TPU v7x, 32 devices: a whole 2x2x4 slice. The times are simulated.
32 devices in a mesh: parts: 2 (over x), ref: 16 (over z, y, core).
Axes of the slice: x: 2, y: 2, z: 4, core: 2. Of those that a mesh axis runs over, the one named last changes fastest.
Arguments:
- queries: float32 [4096, 128], P('parts'), parts along dimension 0, may hold values from -15 to 15, as said below
- references: float32 [65536, 128], P(('parts', 'ref')), parts along dimension 0, may hold values from -15 to 15
- query_ids: int32 [4096], P('parts'), parts along dimension 0, may hold values from 0 to 32767, as said below
- spread: float32 [128], replicated, may hold values from 0.5 to 2
- cotangent: float32 [4096], P('parts'), parts along dimension 0, may hold values from -4 to 4
Outputs:
- query_grad: float32 [4096, 128], P(('parts', 'ref')), parts along dimension 0
- reference_grad: float32 [65536, 128], P(('parts', 'ref')), parts along dimension 0
- spread_grad: float32 [256], P('parts'), parts along dimension 0
There are 2 independent parts, one for each index of `parts`. A program takes and returns all parts, laid end to end along the dimension named above; an argument that names none is the same for every part. Nothing has to cross between parts.
Inputs may be any that keep to these rules, and one draw needn't show every extreme that they name: `query_ids`: distinct rows of the references; query i is the reference row query_ids_i. `queries`: row i equals row query_ids_i of references.
All inputs are finite; a program needn't handle non-finite values.
Results may differ from a plain program's by a relative error of at most 0.014.
Values sent between devices are 32-bit elements; how exact they have to be, the bound alone decides.
No kernel may reach another device: no remote copies, remote signals or barrier semaphores. Data moves between devices by JAX's collectives and lax.ppermute only.
A program may use at most 64 MiB of HBM per device.

v0:
```python
import jax
import jax.numpy as jnp
from jax import lax
from jax.sharding import PartitionSpec as P


def block_score(query_block, id_block, references, rnorm, inv, ref_start):
    cross = lax.dot_general(
        query_block * inv,
        references,
        (((1,), (1,)), ((), ())),
        precision=lax.Precision.HIGHEST,
        preferred_element_type=jnp.float32,
    )
    qnorm = jnp.sum(query_block * query_block * inv, axis=1)
    score = cross - 0.5 * qnorm[:, None] - 0.5 * rnorm[None, :]
    local_ids = id_block - ref_start
    self_mask = local_ids[:, None] == lax.iota(jnp.int32, references.shape[0])[None, :]
    return (jnp.where(self_mask, -jnp.inf, score), self_mask)


def on_device(queries, references, query_ids, spread, cotangent):
    n_query = queries.shape[0]
    n_feat = queries.shape[1]
    n_ref = references.shape[0]
    block_rows = min(512, n_query)
    n_blocks = n_query // block_rows
    inv = 1.0 / (spread * spread)
    rnorm = jnp.sum(references * references * inv, axis=1)
    ref_start = lax.axis_index("ref") * n_ref
    query_blocks = queries.reshape(n_blocks, block_rows, n_feat)
    id_blocks = query_ids.reshape(n_blocks, block_rows)
    weight_blocks = cotangent.reshape(n_blocks, block_rows)

    def local_density(items):
        query_block, id_block = items
        score, self_mask = block_score(query_block, id_block, references, rnorm, inv, ref_start)
        local_peak = jnp.max(score, axis=1)
        local_total = jnp.sum(jnp.exp(score - local_peak[:, None]), axis=1)
        return (local_peak, local_total)

    local_peak, local_total = lax.map(local_density, (query_blocks, id_blocks))
    local_peak = local_peak.reshape(n_query)
    local_total = local_total.reshape(n_query)
    peak = lax.pmax(local_peak, "ref")
    total = lax.psum(local_total * jnp.exp(local_peak - peak), "ref")
    ref_low = references.astype(jnp.bfloat16)
    query_low_blocks = query_blocks.astype(jnp.bfloat16)

    def backward(carry, items):
        pushed, column = carry
        query_block, query_low, id_block, cot_block, peak_block, total_block = items
        score, self_mask = block_score(query_block, id_block, references, rnorm, inv, ref_start)
        weight = jnp.where(
            self_mask,
            0.0,
            cot_block[:, None] * jnp.exp(score - peak_block[:, None]) / total_block[:, None],
        ).astype(jnp.bfloat16)
        pulled = jnp.dot(weight, ref_low, preferred_element_type=jnp.float32)
        pushed = pushed + lax.dot_general(
            weight, query_low, (((0,), (0,)), ((), ())), preferred_element_type=jnp.float32
        )
        column = column + jnp.sum(weight.astype(jnp.float32), axis=0)
        return ((pushed, column), pulled)

    init = (jnp.zeros((n_ref, n_feat), jnp.float32), jnp.zeros((n_ref,), jnp.float32))
    items = (
        query_blocks,
        query_low_blocks,
        id_blocks,
        weight_blocks,
        peak.reshape(n_blocks, block_rows),
        total.reshape(n_blocks, block_rows),
    )
    (pushed, column), pulled = lax.scan(backward, init, items)
    pulled = pulled.reshape(n_query, n_feat)
    reference_grad = (pushed - references * column[:, None]) * inv
    ref_terms = jnp.sum(references * reference_grad, axis=0)
    weight_total = jnp.sum(cotangent)
    own_rows = n_query // lax.axis_size("ref")
    own_start = lax.axis_index("ref") * own_rows
    summed_pull, summed_terms = lax.psum((pulled, ref_terms), "ref")
    every_grad = (summed_pull - queries * cotangent[:, None]) * inv
    summed = jnp.sum(queries * every_grad, axis=0) + summed_terms
    query_grad = lax.dynamic_slice_in_dim(every_grad, own_start, own_rows, 0)
    spread_grad = -summed / spread - weight_total / spread
    return (query_grad, reference_grad, spread_grad)


def solution(mesh):
    placed = (P("parts", None), P(("parts", "ref"), None), P("parts"), P(), P("parts"))
    return jax.shard_map(
        on_device,
        mesh=mesh,
        in_specs=placed,
        out_specs=(P(("parts", "ref"), None), P(("parts", "ref"), None), P("parts")),
        check_vma=False,
    )
```

profile of v0, /device:TPU:0, one launch (start us, length us, event | category | flops | bytes accessed | tf_op | source)
XLA Modules:
  0.0 282.6 jit_solution(32626793319487471)
XLA Ops:
  9.3 1.3 convert_element_type.12
  10.6 1.9 fusion.15
  12.5 30.2 %while.27 = (s32[]{:T(128)}, f32[4,512]{1,0:T(4,128)S(1)}, f32[4,512]{1,0:T(4,128)S(1)}, s32[4,512]{1,0:T(4,128)S(1)}, s32[]{:T(128)}, /*index=5*/f32[4,512,128]...) while((s32[]{:T(128)}, f32[4,512]{1,0:T(4,128)S(1)}, ...), condition=%wide.region_5.6_spmd, body=%wide.region_1.5_spmd.sunk | while | flops 1618216448 | bytes 10015885 | solution.py:42
  13.7 5.6 %fusion.33 = (f32[512]{0:T(512)S(1)}, f32[512,2048]{1,0:T(8,128)S(1)}) fusion(f32[2048]{0:T(1024)S(1)} %broadcast_multiply_fusion.8, f32[512]{0:T(512)S(1)} %broadcast_multiply_fusion.9, f32[2048,128]{1,0:T(8,128)} %get-tuple-element.432, f32[4,512,128]{2,1,0:T(8,128)} %get-tuple-element.430, s32[]{:T(128)S(6)} %copy.16, ...), kind=kOutput, calls=%fused_computation.45.clone.1 | convolution fusion | flops 1615920640 | bytes 5519876 | tf_op jit(solution)/shard_map/while/body/eval_jaxpr/dot_general | solution.py:8
  21.2 5.6 %fusion.33 = (f32[512]{0:T(512)S(1)}, f32[512,2048]{1,0:T(8,128)S(1)}) fusion(f32[2048]{0:T(1024)S(1)} %broadcast_multiply_fusion.8, f32[512]{0:T(512)S(1)} %broadcast_multiply_fusion.9, f32[2048,128]{1,0:T(8,128)} %get-tuple-element.432, f32[4,512,128]{2,1,0:T(8,128)} %get-tuple-element.430, s32[]{:T(128)S(6)} %copy.16, ...), kind=kOutput, calls=%fused_computation.45.clone.1 | convolution fusion | flops 1615920640 | bytes 5519876 | tf_op jit(solution)/shard_map/while/body/eval_jaxpr/dot_general | solution.py:8
  28.8 5.6 %fusion.33 = (f32[512]{0:T(512)S(1)}, f32[512,2048]{1,0:T(8,128)S(1)}) fusion(f32[2048]{0:T(1024)S(1)} %broadcast_multiply_fusion.8, f32[512]{0:T(512)S(1)} %broadcast_multiply_fusion.9, f32[2048,128]{1,0:T(8,128)} %get-tuple-element.432, f32[4,512,128]{2,1,0:T(8,128)} %get-tuple-element.430, s32[]{:T(128)S(6)} %copy.16, ...), kind=kOutput, calls=%fused_computation.45.clone.1 | convolution fusion | flops 1615920640 | bytes 5519876 | tf_op jit(solution)/shard_map/while/body/eval_jaxpr/dot_general | solution.py:8
  36.3 5.6 %fusion.33 = (f32[512]{0:T(512)S(1)}, f32[512,2048]{1,0:T(8,128)S(1)}) fusion(f32[2048]{0:T(1024)S(1)} %broadcast_multiply_fusion.8, f32[512]{0:T(512)S(1)} %broadcast_multiply_fusion.9, f32[2048,128]{1,0:T(8,128)} %get-tuple-element.432, f32[4,512,128]{2,1,0:T(8,128)} %get-tuple-element.430, s32[]{:T(128)S(6)} %copy.16, ...), kind=kOutput, calls=%fused_computation.45.clone.1 | convolution fusion | flops 1615920640 | bytes 5519876 | tf_op jit(solution)/shard_map/while/body/eval_jaxpr/dot_general | solution.py:8
  42.8 35.5 %pmax.7 = f32[2048]{0:T(1024)S(1)} all-reduce(f32[2048]{0:T(1024)S(1)} %bitcast.87), channel_id=1, replica_groups=mesh['parts'=2,'ref'=16] {'ref'}, use_global_device_ids=true, to_apply=%region_6.7 | all-reduce | flops 2048 | bytes 16384 | tf_op jit(solution)/shard_map/pmax | solution.py:45
  78.3 30.2 %psum.21 = f32[4,512]{1,0:T(4,128)S(1)} all-reduce(f32[4,512]{1,0:T(4,128)S(1)} %reshape.78), channel_id=1, replica_groups=mesh['parts'=2,'ref'=16] {'ref'}, use_global_device_ids=true, to_apply=%region_7.8 | all-reduce | flops 2048 | bytes 16384 | tf_op jit(solution)/shard_map/psum | solution.py:46
  108.5 40.9 %while.28 = (s32[]{:T(128)}, f32[2048,128]{1,0:T(8,128)S(1)}, f32[2048]{0:T(1024)S(1)}, f32[4,512,128]{2,1,0:T(8,128)}, s32[4,512]{1,0:T(4,128)S(1)}, /*index=5*...) while((s32[]{:T(128)}, f32[2048,128]{1,0:T(8,128)S(1)}, ...), condition=%wide.region_11.12_spmd.clone, body=%wide.region_8.11_spmd.clone.sunk | while | flops 2159809024 | bytes 10970320 | solution.py:75
  109.7 6.4 %convert_reduce_fusion.2 = (f32[2048]{0:T(1024)S(1)}, bf16[512,2048]{1,0:T(8,128)(2,1)S(1)}) fusion(f32[512]{0:T(512)S(1)} %bitcast.89, f32[512]{0:T(512)S(1)} %bitcast.90, f32[2048]{0:T(1024)S(1)} %broadcast_multiply_fusion.10, f32[512]{0:T(512)S(1)} %broadcast_multiply_fusion.11, f32[2048,128]{1,0:T(8,128)} %get-tuple-element.479, ...), kind=kOutput, calls=%fused_computation.13.clone.1 | convolution fusion | flops 1622210560 | bytes 3435012 | tf_op jit(solution)/shard_map/while/body/eval_jaxpr/dot_general | solution.py:8
  117.3 1.4 fusion.40
  119.9 6.4 %convert_reduce_fusion.2 = (f32[2048]{0:T(1024)S(1)}, bf16[512,2048]{1,0:T(8,128)(2,1)S(1)}) fusion(f32[512]{0:T(512)S(1)} %bitcast.89, f32[512]{0:T(512)S(1)} %bitcast.90, f32[2048]{0:T(1024)S(1)} %broadcast_multiply_fusion.10, f32[512]{0:T(512)S(1)} %broadcast_multiply_fusion.11, f32[2048,128]{1,0:T(8,128)} %get-tuple-element.479, ...), kind=kOutput, calls=%fused_computation.13.clone.1 | convolution fusion | flops 1622210560 | bytes 3435012 | tf_op jit(solution)/shard_map/while/body/eval_jaxpr/dot_general | solution.py:8
  127.5 1.4 fusion.40
  130.1 6.4 %convert_reduce_fusion.2 = (f32[2048]{0:T(1024)S(1)}, bf16[512,2048]{1,0:T(8,128)(2,1)S(1)}) fusion(f32[512]{0:T(512)S(1)} %bitcast.89, f32[512]{0:T(512)S(1)} %bitcast.90, f32[2048]{0:T(1024)S(1)} %broadcast_multiply_fusion.10, f32[512]{0:T(512)S(1)} %broadcast_multiply_fusion.11, f32[2048,128]{1,0:T(8,128)} %get-tuple-element.479, ...), kind=kOutput, calls=%fused_computation.13.clone.1 | convolution fusion | flops 1622210560 | bytes 3435012 | tf_op jit(solution)/shard_map/while/body/eval_jaxpr/dot_general | solution.py:8
  136.5 1.2 convolution_add_fusion.2
  137.7 1.4 fusion.40
  140.3 6.4 %convert_reduce_fusion.2 = (f32[2048]{0:T(1024)S(1)}, bf16[512,2048]{1,0:T(8,128)(2,1)S(1)}) fusion(f32[512]{0:T(512)S(1)} %bitcast.89, f32[512]{0:T(512)S(1)} %bitcast.90, f32[2048]{0:T(1024)S(1)} %broadcast_multiply_fusion.10, f32[512]{0:T(512)S(1)} %broadcast_multiply_fusion.11, f32[2048,128]{1,0:T(8,128)} %get-tuple-element.479, ...), kind=kOutput, calls=%fused_computation.13.clone.1 | convolution fusion | flops 1622210560 | bytes 3435012 | tf_op jit(solution)/shard_map/while/body/eval_jaxpr/dot_general | solution.py:8
  146.7 1.2 convolution_add_fusion.2
  147.9 1.4 fusion.40
  150.0 90.4 %all-reduce.2.cloned.1.call-done = f32[2048,128]{1,0:T(8,128)} async-done(((f32[2048,128]{1,0:T(8,128)}), f32[2048,128]{1,0:T(8,128)}) %all-reduce.2.cloned.1.call-update) | async-done | bytes 1048592 | tf_op jit(solution)/shard_map/psum | solution.py:82
  240.5 3.0 %multiply_reduce_fusion = (f32[128]{0:T(128)S(1)}, f32[2048,128]{1,0:T(8,128)}, f32[128]{0:T(128)S(1)}, f32[2048,128]{1,0:T(8,128)S(1)}) fusion(f32[2048,128]{1,0:T(8,128)} %get-tuple-element.491, f32[128]{0:T(128)S(1)} %get-tuple-element.498, f32[2048,128]{1,0:T(8,128)S(1)} %get-tuple-element.133, f32[2048]{0:T(1024)S(1)} %get-tuple-element.134, ...), kind=kLoop, calls=%fused_computation.36 | loop fusion | flops 2621184 | bytes 6309376 | tf_op jit(solution)/shard_map/reduce_sum | solution.py:78
  243.5 30.4 %psum.23 = f32[128]{0:T(128)S(1)} all-reduce(f32[128]{0:T(128)S(1)} %get-tuple-element.231), channel_id=1, replica_groups=mesh['parts'=2,'ref'=16] {'ref'}, use_global_device_ids=true, to_apply=%region_15.16 | all-reduce | flops 128 | bytes 1024 | tf_op jit(solution)/shard_map/psum | solution.py:82
  274.5 1.2 divide_subtract_fusion
  (79 shorter events, 18.2 us)
Async XLA Ops:
  7.2 233.3 %all-reduce.2.cloned.1.call-start = ((), (), s32[]{:S(2)}) async-start(), calls=%async_computation | async-start | bytes 2097152 | tf_op jit(solution)/shard_map/psum | solution.py:82
  108.5 40.9 %copy-start = (f32[2048]{0:T(1024)S(1)}, f32[2048]{0:T(1024)}, u32[]{:S(2)}) copy-start(f32[2048]{0:T(1024)} %param.13) | copy-start | bytes 24580
  149.3 125.2 %copy-start.1 = (f32[128]{0:T(128)S(1)}, f32[128]{0:T(128)}, u32[]{:S(2)}) copy-start(f32[128]{0:T(128)} %param.12) | copy-start | bytes 1540
Sparse Core Ops, SparseCore 0:
  149.5 90.9 all-reduce.1
where the time goes:
time: 283 us
  blocking collectives  96.1 us (34%)
  waiting for transfers between devices  90.5 us (32%)
  matrix products  58.4 us (21%)
  other arithmetic  20.5 us (7%)
  between operations  14.2 us (5%)
    psum x1, waiting for transfers between devices, on_device(): summed_pull, summed_terms = lax.psum((pulled, ref_terms), 'ref')  90.4 us
    dot_general x8, matrix products, block_score(): lax.dot_general(query_block * inv, references, (((1,), (1,)), ((), ())),...  47.9 us
    pmax x1, blocking collectives, on_device(): peak = lax.pmax(local_peak, 'ref')  35.5 us
    psum x1, blocking collectives, on_device(): summed_pull, summed_terms = lax.psum((pulled, ref_terms), 'ref')  30.4 us
    psum x1, blocking collectives, on_device(): total = lax.psum(local_total * jnp.exp(local_peak - peak), 'ref')  30.2 us
    reduce_sum x8, other arithmetic, block_score(): qnorm = jnp.sum(query_block * query_block * inv, axis=1)  8.81 us
    dot_general x4, matrix products, backward(): pulled = jnp.dot(weight, ref_low, preferred_element_type=jnp.float32)  5.7 us
  transfers between devices with their start and end apart: 1, of which 1 were waited for; matrix products, arithmetic and copies ran while one was open for 0% of the time, Pallas kernels for 0%

commit v1 on v0

--- a/solution.py
+++ b/solution.py
@@ -19,10 +19,44 @@
     return (jnp.where(self_mask, -jnp.inf, score), self_mask)
 
 
+def exchange(x, n_dev, step):
+    return lax.ppermute(x, "ref", [(i, i ^ step) for i in range(n_dev)])
+
+
+def butterfly_stats(peak, total, n_dev):
+    step = 1
+    while step < n_dev:
+        other_peak, other_total = exchange((peak, total), n_dev, step)
+        new_peak = jnp.maximum(peak, other_peak)
+        total = total * jnp.exp(peak - new_peak) + other_total * jnp.exp(other_peak - new_peak)
+        peak = new_peak
+        step *= 2
+    return peak, total
+
+
+def halving_scatter(rows, extra, n_dev):
+    me = lax.axis_index("ref")
+    n_feat = rows.shape[-1]
+    blocks = rows.reshape(n_dev, -1, n_feat)
+    step = 1
+    while step < n_dev:
+        lead = n_dev // (2 * step)
+        split = blocks.reshape(lead, 2, -1, n_feat)
+        bit = (me // step) % 2
+        keep = lax.dynamic_index_in_dim(split, bit, axis=1, keepdims=False)
+        send = lax.dynamic_index_in_dim(split, 1 - bit, axis=1, keepdims=False)
+        got, got_extra = exchange((send, extra), n_dev, step)
+        blocks = keep + got
+        extra = extra + got_extra
+        step *= 2
+    return blocks.reshape(-1, n_feat), extra
+
+
 def on_device(queries, references, query_ids, spread, cotangent):
     n_query = queries.shape[0]
     n_feat = queries.shape[1]
     n_ref = references.shape[0]
+    n_dev = lax.axis_size("ref")
     block_rows = min(512, n_query)
     n_blocks = n_query // block_rows
     inv = 1.0 / (spread * spread)
@@ -40,10 +74,7 @@
         return (local_peak, local_total)
 
     local_peak, local_total = lax.map(local_density, (query_blocks, id_blocks))
-    local_peak = local_peak.reshape(n_query)
-    local_total = local_total.reshape(n_query)
-    peak = lax.pmax(local_peak, "ref")
-    total = lax.psum(local_total * jnp.exp(local_peak - peak), "ref")
+    peak, total = butterfly_stats(local_peak.reshape(n_query), local_total.reshape(n_query), n_dev)
     ref_low = references.astype(jnp.bfloat16)
     query_low_blocks = query_blocks.astype(jnp.bfloat16)
 
@@ -75,14 +106,16 @@
     (pushed, column), pulled = lax.scan(backward, init, items)
     pulled = pulled.reshape(n_query, n_feat)
     reference_grad = (pushed - references * column[:, None]) * inv
-    ref_terms = jnp.sum(references * reference_grad, axis=0)
+    local_terms = jnp.stack([jnp.sum(queries * pulled, axis=0), jnp.sum(references * reference_grad, axis=0)])
+    own_pulled, summed_terms = halving_scatter(pulled, local_terms, n_dev)
+    own_rows = n_query // n_dev
+    own_start = lax.axis_index("ref") * own_rows
+    own_queries = lax.dynamic_slice_in_dim(queries, own_start, own_rows, 0)
+    own_cot = lax.dynamic_slice_in_dim(cotangent, own_start, own_rows, 0)
+    query_grad = (own_pulled - own_queries * own_cot[:, None]) * inv
+    self_terms = jnp.sum(queries * queries * cotangent[:, None], axis=0)
+    summed = (summed_terms[0] - self_terms) * inv + summed_terms[1]
     weight_total = jnp.sum(cotangent)
-    own_rows = n_query // lax.axis_size("ref")
-    own_start = lax.axis_index("ref") * own_rows
-    summed_pull, summed_terms = lax.psum((pulled, ref_terms), "ref")
-    every_grad = (summed_pull - queries * cotangent[:, None]) * inv
-    summed = jnp.sum(queries * every_grad, axis=0) + summed_terms
-    query_grad = lax.dynamic_slice_in_dim(every_grad, own_start, own_rows, 0)
     spread_grad = -summed / spread - weight_total / spread
     return (query_grad, reference_grad, spread_grad)
 

time: 283 us -> 124 us (0.44)
  blocking collectives: 96.1 us -> 0 us
  waiting for transfers between devices: 90.5 us -> 27.8 us
  starting transfers between devices: 0.04 us -> 13.8 us
  between operations: 14.2 us -> 0.9 us
  other arithmetic: 20.5 us -> 23.5 us
  matrix products: 58.4 us -> 55.5 us
    psum x1 -> x0, waiting for transfers between devices: 90.4 us -> none  [on_device(): summed_pull, summed_terms = lax.psum((pulled, ref_terms), 'ref')]
    psum x2 -> x0, blocking collectives: 60.6 us -> none  [the longest x1 30.4 us: on_device(): summed_pull, summed_terms = lax.psum((pulled, ref_terms), 'ref')]
    pmax x1 -> x0, blocking collectives: 35.5 us -> none  [on_device(): peak = lax.pmax(local_peak, 'ref')]
    ppermute x0 -> x16, waiting for transfers between devices: none -> 27.8 us  [exchange(): return lax.ppermute(x, 'ref', [(i, i ^ step) for i in range(n_dev)])]
    ppermute x0 -> x16, starting transfers between devices: none -> 13.8 us  [exchange(): return lax.ppermute(x, 'ref', [(i, i ^ step) for i in range(n_dev)])]
    dot_general x4, matrix products: 5.7 us -> 2.86 us  [backward(): pulled = jnp.dot(weight, ref_low, preferred_element_type=jnp.float32)]
  transfers between devices with their start and end apart: 1 -> 16, of which waited for: 1 -> 13; matrix products, arithmetic and copies ran while one was open for 0% -> 6% of each run, Pallas kernels for 0% -> 0%
where the time goes in v1:
time: 124 us
  matrix products  55.5 us (45%)
  waiting for transfers between devices  27.8 us (22%)
  other arithmetic  23.5 us (19%)
  starting transfers between devices  13.8 us (11%)
  local copies, waits for them, and re-layouts  1.4 us (1%)
    dot_general x8, matrix products, block_score(): lax.dot_general(query_block * inv, references, (((1,), (1,)), ((), ())),...  47.9 us
    ppermute x16, waiting for transfers between devices, exchange(): return lax.ppermute(x, 'ref', [(i, i ^ step) for i in range(n_dev)])  27.8 us
    ppermute x16, starting transfers between devices, exchange(): return lax.ppermute(x, 'ref', [(i, i ^ step) for i in range(n_dev)])  13.8 us
    reduce_sum x8, other arithmetic, block_score(): qnorm = jnp.sum(query_block * query_block * inv, axis=1)  8.81 us
    dot_general x4, matrix products, backward(): lax.dot_general(weight, query_low, (((0,), (0,)), ((), ())), preferred_el...  4.74 us
    dot_general x4, matrix products, backward(): pulled = jnp.dot(weight, ref_low, preferred_element_type=jnp.float32)  2.86 us
    reduce_sum x4, other arithmetic, local_density(): local_total = jnp.sum(jnp.exp(score - local_peak[:, None]), axis=1)  2.84 us
    reduce_sum x1, other arithmetic, on_device(): jnp.sum(references * reference_grad, axis=0)  2.54 us
  transfers between devices with their start and end apart: 16, of which 13 were waited for; matrix products, arithmetic and copies ran while one was open for 6% of the time, Pallas kernels for 0%

profile of v1, /device:TPU:0, one launch (start us, length us, event | category | flops | bytes accessed | tf_op | source)
XLA Modules:
  0.0 123.6 jit_solution(16438219430975874433)
XLA Ops:
  2.0 2.0 %fusion.21 = (bf16[2048,128]{1,0:T(8,128)(2,1)S(1)}, f32[2048]{0:T(1024)S(1)}) fusion(f32[2048,128]{1,0:T(8,128)} %param.10, f32[128]{0:T(128)S(1)} %multiply_divide_fusion), kind=kLoop, calls=%fused_computation.65 | loop fusion | flops 1046528 | bytes 1581568 | tf_op jit(solution)/shard_map/convert_element_type | solution.py:78
  4.0 30.2 %while.27 = (s32[]{:T(128)}, f32[4,512]{1,0:T(4,128)S(1)}, f32[4,512]{1,0:T(4,128)S(1)}, s32[4,512]{1,0:T(4,128)S(1)}, s32[]{:T(128)}, /*index=5*/f32[4,512,128]...) while((s32[]{:T(128)}, f32[4,512]{1,0:T(4,128)S(1)}, ...), condition=%wide.region_5.6_spmd, body=%wide.region_1.5_spmd.sunk | while | flops 1618216448 | bytes 10015885 | solution.py:76
  5.2 5.6 %fusion.40 = (f32[512]{0:T(512)S(1)}, f32[512,2048]{1,0:T(8,128)S(1)}) fusion(f32[2048]{0:T(1024)S(1)} %broadcast_multiply_fusion.8, f32[512]{0:T(512)S(1)} %broadcast_multiply_fusion.9, f32[2048,128]{1,0:T(8,128)} %get-tuple-element.438, f32[4,512,128]{2,1,0:T(8,128)} %get-tuple-element.436, s32[]{:T(128)S(6)} %copy.20, ...), kind=kOutput, calls=%fused_computation.64.clone.1 | convolution fusion | flops 1615920640 | bytes 5519876 | tf_op jit(solution)/shard_map/while/body/eval_jaxpr/dot_general | solution.py:8
  12.7 5.6 %fusion.40 = (f32[512]{0:T(512)S(1)}, f32[512,2048]{1,0:T(8,128)S(1)}) fusion(f32[2048]{0:T(1024)S(1)} %broadcast_multiply_fusion.8, f32[512]{0:T(512)S(1)} %broadcast_multiply_fusion.9, f32[2048,128]{1,0:T(8,128)} %get-tuple-element.438, f32[4,512,128]{2,1,0:T(8,128)} %get-tuple-element.436, s32[]{:T(128)S(6)} %copy.20, ...), kind=kOutput, calls=%fused_computation.64.clone.1 | convolution fusion | flops 1615920640 | bytes 5519876 | tf_op jit(solution)/shard_map/while/body/eval_jaxpr/dot_general | solution.py:8
  20.3 5.6 %fusion.40 = (f32[512]{0:T(512)S(1)}, f32[512,2048]{1,0:T(8,128)S(1)}) fusion(f32[2048]{0:T(1024)S(1)} %broadcast_multiply_fusion.8, f32[512]{0:T(512)S(1)} %broadcast_multiply_fusion.9, f32[2048,128]{1,0:T(8,128)} %get-tuple-element.438, f32[4,512,128]{2,1,0:T(8,128)} %get-tuple-element.436, s32[]{:T(128)S(6)} %copy.20, ...), kind=kOutput, calls=%fused_computation.64.clone.1 | convolution fusion | flops 1615920640 | bytes 5519876 | tf_op jit(solution)/shard_map/while/body/eval_jaxpr/dot_general | solution.py:8
  27.8 5.6 %fusion.40 = (f32[512]{0:T(512)S(1)}, f32[512,2048]{1,0:T(8,128)S(1)}) fusion(f32[2048]{0:T(1024)S(1)} %broadcast_multiply_fusion.8, f32[512]{0:T(512)S(1)} %broadcast_multiply_fusion.9, f32[2048,128]{1,0:T(8,128)} %get-tuple-element.438, f32[4,512,128]{2,1,0:T(8,128)} %get-tuple-element.436, s32[]{:T(128)S(6)} %copy.20, ...), kind=kOutput, calls=%fused_computation.64.clone.1 | convolution fusion | flops 1615920640 | bytes 5519876 | tf_op jit(solution)/shard_map/while/body/eval_jaxpr/dot_general | solution.py:8
  36.0 2.7 %collective-permute-start.5 = (f32[2048]{0:T(1024)S(1)}, f32[2048]{0:T(1024)S(1)}, u32[]{:S(2)}, u32[]{:S(2)}) collective-permute-start(f32[2048]{0:T(1024)S(1)} %get-tuple-element.241), channel_id=1, source_target_pairs={{0,2},{1,3},{2,0},{3,1},{4,6},{5,7},{6,4},{7,5},{8,10},{9,11},{10,... | collective-permute-start | bytes 24584 | tf_op jit(solution)/shard_map/ppermute | solution.py:23
  40.4 2.0 %collective-permute-done.1 = f32[2048]{0:T(1024)S(1)} collective-permute-done((f32[2048]{0:T(1024)S(1)}, f32[2048]{0:T(1024)S(1)}, u32[]{:S(2)}, u32[]{:S(2)}) %collective-permute-start.1) | collective-permute-done | bytes 8224 | tf_op jit(solution)/shard_map/ppermute | solution.py:23
  42.4 1.6 %collective-permute-start.6 = (f32[2048]{0:T(1024)S(1)}, f32[2048]{0:T(1024)S(1)}, u32[]{:S(2)}, u32[]{:S(2)}) collective-permute-start(f32[2048]{0:T(1024)S(1)} %get-tuple-element.239), channel_id=1, source_target_pairs={{0,4},{1,5},{2,6},{3,7},{4,0},{5,1},{6,2},{7,3},{8,12},{9,13},{10,... | collective-permute-start | bytes 24584 | tf_op jit(solution)/shard_map/ppermute | solution.py:23
  44.5 1.6 %collective-permute-done.6 = f32[2048]{0:T(1024)S(1)} collective-permute-done((f32[2048]{0:T(1024)S(1)}, f32[2048]{0:T(1024)S(1)}, u32[]{:S(2)}, u32[]{:S(2)}) %collective-permute-start.6) | collective-permute-done | bytes 8224 | tf_op jit(solution)/shard_map/ppermute | solution.py:23
  47.7 2.7 %collective-permute-start.7 = (f32[2048]{0:T(1024)S(1)}, f32[2048]{0:T(1024)S(1)}, u32[]{:S(2)}, u32[]{:S(2)}) collective-permute-start(f32[2048]{0:T(1024)S(1)} %get-tuple-element.237), channel_id=1, source_target_pairs={{0,8},{1,9},{2,10},{3,11},{4,12},{5,13},{6,14},{7,15},{8,0},{9,1},... | collective-permute-start | bytes 24584 | tf_op jit(solution)/shard_map/ppermute | solution.py:23
  52.3 2.6 %collective-permute-done.3 = f32[2048]{0:T(1024)S(1)} collective-permute-done((f32[2048]{0:T(1024)S(1)}, f32[2048]{0:T(1024)S(1)}, u32[]{:S(2)}, u32[]{:S(2)}) %collective-permute-start.3) | collective-permute-done | bytes 8224 | tf_op jit(solution)/shard_map/ppermute | solution.py:23
  54.9 38.3 %while.28 = (s32[]{:T(128)}, f32[2048,128]{1,0:T(8,128)S(1)}, f32[2048]{0:T(1024)S(1)}, f32[4,512,128]{2,1,0:T(8,128)S(1)}, s32[4,512]{1,0:T(4,128)S(1)}, /*inde...) while((s32[]{:T(128)}, f32[2048,128]{1,0:T(8,128)S(1)}, ...), condition=%wide.region_9.10_spmd.clone, body=%wide.region_6.9_spmd.clone.sunk | while | flops 2159809024 | bytes 10970320 | solution.py:106
  56.3 6.4 %convert_reduce_fusion.2 = (f32[2048]{0:T(1024)S(1)}, bf16[512,2048]{1,0:T(8,128)(2,1)S(1)}) fusion(f32[512]{0:T(512)S(1)} %bitcast.134, f32[512]{0:T(512)S(1)} %bitcast.135, f32[2048]{0:T(1024)S(1)} %broadcast_multiply_fusion.10, f32[512]{0:T(512)S(1)} %broadcast_multiply_fusion.11, f32[2048,128]{1,0:T(8,128)} %get-tuple-element.485, ...), kind=kOutput, calls=%fused_computation.13.clone.1 | convolution fusion | flops 1622210560 | bytes 3435012 | tf_op jit(solution)/shard_map/while/body/eval_jaxpr/dot_general | solution.py:8
  65.9 6.4 %convert_reduce_fusion.2 = (f32[2048]{0:T(1024)S(1)}, bf16[512,2048]{1,0:T(8,128)(2,1)S(1)}) fusion(f32[512]{0:T(512)S(1)} %bitcast.134, f32[512]{0:T(512)S(1)} %bitcast.135, f32[2048]{0:T(1024)S(1)} %broadcast_multiply_fusion.10, f32[512]{0:T(512)S(1)} %broadcast_multiply_fusion.11, f32[2048,128]{1,0:T(8,128)} %get-tuple-element.485, ...), kind=kOutput, calls=%fused_computation.13.clone.1 | convolution fusion | flops 1622210560 | bytes 3435012 | tf_op jit(solution)/shard_map/while/body/eval_jaxpr/dot_general | solution.py:8
  75.4 6.4 %convert_reduce_fusion.2 = (f32[2048]{0:T(1024)S(1)}, bf16[512,2048]{1,0:T(8,128)(2,1)S(1)}) fusion(f32[512]{0:T(512)S(1)} %bitcast.134, f32[512]{0:T(512)S(1)} %bitcast.135, f32[2048]{0:T(1024)S(1)} %broadcast_multiply_fusion.10, f32[512]{0:T(512)S(1)} %broadcast_multiply_fusion.11, f32[2048,128]{1,0:T(8,128)} %get-tuple-element.485, ...), kind=kOutput, calls=%fused_computation.13.clone.1 | convolution fusion | flops 1622210560 | bytes 3435012 | tf_op jit(solution)/shard_map/while/body/eval_jaxpr/dot_general | solution.py:8
  84.9 6.4 %convert_reduce_fusion.2 = (f32[2048]{0:T(1024)S(1)}, bf16[512,2048]{1,0:T(8,128)(2,1)S(1)}) fusion(f32[512]{0:T(512)S(1)} %bitcast.134, f32[512]{0:T(512)S(1)} %bitcast.135, f32[2048]{0:T(1024)S(1)} %broadcast_multiply_fusion.10, f32[512]{0:T(512)S(1)} %broadcast_multiply_fusion.11, f32[2048,128]{1,0:T(8,128)} %get-tuple-element.485, ...), kind=kOutput, calls=%fused_computation.13.clone.1 | convolution fusion | flops 1622210560 | bytes 3435012 | tf_op jit(solution)/shard_map/while/body/eval_jaxpr/dot_general | solution.py:8
  93.5 1.6 %fusion.14 = (f32[128]{0:T(128)S(1)}, f32[128]{0:T(128)S(1)}) fusion(f32[2048,128]{1,0:T(8,128)} %bitcast.124, f32[4,512,128]{2,1,0:T(8,128)S(1)} %get-tuple-element.132, f32[2048]{0:T(1024)S(1)} %copy-done), kind=kLoop, calls=%fused_computation.37 | loop fusion | flops 1310464 | bytes 2106368 | tf_op jit(solution)/shard_map/reduce_sum | solution.py:109
  95.1 2.5 %multiply_reduce_fusion.1 = (f32[128]{0:T(128)S(1)}, f32[2048,128]{1,0:T(8,128)}) fusion(f32[2048,128]{1,0:T(8,128)} %get-tuple-element.496, f32[128]{0:T(128)S(1)} %get-tuple-element.506, f32[2048,128]{1,0:T(8,128)S(1)} %get-tuple-element.133, f32[2048]{0:T(1024)S(1)} %get-tuple-element.134), kind=kLoop, calls=%fused_computation.39 | loop fusion | flops 1310592 | bytes 3154944 | tf_op jit(solution)/shard_map/reduce_sum | solution.py:109
  101.1 5.4 %collective-permute-done.9 = f32[4,128,128]{2,1,0:T(8,128)S(1)} collective-permute-done((f32[4,128,128]{2,1,0:T(8,128)S(1)}, f32[4,128,128]{2,1,0:T(8,128)S(1)}, u32[]{:S(2)}, u32[]{:S(2)}) %collective-permute-start.9) | collective-permute-done | bytes 262176 | tf_op jit(solution)/shard_map/ppermute | solution.py:23
  107.0 1.7 %collective-permute-start.14 = (f32[2,128]{1,0:T(2,128)S(1)}, f32[2,128]{1,0:T(2,128)S(1)}, u32[]{:S(2)}, u32[]{:S(2)}) collective-permute-start(f32[2,128]{1,0:T(2,128)S(1)} %fusion.27), channel_id=1, source_target_pairs={{0,4},{1,5},{2,6},{3,7},{4,0},{5,1},{6,2},{7,3},{8,12},{9,13},{10,... | collective-permute-start | bytes 3080 | tf_op jit(solution)/shard_map/ppermute | solution.py:23
  108.7 2.9 %collective-permute-done.14 = f32[2,128]{1,0:T(2,128)S(1)} collective-permute-done((f32[2,128]{1,0:T(2,128)S(1)}, f32[2,128]{1,0:T(2,128)S(1)}, u32[]{:S(2)}, u32[]{:S(2)}) %collective-permute-start.14) | collective-permute-done | bytes 1056 | tf_op jit(solution)/shard_map/ppermute | solution.py:23
  112.6 3.5 %collective-permute-done.15 = f32[2,128]{1,0:T(2,128)S(1)} collective-permute-done((f32[2,128]{1,0:T(2,128)S(1)}, f32[2,128]{1,0:T(2,128)S(1)}, u32[]{:S(2)}, u32[]{:S(2)}) %collective-permute-start.15) | collective-permute-done | bytes 1056 | tf_op jit(solution)/shard_map/ppermute | solution.py:23
  117.7 4.4 %collective-permute-done.11 = f32[1,128,128]{2,1,0:T(8,128)S(1)} collective-permute-done((f32[1,128,128]{2,1,0:T(8,128)S(1)}, f32[1,128,128]{2,1,0:T(8,128)S(1)}, u32[]{:S(2)}, u32[]{:S(2)}) %collective-permute-start.11) | collective-permute-done | bytes 65568 | tf_op jit(solution)/shard_map/ppermute | solution.py:23
  (122 shorter events, 36.9 us)
Async XLA Ops:
  4.0 48.0 %copy-start = (f32[2048]{0:T(1024)S(1)}, f32[2048]{0:T(1024)}, u32[]{:S(2)}) copy-start(f32[2048]{0:T(1024)} %param.13) | copy-start | bytes 24580
  34.2 1.4 %collective-permute-start = (f32[2048]{0:T(1024)S(1)}, f32[2048]{0:T(1024)S(1)}, u32[]{:S(2)}, u32[]{:S(2)}) collective-permute-start(f32[2048]{0:T(1024)S(1)} %bitcast.139), channel_id=1, source_target_pairs={{0,1},{1,0},{2,3},{3,2},{4,5},{5,4},{6,7},{7,6},{8,9},{9,8},{10,11... | collective-permute-start | bytes 24584 | tf_op jit(solution)/shard_map/ppermute | solution.py:23
  34.8 1.2 collective-permute-start.4
  36.0 4.4 %collective-permute-start.5 = (f32[2048]{0:T(1024)S(1)}, f32[2048]{0:T(1024)S(1)}, u32[]{:S(2)}, u32[]{:S(2)}) collective-permute-start(f32[2048]{0:T(1024)S(1)} %get-tuple-element.241), channel_id=1, source_target_pairs={{0,2},{1,3},{2,0},{3,1},{4,6},{5,7},{6,4},{7,5},{8,10},{9,11},{10,... | collective-permute-start | bytes 24584 | tf_op jit(solution)/shard_map/ppermute | solution.py:23
  38.7 3.7 %collective-permute-start.1 = (f32[2048]{0:T(1024)S(1)}, f32[2048]{0:T(1024)S(1)}, u32[]{:S(2)}, u32[]{:S(2)}) collective-permute-start(f32[2048]{0:T(1024)S(1)} %get-tuple-element.242), channel_id=1, source_target_pairs={{0,2},{1,3},{2,0},{3,1},{4,6},{5,7},{6,4},{7,5},{8,10},{9,11},{10,... | collective-permute-start | bytes 24584 | tf_op jit(solution)/shard_map/ppermute | solution.py:23
  42.4 3.7 %collective-permute-start.6 = (f32[2048]{0:T(1024)S(1)}, f32[2048]{0:T(1024)S(1)}, u32[]{:S(2)}, u32[]{:S(2)}) collective-permute-start(f32[2048]{0:T(1024)S(1)} %get-tuple-element.239), channel_id=1, source_target_pairs={{0,4},{1,5},{2,6},{3,7},{4,0},{5,1},{6,2},{7,3},{8,12},{9,13},{10,... | collective-permute-start | bytes 24584 | tf_op jit(solution)/shard_map/ppermute | solution.py:23
  44.0 3.7 %collective-permute-start.2 = (f32[2048]{0:T(1024)S(1)}, f32[2048]{0:T(1024)S(1)}, u32[]{:S(2)}, u32[]{:S(2)}) collective-permute-start(f32[2048]{0:T(1024)S(1)} %get-tuple-element.240), channel_id=1, source_target_pairs={{0,4},{1,5},{2,6},{3,7},{4,0},{5,1},{6,2},{7,3},{8,12},{9,13},{10,... | collective-permute-start | bytes 24584 | tf_op jit(solution)/shard_map/ppermute | solution.py:23
  47.7 4.6 %collective-permute-start.7 = (f32[2048]{0:T(1024)S(1)}, f32[2048]{0:T(1024)S(1)}, u32[]{:S(2)}, u32[]{:S(2)}) collective-permute-start(f32[2048]{0:T(1024)S(1)} %get-tuple-element.237), channel_id=1, source_target_pairs={{0,8},{1,9},{2,10},{3,11},{4,12},{5,13},{6,14},{7,15},{8,0},{9,1},... | collective-permute-start | bytes 24584 | tf_op jit(solution)/shard_map/ppermute | solution.py:23
  50.4 4.5 %collective-permute-start.3 = (f32[2048]{0:T(1024)S(1)}, f32[2048]{0:T(1024)S(1)}, u32[]{:S(2)}, u32[]{:S(2)}) collective-permute-start(f32[2048]{0:T(1024)S(1)} %get-tuple-element.238), channel_id=1, source_target_pairs={{0,8},{1,9},{2,10},{3,11},{4,12},{5,13},{6,14},{7,15},{8,0},{9,1},... | collective-permute-start | bytes 24584 | tf_op jit(solution)/shard_map/ppermute | solution.py:23
  93.3 4.3 %collective-permute-start.8 = (f32[8,128,128]{2,1,0:T(8,128)S(1)}, f32[8,128,128]{2,1,0:T(8,128)S(1)}, u32[]{:S(2)}, u32[]{:S(2)}) collective-permute-start(f32[8,128,128]{2,1,0:T(8,128)S(1)} %dynamic-slice_bitcast_fusion), channel_id=1, source_target_pairs={{0,1},{1,0},{2,3},{3,2},{4,5},{5,4},{6,7},{7,6},{8,9},{9,8},{10,11... | collective-permute-start | bytes 1572872 | tf_op jit(solution)/shard_map/ppermute | solution.py:23
  93.4 23.1 %copy-start.1 = (f32[128]{0:T(128)S(1)}, f32[128]{0:T(128)}, u32[]{:S(2)}) copy-start(f32[128]{0:T(128)} %param.12) | copy-start | bytes 1540
  97.7 8.7 %collective-permute-start.9 = (f32[4,128,128]{2,1,0:T(8,128)S(1)}, f32[4,128,128]{2,1,0:T(8,128)S(1)}, u32[]{:S(2)}, u32[]{:S(2)}) collective-permute-start(f32[4,128,128]{2,1,0:T(8,128)S(1)} %dynamic-slice_bitcast_fusion.1), channel_id=1, source_target_pairs={{0,2},{1,3},{2,0},{3,1},{4,6},{5,7},{6,4},{7,5},{8,10},{9,11},{10,... | collective-permute-start | bytes 786440 | tf_op jit(solution)/shard_map/ppermute | solution.py:23
  98.3 1.2 collective-permute-start.12
  99.5 7.5 %collective-permute-start.13 = (f32[2,128]{1,0:T(2,128)S(1)}, f32[2,128]{1,0:T(2,128)S(1)}, u32[]{:S(2)}, u32[]{:S(2)}) collective-permute-start(f32[2,128]{1,0:T(2,128)S(1)} %fusion.19), channel_id=1, source_target_pairs={{0,2},{1,3},{2,0},{3,1},{4,6},{5,7},{6,4},{7,5},{8,10},{9,11},{10,... | collective-permute-start | bytes 3080 | tf_op jit(solution)/shard_map/ppermute | solution.py:23
  106.5 9.6 %collective-permute-start.10 = (f32[2,128,128]{2,1,0:T(8,128)S(1)}, f32[2,128,128]{2,1,0:T(8,128)S(1)}, u32[]{:S(2)}, u32[]{:S(2)}) collective-permute-start(f32[2,128,128]{2,1,0:T(8,128)S(1)} %dynamic-slice_bitcast_fusion.2), channel_id=1, source_target_pairs={{0,4},{1,5},{2,6},{3,7},{4,0},{5,1},{6,2},{7,3},{8,12},{9,13},{10,... | collective-permute-start | bytes 393224 | tf_op jit(solution)/shard_map/ppermute | solution.py:23
  107.0 4.6 %collective-permute-start.14 = (f32[2,128]{1,0:T(2,128)S(1)}, f32[2,128]{1,0:T(2,128)S(1)}, u32[]{:S(2)}, u32[]{:S(2)}) collective-permute-start(f32[2,128]{1,0:T(2,128)S(1)} %fusion.27), channel_id=1, source_target_pairs={{0,4},{1,5},{2,6},{3,7},{4,0},{5,1},{6,2},{7,3},{8,12},{9,13},{10,... | collective-permute-start | bytes 3080 | tf_op jit(solution)/shard_map/ppermute | solution.py:23
  111.6 4.5 %collective-permute-start.15 = (f32[2,128]{1,0:T(2,128)S(1)}, f32[2,128]{1,0:T(2,128)S(1)}, u32[]{:S(2)}, u32[]{:S(2)}) collective-permute-start(f32[2,128]{1,0:T(2,128)S(1)} %add.127), channel_id=1, source_target_pairs={{0,8},{1,9},{2,10},{3,11},{4,12},{5,13},{6,14},{7,15},{8,0},{9,1},... | collective-permute-start | bytes 3080 | tf_op jit(solution)/shard_map/ppermute | solution.py:23
  116.1 5.9 %collective-permute-start.11 = (f32[1,128,128]{2,1,0:T(8,128)S(1)}, f32[1,128,128]{2,1,0:T(8,128)S(1)}, u32[]{:S(2)}, u32[]{:S(2)}) collective-permute-start(f32[1,128,128]{2,1,0:T(8,128)S(1)} %constant_dynamic-slice_fusion.3), channel_id=1, source_target_pairs={{0,8},{1,9},{2,10},{3,11},{4,12},{5,13},{6,14},{7,15},{8,0},{9,1},... | collective-permute-start | bytes 196616 | tf_op jit(solution)/shard_map/ppermute | solution.py:23

commit v2 on v1

v2 whole, which is shorter than its diff:
```python
import jax
import jax.numpy as jnp
from jax import lax
from jax.sharding import PartitionSpec as P


def block_score(query_block, id_block, references, rnorm, inv, ref_start):
    cross = lax.dot_general(
        query_block * inv,
        references,
        (((1,), (1,)), ((), ())),
        precision=lax.Precision.HIGHEST,
        preferred_element_type=jnp.float32,
    )
    qnorm = jnp.sum(query_block * query_block * inv, axis=1)
    score = cross - 0.5 * qnorm[:, None] - 0.5 * rnorm[None, :]
    local_ids = id_block - ref_start
    self_mask = local_ids[:, None] == lax.iota(jnp.int32, references.shape[0])[None, :]
    return jnp.where(self_mask, -jnp.inf, score)


def exchange(x, n_dev, step):
    return lax.ppermute(x, "ref", [(i, i ^ step) for i in range(n_dev)])


def butterfly_stats(peak, total, n_dev):
    step = 1
    while step < n_dev:
        other_peak, other_total = exchange((peak, total), n_dev, step)
        new_peak = jnp.maximum(peak, other_peak)
        total = total * jnp.exp(peak - new_peak) + other_total * jnp.exp(other_peak - new_peak)
        peak = new_peak
        step *= 2
    return peak, total


def butterfly_sum(x, n_dev):
    step = 1
    while step < n_dev:
        x = x + exchange(x, n_dev, step)
        step *= 2
    return x


def halving_scatter(rows, n_dev):
    me = lax.axis_index("ref")
    n_feat = rows.shape[-1]
    blocks = rows.reshape(n_dev, -1, n_feat)
    step = 1
    while step < n_dev:
        lead = n_dev // (2 * step)
        split = blocks.reshape(lead, 2, -1, n_feat)
        bit = (me // step) % 2
        keep = lax.dynamic_index_in_dim(split, bit, axis=1, keepdims=False)
        send = lax.dynamic_index_in_dim(split, 1 - bit, axis=1, keepdims=False)
        blocks = keep + exchange(send, n_dev, step)
        step *= 2
    return blocks.reshape(-1, n_feat)


def on_device(queries, references, query_ids, spread, cotangent):
    n_query = queries.shape[0]
    n_feat = queries.shape[1]
    n_ref = references.shape[0]
    n_dev = lax.axis_size("ref")
    own_rows = n_query // n_dev
    n_blocks = 4 if own_rows % 4 == 0 else 1
    part_rows = own_rows // n_blocks
    inv = 1.0 / (spread * spread)
    rnorm = jnp.sum(references * references * inv, axis=1)
    ref_start = lax.axis_index("ref") * n_ref
    ref_low = references.astype(jnp.bfloat16)

    def interleave(x):
        tail = x.shape[1:]
        x = x.reshape((n_dev, n_blocks, part_rows) + tail)
        return jnp.moveaxis(x, 1, 0).reshape((n_blocks, n_dev * part_rows) + tail)

    query_blocks = interleave(queries)
    id_blocks = interleave(query_ids)
    cot_blocks = interleave(cotangent)

    kept = []
    for b in range(n_blocks):
        score = block_score(query_blocks[b], id_blocks[b], references, rnorm, inv, ref_start)
        local_peak = jnp.max(score, axis=1)
        expd = jnp.exp(score - local_peak[:, None])
        local_total = jnp.sum(expd, axis=1)
        expd_low = expd.astype(jnp.bfloat16)
        unscaled = jnp.dot(expd_low, ref_low, preferred_element_type=jnp.float32)
        peak, total = butterfly_stats(local_peak, local_total, n_dev)
        scale = cot_blocks[b] * jnp.exp(local_peak - peak) / total
        kept.append((expd_low, unscaled, scale))

    pushed = jnp.zeros((n_ref, n_feat), jnp.float32)
    column = jnp.zeros((n_ref,), jnp.float32)
    own_parts = []
    pull_terms = jnp.zeros((n_feat,), jnp.float32)
    for b in range(n_blocks):
        expd_low, unscaled, scale = kept[b]
        pulled = unscaled * scale[:, None]
        pull_terms = pull_terms + jnp.sum(query_blocks[b] * pulled, axis=0)
        own_parts.append(halving_scatter(pulled, n_dev))
        weight = (expd_low.astype(jnp.float32) * scale[:, None]).astype(jnp.bfloat16)
        pushed = pushed + lax.dot_general(
            weight, query_blocks[b].astype(jnp.bfloat16), (((0,), (0,)), ((), ())),
            preferred_element_type=jnp.float32,
        )
        column = column + jnp.sum(weight.astype(jnp.float32), axis=0)

    reference_grad = (pushed - references * column[:, None]) * inv
    local_terms = jnp.stack([pull_terms, jnp.sum(references * reference_grad, axis=0)])
    summed_terms = butterfly_sum(local_terms, n_dev)
    own_pulled = jnp.stack(own_parts).reshape(own_rows, n_feat)
    own_start = lax.axis_index("ref") * own_rows
    own_queries = lax.dynamic_slice_in_dim(queries, own_start, own_rows, 0)
    own_cot = lax.dynamic_slice_in_dim(cotangent, own_start, own_rows, 0)
    query_grad = (own_pulled - own_queries * own_cot[:, None]) * inv
    self_terms = jnp.sum(queries * queries * cotangent[:, None], axis=0)
    summed = (summed_terms[0] - self_terms) * inv + summed_terms[1]
    weight_total = jnp.sum(cotangent)
    spread_grad = -summed / spread - weight_total / spread
    return (query_grad, reference_grad, spread_grad)


def solution(mesh):
    placed = (P("parts", None), P(("parts", "ref"), None), P("parts"), P(), P("parts"))
    return jax.shard_map(
        on_device,
        mesh=mesh,
        in_specs=placed,
        out_specs=(P(("parts", "ref"), None), P(("parts", "ref"), None), P("parts")),
        check_vma=False,
    )
```

time: 124 us -> 139 us (1.12)
  starting transfers between devices: 13.8 us -> 53.7 us
  matrix products: 55.5 us -> 31.4 us
  waiting for transfers between devices: 27.8 us -> 11.7 us
  local copies, waits for them, and re-layouts: 1.4 us -> 12.4 us
  other arithmetic: 23.5 us -> 27.4 us
    ppermute x16 -> x52, starting transfers between devices: 13.8 us -> 53.7 us  [exchange(): return lax.ppermute(x, 'ref', [(i, i ^ step) for i in range(n_dev)])]
    dot_general x8 -> x4, matrix products: 47.9 us -> 22.7 us  [block_score(): lax.dot_general(query_block * inv, references, (((1,), (1,)), ((), ())),...]
    ppermute x16 -> x52, waiting for transfers between devices: 27.8 us -> 11.7 us  [exchange(): return lax.ppermute(x, 'ref', [(i, i ^ step) for i in range(n_dev)])]
    reduce_sum x6 -> x10, other arithmetic: 7.01 us -> 17.4 us  [the longest x4 8.83 us: on_device(): local_total = jnp.sum(expd, axis=1)]
    reduce_sum x8 -> x1, other arithmetic: 8.81 us -> 0.35 us  [block_score(): qnorm = jnp.sum(query_block * query_block * inv, axis=1)]
    squeeze x0 -> x4, local copies, waits for them, and re-layouts: none -> 5.42 us  [on_device(): scale = cot_blocks[b] * jnp.exp(local_peak - peak) / total]
    add x4 -> x12, other arithmetic: 0.05 us -> 3.11 us  [butterfly_stats(): total * jnp.exp(peak - new_peak)]
    convert_element_type x2 -> x4, other arithmetic: 3.28 us -> 0.72 us  [on_device(): query_blocks[b].astype(jnp.bfloat16)]
  transfers between devices with their start and end apart: 16 -> 52, of which waited for: 13 -> 9; matrix products, arithmetic and copies ran while one was open for 6% -> 37% of each run, Pallas kernels for 0% -> 0%
where the time goes in v2:
time: 139 us; the launch traced here: 138 us
  starting transfers between devices  53.7 us (39%)
  matrix products  31.4 us (23%)
  other arithmetic  27.4 us (20%)
  local copies, waits for them, and re-layouts  12.4 us (9%)
  waiting for transfers between devices  11.7 us (8%)
    ppermute x52, starting transfers between devices, exchange(): return lax.ppermute(x, 'ref', [(i, i ^ step) for i in range(n_dev)])  53.7 us
    dot_general x4, matrix products, block_score(): lax.dot_general(query_block * inv, references, (((1,), (1,)), ((), ())),...  22.7 us
    ppermute x52, waiting for transfers between devices, exchange(): return lax.ppermute(x, 'ref', [(i, i ^ step) for i in range(n_dev)])  11.7 us
    reduce_sum x4, other arithmetic, on_device(): local_total = jnp.sum(expd, axis=1)  8.83 us
    reduce_sum x4, other arithmetic, on_device(): column = column + jnp.sum(weight.astype(jnp.float32), axis=0)  7.29 us
    dot_general x4, matrix products, on_device(): lax.dot_general(weight, query_blocks[b].astype(jnp.bfloat16), (((0,), (0,...  5.69 us
    squeeze x4, local copies, waits for them, and re-layouts, on_device(): scale = cot_blocks[b] * jnp.exp(local_peak - peak) / total  5.42 us
    add x12, other arithmetic, butterfly_stats(): total * jnp.exp(peak - new_peak)  3.11 us
  transfers between devices with their start and end apart: 52, of which 9 were waited for; matrix products, arithmetic and copies ran while one was open for 37% of the time, Pallas kernels for 0%

profile of v2, /device:TPU:0, one launch (start us, length us, event | category | flops | bytes accessed | tf_op | source)
XLA Modules:
  0.0 137.9 jit_solution(1678556381210097206)
XLA Ops:
  3.9 4.3 %fusion.36 = (f32[512]{0:T(512)S(1)}, f32[512,2048]{1,0:T(8,128)S(1)}) fusion(f32[2048]{0:T(1024)S(1)} %broadcast_multiply_fusion.4, f32[512]{0:T(512)S(1)} %mul.438, f32[512,128]{1,0:T(8,128)S(1)} %get-tuple-element.64, f32[2048,128]{1,0:T(8,128)S(1)} %copy-done.7, s32[512]{0:T(512)S(1)} %sub.361), kind=kOutput, calls=%fused_computation.153 | convolution fusion | flops 1615855104 | bytes 5519360 | tf_op jit(solution)/shard_map/dot_general | solution.py:8
  12.1 5.8 %fusion.39 = (f32[512]{0:T(512)S(1)}, f32[512,2048]{1,0:T(8,128)}) fusion(f32[2048]{0:T(1024)S(1)} %broadcast_multiply_fusion.4, f32[512]{0:T(512)S(1)} %mul.422, f32[512,128]{1,0:T(8,128)S(1)} %get-tuple-element.63, f32[2048,128]{1,0:T(8,128)S(1)} %copy-done.7, s32[512]{0:T(512)S(1)} %sub.345), kind=kOutput, calls=%fused_computation.156 | convolution fusion | flops 1615855104 | bytes 5519360 | tf_op jit(solution)/shard_map/dot_general | solution.py:8
  18.0 6.3 %fusion.37 = (f32[512]{0:T(512)}, f32[512,2048]{1,0:T(8,128)}) fusion(f32[2048]{0:T(1024)S(1)} %broadcast_multiply_fusion.4, f32[512]{0:T(512)S(1)} %mul.386, f32[512,128]{1,0:T(8,128)S(1)} %get-tuple-element.61, f32[2048,128]{1,0:T(8,128)S(1)} %copy-done.7, s32[512]{0:T(512)S(1)} %sub.305), kind=kOutput, calls=%fused_computation.154 | convolution fusion | flops 1615855104 | bytes 5519360 | tf_op jit(solution)/shard_map/dot_general | solution.py:8
  25.0 6.3 %fusion.38 = (f32[512]{0:T(512)}, f32[512,2048]{1,0:T(8,128)}) fusion(f32[2048]{0:T(1024)S(1)} %broadcast_multiply_fusion.4, f32[512]{0:T(512)S(1)} %mul.406, f32[512,128]{1,0:T(8,128)S(1)} %get-tuple-element.62, f32[2048,128]{1,0:T(8,128)S(1)} %copy-done.7, s32[512]{0:T(512)S(1)} %sub.329), kind=kOutput, calls=%fused_computation.155 | convolution fusion | flops 1615855104 | bytes 5519360 | tf_op jit(solution)/shard_map/dot_general | solution.py:8
  35.7 3.6 %fusion.4 = f32[512]{0:T(512)} fusion(f32[512,2048]{1,0:T(8,128)} %get-tuple-element.72, f32[512]{0:T(512)S(1)} %get-tuple-element.71), kind=kLoop, calls=%fused_computation.24 | loop fusion | flops 2096640 | bytes 4198400 | tf_op jit(solution)/shard_map/reduce_sum | solution.py:88
  39.3 2.0 %fusion = f32[512]{0:T(512)} fusion(f32[512,2048]{1,0:T(8,128)S(1)} %copy-done.2, f32[512]{0:T(512)} %get-tuple-element.67), kind=kLoop, calls=%fused_computation.20 | loop fusion | flops 2096640 | bytes 4198400 | tf_op jit(solution)/shard_map/reduce_sum | solution.py:88
  41.3 2.0 %fusion.2 = f32[512]{0:T(512)} fusion(f32[512,2048]{1,0:T(8,128)S(1)} %copy-done.4, f32[512]{0:T(512)} %get-tuple-element.69), kind=kLoop, calls=%fused_computation.22 | loop fusion | flops 2096640 | bytes 4198400 | tf_op jit(solution)/shard_map/reduce_sum | solution.py:88
  51.9 2.6 %collective-permute-start.41 = (f32[512]{0:T(512)S(1)}, f32[512]{0:T(512)S(1)}, u32[]{:S(2)}, u32[]{:S(2)}) collective-permute-start(f32[512]{0:T(512)S(1)} %get-tuple-element.53), channel_id=1, source_target_pairs={{0,2},{1,3},{2,0},{3,1},{4,6},{5,7},{6,4},{7,5},{8,10},{9,11},{10,... | collective-permute-start | bytes 6152 | tf_op jit(solution)/shard_map/ppermute | solution.py:23
  55.3 2.0 %collective-permute-start.29 = (f32[512]{0:T(512)S(1)}, f32[512]{0:T(512)S(1)}, u32[]{:S(2)}, u32[]{:S(2)}) collective-permute-start(f32[512]{0:T(512)S(1)} %get-tuple-element.47), channel_id=1, source_target_pairs={{0,2},{1,3},{2,0},{3,1},{4,6},{5,7},{6,4},{7,5},{8,10},{9,11},{10,... | collective-permute-start | bytes 6152 | tf_op jit(solution)/shard_map/ppermute | solution.py:23
  60.9 1.9 %collective-permute-start.17 = (f32[512]{0:T(512)S(1)}, f32[512]{0:T(512)S(1)}, u32[]{:S(2)}, u32[]{:S(2)}) collective-permute-start(f32[512]{0:T(512)S(1)} %get-tuple-element.41), channel_id=1, source_target_pairs={{0,2},{1,3},{2,0},{3,1},{4,6},{5,7},{6,4},{7,5},{8,10},{9,11},{10,... | collective-permute-start | bytes 6152 | tf_op jit(solution)/shard_map/ppermute | solution.py:23
  63.0 2.0 %collective-permute-start.42 = (f32[512]{0:T(512)S(1)}, f32[512]{0:T(512)S(1)}, u32[]{:S(2)}, u32[]{:S(2)}) collective-permute-start(f32[512]{0:T(512)S(1)} %get-tuple-element.51), channel_id=1, source_target_pairs={{0,4},{1,5},{2,6},{3,7},{4,0},{5,1},{6,2},{7,3},{8,12},{9,13},{10,... | collective-permute-start | bytes 6152 | tf_op jit(solution)/shard_map/ppermute | solution.py:23
  65.1 2.0 %collective-permute-start.30 = (f32[512]{0:T(512)S(1)}, f32[512]{0:T(512)S(1)}, u32[]{:S(2)}, u32[]{:S(2)}) collective-permute-start(f32[512]{0:T(512)S(1)} %get-tuple-element.45), channel_id=1, source_target_pairs={{0,4},{1,5},{2,6},{3,7},{4,0},{5,1},{6,2},{7,3},{8,12},{9,13},{10,... | collective-permute-start | bytes 6152 | tf_op jit(solution)/shard_map/ppermute | solution.py:23
  71.5 2.9 %collective-permute-start.43 = (f32[512]{0:T(512)S(1)}, f32[512]{0:T(512)S(1)}, u32[]{:S(2)}, u32[]{:S(2)}) collective-permute-start(f32[512]{0:T(512)S(1)} %get-tuple-element.49), channel_id=1, source_target_pairs={{0,8},{1,9},{2,10},{3,11},{4,12},{5,13},{6,14},{7,15},{8,0},{9,1},... | collective-permute-start | bytes 6152 | tf_op jit(solution)/shard_map/ppermute | solution.py:23
  74.6 2.9 %collective-permute-start.31 = (f32[512]{0:T(512)S(1)}, f32[512]{0:T(512)S(1)}, u32[]{:S(2)}, u32[]{:S(2)}) collective-permute-start(f32[512]{0:T(512)S(1)} %get-tuple-element.43), channel_id=1, source_target_pairs={{0,8},{1,9},{2,10},{3,11},{4,12},{5,13},{6,14},{7,15},{8,0},{9,1},... | collective-permute-start | bytes 6152 | tf_op jit(solution)/shard_map/ppermute | solution.py:23
  77.6 2.8 %collective-permute-start.7 = (f32[512]{0:T(512)S(1)}, f32[512]{0:T(512)S(1)}, u32[]{:S(2)}, u32[]{:S(2)}) collective-permute-start(f32[512]{0:T(512)S(1)} %get-tuple-element.31), channel_id=1, source_target_pairs={{0,8},{1,9},{2,10},{3,11},{4,12},{5,13},{6,14},{7,15},{8,0},{9,1},... | collective-permute-start | bytes 6152 | tf_op jit(solution)/shard_map/ppermute | solution.py:23
  80.7 2.8 %collective-permute-start.19 = (f32[512]{0:T(512)S(1)}, f32[512]{0:T(512)S(1)}, u32[]{:S(2)}, u32[]{:S(2)}) collective-permute-start(f32[512]{0:T(512)S(1)} %get-tuple-element.37), channel_id=1, source_target_pairs={{0,8},{1,9},{2,10},{3,11},{4,12},{5,13},{6,14},{7,15},{8,0},{9,1},... | collective-permute-start | bytes 6152 | tf_op jit(solution)/shard_map/ppermute | solution.py:23
  84.2 3.0 %convert_reduce_fusion = (f32[2048]{0:T(1024)S(1)}, bf16[512,2048]{1,0:T(8,128)(2,1)S(1)}) fusion(f32[512]{0:T(512)S(1)} %add_divide_fusion, f32[512,2048]{1,0:T(8,128)} %copy-done.1, f32[512]{0:T(512)S(1)} %get-tuple-element.65), kind=kLoop, calls=%fused_computation | loop fusion | flops 7337984 | bytes 6303744 | tf_op jit(solution)/shard_map/reduce_sum | solution.py:109
  97.5 2.3 %multiply_reduce_fusion.1 = (f32[128]{0:T(128)S(1)}, bf16[2048,128]{1,0:T(8,128)(2,1)S(1)}, f32[2048,128]{1,0:T(8,128)}) fusion(f32[2048,128]{1,0:T(8,128)S(1)} %copy-done.7, f32[128]{0:T(128)S(1)} %copy-done.11, f32[2048]{0:T(1024)S(1)} %add_add_fusion, f32[2048,128]{1,0:T(8,128)S(1)} %convolution_add_fusion.1, ...), kind=kOutput, calls=%fused_computation.35 | convolution fusion | flops 273416064 | bytes 5909504 | tf_op jit(solution)/shard_map/dot_general | solution.py:105
  105.7 2.0 %collective-permute-done.49 = f32[2,128]{1,0:T(2,128)S(1)} collective-permute-done((f32[2,128]{1,0:T(2,128)S(1)}, f32[2,128]{1,0:T(2,128)S(1)}, u32[]{:S(2)}, u32[]{:S(2)}) %collective-permute-start.49) | collective-permute-done | bytes 1056 | tf_op jit(solution)/shard_map/ppermute | solution.py:23
  111.4 2.1 %collective-permute-start.51 = (f32[2,128]{1,0:T(2,128)S(1)}, f32[2,128]{1,0:T(2,128)S(1)}, u32[]{:S(2)}, u32[]{:S(2)}) collective-permute-start(f32[2,128]{1,0:T(2,128)S(1)} %add.322), channel_id=1, source_target_pairs={{0,8},{1,9},{2,10},{3,11},{4,12},{5,13},{6,14},{7,15},{8,0},{9,1},... | collective-permute-start | bytes 3080 | tf_op jit(solution)/shard_map/ppermute | solution.py:23
  113.5 2.3 %collective-permute-done.51 = f32[2,128]{1,0:T(2,128)S(1)} collective-permute-done((f32[2,128]{1,0:T(2,128)S(1)}, f32[2,128]{1,0:T(2,128)S(1)}, u32[]{:S(2)}, u32[]{:S(2)}) %collective-permute-start.51) | collective-permute-done | bytes 1056 | tf_op jit(solution)/shard_map/ppermute | solution.py:23
  126.9 2.2 %collective-permute-start.47 = (f32[1,32,128]{2,1,0:T(8,128)S(1)}, f32[1,32,128]{2,1,0:T(8,128)S(1)}, u32[]{:S(2)}, u32[]{:S(2)}) collective-permute-start(f32[1,32,128]{2,1,0:T(8,128)S(1)} %constant_dynamic-slice_fusion), channel_id=1, source_target_pairs={{0,8},{1,9},{2,10},{3,11},{4,12},{5,13},{6,14},{7,15},{8,0},{9,1},... | collective-permute-start | bytes 49160 | tf_op jit(solution)/shard_map/ppermute | solution.py:23
  130.1 2.2 %collective-permute-start.23 = (f32[1,32,128]{2,1,0:T(8,128)S(1)}, f32[1,32,128]{2,1,0:T(8,128)S(1)}, u32[]{:S(2)}, u32[]{:S(2)}) collective-permute-start(f32[1,32,128]{2,1,0:T(8,128)S(1)} %constant_dynamic-slice_fusion.2), channel_id=1, source_target_pairs={{0,8},{1,9},{2,10},{3,11},{4,12},{5,13},{6,14},{7,15},{8,0},{9,1},... | collective-permute-start | bytes 49160 | tf_op jit(solution)/shard_map/ppermute | solution.py:23
  134.8 2.4 %collective-permute-done.11 = f32[1,32,128]{2,1,0:T(8,128)S(1)} collective-permute-done((f32[1,32,128]{2,1,0:T(8,128)S(1)}, f32[1,32,128]{2,1,0:T(8,128)S(1)}, u32[]{:S(2)}, u32[]{:S(2)}) %collective-permute-start.11) | collective-permute-done | bytes 16416 | tf_op jit(solution)/shard_map/ppermute | solution.py:23
  (227 shorter events, 65.7 us)
Async XLA Ops:
  8.2 42.1 %collective-permute-start.36 = (f32[512]{0:T(512)S(1)}, f32[512]{0:T(512)}, u32[]{:S(2)}, u32[]{:S(2)}) collective-permute-start(f32[512]{0:T(512)S(1)} %get-tuple-element.65), channel_id=1, source_target_pairs={{0,1},{1,0},{2,3},{3,2},{4,5},{5,4},{6,7},{7,6},{8,9},{9,8},{10,11... | collective-permute-start | bytes 6152 | tf_op jit(solution)/shard_map/ppermute | solution.py:23
  11.4 38.4 %collective-permute-start.40 = (f32[512]{0:T(512)}, f32[512]{0:T(512)}, u32[]{:S(2)}, u32[]{:S(2)}) collective-permute-start(f32[512]{0:T(512)} %fusion.6), channel_id=1, source_target_pairs={{0,1},{1,0},{2,3},{3,2},{4,5},{5,4},{6,7},{7,6},{8,9},{9,8},{10,11... | collective-permute-start | bytes 6152 | tf_op jit(solution)/shard_map/ppermute | solution.py:23
  17.9 34.0 %collective-permute-start.24 = (f32[512]{0:T(512)S(1)}, f32[512]{0:T(512)}, u32[]{:S(2)}, u32[]{:S(2)}) collective-permute-start(f32[512]{0:T(512)S(1)} %get-tuple-element.71), channel_id=1, source_target_pairs={{0,1},{1,0},{2,3},{3,2},{4,5},{5,4},{6,7},{7,6},{8,9},{9,8},{10,11... | collective-permute-start | bytes 6152 | tf_op jit(solution)/shard_map/ppermute | solution.py:23
  24.4 30.9 %collective-permute-start = (f32[512]{0:T(512)}, f32[512]{0:T(512)}, u32[]{:S(2)}, u32[]{:S(2)}) collective-permute-start(f32[512]{0:T(512)} %get-tuple-element.67), channel_id=1, source_target_pairs={{0,1},{1,0},{2,3},{3,2},{4,5},{5,4},{6,7},{7,6},{8,9},{9,8},{10,11... | collective-permute-start | bytes 6152 | tf_op jit(solution)/shard_map/ppermute | solution.py:23
  31.3 26.8 %collective-permute-start.12 = (f32[512]{0:T(512)}, f32[512]{0:T(512)}, u32[]{:S(2)}, u32[]{:S(2)}) collective-permute-start(f32[512]{0:T(512)} %get-tuple-element.69), channel_id=1, source_target_pairs={{0,1},{1,0},{2,3},{3,2},{4,5},{5,4},{6,7},{7,6},{8,9},{9,8},{10,11... | collective-permute-start | bytes 6152 | tf_op jit(solution)/shard_map/ppermute | solution.py:23
  51.4 6.6 %collective-permute-start.16 = (f32[512]{0:T(512)}, f32[512]{0:T(512)S(1)}, u32[]{:S(2)}, u32[]{:S(2)}) collective-permute-start(f32[512]{0:T(512)} %fusion.2), channel_id=1, source_target_pairs={{0,1},{1,0},{2,3},{3,2},{4,5},{5,4},{6,7},{7,6},{8,9},{9,8},{10,11... | collective-permute-start | bytes 6152 | tf_op jit(solution)/shard_map/ppermute | solution.py:23
  51.9 8.9 %collective-permute-start.41 = (f32[512]{0:T(512)S(1)}, f32[512]{0:T(512)S(1)}, u32[]{:S(2)}, u32[]{:S(2)}) collective-permute-start(f32[512]{0:T(512)S(1)} %get-tuple-element.53), channel_id=1, source_target_pairs={{0,2},{1,3},{2,0},{3,1},{4,6},{5,7},{6,4},{7,5},{8,10},{9,11},{10,... | collective-permute-start | bytes 6152 | tf_op jit(solution)/shard_map/ppermute | solution.py:23
  55.3 7.6 %collective-permute-start.29 = (f32[512]{0:T(512)S(1)}, f32[512]{0:T(512)S(1)}, u32[]{:S(2)}, u32[]{:S(2)}) collective-permute-start(f32[512]{0:T(512)S(1)} %get-tuple-element.47), channel_id=1, source_target_pairs={{0,2},{1,3},{2,0},{3,1},{4,6},{5,7},{6,4},{7,5},{8,10},{9,11},{10,... | collective-permute-start | bytes 6152 | tf_op jit(solution)/shard_map/ppermute | solution.py:23
  58.1 6.9 %collective-permute-start.5 = (f32[512]{0:T(512)S(1)}, f32[512]{0:T(512)S(1)}, u32[]{:S(2)}, u32[]{:S(2)}) collective-permute-start(f32[512]{0:T(512)S(1)} %get-tuple-element.35), channel_id=1, source_target_pairs={{0,2},{1,3},{2,0},{3,1},{4,6},{5,7},{6,4},{7,5},{8,10},{9,11},{10,... | collective-permute-start | bytes 6152 | tf_op jit(solution)/shard_map/ppermute | solution.py:23
  60.9 6.2 %collective-permute-start.17 = (f32[512]{0:T(512)S(1)}, f32[512]{0:T(512)S(1)}, u32[]{:S(2)}, u32[]{:S(2)}) collective-permute-start(f32[512]{0:T(512)S(1)} %get-tuple-element.41), channel_id=1, source_target_pairs={{0,2},{1,3},{2,0},{3,1},{4,6},{5,7},{6,4},{7,5},{8,10},{9,11},{10,... | collective-permute-start | bytes 6152 | tf_op jit(solution)/shard_map/ppermute | solution.py:23
  67.3 7.2 %collective-permute-start.6 = (f32[512]{0:T(512)S(1)}, f32[512]{0:T(512)S(1)}, u32[]{:S(2)}, u32[]{:S(2)}) collective-permute-start(f32[512]{0:T(512)S(1)} %get-tuple-element.33), channel_id=1, source_target_pairs={{0,4},{1,5},{2,6},{3,7},{4,0},{5,1},{6,2},{7,3},{8,12},{9,13},{10,... | collective-permute-start | bytes 6152 | tf_op jit(solution)/shard_map/ppermute | solution.py:23
  69.4 8.1 %collective-permute-start.18 = (f32[512]{0:T(512)S(1)}, f32[512]{0:T(512)S(1)}, u32[]{:S(2)}, u32[]{:S(2)}) collective-permute-start(f32[512]{0:T(512)S(1)} %get-tuple-element.39), channel_id=1, source_target_pairs={{0,4},{1,5},{2,6},{3,7},{4,0},{5,1},{6,2},{7,3},{8,12},{9,13},{10,... | collective-permute-start | bytes 6152 | tf_op jit(solution)/shard_map/ppermute | solution.py:23
  71.4 6.3 %collective-permute-start.14 = (f32[512]{0:T(512)S(1)}, f32[512]{0:T(512)S(1)}, u32[]{:S(2)}, u32[]{:S(2)}) collective-permute-start(f32[512]{0:T(512)S(1)} %get-tuple-element.40), channel_id=1, source_target_pairs={{0,4},{1,5},{2,6},{3,7},{4,0},{5,1},{6,2},{7,3},{8,12},{9,13},{10,... | collective-permute-start | bytes 6152 | tf_op jit(solution)/shard_map/ppermute | solution.py:23
  71.5 9.0 %collective-permute-start.43 = (f32[512]{0:T(512)S(1)}, f32[512]{0:T(512)S(1)}, u32[]{:S(2)}, u32[]{:S(2)}) collective-permute-start(f32[512]{0:T(512)S(1)} %get-tuple-element.49), channel_id=1, source_target_pairs={{0,8},{1,9},{2,10},{3,11},{4,12},{5,13},{6,14},{7,15},{8,0},{9,1},... | collective-permute-start | bytes 6152 | tf_op jit(solution)/shard_map/ppermute | solution.py:23
  74.6 12.7 %collective-permute-start.31 = (f32[512]{0:T(512)S(1)}, f32[512]{0:T(512)S(1)}, u32[]{:S(2)}, u32[]{:S(2)}) collective-permute-start(f32[512]{0:T(512)S(1)} %get-tuple-element.43), channel_id=1, source_target_pairs={{0,8},{1,9},{2,10},{3,11},{4,12},{5,13},{6,14},{7,15},{8,0},{9,1},... | collective-permute-start | bytes 6152 | tf_op jit(solution)/shard_map/ppermute | solution.py:23
  77.5 9.9 %collective-permute-start.27 = (f32[512]{0:T(512)S(1)}, f32[512]{0:T(512)S(1)}, u32[]{:S(2)}, u32[]{:S(2)}) collective-permute-start(f32[512]{0:T(512)S(1)} %get-tuple-element.44), channel_id=1, source_target_pairs={{0,8},{1,9},{2,10},{3,11},{4,12},{5,13},{6,14},{7,15},{8,0},{9,1},... | collective-permute-start | bytes 6152 | tf_op jit(solution)/shard_map/ppermute | solution.py:23
  77.6 10.7 %collective-permute-start.7 = (f32[512]{0:T(512)S(1)}, f32[512]{0:T(512)S(1)}, u32[]{:S(2)}, u32[]{:S(2)}) collective-permute-start(f32[512]{0:T(512)S(1)} %get-tuple-element.31), channel_id=1, source_target_pairs={{0,8},{1,9},{2,10},{3,11},{4,12},{5,13},{6,14},{7,15},{8,0},{9,1},... | collective-permute-start | bytes 6152 | tf_op jit(solution)/shard_map/ppermute | solution.py:23
  80.5 7.9 %collective-permute-start.3 = (f32[512]{0:T(512)S(1)}, f32[512]{0:T(512)S(1)}, u32[]{:S(2)}, u32[]{:S(2)}) collective-permute-start(f32[512]{0:T(512)S(1)} %get-tuple-element.32), channel_id=1, source_target_pairs={{0,8},{1,9},{2,10},{3,11},{4,12},{5,13},{6,14},{7,15},{8,0},{9,1},... | collective-permute-start | bytes 6152 | tf_op jit(solution)/shard_map/ppermute | solution.py:23
  80.7 10.6 %collective-permute-start.19 = (f32[512]{0:T(512)S(1)}, f32[512]{0:T(512)S(1)}, u32[]{:S(2)}, u32[]{:S(2)}) collective-permute-start(f32[512]{0:T(512)S(1)} %get-tuple-element.37), channel_id=1, source_target_pairs={{0,8},{1,9},{2,10},{3,11},{4,12},{5,13},{6,14},{7,15},{8,0},{9,1},... | collective-permute-start | bytes 6152 | tf_op jit(solution)/shard_map/ppermute | solution.py:23
  102.9 14.1 %collective-permute-start.44 = (f32[8,32,128]{2,1,0:T(8,128)S(1)}, f32[8,32,128]{2,1,0:T(8,128)S(1)}, u32[]{:S(2)}, u32[]{:S(2)}) collective-permute-start(f32[8,32,128]{2,1,0:T(8,128)S(1)} %dynamic-slice_bitcast_fusion), channel_id=1, source_target_pairs={{0,1},{1,0},{2,3},{3,2},{4,5},{5,4},{6,7},{7,6},{8,9},{9,8},{10,11... | collective-permute-start | bytes 393224 | tf_op jit(solution)/shard_map/ppermute | solution.py:23
  105.7 13.0 %collective-permute-start.32 = (f32[8,32,128]{2,1,0:T(8,128)S(1)}, f32[8,32,128]{2,1,0:T(8,128)S(1)}, u32[]{:S(2)}, u32[]{:S(2)}) collective-permute-start(f32[8,32,128]{2,1,0:T(8,128)S(1)} %dynamic-slice_bitcast_fusion.1), channel_id=1, source_target_pairs={{0,1},{1,0},{2,3},{3,2},{4,5},{5,4},{6,7},{7,6},{8,9},{9,8},{10,11... | collective-permute-start | bytes 393224 | tf_op jit(solution)/shard_map/ppermute | solution.py:23
  109.4 9.9 %collective-permute-start.20 = (f32[8,32,128]{2,1,0:T(8,128)S(1)}, f32[8,32,128]{2,1,0:T(8,128)S(1)}, u32[]{:S(2)}, u32[]{:S(2)}) collective-permute-start(f32[8,32,128]{2,1,0:T(8,128)S(1)} %dynamic-slice_bitcast_fusion.2), channel_id=1, source_target_pairs={{0,1},{1,0},{2,3},{3,2},{4,5},{5,4},{6,7},{7,6},{8,9},{9,8},{10,11... | collective-permute-start | bytes 393224 | tf_op jit(solution)/shard_map/ppermute | solution.py:23
  113.5 7.4 %collective-permute-start.8 = (f32[8,32,128]{2,1,0:T(8,128)S(1)}, f32[8,32,128]{2,1,0:T(8,128)S(1)}, u32[]{:S(2)}, u32[]{:S(2)}) collective-permute-start(f32[8,32,128]{2,1,0:T(8,128)S(1)} %dynamic-slice_bitcast_fusion.3), channel_id=1, source_target_pairs={{0,1},{1,0},{2,3},{3,2},{4,5},{5,4},{6,7},{7,6},{8,9},{9,8},{10,11... | collective-permute-start | bytes 393224 | tf_op jit(solution)/shard_map/ppermute | solution.py:23
  125.7 6.5 %collective-permute-start.10 = (f32[2,32,128]{2,1,0:T(8,128)S(1)}, f32[2,32,128]{2,1,0:T(8,128)S(1)}, u32[]{:S(2)}, u32[]{:S(2)}) collective-permute-start(f32[2,32,128]{2,1,0:T(8,128)S(1)} %dynamic-slice_bitcast_fusion.11), channel_id=1, source_target_pairs={{0,4},{1,5},{2,6},{3,7},{4,0},{5,1},{6,2},{7,3},{8,12},{9,13},{10,... | collective-permute-start | bytes 98312 | tf_op jit(solution)/shard_map/ppermute | solution.py:23
  (47 other events, 330.5 us)

commit v3 on v1

v3 whole, which is shorter than its diff:
```python
import jax
import jax.numpy as jnp
from jax import lax
from jax.experimental import pallas as pl
from jax.experimental.pallas import tpu as pltpu
from jax.sharding import PartitionSpec as P

TILE = 256


def forward_kernel(qs_ref, qn_ref, id_ref, r_ref, rn_ref, rlow_ref, e_ref, u_ref, p_ref, t_ref):
    cross = lax.dot_general(
        qs_ref[...], r_ref[...], (((1,), (1,)), ((), ())),
        precision=lax.Precision.HIGHEST, preferred_element_type=jnp.float32,
    )
    score = cross - qn_ref[...] - rn_ref[...]
    col = lax.broadcasted_iota(jnp.int32, score.shape, 1)
    score = jnp.where(col == id_ref[...], -jnp.inf, score)
    peak = jnp.max(score, axis=1, keepdims=True)
    expd = jnp.exp(score - peak)
    p_ref[...] = peak
    t_ref[...] = jnp.sum(expd, axis=1, keepdims=True)
    expd_low = expd.astype(jnp.bfloat16)
    e_ref[...] = expd_low
    u_ref[...] = jnp.dot(expd_low, rlow_ref[...], preferred_element_type=jnp.float32)


def backward_kernel(e_ref, sc_ref, qlt_ref, pt_ref, col_ref):
    @pl.when(pl.program_id(0) == 0)
    def _():
        pt_ref[...] = jnp.zeros_like(pt_ref)
        col_ref[...] = jnp.zeros_like(col_ref)

    weight = (e_ref[...].astype(jnp.float32) * sc_ref[...]).astype(jnp.bfloat16)
    pt_ref[...] += jnp.dot(qlt_ref[...], weight, preferred_element_type=jnp.float32)
    col_ref[...] += jnp.sum(weight.astype(jnp.float32), axis=0, keepdims=True)


def local_forward(scaled, half_qnorm, local_ids, references, half_rnorm, ref_low):
    n_query, n_feat = scaled.shape
    n_ref = references.shape[0]
    tile = min(TILE, n_query)
    row = lambda i: (i, 0)
    whole = lambda i: (0, 0)
    return pl.pallas_call(
        forward_kernel,
        grid=(n_query // tile,),
        in_specs=[
            pl.BlockSpec((tile, n_feat), row),
            pl.BlockSpec((tile, 1), row),
            pl.BlockSpec((tile, 1), row),
            pl.BlockSpec((n_ref, n_feat), whole),
            pl.BlockSpec((1, n_ref), whole),
            pl.BlockSpec((n_ref, n_feat), whole),
        ],
        out_specs=[
            pl.BlockSpec((tile, n_ref), row),
            pl.BlockSpec((tile, n_feat), row),
            pl.BlockSpec((tile, 1), row),
            pl.BlockSpec((tile, 1), row),
        ],
        out_shape=[
            jax.ShapeDtypeStruct((n_query, n_ref), jnp.bfloat16),
            jax.ShapeDtypeStruct((n_query, n_feat), jnp.float32),
            jax.ShapeDtypeStruct((n_query, 1), jnp.float32),
            jax.ShapeDtypeStruct((n_query, 1), jnp.float32),
        ],
        compiler_params=pltpu.CompilerParams(dimension_semantics=("arbitrary",)),
    )(scaled, half_qnorm, local_ids, references, half_rnorm, ref_low)


def local_backward(expd_low, scale, query_low_t):
    n_query, n_ref = expd_low.shape
    n_feat = query_low_t.shape[0]
    tile = min(TILE, n_query)
    return pl.pallas_call(
        backward_kernel,
        grid=(n_query // tile,),
        in_specs=[
            pl.BlockSpec((tile, n_ref), lambda i: (i, 0)),
            pl.BlockSpec((tile, 1), lambda i: (i, 0)),
            pl.BlockSpec((n_feat, tile), lambda i: (0, i)),
        ],
        out_specs=[
            pl.BlockSpec((n_feat, n_ref), lambda i: (0, 0)),
            pl.BlockSpec((1, n_ref), lambda i: (0, 0)),
        ],
        out_shape=[
            jax.ShapeDtypeStruct((n_feat, n_ref), jnp.float32),
            jax.ShapeDtypeStruct((1, n_ref), jnp.float32),
        ],
        compiler_params=pltpu.CompilerParams(dimension_semantics=("arbitrary",)),
    )(expd_low, scale, query_low_t)


def exchange(x, n_dev, step):
    return lax.ppermute(x, "ref", [(i, i ^ step) for i in range(n_dev)])


def butterfly_stats(peak, total, n_dev):
    step = 1
    while step < n_dev:
        other_peak, other_total = exchange((peak, total), n_dev, step)
        new_peak = jnp.maximum(peak, other_peak)
        total = total * jnp.exp(peak - new_peak) + other_total * jnp.exp(other_peak - new_peak)
        peak = new_peak
        step *= 2
    return peak, total


def halving_scatter(rows, extra, n_dev):
    me = lax.axis_index("ref")
    n_feat = rows.shape[-1]
    blocks = rows.reshape(n_dev, -1, n_feat)
    step = 1
    while step < n_dev:
        lead = n_dev // (2 * step)
        split = blocks.reshape(lead, 2, -1, n_feat)
        bit = (me // step) % 2
        keep = lax.dynamic_index_in_dim(split, bit, axis=1, keepdims=False)
        send = lax.dynamic_index_in_dim(split, 1 - bit, axis=1, keepdims=False)
        got, got_extra = exchange((send, extra), n_dev, step)
        blocks = keep + got
        extra = extra + got_extra
        step *= 2
    return blocks.reshape(-1, n_feat), extra


def on_device(queries, references, query_ids, spread, cotangent):
    n_query = queries.shape[0]
    n_feat = queries.shape[1]
    n_ref = references.shape[0]
    n_dev = lax.axis_size("ref")
    inv = 1.0 / (spread * spread)
    rnorm = jnp.sum(references * references * inv, axis=1)
    qnorm = jnp.sum(queries * queries * inv, axis=1)
    ref_start = lax.axis_index("ref") * n_ref
    ref_low = references.astype(jnp.bfloat16)
    local_ids = (query_ids - ref_start)[:, None]

    expd_low, unscaled, local_peak, local_total = local_forward(
        queries * inv, (0.5 * qnorm)[:, None], local_ids, references, (0.5 * rnorm)[None, :], ref_low
    )
    peak, total = butterfly_stats(local_peak[:, 0], local_total[:, 0], n_dev)
    scale = cotangent * jnp.exp(local_peak[:, 0] - peak) / total
    pulled = unscaled * scale[:, None]
    pushed_t, column = local_backward(expd_low, scale[:, None], queries.astype(jnp.bfloat16).T)
    reference_grad = (pushed_t.T - references * column[0][:, None]) * inv
    local_terms = jnp.stack([jnp.sum(queries * pulled, axis=0), jnp.sum(references * reference_grad, axis=0)])
    own_pulled, summed_terms = halving_scatter(pulled, local_terms, n_dev)
    own_rows = n_query // n_dev
    own_start = lax.axis_index("ref") * own_rows
    own_queries = lax.dynamic_slice_in_dim(queries, own_start, own_rows, 0)
    own_cot = lax.dynamic_slice_in_dim(cotangent, own_start, own_rows, 0)
    query_grad = (own_pulled - own_queries * own_cot[:, None]) * inv
    self_terms = jnp.sum(queries * queries * cotangent[:, None], axis=0)
    summed = (summed_terms[0] - self_terms) * inv + summed_terms[1]
    weight_total = jnp.sum(cotangent)
    spread_grad = -summed / spread - weight_total / spread
    return (query_grad, reference_grad, spread_grad)


def solution(mesh):
    placed = (P("parts", None), P(("parts", "ref"), None), P("parts"), P(), P("parts"))
    return jax.shard_map(
        on_device,
        mesh=mesh,
        in_specs=placed,
        out_specs=(P(("parts", "ref"), None), P(("parts", "ref"), None), P("parts")),
        check_vma=False,
    )
```

time: 124 us -> 107 us (0.86)
  matrix products: 55.5 us -> 0 us
  Pallas kernels: 0 us -> 33.6 us
  local copies, waits for them, and re-layouts: 1.4 us -> 12.9 us
  other arithmetic: 23.5 us -> 16.4 us
    dot_general x16 -> x0, matrix products: 55.5 us -> none  [the longest x8 47.9 us: block_score(): lax.dot_general(query_block * inv, references, (((1,), (1,)), ((), ())),...]
    pallas_call x0 -> x2, Pallas kernels: none -> 33.6 us  [the longest x1 24 us: local_forward(): pl.pallas_call(forward_kernel, grid=(n_query // tile,), in_specs=[pl.Bloc...]
    reduce_sum x12 -> x1, other arithmetic: 11.7 us -> 2.88 us  [on_device(): self_terms = jnp.sum(queries * queries * cotangent[:, None], axis=0)]
    unnamed x6 -> x13, local copies, waits for them, and re-layouts: 0.02 us -> 6.47 us
    pallas_call x0 -> x2, other arithmetic: none -> 3.12 us  [local_forward(): pl.pallas_call(forward_kernel, grid=(n_query // tile,), in_specs=[pl.Bloc...]
    broadcast_in_dim x0 -> x2, local copies, waits for them, and re-layouts: none -> 2.79 us  [the longest x1 1.42 us: on_device(): pulled = unscaled * scale[:, None]]
    mul x0 -> x2, local copies, waits for them, and re-layouts: none -> 2.64 us  [the longest x1 1.34 us: on_device(): 0.5 * qnorm]
    convert_element_type x1 -> x0, other arithmetic: 1.29 us -> none  [on_device(): query_low_blocks = query_blocks.astype(jnp.bfloat16)]
  transfers between devices with their start and end apart: 16 -> 16, of which waited for: 13 -> 12; matrix products, arithmetic and copies ran while one was open for 6% -> 7% of each run, Pallas kernels for 0% -> 9%
where the time goes in v3:
time: 107 us; the launch traced here: 106 us
  Pallas kernels  33.6 us (31%)
  waiting for transfers between devices  28.7 us (27%)
  other arithmetic  16.4 us (15%)
  starting transfers between devices  13.8 us (13%)
  local copies, waits for them, and re-layouts  12.9 us (12%)
    ppermute x16, waiting for transfers between devices, exchange(): return lax.ppermute(x, 'ref', [(i, i ^ step) for i in range(n_dev)])  28.7 us
    pallas_call x1, Pallas kernels, local_forward(): pl.pallas_call(forward_kernel, grid=(n_query // tile,), in_specs=[pl.Bloc...  24 us
    ppermute x16, starting transfers between devices, exchange(): return lax.ppermute(x, 'ref', [(i, i ^ step) for i in range(n_dev)])  13.8 us
    pallas_call x1, Pallas kernels, local_backward(): pl.pallas_call(backward_kernel, grid=(n_query // tile,), in_specs=[pl.Blo...  9.6 us
    unnamed x13, local copies, waits for them, and re-layouts  6.47 us
    pallas_call x2, other arithmetic, local_forward(): pl.pallas_call(forward_kernel, grid=(n_query // tile,), in_specs=[pl.Bloc...  3.12 us
    reduce_sum x1, other arithmetic, on_device(): self_terms = jnp.sum(queries * queries * cotangent[:, None], axis=0)  2.88 us
  transfers between devices with their start and end apart: 16, of which 12 were waited for; matrix products, arithmetic and copies ran while one was open for 7% of the time, Pallas kernels for 9%

profile of v3, /device:TPU:0, one launch (start us, length us, event | category | flops | bytes accessed | tf_op | source)
XLA Modules:
  0.0 106.1 jit_solution(13528567684413242424)
XLA Ops:
  0.6 1.6 %copy.34 = f32[2048,128]{0,1:T(8,128)S(1)} copy(f32[2048,128]{1,0:T(8,128)} %r_ref.1) | data formatting | bytes 2097152 | tf_op args[1]
  2.2 2.1 %convert_element_type.6.rlow_ref = bf16[2048,128]{1,0:T(8,128)(2,1)} convert(f32[2048,128]{1,0:T(8,128)} %r_ref.1) | non-fusion elementwise | flops 262144 | bytes 1572864 | tf_op jit(solution)/shard_map/convert_element_type | solution.py:138
  4.9 2.6 %copy.31 = f32[2048,128]{0,1:T(8,128)} copy(f32[2048,128]{1,0:T(8,128)} %param.5) | data formatting | bytes 2097152 | tf_op args[0]
  7.5 2.9 %multiply_reduce_fusion = (f32[128]{0:T(128)S(1)}, f32[2048]{0:T(1024)S(1)}, f32[2048]{0:T(1024)S(1)}, f32[2048,128]{0,1:T(8,128)S(1)}, bf16[128,2048]{1,0:T(8,128)(2,1)}) fusion(f32[2048,128]{0,1:T(8,128)} %copy.31, f32[2048]{0:T(1024)} %param.9, f32[128]{0:T(128)S(1)} %multiply_divide_fusion, f32[2048,128]{0,1:T(8,128)S(1)} %copy.34), kind=kLoop, calls=%fused_computation.2 | loop fusion | flops 2617216 | bytes 3695616 | tf_op jit(solution)/shard_map/reduce_sum | solution.py:156
  15.0 24.0 %shard_map.76 = (bf16[2048,2048]{1,0:T(8,128)(2,1)}, f32[2048,128]{1,0:T(8,128)}, f32[2048,1]{1,0:T(8,128)}, f32[2048,1]{1,0:T(8,128)}) custom-call(f32[2048,128]{1,0:T(8,128)} %copy.36.qs_ref, f32[2048,1]{1,0:T(8,128)} %copy.37.qn_ref, s32[2048,1]{1,0:T(8,128)} %copy.38.id_ref, f32[2048,128]{1,0:T(8,128)} %r_ref.1, f32[1,2048]{1,0:T(1,128)} %bitcast.55, ...), custom_call_target="tpu_custom_call" | custom-call | tf_op jit(solution)/shard_map/pallas_call | solution.py:45
  39.0 1.6 %reduce = f32[2048]{0:T(1024)S(1)} reduce(f32[2048,1]{1,0:T(8,128)} %get-tuple-element.10, f32[]{:T(128)} %constant.108), dimensions={1}, to_apply=%get-tuple-element.10.reduce_sub_computation | reduce | bytes 16388 | tf_op jit(solution)/shard_map/pallas_call | solution.py:45
  41.1 1.6 %reduce.1 = f32[2048]{0:T(1024)S(1)} reduce(f32[2048,1]{1,0:T(8,128)} %get-tuple-element.11, f32[]{:T(128)} %constant.108), dimensions={1}, to_apply=%get-tuple-element.11.reduce_sub_computation | reduce | bytes 16388 | tf_op jit(solution)/shard_map/pallas_call | solution.py:45
  44.0 2.7 %collective-permute-start.1 = (f32[2048]{0:T(1024)S(1)}, f32[2048]{0:T(1024)S(1)}, u32[]{:S(2)}, u32[]{:S(2)}) collective-permute-start(f32[2048]{0:T(1024)S(1)} %get-tuple-element.36), channel_id=1, source_target_pairs={{0,2},{1,3},{2,0},{3,1},{4,6},{5,7},{6,4},{7,5},{8,10},{9,11},{10,... | collective-permute-start | bytes 24584 | tf_op jit(solution)/shard_map/ppermute | solution.py:97
  48.3 2.0 %collective-permute-done.5 = f32[2048]{0:T(1024)S(1)} collective-permute-done((f32[2048]{0:T(1024)S(1)}, f32[2048]{0:T(1024)S(1)}, u32[]{:S(2)}, u32[]{:S(2)}) %collective-permute-start.5) | collective-permute-done | bytes 8224 | tf_op jit(solution)/shard_map/ppermute | solution.py:97
  50.4 1.6 %collective-permute-start.2 = (f32[2048]{0:T(1024)S(1)}, f32[2048]{0:T(1024)S(1)}, u32[]{:S(2)}, u32[]{:S(2)}) collective-permute-start(f32[2048]{0:T(1024)S(1)} %get-tuple-element.34), channel_id=1, source_target_pairs={{0,4},{1,5},{2,6},{3,7},{4,0},{5,1},{6,2},{7,3},{8,12},{9,13},{10,... | collective-permute-start | bytes 24584 | tf_op jit(solution)/shard_map/ppermute | solution.py:97
  52.4 1.6 %collective-permute-done.2 = f32[2048]{0:T(1024)S(1)} collective-permute-done((f32[2048]{0:T(1024)S(1)}, f32[2048]{0:T(1024)S(1)}, u32[]{:S(2)}, u32[]{:S(2)}) %collective-permute-start.2) | collective-permute-done | bytes 8224 | tf_op jit(solution)/shard_map/ppermute | solution.py:97
  54.1 1.6 %collective-permute-done.6 = f32[2048]{0:T(1024)S(1)} collective-permute-done((f32[2048]{0:T(1024)S(1)}, f32[2048]{0:T(1024)S(1)}, u32[]{:S(2)}, u32[]{:S(2)}) %collective-permute-start.6) | collective-permute-done | bytes 8224 | tf_op jit(solution)/shard_map/ppermute | solution.py:97
  55.7 2.7 %collective-permute-start.3 = (f32[2048]{0:T(1024)S(1)}, f32[2048]{0:T(1024)S(1)}, u32[]{:S(2)}, u32[]{:S(2)}) collective-permute-start(f32[2048]{0:T(1024)S(1)} %get-tuple-element.32), channel_id=1, source_target_pairs={{0,8},{1,9},{2,10},{3,11},{4,12},{5,13},{6,14},{7,15},{8,0},{9,1},... | collective-permute-start | bytes 24584 | tf_op jit(solution)/shard_map/ppermute | solution.py:97
  58.7 1.6 %collective-permute-done.3 = f32[2048]{0:T(1024)S(1)} collective-permute-done((f32[2048]{0:T(1024)S(1)}, f32[2048]{0:T(1024)S(1)}, u32[]{:S(2)}, u32[]{:S(2)}) %collective-permute-start.3) | collective-permute-done | bytes 8224 | tf_op jit(solution)/shard_map/ppermute | solution.py:97
  60.3 2.6 %collective-permute-done.7 = f32[2048]{0:T(1024)S(1)} collective-permute-done((f32[2048]{0:T(1024)S(1)}, f32[2048]{0:T(1024)S(1)}, u32[]{:S(2)}, u32[]{:S(2)}) %collective-permute-start.7) | collective-permute-done | bytes 8224 | tf_op jit(solution)/shard_map/ppermute | solution.py:97
  63.5 1.6 %multiply_reduce_fusion.2 = (f32[128]{0:T(128)S(1)}, f32[2048,128]{1,0:T(8,128)S(1)}) fusion(f32[2048,128]{1,0:T(8,128)S(1)} %copy-done, f32[2048,128]{1,0:T(8,128)} %get-tuple-element.9, f32[2048]{0:T(1024)S(1)} %get-tuple-element.40), kind=kLoop, calls=%fused_computation.4 | loop fusion | flops 786304 | bytes 3154432 | tf_op jit(solution)/shard_map/reduce_sum | solution.py:149
  68.4 9.6 %shard_map.77 = (f32[128,2048]{1,0:T(8,128)}, f32[1,2048]{1,0:T(1,128)}) custom-call(bf16[2048,2048]{1,0:T(8,128)(2,1)} %get-tuple-element.12.e_ref, f32[2048,1]{1,0:T(8,128)} %copy.40.sc_ref, bf16[128,2048]{1,0:T(8,128)(2,1)} %get-tuple-element.38.qlt_ref), custom_call_target="tpu_custom_call" | custom-call | tf_op jit(solution)/shard_map/pallas_call | solution.py:76
  78.0 1.6 %multiply_reduce_fusion.1 = (f32[128]{0:T(128)S(1)}, f32[2048,128]{0,1:T(8,128)S(1)}) fusion(f32[2048,128]{0,1:T(8,128)S(1)} %copy.34, f32[128]{0:T(128)S(1)} %multiply_divide_fusion, f32[2048]{0:T(1024)} %bitcast.57, f32[128,2048]{1,0:T(8,128)} %get-tuple-element.13), kind=kLoop, calls=%fused_computation.3 | loop fusion | flops 1310592 | bytes 3154944 | tf_op jit(solution)/shard_map/reduce_sum | solution.py:149
  82.7 1.6 %collective-permute-start.13 = (f32[2,128]{1,0:T(2,128)S(1)}, f32[2,128]{1,0:T(2,128)S(1)}, u32[]{:S(2)}, u32[]{:S(2)}) collective-permute-start(f32[2,128]{1,0:T(2,128)S(1)} %fusion.7), channel_id=1, source_target_pairs={{0,2},{1,3},{2,0},{3,1},{4,6},{5,7},{6,4},{7,5},{8,10},{9,11},{10,... | collective-permute-start | bytes 3080 | tf_op jit(solution)/shard_map/ppermute | solution.py:97
  84.2 5.5 %collective-permute-done.9 = f32[4,128,128]{2,1,0:T(8,128)S(1)} collective-permute-done((f32[4,128,128]{2,1,0:T(8,128)S(1)}, f32[4,128,128]{2,1,0:T(8,128)S(1)}, u32[]{:S(2)}, u32[]{:S(2)}) %collective-permute-start.9) | collective-permute-done | bytes 262176 | tf_op jit(solution)/shard_map/ppermute | solution.py:97
  90.3 1.6 %collective-permute-start.14 = (f32[2,128]{1,0:T(2,128)S(1)}, f32[2,128]{1,0:T(2,128)S(1)}, u32[]{:S(2)}, u32[]{:S(2)}) collective-permute-start(f32[2,128]{1,0:T(2,128)S(1)} %fusion.10), channel_id=1, source_target_pairs={{0,4},{1,5},{2,6},{3,7},{4,0},{5,1},{6,2},{7,3},{8,12},{9,13},{10,... | collective-permute-start | bytes 3080 | tf_op jit(solution)/shard_map/ppermute | solution.py:97
  91.9 3.0 %collective-permute-done.14 = f32[2,128]{1,0:T(2,128)S(1)} collective-permute-done((f32[2,128]{1,0:T(2,128)S(1)}, f32[2,128]{1,0:T(2,128)S(1)}, u32[]{:S(2)}, u32[]{:S(2)}) %collective-permute-start.14) | collective-permute-done | bytes 1056 | tf_op jit(solution)/shard_map/ppermute | solution.py:97
  96.6 2.8 %collective-permute-done.15 = f32[2,128]{1,0:T(2,128)S(1)} collective-permute-done((f32[2,128]{1,0:T(2,128)S(1)}, f32[2,128]{1,0:T(2,128)S(1)}, u32[]{:S(2)}, u32[]{:S(2)}) %collective-permute-start.15) | collective-permute-done | bytes 1056 | tf_op jit(solution)/shard_map/ppermute | solution.py:97
  101.0 4.4 %collective-permute-done.11 = f32[1,128,128]{2,1,0:T(8,128)S(1)} collective-permute-done((f32[1,128,128]{2,1,0:T(8,128)S(1)}, f32[1,128,128]{2,1,0:T(8,128)S(1)}, u32[]{:S(2)}, u32[]{:S(2)}) %collective-permute-start.11) | collective-permute-done | bytes 65568 | tf_op jit(solution)/shard_map/ppermute | solution.py:97
  (55 shorter events, 21.1 us)
Async XLA Ops:
  0.6 13.0 %copy-start.3 = (s32[2048]{0:T(1024)S(1)}, s32[2048]{0:T(1024)}, u32[]{:S(2)}) copy-start(s32[2048]{0:T(1024)} %param.7) | copy-start | bytes 24580
  4.9 58.0 %copy-start.2 = (f32[2048]{0:T(1024)S(1)}, f32[2048]{0:T(1024)}, u32[]{:S(2)}) copy-start(f32[2048]{0:T(1024)} %param.9) | copy-start | bytes 24580
  4.9 58.6 %copy-start = (f32[2048,128]{1,0:T(8,128)S(1)}, f32[2048,128]{1,0:T(8,128)}, u32[]{:S(2)}) copy-start(f32[2048,128]{1,0:T(8,128)} %param.5) | copy-start | bytes 3145732
  40.6 2.2 %collective-permute-start = (f32[2048]{0:T(1024)S(1)}, f32[2048]{0:T(1024)S(1)}, u32[]{:S(2)}, u32[]{:S(2)}) collective-permute-start(f32[2048]{0:T(1024)S(1)} %reduce), channel_id=1, source_target_pairs={{0,1},{1,0},{2,3},{3,2},{4,5},{5,4},{6,7},{7,6},{8,9},{9,8},{10,11... | collective-permute-start | bytes 24584 | tf_op jit(solution)/shard_map/ppermute | solution.py:97
  42.7 1.2 %collective-permute-start.4 = (f32[2048]{0:T(1024)S(1)}, f32[2048]{0:T(1024)S(1)}, u32[]{:S(2)}, u32[]{:S(2)}) collective-permute-start(f32[2048]{0:T(1024)S(1)} %reduce.1), channel_id=1, source_target_pairs={{0,1},{1,0},{2,3},{3,2},{4,5},{5,4},{6,7},{7,6},{8,9},{9,8},{10,11... | collective-permute-start | bytes 24584 | tf_op jit(solution)/shard_map/ppermute | solution.py:97
  44.0 4.4 %collective-permute-start.1 = (f32[2048]{0:T(1024)S(1)}, f32[2048]{0:T(1024)S(1)}, u32[]{:S(2)}, u32[]{:S(2)}) collective-permute-start(f32[2048]{0:T(1024)S(1)} %get-tuple-element.36), channel_id=1, source_target_pairs={{0,2},{1,3},{2,0},{3,1},{4,6},{5,7},{6,4},{7,5},{8,10},{9,11},{10,... | collective-permute-start | bytes 24584 | tf_op jit(solution)/shard_map/ppermute | solution.py:97
  46.7 3.7 %collective-permute-start.5 = (f32[2048]{0:T(1024)S(1)}, f32[2048]{0:T(1024)S(1)}, u32[]{:S(2)}, u32[]{:S(2)}) collective-permute-start(f32[2048]{0:T(1024)S(1)} %get-tuple-element.35), channel_id=1, source_target_pairs={{0,2},{1,3},{2,0},{3,1},{4,6},{5,7},{6,4},{7,5},{8,10},{9,11},{10,... | collective-permute-start | bytes 24584 | tf_op jit(solution)/shard_map/ppermute | solution.py:97
  50.4 3.7 %collective-permute-start.2 = (f32[2048]{0:T(1024)S(1)}, f32[2048]{0:T(1024)S(1)}, u32[]{:S(2)}, u32[]{:S(2)}) collective-permute-start(f32[2048]{0:T(1024)S(1)} %get-tuple-element.34), channel_id=1, source_target_pairs={{0,4},{1,5},{2,6},{3,7},{4,0},{5,1},{6,2},{7,3},{8,12},{9,13},{10,... | collective-permute-start | bytes 24584 | tf_op jit(solution)/shard_map/ppermute | solution.py:97
  52.0 3.7 %collective-permute-start.6 = (f32[2048]{0:T(1024)S(1)}, f32[2048]{0:T(1024)S(1)}, u32[]{:S(2)}, u32[]{:S(2)}) collective-permute-start(f32[2048]{0:T(1024)S(1)} %get-tuple-element.33), channel_id=1, source_target_pairs={{0,4},{1,5},{2,6},{3,7},{4,0},{5,1},{6,2},{7,3},{8,12},{9,13},{10,... | collective-permute-start | bytes 24584 | tf_op jit(solution)/shard_map/ppermute | solution.py:97
  55.7 4.6 %collective-permute-start.3 = (f32[2048]{0:T(1024)S(1)}, f32[2048]{0:T(1024)S(1)}, u32[]{:S(2)}, u32[]{:S(2)}) collective-permute-start(f32[2048]{0:T(1024)S(1)} %get-tuple-element.32), channel_id=1, source_target_pairs={{0,8},{1,9},{2,10},{3,11},{4,12},{5,13},{6,14},{7,15},{8,0},{9,1},... | collective-permute-start | bytes 24584 | tf_op jit(solution)/shard_map/ppermute | solution.py:97
  58.3 4.5 %collective-permute-start.7 = (f32[2048]{0:T(1024)S(1)}, f32[2048]{0:T(1024)S(1)}, u32[]{:S(2)}, u32[]{:S(2)}) collective-permute-start(f32[2048]{0:T(1024)S(1)} %get-tuple-element.31), channel_id=1, source_target_pairs={{0,8},{1,9},{2,10},{3,11},{4,12},{5,13},{6,14},{7,15},{8,0},{9,1},... | collective-permute-start | bytes 24584 | tf_op jit(solution)/shard_map/ppermute | solution.py:97
  65.1 1.0 copy-start.1
  66.9 12.7 %collective-permute-start.8 = (f32[8,128,128]{2,1,0:T(8,128)}, f32[8,128,128]{2,1,0:T(8,128)}, u32[]{:S(2)}, u32[]{:S(2)}) collective-permute-start(f32[8,128,128]{2,1,0:T(8,128)} %dynamic-slice_bitcast_fusion), channel_id=1, source_target_pairs={{0,1},{1,0},{2,3},{3,2},{4,5},{5,4},{6,7},{7,6},{8,9},{9,8},{10,11... | collective-permute-start | bytes 1572872 | tf_op jit(solution)/shard_map/ppermute | solution.py:97
  68.4 31.5 %copy-start.4 = (f32[128]{0:T(128)S(1)}, f32[128]{0:T(128)}, u32[]{:S(2)}) copy-start(f32[128]{0:T(128)} %param.8) | copy-start | bytes 1540
  80.9 8.8 %collective-permute-start.9 = (f32[4,128,128]{2,1,0:T(8,128)S(1)}, f32[4,128,128]{2,1,0:T(8,128)S(1)}, u32[]{:S(2)}, u32[]{:S(2)}) collective-permute-start(f32[4,128,128]{2,1,0:T(8,128)S(1)} %dynamic-slice_bitcast_fusion.1), channel_id=1, source_target_pairs={{0,2},{1,3},{2,0},{3,1},{4,6},{5,7},{6,4},{7,5},{8,10},{9,11},{10,... | collective-permute-start | bytes 786440 | tf_op jit(solution)/shard_map/ppermute | solution.py:97
  81.5 1.2 %collective-permute-start.12 = (f32[2,128]{1,0:T(2,128)S(1)}, f32[2,128]{1,0:T(2,128)S(1)}, u32[]{:S(2)}, u32[]{:S(2)}) collective-permute-start(f32[2,128]{1,0:T(2,128)S(1)} %pad_maximum_fusion), channel_id=1, source_target_pairs={{0,1},{1,0},{2,3},{3,2},{4,5},{5,4},{6,7},{7,6},{8,9},{9,8},{10,11... | collective-permute-start | bytes 3080 | tf_op jit(solution)/shard_map/ppermute | solution.py:97
  82.7 7.6 %collective-permute-start.13 = (f32[2,128]{1,0:T(2,128)S(1)}, f32[2,128]{1,0:T(2,128)S(1)}, u32[]{:S(2)}, u32[]{:S(2)}) collective-permute-start(f32[2,128]{1,0:T(2,128)S(1)} %fusion.7), channel_id=1, source_target_pairs={{0,2},{1,3},{2,0},{3,1},{4,6},{5,7},{6,4},{7,5},{8,10},{9,11},{10,... | collective-permute-start | bytes 3080 | tf_op jit(solution)/shard_map/ppermute | solution.py:97
  89.8 9.7 %collective-permute-start.10 = (f32[2,128,128]{2,1,0:T(8,128)S(1)}, f32[2,128,128]{2,1,0:T(8,128)S(1)}, u32[]{:S(2)}, u32[]{:S(2)}) collective-permute-start(f32[2,128,128]{2,1,0:T(8,128)S(1)} %dynamic-slice_bitcast_fusion.2), channel_id=1, source_target_pairs={{0,4},{1,5},{2,6},{3,7},{4,0},{5,1},{6,2},{7,3},{8,12},{9,13},{10,... | collective-permute-start | bytes 393224 | tf_op jit(solution)/shard_map/ppermute | solution.py:97
  90.3 4.6 %collective-permute-start.14 = (f32[2,128]{1,0:T(2,128)S(1)}, f32[2,128]{1,0:T(2,128)S(1)}, u32[]{:S(2)}, u32[]{:S(2)}) collective-permute-start(f32[2,128]{1,0:T(2,128)S(1)} %fusion.10), channel_id=1, source_target_pairs={{0,4},{1,5},{2,6},{3,7},{4,0},{5,1},{6,2},{7,3},{8,12},{9,13},{10,... | collective-permute-start | bytes 3080 | tf_op jit(solution)/shard_map/ppermute | solution.py:97
  94.9 4.5 %collective-permute-start.15 = (f32[2,128]{1,0:T(2,128)S(1)}, f32[2,128]{1,0:T(2,128)S(1)}, u32[]{:S(2)}, u32[]{:S(2)}) collective-permute-start(f32[2,128]{1,0:T(2,128)S(1)} %add.115), channel_id=1, source_target_pairs={{0,8},{1,9},{2,10},{3,11},{4,12},{5,13},{6,14},{7,15},{8,0},{9,1},... | collective-permute-start | bytes 3080 | tf_op jit(solution)/shard_map/ppermute | solution.py:97
  99.5 5.9 %collective-permute-start.11 = (f32[1,128,128]{2,1,0:T(8,128)S(1)}, f32[1,128,128]{2,1,0:T(8,128)S(1)}, u32[]{:S(2)}, u32[]{:S(2)}) collective-permute-start(f32[1,128,128]{2,1,0:T(8,128)S(1)} %constant_dynamic-slice_fusion), channel_id=1, source_target_pairs={{0,8},{1,9},{2,10},{3,11},{4,12},{5,13},{6,14},{7,15},{8,0},{9,1},... | collective-permute-start | bytes 196616 | tf_op jit(solution)/shard_map/ppermute | solution.py:97

commit v4 on v3

v4 whole, which is shorter than its diff:
```python
import jax
import jax.numpy as jnp
from jax import lax
from jax.experimental import pallas as pl
from jax.experimental.pallas import tpu as pltpu
from jax.sharding import PartitionSpec as P

TILE = 256


def forward_kernel(q_ref, inv_ref, lid_ref, r_ref, e_ref, ut_ref, p_ref, t_ref, rn_sc, rlt_sc):
    inv = inv_ref[...]

    @pl.when(pl.program_id(0) == 0)
    def _():
        refs = r_ref[...]
        rn_sc[...] = 0.5 * jnp.sum(refs * refs * inv, axis=1, keepdims=True)
        rlt_sc[...] = refs.T.astype(jnp.bfloat16)

    q = q_ref[...]
    ones = jnp.ones((8, q.shape[1]), jnp.float32)
    qnorm = lax.dot_general(
        ones, q * q * inv, (((1,), (1,)), ((), ())),
        precision=lax.Precision.HIGHEST, preferred_element_type=jnp.float32,
    )[0:1, :]
    cross = lax.dot_general(
        r_ref[...], q * inv, (((1,), (1,)), ((), ())),
        precision=lax.Precision.HIGHEST, preferred_element_type=jnp.float32,
    )
    score = cross - 0.5 * qnorm - rn_sc[...]
    row = lax.broadcasted_iota(jnp.int32, score.shape, 0)
    score = jnp.where(row == lid_ref[...], -jnp.inf, score)
    peak = jnp.max(score, axis=0, keepdims=True)
    expd = jnp.exp(score - peak)
    p_ref[...] = peak
    t_ref[...] = jnp.sum(expd, axis=0, keepdims=True)
    expd_low = expd.astype(jnp.bfloat16)
    e_ref[...] = expd_low
    ut_ref[...] = jnp.dot(rlt_sc[...], expd_low, preferred_element_type=jnp.float32)


def backward_kernel(e_ref, sc_ref, qa_ref, pa_ref):
    @pl.when(pl.program_id(0) == 0)
    def _():
        pa_ref[...] = jnp.zeros_like(pa_ref)

    weight = (e_ref[...].astype(jnp.float32) * sc_ref[...]).astype(jnp.bfloat16)
    pa_ref[...] += jnp.dot(weight, qa_ref[...], preferred_element_type=jnp.float32)


def local_forward(queries, inv, local_ids, references):
    n_query, n_feat = queries.shape
    n_ref = references.shape[0]
    tile = min(TILE, n_query)
    return pl.pallas_call(
        forward_kernel,
        grid=(n_query // tile,),
        in_specs=[
            pl.BlockSpec((tile, n_feat), lambda i: (i, 0)),
            pl.BlockSpec((1, n_feat), lambda i: (0, 0)),
            pl.BlockSpec((1, tile), lambda i: (0, i)),
            pl.BlockSpec((n_ref, n_feat), lambda i: (0, 0)),
        ],
        out_specs=[
            pl.BlockSpec((n_ref, tile), lambda i: (0, i)),
            pl.BlockSpec((n_feat, tile), lambda i: (0, i)),
            pl.BlockSpec((1, tile), lambda i: (0, i)),
            pl.BlockSpec((1, tile), lambda i: (0, i)),
        ],
        out_shape=[
            jax.ShapeDtypeStruct((n_ref, n_query), jnp.bfloat16),
            jax.ShapeDtypeStruct((n_feat, n_query), jnp.float32),
            jax.ShapeDtypeStruct((1, n_query), jnp.float32),
            jax.ShapeDtypeStruct((1, n_query), jnp.float32),
        ],
        scratch_shapes=[
            pltpu.VMEM((n_ref, 1), jnp.float32),
            pltpu.VMEM((n_feat, n_ref), jnp.bfloat16),
        ],
        compiler_params=pltpu.CompilerParams(dimension_semantics=("arbitrary",)),
    )(queries, inv, local_ids, references)


def local_backward(expd_low, scale, query_aug):
    n_ref, n_query = expd_low.shape
    width = query_aug.shape[1]
    tile = min(TILE, n_query)
    return pl.pallas_call(
        backward_kernel,
        grid=(n_query // tile,),
        in_specs=[
            pl.BlockSpec((n_ref, tile), lambda i: (0, i)),
            pl.BlockSpec((1, tile), lambda i: (0, i)),
            pl.BlockSpec((tile, width), lambda i: (i, 0)),
        ],
        out_specs=pl.BlockSpec((n_ref, width), lambda i: (0, 0)),
        out_shape=jax.ShapeDtypeStruct((n_ref, width), jnp.float32),
        compiler_params=pltpu.CompilerParams(dimension_semantics=("arbitrary",)),
    )(expd_low, scale, query_aug)


def exchange(x, n_dev, step):
    return lax.ppermute(x, "ref", [(i, i ^ step) for i in range(n_dev)])


def butterfly_stats(peak, total, n_dev):
    step = 1
    while step < n_dev:
        other_peak, other_total = exchange((peak, total), n_dev, step)
        new_peak = jnp.maximum(peak, other_peak)
        total = total * jnp.exp(peak - new_peak) + other_total * jnp.exp(other_peak - new_peak)
        peak = new_peak
        step *= 2
    return peak, total


def halving_scatter(rows, extra, n_dev):
    me = lax.axis_index("ref")
    n_feat = rows.shape[-1]
    blocks = rows.reshape(n_dev, -1, n_feat)
    step = 1
    while step < n_dev:
        lead = n_dev // (2 * step)
        split = blocks.reshape(lead, 2, -1, n_feat)
        bit = (me // step) % 2
        keep = lax.dynamic_index_in_dim(split, bit, axis=1, keepdims=False)
        send = lax.dynamic_index_in_dim(split, 1 - bit, axis=1, keepdims=False)
        got, got_extra = exchange((send, extra), n_dev, step)
        blocks = keep + got
        extra = extra + got_extra
        step *= 2
    return blocks.reshape(-1, n_feat), extra


def on_device(queries, references, query_ids, spread, cotangent):
    n_query = queries.shape[0]
    n_feat = queries.shape[1]
    n_ref = references.shape[0]
    n_dev = lax.axis_size("ref")
    inv = 1.0 / (spread * spread)
    ref_start = lax.axis_index("ref") * n_ref
    local_ids = (query_ids - ref_start)[None, :]
    expd_low, unscaled_t, local_peak, local_total = local_forward(queries, inv[None, :], local_ids, references)
    peak, total = butterfly_stats(local_peak[0], local_total[0], n_dev)
    scale = cotangent * jnp.exp(local_peak[0] - peak) / total
    pulled = (unscaled_t * scale[None, :]).T
    query_low = queries.astype(jnp.bfloat16)
    query_aug = jnp.concatenate(
        [query_low, jnp.ones((n_query, 1), jnp.bfloat16), jnp.zeros((n_query, n_feat - 1), jnp.bfloat16)], axis=1
    )
    pushed_aug = local_backward(expd_low, scale[None, :], query_aug)
    pushed = pushed_aug[:, :n_feat]
    column = pushed_aug[:, n_feat]
    reference_grad = (pushed - references * column[:, None]) * inv
    local_terms = jnp.stack([jnp.sum(queries * pulled, axis=0), jnp.sum(references * reference_grad, axis=0)])
    own_pulled, summed_terms = halving_scatter(pulled, local_terms, n_dev)
    own_rows = n_query // n_dev
    own_start = lax.axis_index("ref") * own_rows
    own_queries = lax.dynamic_slice_in_dim(queries, own_start, own_rows, 0)
    own_cot = lax.dynamic_slice_in_dim(cotangent, own_start, own_rows, 0)
    query_grad = (own_pulled - own_queries * own_cot[:, None]) * inv
    self_terms = jnp.sum(queries * queries * cotangent[:, None], axis=0)
    summed = (summed_terms[0] - self_terms) * inv + summed_terms[1]
    weight_total = jnp.sum(cotangent)
    spread_grad = -summed / spread - weight_total / spread
    return (query_grad, reference_grad, spread_grad)


def solution(mesh):
    placed = (P("parts", None), P(("parts", "ref"), None), P("parts"), P(), P("parts"))
    return jax.shard_map(
        on_device,
        mesh=mesh,
        in_specs=placed,
        out_specs=(P(("parts", "ref"), None), P(("parts", "ref"), None), P("parts")),
        check_vma=False,
    )
```

time: 107 us -> 96.4 us (0.901)
  local copies, waits for them, and re-layouts: 12.9 us -> 5.41 us
  other arithmetic: 16.4 us -> 12.5 us
  Pallas kernels: 33.6 us -> 35.2 us
    unnamed x13, local copies, waits for them, and re-layouts: 6.47 us -> 0.36 us
    pallas_call x2 -> x0, other arithmetic: 3.12 us -> none  [local_forward(): pl.pallas_call(forward_kernel, grid=(n_query // tile,), in_specs=[pl.Bloc...]
    broadcast_in_dim x2 -> x1, local copies, waits for them, and re-layouts: 2.79 us -> 0.01 us  [on_device(): jnp.zeros((n_query, n_feat - 1), jnp.bfloat16)]
    mul x2 -> x0, local copies, waits for them, and re-layouts: 2.64 us -> none  [the longest x1 1.34 us: on_device(): 0.5 * qnorm]
    reduce_sum x1, other arithmetic: 2.88 us -> 0.37 us  [on_device(): self_terms = jnp.sum(queries * queries * cotangent[:, None], axis=0)]
    dynamic_slice x0 -> x3, local copies, waits for them, and re-layouts: none -> 2.38 us  [the longest x2 1.3 us: halving_scatter(): keep = lax.dynamic_index_in_dim(split, bit, axis=1, keepdims=False)]
    pallas_call x1, Pallas kernels: 24 us -> 26 us  [local_forward(): pl.pallas_call(forward_kernel, grid=(n_query // tile,), in_specs=[pl.Bloc...]
    convert_element_type x1 -> x0, other arithmetic: 2.05 us -> none  [on_device(): ref_low = references.astype(jnp.bfloat16)]
  transfers between devices with their start and end apart: 16 -> 16, of which waited for: 12 -> 13; matrix products, arithmetic and copies ran while one was open for 7% -> 8% of each run, Pallas kernels for 9% -> 10%
where the time goes in v4:
time: 96.4 us; the launch traced here: 95.8 us
  Pallas kernels  35.2 us (37%)
  waiting for transfers between devices  28.2 us (29%)
  starting transfers between devices  13.7 us (14%)
  other arithmetic  12.5 us (13%)
  local copies, waits for them, and re-layouts  5.41 us (6%)
    ppermute x16, waiting for transfers between devices, exchange(): return lax.ppermute(x, 'ref', [(i, i ^ step) for i in range(n_dev)])  28.2 us
    pallas_call x1, Pallas kernels, local_forward(): pl.pallas_call(forward_kernel, grid=(n_query // tile,), in_specs=[pl.Bloc...  26 us
    ppermute x16, starting transfers between devices, exchange(): return lax.ppermute(x, 'ref', [(i, i ^ step) for i in range(n_dev)])  13.7 us
    pallas_call x1, Pallas kernels, local_backward(): pl.pallas_call(backward_kernel, grid=(n_query // tile,), in_specs=[pl.Blo...  9.16 us
    reduce_sum x1, other arithmetic, on_device(): jnp.sum(references * reference_grad, axis=0)  2.54 us
  transfers between devices with their start and end apart: 16, of which 13 were waited for; matrix products, arithmetic and copies ran while one was open for 8% of the time, Pallas kernels for 10%

profile of v4, /device:TPU:0, one launch (start us, length us, event | category | flops | bytes accessed | tf_op | source)
XLA Modules:
  0.0 95.8 jit_solution(8519845558611453417)
XLA Ops:
  0.7 1.3 %fusion.11.inv_ref = f32[1,128]{1,0:T(1,128)} fusion(f32[128]{0:T(128)} %param.8), kind=kLoop, calls=%fused_computation.37 | loop fusion | flops 256 | bytes 1024 | tf_op jit(solution)/shard_map/broadcast_in_dim | solution.py:143
  1.9 1.3 %broadcast_subtract_fusion = s32[2048]{0:T(1024)} fusion(s32[2048]{0:T(1024)} %param.7, s32[]{:T(128)S(6)} %mul.99), kind=kLoop, calls=%fused_computation.22 | loop fusion | flops 2048 | bytes 16388 | tf_op jit(solution)/shard_map/sub | solution.py:142
  3.2 26.0 %shard_map.76 = (bf16[2048,2048]{1,0:T(8,128)(2,1)}, f32[128,2048]{1,0:T(8,128)}, f32[1,2048]{1,0:T(1,128)}, f32[1,2048]{1,0:T(1,128)}) custom-call(f32[2048,128]{1,0:T(8,128)} %q_ref.1, f32[1,128]{1,0:T(1,128)} %fusion.11.inv_ref, s32[1,2048]{1,0:T(1,128)} %bitcast.50, f32[2048,128]{1,0:T(8,128)} %r_ref.1), custom_call_target="tpu_custom_call" | custom-call | tf_op jit(solution)/shard_map/pallas_call | solution.py:55
  31.9 2.7 %collective-permute-start.5 = (f32[2048]{0:T(1024)S(1)}, f32[2048]{0:T(1024)S(1)}, u32[]{:S(2)}, u32[]{:S(2)}) collective-permute-start(f32[2048]{0:T(1024)S(1)} %get-tuple-element.19), channel_id=1, source_target_pairs={{0,2},{1,3},{2,0},{3,1},{4,6},{5,7},{6,4},{7,5},{8,10},{9,11},{10,... | collective-permute-start | bytes 24584 | tf_op jit(solution)/shard_map/ppermute | solution.py:103
  34.7 1.6 %collective-permute-done.5 = f32[2048]{0:T(1024)S(1)} collective-permute-done((f32[2048]{0:T(1024)S(1)}, f32[2048]{0:T(1024)S(1)}, u32[]{:S(2)}, u32[]{:S(2)}) %collective-permute-start.5) | collective-permute-done | bytes 8224 | tf_op jit(solution)/shard_map/ppermute | solution.py:103
  36.3 2.0 %collective-permute-done.1 = f32[2048]{0:T(1024)S(1)} collective-permute-done((f32[2048]{0:T(1024)S(1)}, f32[2048]{0:T(1024)S(1)}, u32[]{:S(2)}, u32[]{:S(2)}) %collective-permute-start.1) | collective-permute-done | bytes 8224 | tf_op jit(solution)/shard_map/ppermute | solution.py:103
  38.3 1.6 %collective-permute-start.6 = (f32[2048]{0:T(1024)S(1)}, f32[2048]{0:T(1024)S(1)}, u32[]{:S(2)}, u32[]{:S(2)}) collective-permute-start(f32[2048]{0:T(1024)S(1)} %get-tuple-element.17), channel_id=1, source_target_pairs={{0,4},{1,5},{2,6},{3,7},{4,0},{5,1},{6,2},{7,3},{8,12},{9,13},{10,... | collective-permute-start | bytes 24584 | tf_op jit(solution)/shard_map/ppermute | solution.py:103
  40.9 1.1 %collective-permute-done.6 = f32[2048]{0:T(1024)S(1)} collective-permute-done((f32[2048]{0:T(1024)S(1)}, f32[2048]{0:T(1024)S(1)}, u32[]{:S(2)}, u32[]{:S(2)}) %collective-permute-start.6) | collective-permute-done | bytes 8224 | tf_op jit(solution)/shard_map/ppermute | solution.py:103
  42.0 1.6 %collective-permute-done.2 = f32[2048]{0:T(1024)S(1)} collective-permute-done((f32[2048]{0:T(1024)S(1)}, f32[2048]{0:T(1024)S(1)}, u32[]{:S(2)}, u32[]{:S(2)}) %collective-permute-start.2) | collective-permute-done | bytes 8224 | tf_op jit(solution)/shard_map/ppermute | solution.py:103
  43.6 2.7 %collective-permute-start.7 = (f32[2048]{0:T(1024)S(1)}, f32[2048]{0:T(1024)S(1)}, u32[]{:S(2)}, u32[]{:S(2)}) collective-permute-start(f32[2048]{0:T(1024)S(1)} %get-tuple-element.15), channel_id=1, source_target_pairs={{0,8},{1,9},{2,10},{3,11},{4,12},{5,13},{6,14},{7,15},{8,0},{9,1},... | collective-permute-start | bytes 24584 | tf_op jit(solution)/shard_map/ppermute | solution.py:103
  46.6 1.1 %maximum_maximum_fusion.qa_ref = bf16[2048,256]{1,0:T(8,128)(2,1)} fusion(bf16[2048,128]{1,0:T(8,128)(2,1)S(1)} %get-tuple-element.22, bf16[256]{0:T(256)(128)(2,1)S(1)} %pad.4.clone, bf16[256]{0:T(256)(128)(2,1)S(1)} %pad.3.clone), kind=kLoop, calls=%fused_computation.3 | loop fusion | flops 3145728 | bytes 1573888 | tf_op jit(solution)/shard_map/concatenate | solution.py:148
  48.2 2.6 %collective-permute-done.3 = f32[2048]{0:T(1024)S(1)} collective-permute-done((f32[2048]{0:T(1024)S(1)}, f32[2048]{0:T(1024)S(1)}, u32[]{:S(2)}, u32[]{:S(2)}) %collective-permute-start.3) | collective-permute-done | bytes 8224 | tf_op jit(solution)/shard_map/ppermute | solution.py:103
  51.5 1.4 %multiply_reduce_fusion.2 = (f32[128]{0:T(128)S(1)}, f32[2048,128]{0,1:T(8,128)S(1)}) fusion(f32[2048,128]{0,1:T(8,128)S(1)} %copy.12, f32[128,2048]{1,0:T(8,128)} %get-tuple-element.7, f32[2048]{0:T(1024)S(1)} %get-tuple-element.26), kind=kLoop, calls=%fused_computation.6 | loop fusion | flops 786304 | bytes 3154432 | tf_op jit(solution)/shard_map/reduce_sum | solution.py:155
  56.3 9.2 %shard_map.77 = f32[2048,256]{1,0:T(8,128)} custom-call(bf16[2048,2048]{1,0:T(8,128)(2,1)} %get-tuple-element.10.e_ref, f32[1,2048]{1,0:T(1,128)} %bitcast.49, bf16[2048,256]{1,0:T(8,128)(2,1)} %maximum_maximum_fusion.qa_ref), custom_call_target="tpu_custom_call" | custom-call | tf_op jit(solution)/shard_map/pallas_call | solution.py:88
  65.5 1.6 %slice_reduce_fusion = f32[2048]{0:T(1024)S(1)} fusion(f32[2048,256]{1,0:T(8,128)} %shard_map.77), kind=kLoop, calls=%fused_computation | loop fusion | bytes 16384 | tf_op jit(solution)/shard_map/slice | solution.py:153
  67.1 2.5 %multiply_reduce_fusion.1 = (f32[128]{0:T(128)S(1)}, f32[2048,128]{1,0:T(8,128)}) fusion(f32[2048,128]{1,0:T(8,128)S(1)} %copy-done.1, f32[128]{0:T(128)S(1)} %multiply_divide_fusion, f32[2048]{0:T(1024)S(1)} %slice_reduce_fusion, f32[2048,256]{1,0:T(8,128)} %shard_map.77), kind=kLoop, calls=%fused_computation.5 | loop fusion | flops 1310592 | bytes 3154944 | tf_op jit(solution)/shard_map/reduce_sum | solution.py:155
  69.6 1.1 %bitcast_add_fusion = f32[8,128,128]{2,1,0:T(8,128)S(1)} fusion(f32[8,128,128]{2,1,0:T(8,128)} %collective-permute-done.8, f32[8,1,128,128]{3,2,0,1:T(8,128)S(1)} %copy.10), kind=kLoop, calls=%fused_computation.8 | loop fusion | flops 131072 | bytes 1572864 | tf_op jit(solution)/shard_map/add | solution.py:129
  72.5 1.6 %collective-permute-start.13 = (f32[2,128]{1,0:T(2,128)S(1)}, f32[2,128]{1,0:T(2,128)S(1)}, u32[]{:S(2)}, u32[]{:S(2)}) collective-permute-start(f32[2,128]{1,0:T(2,128)S(1)} %fusion.7), channel_id=1, source_target_pairs={{0,2},{1,3},{2,0},{3,1},{4,6},{5,7},{6,4},{7,5},{8,10},{9,11},{10,... | collective-permute-start | bytes 3080 | tf_op jit(solution)/shard_map/ppermute | solution.py:103
  74.1 5.4 %collective-permute-done.9 = f32[4,128,128]{2,1,0:T(8,128)S(1)} collective-permute-done((f32[4,128,128]{2,1,0:T(8,128)S(1)}, f32[4,128,128]{2,1,0:T(8,128)S(1)}, u32[]{:S(2)}, u32[]{:S(2)}) %collective-permute-start.9) | collective-permute-done | bytes 262176 | tf_op jit(solution)/shard_map/ppermute | solution.py:103
  80.1 1.6 %collective-permute-start.14 = (f32[2,128]{1,0:T(2,128)S(1)}, f32[2,128]{1,0:T(2,128)S(1)}, u32[]{:S(2)}, u32[]{:S(2)}) collective-permute-start(f32[2,128]{1,0:T(2,128)S(1)} %fusion.10), channel_id=1, source_target_pairs={{0,4},{1,5},{2,6},{3,7},{4,0},{5,1},{6,2},{7,3},{8,12},{9,13},{10,... | collective-permute-start | bytes 3080 | tf_op jit(solution)/shard_map/ppermute | solution.py:103
  81.7 2.9 %collective-permute-done.14 = f32[2,128]{1,0:T(2,128)S(1)} collective-permute-done((f32[2,128]{1,0:T(2,128)S(1)}, f32[2,128]{1,0:T(2,128)S(1)}, u32[]{:S(2)}, u32[]{:S(2)}) %collective-permute-start.14) | collective-permute-done | bytes 1056 | tf_op jit(solution)/shard_map/ppermute | solution.py:103
  85.0 4.1 %collective-permute-done.15 = f32[2,128]{1,0:T(2,128)S(1)} collective-permute-done((f32[2,128]{1,0:T(2,128)S(1)}, f32[2,128]{1,0:T(2,128)S(1)}, u32[]{:S(2)}, u32[]{:S(2)}) %collective-permute-start.15) | collective-permute-done | bytes 1056 | tf_op jit(solution)/shard_map/ppermute | solution.py:103
  89.6 1.2 %divide_subtract_fusion = f32[128]{0:T(128)} fusion(f32[128]{0:T(128)S(1)} %copy-done.5, f32[128]{0:T(128)S(1)} %get-tuple-element.21, f32[2,128]{1,0:T(2,128)S(1)} %add.116, f32[]{:T(128)} %get-tuple-element.25), kind=kLoop, calls=%fused_computation.27 | loop fusion | flops 1152 | bytes 2564 | tf_op jit(solution)/shard_map/sub | solution.py:165
  90.7 4.4 %collective-permute-done.11 = f32[1,128,128]{2,1,0:T(8,128)S(1)} collective-permute-done((f32[1,128,128]{2,1,0:T(8,128)S(1)}, f32[1,128,128]{2,1,0:T(8,128)S(1)}, u32[]{:S(2)}, u32[]{:S(2)}) %collective-permute-start.11) | collective-permute-done | bytes 65568 | tf_op jit(solution)/shard_map/ppermute | solution.py:103
  (56 shorter events, 12.3 us)
Async XLA Ops:
  0.6 39.8 %copy-start = (f32[2048,128]{1,0:T(8,128)S(1)}, f32[2048,128]{1,0:T(8,128)}, u32[]{:S(2)}) copy-start(f32[2048,128]{1,0:T(8,128)} %q_ref.1) | copy-start | bytes 3145732
  0.6 39.8 %copy-start.3 = (f32[2048]{0:T(1024)S(1)}, f32[2048]{0:T(1024)}, u32[]{:S(2)}) copy-start(f32[2048]{0:T(1024)} %param.9) | copy-start | bytes 24580
  29.3 1.6 %collective-permute-start.4 = (f32[2048]{0:T(1024)}, f32[2048]{0:T(1024)S(1)}, u32[]{:S(2)}, u32[]{:S(2)}) collective-permute-start(f32[2048]{0:T(1024)} %bitcast.57), channel_id=1, source_target_pairs={{0,1},{1,0},{2,3},{3,2},{4,5},{5,4},{6,7},{7,6},{8,9},{9,8},{10,11... | collective-permute-start | bytes 24584 | tf_op jit(solution)/shard_map/ppermute | solution.py:103
  29.8 1.4 %collective-permute-start = (f32[2048]{0:T(1024)}, f32[2048]{0:T(1024)S(1)}, u32[]{:S(2)}, u32[]{:S(2)}) collective-permute-start(f32[2048]{0:T(1024)} %bitcast.51), channel_id=1, source_target_pairs={{0,1},{1,0},{2,3},{3,2},{4,5},{5,4},{6,7},{7,6},{8,9},{9,8},{10,11... | collective-permute-start | bytes 24584 | tf_op jit(solution)/shard_map/ppermute | solution.py:103
  31.9 4.4 %collective-permute-start.5 = (f32[2048]{0:T(1024)S(1)}, f32[2048]{0:T(1024)S(1)}, u32[]{:S(2)}, u32[]{:S(2)}) collective-permute-start(f32[2048]{0:T(1024)S(1)} %get-tuple-element.19), channel_id=1, source_target_pairs={{0,2},{1,3},{2,0},{3,1},{4,6},{5,7},{6,4},{7,5},{8,10},{9,11},{10,... | collective-permute-start | bytes 24584 | tf_op jit(solution)/shard_map/ppermute | solution.py:103
  34.7 3.7 %collective-permute-start.1 = (f32[2048]{0:T(1024)S(1)}, f32[2048]{0:T(1024)S(1)}, u32[]{:S(2)}, u32[]{:S(2)}) collective-permute-start(f32[2048]{0:T(1024)S(1)} %get-tuple-element.20), channel_id=1, source_target_pairs={{0,2},{1,3},{2,0},{3,1},{4,6},{5,7},{6,4},{7,5},{8,10},{9,11},{10,... | collective-permute-start | bytes 24584 | tf_op jit(solution)/shard_map/ppermute | solution.py:103
  38.3 3.7 %collective-permute-start.6 = (f32[2048]{0:T(1024)S(1)}, f32[2048]{0:T(1024)S(1)}, u32[]{:S(2)}, u32[]{:S(2)}) collective-permute-start(f32[2048]{0:T(1024)S(1)} %get-tuple-element.17), channel_id=1, source_target_pairs={{0,4},{1,5},{2,6},{3,7},{4,0},{5,1},{6,2},{7,3},{8,12},{9,13},{10,... | collective-permute-start | bytes 24584 | tf_op jit(solution)/shard_map/ppermute | solution.py:103
  40.0 3.7 %collective-permute-start.2 = (f32[2048]{0:T(1024)S(1)}, f32[2048]{0:T(1024)S(1)}, u32[]{:S(2)}, u32[]{:S(2)}) collective-permute-start(f32[2048]{0:T(1024)S(1)} %get-tuple-element.18), channel_id=1, source_target_pairs={{0,4},{1,5},{2,6},{3,7},{4,0},{5,1},{6,2},{7,3},{8,12},{9,13},{10,... | collective-permute-start | bytes 24584 | tf_op jit(solution)/shard_map/ppermute | solution.py:103
  40.8 10.1 %copy-start.4 = (f32[1,2048]{1,0:T(1,128)S(1)}, f32[1,2048]{1,0:T(1,128)}, u32[]{:S(2)}) copy-start(f32[1,2048]{1,0:T(1,128)} %get-tuple-element.8) | copy-start | bytes 24580
  43.6 4.6 %collective-permute-start.7 = (f32[2048]{0:T(1024)S(1)}, f32[2048]{0:T(1024)S(1)}, u32[]{:S(2)}, u32[]{:S(2)}) collective-permute-start(f32[2048]{0:T(1024)S(1)} %get-tuple-element.15), channel_id=1, source_target_pairs={{0,8},{1,9},{2,10},{3,11},{4,12},{5,13},{6,14},{7,15},{8,0},{9,1},... | collective-permute-start | bytes 24584 | tf_op jit(solution)/shard_map/ppermute | solution.py:103
  46.3 4.5 %collective-permute-start.3 = (f32[2048]{0:T(1024)S(1)}, f32[2048]{0:T(1024)S(1)}, u32[]{:S(2)}, u32[]{:S(2)}) collective-permute-start(f32[2048]{0:T(1024)S(1)} %get-tuple-element.16), channel_id=1, source_target_pairs={{0,8},{1,9},{2,10},{3,11},{4,12},{5,13},{6,14},{7,15},{8,0},{9,1},... | collective-permute-start | bytes 24584 | tf_op jit(solution)/shard_map/ppermute | solution.py:103
  51.5 2.3 %copy-start.2 = (f32[2048]{0:T(1024)}, f32[2048]{0:T(1024)S(1)}, u32[]{:S(2)}) copy-start(f32[2048]{0:T(1024)S(1)} %get-tuple-element.26) | copy-start | bytes 24580
  53.8 2.0 %copy-start.5 = (f32[128]{0:T(128)S(1)}, f32[128]{0:T(128)}, u32[]{:S(2)}) copy-start(f32[128]{0:T(128)} %param.8) | copy-start | bytes 1540
  55.9 13.7 %collective-permute-start.8 = (f32[8,128,128]{2,1,0:T(8,128)}, f32[8,128,128]{2,1,0:T(8,128)}, u32[]{:S(2)}, u32[]{:S(2)}) collective-permute-start(f32[8,128,128]{2,1,0:T(8,128)} %bitcast.6), channel_id=1, source_target_pairs={{0,1},{1,0},{2,3},{3,2},{4,5},{5,4},{6,7},{7,6},{8,9},{9,8},{10,11... | collective-permute-start | bytes 1572872 | tf_op jit(solution)/shard_map/ppermute | solution.py:103
  56.3 10.7 %copy-start.1 = (f32[2048,128]{1,0:T(8,128)S(1)}, f32[2048,128]{1,0:T(8,128)}, u32[]{:S(2)}) copy-start(f32[2048,128]{1,0:T(8,128)} %r_ref.1) | copy-start | bytes 3145732
  70.7 8.7 %collective-permute-start.9 = (f32[4,128,128]{2,1,0:T(8,128)S(1)}, f32[4,128,128]{2,1,0:T(8,128)S(1)}, u32[]{:S(2)}, u32[]{:S(2)}) collective-permute-start(f32[4,128,128]{2,1,0:T(8,128)S(1)} %dynamic-slice_bitcast_fusion), channel_id=1, source_target_pairs={{0,2},{1,3},{2,0},{3,1},{4,6},{5,7},{6,4},{7,5},{8,10},{9,11},{10,... | collective-permute-start | bytes 786440 | tf_op jit(solution)/shard_map/ppermute | solution.py:103
  71.3 1.2 %collective-permute-start.12 = (f32[2,128]{1,0:T(2,128)S(1)}, f32[2,128]{1,0:T(2,128)S(1)}, u32[]{:S(2)}, u32[]{:S(2)}) collective-permute-start(f32[2,128]{1,0:T(2,128)S(1)} %pad_maximum_fusion), channel_id=1, source_target_pairs={{0,1},{1,0},{2,3},{3,2},{4,5},{5,4},{6,7},{7,6},{8,9},{9,8},{10,11... | collective-permute-start | bytes 3080 | tf_op jit(solution)/shard_map/ppermute | solution.py:103
  72.5 7.6 %collective-permute-start.13 = (f32[2,128]{1,0:T(2,128)S(1)}, f32[2,128]{1,0:T(2,128)S(1)}, u32[]{:S(2)}, u32[]{:S(2)}) collective-permute-start(f32[2,128]{1,0:T(2,128)S(1)} %fusion.7), channel_id=1, source_target_pairs={{0,2},{1,3},{2,0},{3,1},{4,6},{5,7},{6,4},{7,5},{8,10},{9,11},{10,... | collective-permute-start | bytes 3080 | tf_op jit(solution)/shard_map/ppermute | solution.py:103
  79.5 9.6 %collective-permute-start.10 = (f32[2,128,128]{2,1,0:T(8,128)S(1)}, f32[2,128,128]{2,1,0:T(8,128)S(1)}, u32[]{:S(2)}, u32[]{:S(2)}) collective-permute-start(f32[2,128,128]{2,1,0:T(8,128)S(1)} %dynamic-slice_bitcast_fusion.1), channel_id=1, source_target_pairs={{0,4},{1,5},{2,6},{3,7},{4,0},{5,1},{6,2},{7,3},{8,12},{9,13},{10,... | collective-permute-start | bytes 393224 | tf_op jit(solution)/shard_map/ppermute | solution.py:103
  80.1 4.6 %collective-permute-start.14 = (f32[2,128]{1,0:T(2,128)S(1)}, f32[2,128]{1,0:T(2,128)S(1)}, u32[]{:S(2)}, u32[]{:S(2)}) collective-permute-start(f32[2,128]{1,0:T(2,128)S(1)} %fusion.10), channel_id=1, source_target_pairs={{0,4},{1,5},{2,6},{3,7},{4,0},{5,1},{6,2},{7,3},{8,12},{9,13},{10,... | collective-permute-start | bytes 3080 | tf_op jit(solution)/shard_map/ppermute | solution.py:103
  84.7 4.5 %collective-permute-start.15 = (f32[2,128]{1,0:T(2,128)S(1)}, f32[2,128]{1,0:T(2,128)S(1)}, u32[]{:S(2)}, u32[]{:S(2)}) collective-permute-start(f32[2,128]{1,0:T(2,128)S(1)} %add.115), channel_id=1, source_target_pairs={{0,8},{1,9},{2,10},{3,11},{4,12},{5,13},{6,14},{7,15},{8,0},{9,1},... | collective-permute-start | bytes 3080 | tf_op jit(solution)/shard_map/ppermute | solution.py:103
  89.2 5.9 %collective-permute-start.11 = (f32[1,128,128]{2,1,0:T(8,128)S(1)}, f32[1,128,128]{2,1,0:T(8,128)S(1)}, u32[]{:S(2)}, u32[]{:S(2)}) collective-permute-start(f32[1,128,128]{2,1,0:T(8,128)S(1)} %constant_dynamic-slice_fusion), channel_id=1, source_target_pairs={{0,8},{1,9},{2,10},{3,11},{4,12},{5,13},{6,14},{7,15},{8,0},{9,1},... | collective-permute-start | bytes 196616 | tf_op jit(solution)/shard_map/ppermute | solution.py:103

commit v5 on v4

--- a/solution.py
+++ b/solution.py
@@ -5,10 +5,18 @@
 from jax.experimental.pallas import tpu as pltpu
 from jax.sharding import PartitionSpec as P
 
-TILE = 256
+TILE = 512
 
 
-def forward_kernel(q_ref, inv_ref, lid_ref, r_ref, e_ref, ut_ref, p_ref, t_ref, rn_sc, rlt_sc):
+def split3(x):
+    x1 = x.astype(jnp.bfloat16)
+    rest = x - x1.astype(jnp.float32)
+    x2 = rest.astype(jnp.bfloat16)
+    x3 = (rest - x2.astype(jnp.float32)).astype(jnp.bfloat16)
+    return x1, x2, x3
+
+
+def forward_kernel(q_ref, inv_ref, lid_ref, r_ref, e_ref, ut_ref, p_ref, t_ref, rn_sc, rlt_sc, rs_sc):
     inv = inv_ref[...]
 
     @pl.when(pl.program_id(0) == 0)
@@ -16,6 +24,8 @@
         refs = r_ref[...]
         rn_sc[...] = 0.5 * jnp.sum(refs * refs * inv, axis=1, keepdims=True)
         rlt_sc[...] = refs.T.astype(jnp.bfloat16)
+        r1, r2, r3 = split3(refs)
+        rs_sc[...] = jnp.concatenate([r1, r1, r1, r2, r2, r3], axis=1)
 
     q = q_ref[...]
     ones = jnp.ones((8, q.shape[1]), jnp.float32)
@@ -23,9 +33,10 @@
         ones, q * q * inv, (((1,), (1,)), ((), ())),
         precision=lax.Precision.HIGHEST, preferred_element_type=jnp.float32,
     )[0:1, :]
+    q1, q2, q3 = split3(q * inv)
     cross = lax.dot_general(
-        r_ref[...], q * inv, (((1,), (1,)), ((), ())),
-        precision=lax.Precision.HIGHEST, preferred_element_type=jnp.float32,
+        rs_sc[...], jnp.concatenate([q1, q2, q3, q1, q2, q1], axis=1), (((1,), (1,)), ((), ())),
+        preferred_element_type=jnp.float32,
     )
     score = cross - 0.5 * qnorm - rn_sc[...]
     row = lax.broadcasted_iota(jnp.int32, score.shape, 0)
@@ -76,6 +87,7 @@
         scratch_shapes=[
             pltpu.VMEM((n_ref, 1), jnp.float32),
             pltpu.VMEM((n_feat, n_ref), jnp.bfloat16),
+            pltpu.VMEM((n_ref, 6 * n_feat), jnp.bfloat16),
         ],
         compiler_params=pltpu.CompilerParams(dimension_semantics=("arbitrary",)),
     )(queries, inv, local_ids, references)

time: 96.4 us -> 86.3 us (0.90)
  Pallas kernels: 35.2 us -> 25.2 us
    pallas_call x1, Pallas kernels: 26 us -> 18 us  [local_forward(): pl.pallas_call(forward_kernel, grid=(n_query // tile,), in_specs=[pl.Bloc...]
    pallas_call x1, Pallas kernels: 9.16 us -> 7.2 us  [local_backward(): pl.pallas_call(backward_kernel, grid=(n_query // tile,), in_specs=[pl.Blo...]
  transfers between devices with their start and end apart: 16 -> 16, of which waited for: 13 -> 13; matrix products, arithmetic and copies ran while one was open for 8% -> 9% of each run, Pallas kernels for 10% -> 8%
where the time goes in v5:
time: 86.3 us; the launch traced here: 85.8 us
  waiting for transfers between devices  28.1 us (33%)
  Pallas kernels  25.2 us (29%)
  starting transfers between devices  13.7 us (16%)
  other arithmetic  12.5 us (14%)
  local copies, waits for them, and re-layouts  5.41 us (6%)
  between operations  0.88 us (1%)
    ppermute x16, waiting for transfers between devices, exchange(): return lax.ppermute(x, 'ref', [(i, i ^ step) for i in range(n_dev)])  28.1 us
    pallas_call x1, Pallas kernels, local_forward(): pl.pallas_call(forward_kernel, grid=(n_query // tile,), in_specs=[pl.Bloc...  18 us
    ppermute x16, starting transfers between devices, exchange(): return lax.ppermute(x, 'ref', [(i, i ^ step) for i in range(n_dev)])  13.7 us
    pallas_call x1, Pallas kernels, local_backward(): pl.pallas_call(backward_kernel, grid=(n_query // tile,), in_specs=[pl.Blo...  7.2 us
    reduce_sum x1, other arithmetic, on_device(): jnp.sum(references * reference_grad, axis=0)  2.54 us
  transfers between devices with their start and end apart: 16, of which 13 were waited for; matrix products, arithmetic and copies ran while one was open for 9% of the time, Pallas kernels for 8%

profile of v5, /device:TPU:0, one launch (start us, length us, event | category | flops | bytes accessed | tf_op | source)
XLA Modules:
  0.0 85.8 jit_solution(1612102213900765325)
XLA Ops:
  0.7 1.3 %fusion.11.inv_ref = f32[1,128]{1,0:T(1,128)} fusion(f32[128]{0:T(128)} %param.8), kind=kLoop, calls=%fused_computation.37 | loop fusion | flops 256 | bytes 1024 | tf_op jit(solution)/shard_map/broadcast_in_dim | solution.py:155
  1.9 1.3 %broadcast_subtract_fusion = s32[2048]{0:T(1024)} fusion(s32[2048]{0:T(1024)} %param.7, s32[]{:T(128)S(6)} %mul.99), kind=kLoop, calls=%fused_computation.22 | loop fusion | flops 2048 | bytes 16388 | tf_op jit(solution)/shard_map/sub | solution.py:154
  3.2 18.0 %shard_map.76 = (bf16[2048,2048]{1,0:T(8,128)(2,1)}, f32[128,2048]{1,0:T(8,128)}, f32[1,2048]{1,0:T(1,128)}, f32[1,2048]{1,0:T(1,128)}) custom-call(f32[2048,128]{1,0:T(8,128)} %q_ref.1, f32[1,128]{1,0:T(1,128)} %fusion.11.inv_ref, s32[1,2048]{1,0:T(1,128)} %bitcast.50, f32[2048,128]{1,0:T(8,128)} %r_ref.1), custom_call_target="tpu_custom_call" | custom-call | tf_op jit(solution)/shard_map/pallas_call | solution.py:66
  23.9 2.7 %collective-permute-start.5 = (f32[2048]{0:T(1024)S(1)}, f32[2048]{0:T(1024)S(1)}, u32[]{:S(2)}, u32[]{:S(2)}) collective-permute-start(f32[2048]{0:T(1024)S(1)} %get-tuple-element.19), channel_id=1, source_target_pairs={{0,2},{1,3},{2,0},{3,1},{4,6},{5,7},{6,4},{7,5},{8,10},{9,11},{10,... | collective-permute-start | bytes 24584 | tf_op jit(solution)/shard_map/ppermute | solution.py:115
  26.7 1.6 %collective-permute-done.5 = f32[2048]{0:T(1024)S(1)} collective-permute-done((f32[2048]{0:T(1024)S(1)}, f32[2048]{0:T(1024)S(1)}, u32[]{:S(2)}, u32[]{:S(2)}) %collective-permute-start.5) | collective-permute-done | bytes 8224 | tf_op jit(solution)/shard_map/ppermute | solution.py:115
  28.2 2.0 %collective-permute-done.1 = f32[2048]{0:T(1024)S(1)} collective-permute-done((f32[2048]{0:T(1024)S(1)}, f32[2048]{0:T(1024)S(1)}, u32[]{:S(2)}, u32[]{:S(2)}) %collective-permute-start.1) | collective-permute-done | bytes 8224 | tf_op jit(solution)/shard_map/ppermute | solution.py:115
  30.3 1.6 %collective-permute-start.6 = (f32[2048]{0:T(1024)S(1)}, f32[2048]{0:T(1024)S(1)}, u32[]{:S(2)}, u32[]{:S(2)}) collective-permute-start(f32[2048]{0:T(1024)S(1)} %get-tuple-element.17), channel_id=1, source_target_pairs={{0,4},{1,5},{2,6},{3,7},{4,0},{5,1},{6,2},{7,3},{8,12},{9,13},{10,... | collective-permute-start | bytes 24584 | tf_op jit(solution)/shard_map/ppermute | solution.py:115
  32.9 1.1 %collective-permute-done.6 = f32[2048]{0:T(1024)S(1)} collective-permute-done((f32[2048]{0:T(1024)S(1)}, f32[2048]{0:T(1024)S(1)}, u32[]{:S(2)}, u32[]{:S(2)}) %collective-permute-start.6) | collective-permute-done | bytes 8224 | tf_op jit(solution)/shard_map/ppermute | solution.py:115
  34.0 1.6 %collective-permute-done.2 = f32[2048]{0:T(1024)S(1)} collective-permute-done((f32[2048]{0:T(1024)S(1)}, f32[2048]{0:T(1024)S(1)}, u32[]{:S(2)}, u32[]{:S(2)}) %collective-permute-start.2) | collective-permute-done | bytes 8224 | tf_op jit(solution)/shard_map/ppermute | solution.py:115
  35.6 2.7 %collective-permute-start.7 = (f32[2048]{0:T(1024)S(1)}, f32[2048]{0:T(1024)S(1)}, u32[]{:S(2)}, u32[]{:S(2)}) collective-permute-start(f32[2048]{0:T(1024)S(1)} %get-tuple-element.15), channel_id=1, source_target_pairs={{0,8},{1,9},{2,10},{3,11},{4,12},{5,13},{6,14},{7,15},{8,0},{9,1},... | collective-permute-start | bytes 24584 | tf_op jit(solution)/shard_map/ppermute | solution.py:115
  38.6 1.1 %maximum_maximum_fusion.qa_ref = bf16[2048,256]{1,0:T(8,128)(2,1)} fusion(bf16[2048,128]{1,0:T(8,128)(2,1)S(1)} %get-tuple-element.22, bf16[256]{0:T(256)(128)(2,1)S(1)} %pad.4.clone, bf16[256]{0:T(256)(128)(2,1)S(1)} %pad.3.clone), kind=kLoop, calls=%fused_computation.3 | loop fusion | flops 3145728 | bytes 1573888 | tf_op jit(solution)/shard_map/concatenate | solution.py:160
  40.2 2.6 %collective-permute-done.3 = f32[2048]{0:T(1024)S(1)} collective-permute-done((f32[2048]{0:T(1024)S(1)}, f32[2048]{0:T(1024)S(1)}, u32[]{:S(2)}, u32[]{:S(2)}) %collective-permute-start.3) | collective-permute-done | bytes 8224 | tf_op jit(solution)/shard_map/ppermute | solution.py:115
  43.5 1.4 %multiply_reduce_fusion.2 = (f32[128]{0:T(128)S(1)}, f32[2048,128]{0,1:T(8,128)S(1)}) fusion(f32[2048,128]{0,1:T(8,128)S(1)} %copy.12, f32[128,2048]{1,0:T(8,128)} %get-tuple-element.7, f32[2048]{0:T(1024)S(1)} %get-tuple-element.26), kind=kLoop, calls=%fused_computation.6 | loop fusion | flops 786304 | bytes 3154432 | tf_op jit(solution)/shard_map/reduce_sum | solution.py:167
  48.3 7.2 %shard_map.77 = f32[2048,256]{1,0:T(8,128)} custom-call(bf16[2048,2048]{1,0:T(8,128)(2,1)} %get-tuple-element.10.e_ref, f32[1,2048]{1,0:T(1,128)} %bitcast.49, bf16[2048,256]{1,0:T(8,128)(2,1)} %maximum_maximum_fusion.qa_ref), custom_call_target="tpu_custom_call" | custom-call | tf_op jit(solution)/shard_map/pallas_call | solution.py:100
  55.5 1.6 %slice_reduce_fusion = f32[2048]{0:T(1024)S(1)} fusion(f32[2048,256]{1,0:T(8,128)} %shard_map.77), kind=kLoop, calls=%fused_computation | loop fusion | bytes 16384 | tf_op jit(solution)/shard_map/slice | solution.py:165
  57.1 2.5 %multiply_reduce_fusion.1 = (f32[128]{0:T(128)S(1)}, f32[2048,128]{1,0:T(8,128)}) fusion(f32[2048,128]{1,0:T(8,128)S(1)} %copy-done.1, f32[128]{0:T(128)S(1)} %multiply_divide_fusion, f32[2048]{0:T(1024)S(1)} %slice_reduce_fusion, f32[2048,256]{1,0:T(8,128)} %shard_map.77), kind=kLoop, calls=%fused_computation.5 | loop fusion | flops 1310592 | bytes 3154944 | tf_op jit(solution)/shard_map/reduce_sum | solution.py:167
  59.6 1.1 %bitcast_add_fusion = f32[8,128,128]{2,1,0:T(8,128)S(1)} fusion(f32[8,128,128]{2,1,0:T(8,128)} %collective-permute-done.8, f32[8,1,128,128]{3,2,0,1:T(8,128)S(1)} %copy.10), kind=kLoop, calls=%fused_computation.8 | loop fusion | flops 131072 | bytes 1572864 | tf_op jit(solution)/shard_map/add | solution.py:141
  62.5 1.6 %collective-permute-start.13 = (f32[2,128]{1,0:T(2,128)S(1)}, f32[2,128]{1,0:T(2,128)S(1)}, u32[]{:S(2)}, u32[]{:S(2)}) collective-permute-start(f32[2,128]{1,0:T(2,128)S(1)} %fusion.7), channel_id=1, source_target_pairs={{0,2},{1,3},{2,0},{3,1},{4,6},{5,7},{6,4},{7,5},{8,10},{9,11},{10,... | collective-permute-start | bytes 3080 | tf_op jit(solution)/shard_map/ppermute | solution.py:115
  64.1 5.4 %collective-permute-done.9 = f32[4,128,128]{2,1,0:T(8,128)S(1)} collective-permute-done((f32[4,128,128]{2,1,0:T(8,128)S(1)}, f32[4,128,128]{2,1,0:T(8,128)S(1)}, u32[]{:S(2)}, u32[]{:S(2)}) %collective-permute-start.9) | collective-permute-done | bytes 262176 | tf_op jit(solution)/shard_map/ppermute | solution.py:115
  70.1 1.6 %collective-permute-start.14 = (f32[2,128]{1,0:T(2,128)S(1)}, f32[2,128]{1,0:T(2,128)S(1)}, u32[]{:S(2)}, u32[]{:S(2)}) collective-permute-start(f32[2,128]{1,0:T(2,128)S(1)} %fusion.10), channel_id=1, source_target_pairs={{0,4},{1,5},{2,6},{3,7},{4,0},{5,1},{6,2},{7,3},{8,12},{9,13},{10,... | collective-permute-start | bytes 3080 | tf_op jit(solution)/shard_map/ppermute | solution.py:115
  71.7 2.9 %collective-permute-done.14 = f32[2,128]{1,0:T(2,128)S(1)} collective-permute-done((f32[2,128]{1,0:T(2,128)S(1)}, f32[2,128]{1,0:T(2,128)S(1)}, u32[]{:S(2)}, u32[]{:S(2)}) %collective-permute-start.14) | collective-permute-done | bytes 1056 | tf_op jit(solution)/shard_map/ppermute | solution.py:115
  75.1 4.1 %collective-permute-done.15 = f32[2,128]{1,0:T(2,128)S(1)} collective-permute-done((f32[2,128]{1,0:T(2,128)S(1)}, f32[2,128]{1,0:T(2,128)S(1)}, u32[]{:S(2)}, u32[]{:S(2)}) %collective-permute-start.15) | collective-permute-done | bytes 1056 | tf_op jit(solution)/shard_map/ppermute | solution.py:115
  79.6 1.2 %divide_subtract_fusion = f32[128]{0:T(128)} fusion(f32[128]{0:T(128)S(1)} %copy-done.5, f32[128]{0:T(128)S(1)} %get-tuple-element.21, f32[2,128]{1,0:T(2,128)S(1)} %add.116, f32[]{:T(128)} %get-tuple-element.25), kind=kLoop, calls=%fused_computation.27 | loop fusion | flops 1152 | bytes 2564 | tf_op jit(solution)/shard_map/sub | solution.py:177
  80.7 4.4 %collective-permute-done.11 = f32[1,128,128]{2,1,0:T(8,128)S(1)} collective-permute-done((f32[1,128,128]{2,1,0:T(8,128)S(1)}, f32[1,128,128]{2,1,0:T(8,128)S(1)}, u32[]{:S(2)}, u32[]{:S(2)}) %collective-permute-start.11) | collective-permute-done | bytes 65568 | tf_op jit(solution)/shard_map/ppermute | solution.py:115
  (56 shorter events, 12.3 us)
Async XLA Ops:
  0.6 31.7 %copy-start = (f32[2048,128]{1,0:T(8,128)S(1)}, f32[2048,128]{1,0:T(8,128)}, u32[]{:S(2)}) copy-start(f32[2048,128]{1,0:T(8,128)} %q_ref.1) | copy-start | bytes 3145732
  0.6 31.7 %copy-start.3 = (f32[2048]{0:T(1024)S(1)}, f32[2048]{0:T(1024)}, u32[]{:S(2)}) copy-start(f32[2048]{0:T(1024)} %param.9) | copy-start | bytes 24580
  21.2 1.6 %collective-permute-start.4 = (f32[2048]{0:T(1024)}, f32[2048]{0:T(1024)S(1)}, u32[]{:S(2)}, u32[]{:S(2)}) collective-permute-start(f32[2048]{0:T(1024)} %bitcast.57), channel_id=1, source_target_pairs={{0,1},{1,0},{2,3},{3,2},{4,5},{5,4},{6,7},{7,6},{8,9},{9,8},{10,11... | collective-permute-start | bytes 24584 | tf_op jit(solution)/shard_map/ppermute | solution.py:115
  21.8 1.4 %collective-permute-start = (f32[2048]{0:T(1024)}, f32[2048]{0:T(1024)S(1)}, u32[]{:S(2)}, u32[]{:S(2)}) collective-permute-start(f32[2048]{0:T(1024)} %bitcast.51), channel_id=1, source_target_pairs={{0,1},{1,0},{2,3},{3,2},{4,5},{5,4},{6,7},{7,6},{8,9},{9,8},{10,11... | collective-permute-start | bytes 24584 | tf_op jit(solution)/shard_map/ppermute | solution.py:115
  23.9 4.4 %collective-permute-start.5 = (f32[2048]{0:T(1024)S(1)}, f32[2048]{0:T(1024)S(1)}, u32[]{:S(2)}, u32[]{:S(2)}) collective-permute-start(f32[2048]{0:T(1024)S(1)} %get-tuple-element.19), channel_id=1, source_target_pairs={{0,2},{1,3},{2,0},{3,1},{4,6},{5,7},{6,4},{7,5},{8,10},{9,11},{10,... | collective-permute-start | bytes 24584 | tf_op jit(solution)/shard_map/ppermute | solution.py:115
  26.6 3.7 %collective-permute-start.1 = (f32[2048]{0:T(1024)S(1)}, f32[2048]{0:T(1024)S(1)}, u32[]{:S(2)}, u32[]{:S(2)}) collective-permute-start(f32[2048]{0:T(1024)S(1)} %get-tuple-element.20), channel_id=1, source_target_pairs={{0,2},{1,3},{2,0},{3,1},{4,6},{5,7},{6,4},{7,5},{8,10},{9,11},{10,... | collective-permute-start | bytes 24584 | tf_op jit(solution)/shard_map/ppermute | solution.py:115
  30.3 3.7 %collective-permute-start.6 = (f32[2048]{0:T(1024)S(1)}, f32[2048]{0:T(1024)S(1)}, u32[]{:S(2)}, u32[]{:S(2)}) collective-permute-start(f32[2048]{0:T(1024)S(1)} %get-tuple-element.17), channel_id=1, source_target_pairs={{0,4},{1,5},{2,6},{3,7},{4,0},{5,1},{6,2},{7,3},{8,12},{9,13},{10,... | collective-permute-start | bytes 24584 | tf_op jit(solution)/shard_map/ppermute | solution.py:115
  31.9 3.7 %collective-permute-start.2 = (f32[2048]{0:T(1024)S(1)}, f32[2048]{0:T(1024)S(1)}, u32[]{:S(2)}, u32[]{:S(2)}) collective-permute-start(f32[2048]{0:T(1024)S(1)} %get-tuple-element.18), channel_id=1, source_target_pairs={{0,4},{1,5},{2,6},{3,7},{4,0},{5,1},{6,2},{7,3},{8,12},{9,13},{10,... | collective-permute-start | bytes 24584 | tf_op jit(solution)/shard_map/ppermute | solution.py:115
  32.7 10.1 %copy-start.4 = (f32[1,2048]{1,0:T(1,128)S(1)}, f32[1,2048]{1,0:T(1,128)}, u32[]{:S(2)}) copy-start(f32[1,2048]{1,0:T(1,128)} %get-tuple-element.8) | copy-start | bytes 24580
  35.6 4.6 %collective-permute-start.7 = (f32[2048]{0:T(1024)S(1)}, f32[2048]{0:T(1024)S(1)}, u32[]{:S(2)}, u32[]{:S(2)}) collective-permute-start(f32[2048]{0:T(1024)S(1)} %get-tuple-element.15), channel_id=1, source_target_pairs={{0,8},{1,9},{2,10},{3,11},{4,12},{5,13},{6,14},{7,15},{8,0},{9,1},... | collective-permute-start | bytes 24584 | tf_op jit(solution)/shard_map/ppermute | solution.py:115
  38.3 4.5 %collective-permute-start.3 = (f32[2048]{0:T(1024)S(1)}, f32[2048]{0:T(1024)S(1)}, u32[]{:S(2)}, u32[]{:S(2)}) collective-permute-start(f32[2048]{0:T(1024)S(1)} %get-tuple-element.16), channel_id=1, source_target_pairs={{0,8},{1,9},{2,10},{3,11},{4,12},{5,13},{6,14},{7,15},{8,0},{9,1},... | collective-permute-start | bytes 24584 | tf_op jit(solution)/shard_map/ppermute | solution.py:115
  43.5 2.3 %copy-start.2 = (f32[2048]{0:T(1024)}, f32[2048]{0:T(1024)S(1)}, u32[]{:S(2)}) copy-start(f32[2048]{0:T(1024)S(1)} %get-tuple-element.26) | copy-start | bytes 24580
  45.8 2.0 %copy-start.5 = (f32[128]{0:T(128)S(1)}, f32[128]{0:T(128)}, u32[]{:S(2)}) copy-start(f32[128]{0:T(128)} %param.8) | copy-start | bytes 1540
  47.8 11.8 %collective-permute-start.8 = (f32[8,128,128]{2,1,0:T(8,128)}, f32[8,128,128]{2,1,0:T(8,128)}, u32[]{:S(2)}, u32[]{:S(2)}) collective-permute-start(f32[8,128,128]{2,1,0:T(8,128)} %bitcast.6), channel_id=1, source_target_pairs={{0,1},{1,0},{2,3},{3,2},{4,5},{5,4},{6,7},{7,6},{8,9},{9,8},{10,11... | collective-permute-start | bytes 1572872 | tf_op jit(solution)/shard_map/ppermute | solution.py:115
  48.3 8.8 %copy-start.1 = (f32[2048,128]{1,0:T(8,128)S(1)}, f32[2048,128]{1,0:T(8,128)}, u32[]{:S(2)}) copy-start(f32[2048,128]{1,0:T(8,128)} %r_ref.1) | copy-start | bytes 3145732
  60.7 8.7 %collective-permute-start.9 = (f32[4,128,128]{2,1,0:T(8,128)S(1)}, f32[4,128,128]{2,1,0:T(8,128)S(1)}, u32[]{:S(2)}, u32[]{:S(2)}) collective-permute-start(f32[4,128,128]{2,1,0:T(8,128)S(1)} %dynamic-slice_bitcast_fusion), channel_id=1, source_target_pairs={{0,2},{1,3},{2,0},{3,1},{4,6},{5,7},{6,4},{7,5},{8,10},{9,11},{10,... | collective-permute-start | bytes 786440 | tf_op jit(solution)/shard_map/ppermute | solution.py:115
  61.3 1.2 %collective-permute-start.12 = (f32[2,128]{1,0:T(2,128)S(1)}, f32[2,128]{1,0:T(2,128)S(1)}, u32[]{:S(2)}, u32[]{:S(2)}) collective-permute-start(f32[2,128]{1,0:T(2,128)S(1)} %pad_maximum_fusion), channel_id=1, source_target_pairs={{0,1},{1,0},{2,3},{3,2},{4,5},{5,4},{6,7},{7,6},{8,9},{9,8},{10,11... | collective-permute-start | bytes 3080 | tf_op jit(solution)/shard_map/ppermute | solution.py:115
  62.5 7.6 %collective-permute-start.13 = (f32[2,128]{1,0:T(2,128)S(1)}, f32[2,128]{1,0:T(2,128)S(1)}, u32[]{:S(2)}, u32[]{:S(2)}) collective-permute-start(f32[2,128]{1,0:T(2,128)S(1)} %fusion.7), channel_id=1, source_target_pairs={{0,2},{1,3},{2,0},{3,1},{4,6},{5,7},{6,4},{7,5},{8,10},{9,11},{10,... | collective-permute-start | bytes 3080 | tf_op jit(solution)/shard_map/ppermute | solution.py:115
  69.5 9.6 %collective-permute-start.10 = (f32[2,128,128]{2,1,0:T(8,128)S(1)}, f32[2,128,128]{2,1,0:T(8,128)S(1)}, u32[]{:S(2)}, u32[]{:S(2)}) collective-permute-start(f32[2,128,128]{2,1,0:T(8,128)S(1)} %dynamic-slice_bitcast_fusion.1), channel_id=1, source_target_pairs={{0,4},{1,5},{2,6},{3,7},{4,0},{5,1},{6,2},{7,3},{8,12},{9,13},{10,... | collective-permute-start | bytes 393224 | tf_op jit(solution)/shard_map/ppermute | solution.py:115
  70.1 4.6 %collective-permute-start.14 = (f32[2,128]{1,0:T(2,128)S(1)}, f32[2,128]{1,0:T(2,128)S(1)}, u32[]{:S(2)}, u32[]{:S(2)}) collective-permute-start(f32[2,128]{1,0:T(2,128)S(1)} %fusion.10), channel_id=1, source_target_pairs={{0,4},{1,5},{2,6},{3,7},{4,0},{5,1},{6,2},{7,3},{8,12},{9,13},{10,... | collective-permute-start | bytes 3080 | tf_op jit(solution)/shard_map/ppermute | solution.py:115
  74.7 4.5 %collective-permute-start.15 = (f32[2,128]{1,0:T(2,128)S(1)}, f32[2,128]{1,0:T(2,128)S(1)}, u32[]{:S(2)}, u32[]{:S(2)}) collective-permute-start(f32[2,128]{1,0:T(2,128)S(1)} %add.115), channel_id=1, source_target_pairs={{0,8},{1,9},{2,10},{3,11},{4,12},{5,13},{6,14},{7,15},{8,0},{9,1},... | collective-permute-start | bytes 3080 | tf_op jit(solution)/shard_map/ppermute | solution.py:115
  79.2 5.9 %collective-permute-start.11 = (f32[1,128,128]{2,1,0:T(8,128)S(1)}, f32[1,128,128]{2,1,0:T(8,128)S(1)}, u32[]{:S(2)}, u32[]{:S(2)}) collective-permute-start(f32[1,128,128]{2,1,0:T(8,128)S(1)} %constant_dynamic-slice_fusion), channel_id=1, source_target_pairs={{0,8},{1,9},{2,10},{3,11},{4,12},{5,13},{6,14},{7,15},{8,0},{9,1},... | collective-permute-start | bytes 196616 | tf_op jit(solution)/shard_map/ppermute | solution.py:115

commit v6 on v5

--- a/solution.py
+++ b/solution.py
@@ -118,7 +118,8 @@
 def butterfly_stats(peak, total, n_dev):
     step = 1
     while step < n_dev:
-        other_peak, other_total = exchange((peak, total), n_dev, step)
+        other = exchange(jnp.stack([peak, total]), n_dev, step)
+        other_peak, other_total = other[0], other[1]
         new_peak = jnp.maximum(peak, other_peak)
         total = total * jnp.exp(peak - new_peak) + other_total * jnp.exp(other_peak - new_peak)
         peak = new_peak
@@ -137,9 +138,10 @@
         bit = (me // step) % 2
         keep = lax.dynamic_index_in_dim(split, bit, axis=1, keepdims=False)
         send = lax.dynamic_index_in_dim(split, 1 - bit, axis=1, keepdims=False)
-        got, got_extra = exchange((send, extra), n_dev, step)
-        blocks = keep + got
-        extra = extra + got_extra
+        n_send = send.shape[0] * send.shape[1]
+        got = exchange(jnp.concatenate([send.reshape(n_send, n_feat), extra]), n_dev, step)
+        blocks = keep + got[:n_send].reshape(keep.shape)
+        extra = extra + got[n_send:]
         step *= 2
     return blocks.reshape(-1, n_feat), extra
 

time: 86.3 us -> 84 us (0.973)
  waiting for transfers between devices: 28.1 us -> 16.8 us
  local copies, waits for them, and re-layouts: 5.41 us -> 12.1 us
  starting transfers between devices: 13.7 us -> 15.4 us
    ppermute x16 -> x8, waiting for transfers between devices: 28.1 us -> 16.8 us  [exchange(): return lax.ppermute(x, 'ref', [(i, i ^ step) for i in range(n_dev)])]
    dynamic_slice x2, local copies, waits for them, and re-layouts: 1.3 us -> 3.78 us  [halving_scatter(): keep = lax.dynamic_index_in_dim(split, bit, axis=1, keepdims=False)]
    ppermute x16 -> x8, starting transfers between devices: 13.7 us -> 15.4 us  [exchange(): return lax.ppermute(x, 'ref', [(i, i ^ step) for i in range(n_dev)])]
    unnamed x13 -> x16, local copies, waits for them, and re-layouts: 0.36 us -> 1.61 us
    concatenate x0 -> x1, local copies, waits for them, and re-layouts: none -> 1.08 us  [halving_scatter(): jnp.concatenate([send.reshape(n_send, n_feat), extra])]
    add x7, other arithmetic: 1.17 us -> 0.18 us  [the longest x3 0.15 us: halving_scatter(): blocks = keep + got[:n_send].reshape(keep.shape)]
    another operation x1, local copies, waits for them, and re-layouts: 0.89 us -> 1.86 us  [halving_scatter(): split = blocks.reshape(lead, 2, -1, n_feat)]
    dynamic_slice x1 -> x2, local copies, waits for them, and re-layouts: 1.09 us -> 1.94 us  [halving_scatter(): send = lax.dynamic_index_in_dim(split, 1 - bit, axis=1, keepdims=False)]
  transfers between devices with their start and end apart: 16 -> 8, of which waited for: 13 -> 8; matrix products, arithmetic and copies ran while one was open for 9% -> 4% of each run, Pallas kernels for 8% -> 0%
where the time goes in v6:
time: 84 us; the launch traced here: 83.5 us
  Pallas kernels  25.1 us (30%)
  waiting for transfers between devices  16.8 us (20%)
  starting transfers between devices  15.4 us (18%)
  other arithmetic  13.1 us (16%)
  local copies, waits for them, and re-layouts  12.1 us (14%)
  between operations  0.94 us (1%)
    pallas_call x1, Pallas kernels, local_forward(): pl.pallas_call(forward_kernel, grid=(n_query // tile,), in_specs=[pl.Bloc...  18 us
    ppermute x8, waiting for transfers between devices, exchange(): return lax.ppermute(x, 'ref', [(i, i ^ step) for i in range(n_dev)])  16.8 us
    ppermute x8, starting transfers between devices, exchange(): return lax.ppermute(x, 'ref', [(i, i ^ step) for i in range(n_dev)])  15.4 us
    pallas_call x1, Pallas kernels, local_backward(): pl.pallas_call(backward_kernel, grid=(n_query // tile,), in_specs=[pl.Blo...  7.11 us
    dynamic_slice x2, local copies, waits for them, and re-layouts, halving_scatter(): keep = lax.dynamic_index_in_dim(split, bit, axis=1, keepdims=False)  3.78 us
    reduce_sum x1, other arithmetic, on_device(): jnp.sum(references * reference_grad, axis=0)  2.54 us
    dynamic_slice x2, local copies, waits for them, and re-layouts, halving_scatter(): send = lax.dynamic_index_in_dim(split, 1 - bit, axis=1, keepdims=False)  1.94 us
    another operation x1, local copies, waits for them, and re-layouts, halving_scatter(): split = blocks.reshape(lead, 2, -1, n_feat)  1.86 us
  transfers between devices with their start and end apart: 8, of which 8 were waited for; matrix products, arithmetic and copies ran while one was open for 4% of the time, Pallas kernels for 0%

profile of v6, /device:TPU:0, one launch (start us, length us, event | category | flops | bytes accessed | tf_op | source)
XLA Modules:
  0.0 83.5 jit_solution(15972288356565356177)
XLA Ops:
  0.7 1.3 %fusion.20.inv_ref = f32[1,128]{1,0:T(1,128)} fusion(f32[128]{0:T(128)} %param.8), kind=kLoop, calls=%fused_computation.63 | loop fusion | flops 256 | bytes 1024 | tf_op jit(solution)/shard_map/broadcast_in_dim | solution.py:157
  1.9 1.3 %broadcast_subtract_fusion = s32[2048]{0:T(1024)} fusion(s32[2048]{0:T(1024)} %param.7, s32[]{:T(128)S(6)} %mul.123), kind=kLoop, calls=%fused_computation.41 | loop fusion | flops 2048 | bytes 16388 | tf_op jit(solution)/shard_map/sub | solution.py:156
  3.2 18.0 %shard_map.76 = (bf16[2048,2048]{1,0:T(8,128)(2,1)}, f32[128,2048]{1,0:T(8,128)}, f32[1,2048]{1,0:T(1,128)}, f32[1,2048]{1,0:T(1,128)}) custom-call(f32[2048,128]{1,0:T(8,128)} %q_ref.1, f32[1,128]{1,0:T(1,128)} %fusion.20.inv_ref, s32[1,2048]{1,0:T(1,128)} %bitcast.63, f32[2048,128]{1,0:T(8,128)} %r_ref.1), custom_call_target="tpu_custom_call" | custom-call | tf_op jit(solution)/shard_map/pallas_call | solution.py:66
  24.1 2.9 %collective-permute-start.1 = (f32[2,2048]{1,0:T(2,128)S(1)}, f32[2,2048]{1,0:T(2,128)S(1)}, u32[]{:S(2)}, u32[]{:S(2)}) collective-permute-start(f32[2,2048]{1,0:T(2,128)S(1)} %pad_maximum_fusion.4), channel_id=1, source_target_pairs={{0,2},{1,3},{2,0},{3,1},{4,6},{5,7},{6,4},{7,5},{8,10},{9,11},{10,... | collective-permute-start | bytes 49160 | tf_op jit(solution)/shard_map/ppermute | solution.py:115
  27.5 1.2 %collective-permute-done.1 = f32[2,2048]{1,0:T(2,128)S(1)} collective-permute-done((f32[2,2048]{1,0:T(2,128)S(1)}, f32[2,2048]{1,0:T(2,128)S(1)}, u32[]{:S(2)}, u32[]{:S(2)}) %collective-permute-start.1) | collective-permute-done | bytes 16416 | tf_op jit(solution)/shard_map/ppermute | solution.py:115
  28.8 2.1 %collective-permute-start.2 = (f32[2,2048]{1,0:T(2,128)S(1)}, f32[2,2048]{1,0:T(2,128)S(1)}, u32[]{:S(2)}, u32[]{:S(2)}) collective-permute-start(f32[2,2048]{1,0:T(2,128)S(1)} %pad_maximum_fusion.5), channel_id=1, source_target_pairs={{0,4},{1,5},{2,6},{3,7},{4,0},{5,1},{6,2},{7,3},{8,12},{9,13},{10,... | collective-permute-start | bytes 49160 | tf_op jit(solution)/shard_map/ppermute | solution.py:115
  32.7 3.1 %collective-permute-start.3 = (f32[2,2048]{1,0:T(2,128)S(1)}, f32[2,2048]{1,0:T(2,128)S(1)}, u32[]{:S(2)}, u32[]{:S(2)}) collective-permute-start(f32[2,2048]{1,0:T(2,128)S(1)} %pad_maximum_fusion.6), channel_id=1, source_target_pairs={{0,8},{1,9},{2,10},{3,11},{4,12},{5,13},{6,14},{7,15},{8,0},{9,1},... | collective-permute-start | bytes 49160 | tf_op jit(solution)/shard_map/ppermute | solution.py:115
  36.2 1.3 %collective-permute-done.3 = f32[2,2048]{1,0:T(2,128)S(1)} collective-permute-done((f32[2,2048]{1,0:T(2,128)S(1)}, f32[2,2048]{1,0:T(2,128)S(1)}, u32[]{:S(2)}, u32[]{:S(2)}) %collective-permute-start.3) | collective-permute-done | bytes 16416 | tf_op jit(solution)/shard_map/ppermute | solution.py:115
  37.6 1.3 %fusion.19 = (f32[]{:T(128)}, f32[2048]{0:T(1024)}) fusion(f32[2048]{0:T(1024)S(1)} %copy-done.5, f32[2048]{0:T(1024)S(1)} %bitcast.65, f32[2048]{0:T(1024)S(1)} %bitcast.64, f32[2048]{0:T(1024)S(1)} %bitcast.71, f32[2048]{0:T(1024)S(1)} %bitcast.70, f32[2048]{0:T(1024)S(1)} %bitcast.69, f32[2048]{0:T(1024)S(1)} %bitcast.68, f32[2048]{0:T(1024)S(1)} %bitcast.66, ...), kind=kLoop, calls=%fused_computation.62 | loop fusion | flops 57343 | bytes 98308 | tf_op jit(solution)/shard_map/reduce_sum | solution.py:178
  38.9 7.1 %shard_map.77 = f32[2048,256]{1,0:T(8,128)} custom-call(bf16[2048,2048]{1,0:T(8,128)(2,1)} %get-tuple-element.10.e_ref, f32[1,2048]{1,0:T(1,128)} %bitcast.60, bf16[2048,256]{1,0:T(8,128)(2,1)} %maximum_maximum_fusion.qa_ref), custom_call_target="tpu_custom_call" | custom-call | tf_op jit(solution)/shard_map/pallas_call | solution.py:100
  46.0 1.6 %slice_reduce_fusion = f32[2048]{0:T(1024)S(1)} fusion(f32[2048,256]{1,0:T(8,128)} %shard_map.77), kind=kLoop, calls=%fused_computation | loop fusion | bytes 16384 | tf_op jit(solution)/shard_map/slice | solution.py:167
  47.6 1.4 %multiply_reduce_fusion.2 = (f32[128]{0:T(128)S(1)}, f32[2048,128]{0,1:T(8,128)S(1)}) fusion(f32[2048,128]{0,1:T(8,128)S(1)} %copy.14, f32[128,2048]{1,0:T(8,128)} %get-tuple-element.7, f32[2048]{0:T(1024)S(1)} %copy-done.2), kind=kLoop, calls=%fused_computation.6 | loop fusion | flops 786304 | bytes 3154432 | tf_op jit(solution)/shard_map/reduce_sum | solution.py:169
  49.0 1.9 %reshape_reshape.3 = f32[8,2,128,128]{2,1,0,3:T(2,128)} reshape(f32[2048,128]{0,1:T(8,128)S(1)} %get-tuple-element.14) | data formatting | bytes 2097152 | tf_op jit(solution)/shard_map/reshape;reshape | solution.py:137
  50.9 3.7 %constant_dynamic-slice_fusion.4 = (f32[8,1,128,128]{2,1,0,3:T(1,128)}, f32[8,1,128,128]{2,1,0,3:T(1,128)}) fusion(f32[8,2,128,128]{2,1,0,3:T(2,128)} %reshape_reshape.3, s32[]{:T(128)S(6)} %select_n.63, s32[]{:T(128)S(6)} %select_n.64), kind=kLoop, calls=%fused_computation.46 | loop fusion | bytes 2097160 | tf_op jit(solution)/shard_map/jit(dynamic_index_in_dim)/dynamic_slice | solution.py:139
  54.6 1.9 %copy.13 = f32[8,1,128,128]{3,2,0,1:T(8,128)} copy(f32[8,1,128,128]{2,1,0,3:T(1,128)} %get-tuple-element.22) | data formatting | bytes 1048576 | tf_op jit(solution)/shard_map/jit(dynamic_index_in_dim)/dynamic_slice | solution.py:140
  56.6 2.5 %multiply_reduce_fusion.1 = (f32[128]{0:T(128)S(1)}, f32[2048,128]{1,0:T(8,128)}) fusion(f32[2048,128]{1,0:T(8,128)} %r_ref.1, f32[128]{0:T(128)S(1)} %multiply_divide_fusion, f32[2048]{0:T(1024)S(1)} %slice_reduce_fusion, f32[2048,256]{1,0:T(8,128)S(1)} %copy-done.1), kind=kLoop, calls=%fused_computation.5 | loop fusion | flops 1310592 | bytes 3154944 | tf_op jit(solution)/shard_map/reduce_sum | solution.py:169
  60.3 1.2 %copy.15 = f32[8,1,128,128]{3,2,0,1:T(8,128)S(1)} copy(f32[8,1,128,128]{2,1,0,3:T(1,128)} %get-tuple-element.21) | data formatting | bytes 1048576
  62.4 1.9 %collective-permute-start.5 = (f32[514,128]{1,0:T(8,128)S(1)}, f32[514,128]{1,0:T(8,128)S(1)}, u32[]{:S(2)}, u32[]{:S(2)}) collective-permute-start(f32[514,128]{1,0:T(8,128)S(1)} %pad_maximum_fusion), channel_id=1, source_target_pairs={{0,2},{1,3},{2,0},{3,1},{4,6},{5,7},{6,4},{7,5},{8,10},{9,11},{10,... | collective-permute-start | bytes 789512 | tf_op jit(solution)/shard_map/ppermute | solution.py:115
  64.3 6.7 %collective-permute-done.5 = f32[514,128]{1,0:T(8,128)S(1)} collective-permute-done((f32[514,128]{1,0:T(8,128)S(1)}, f32[514,128]{1,0:T(8,128)S(1)}, u32[]{:S(2)}, u32[]{:S(2)}) %collective-permute-start.5) | collective-permute-done | bytes 263200 | tf_op jit(solution)/shard_map/ppermute | solution.py:115
  71.1 1.9 %collective-permute-start.6 = (f32[258,128]{1,0:T(8,128)S(1)}, f32[258,128]{1,0:T(8,128)S(1)}, u32[]{:S(2)}, u32[]{:S(2)}) collective-permute-start(f32[258,128]{1,0:T(8,128)S(1)} %pad_maximum_fusion.1), channel_id=1, source_target_pairs={{0,4},{1,5},{2,6},{3,7},{4,0},{5,1},{6,2},{7,3},{8,12},{9,13},{10,... | collective-permute-start | bytes 396296 | tf_op jit(solution)/shard_map/ppermute | solution.py:115
  73.0 3.2 %collective-permute-done.6 = f32[258,128]{1,0:T(8,128)S(1)} collective-permute-done((f32[258,128]{1,0:T(8,128)S(1)}, f32[258,128]{1,0:T(8,128)S(1)}, u32[]{:S(2)}, u32[]{:S(2)}) %collective-permute-start.6) | collective-permute-done | bytes 132128 | tf_op jit(solution)/shard_map/ppermute | solution.py:115
  76.3 2.9 %collective-permute-start.7 = (f32[130,128]{1,0:T(8,128)S(1)}, f32[130,128]{1,0:T(8,128)S(1)}, u32[]{:S(2)}, u32[]{:S(2)}) collective-permute-start(f32[130,128]{1,0:T(8,128)S(1)} %pad_maximum_fusion.2), channel_id=1, source_target_pairs={{0,8},{1,9},{2,10},{3,11},{4,12},{5,13},{6,14},{7,15},{8,0},{9,1},... | collective-permute-start | bytes 199688 | tf_op jit(solution)/shard_map/ppermute | solution.py:115
  79.2 2.3 %collective-permute-done.7 = f32[130,128]{1,0:T(8,128)S(1)} collective-permute-done((f32[130,128]{1,0:T(8,128)S(1)}, f32[130,128]{1,0:T(8,128)S(1)}, u32[]{:S(2)}, u32[]{:S(2)}) %collective-permute-start.7) | collective-permute-done | bytes 66592 | tf_op jit(solution)/shard_map/ppermute | solution.py:115
  81.5 1.2 %divide_subtract_fusion = f32[128]{0:T(128)} fusion(f32[128]{0:T(128)S(1)} %copy-done.6, f32[128]{0:T(128)S(1)} %get-tuple-element.19, f32[2,128]{1,0:T(2,128)S(1)} %slice_add_fusion.1, f32[]{:T(128)} %get-tuple-element.35), kind=kLoop, calls=%fused_computation.51 | loop fusion | flops 1152 | bytes 2564 | tf_op jit(solution)/shard_map/sub | solution.py:179
  (53 shorter events, 8.5 us)
Async XLA Ops:
  0.6 26.4 %copy-start = (f32[2048,128]{1,0:T(8,128)S(1)}, f32[2048,128]{1,0:T(8,128)}, u32[]{:S(2)}) copy-start(f32[2048,128]{1,0:T(8,128)} %q_ref.1) | copy-start | bytes 3145732
  0.6 26.4 %copy-start.5 = (f32[2048]{0:T(1024)S(1)}, f32[2048]{0:T(1024)}, u32[]{:S(2)}) copy-start(f32[2048]{0:T(1024)} %param.9) | copy-start | bytes 24580
  21.2 14.7 %copy-start.6 = (f32[128]{0:T(128)S(1)}, f32[128]{0:T(128)}, u32[]{:S(2)}) copy-start(f32[128]{0:T(128)} %param.8) | copy-start | bytes 1540
  21.9 1.4 %collective-permute-start = (f32[2,2048]{1,0:T(2,128)S(1)}, f32[2,2048]{1,0:T(2,128)S(1)}, u32[]{:S(2)}, u32[]{:S(2)}) collective-permute-start(f32[2,2048]{1,0:T(2,128)S(1)} %pad_maximum_fusion.3), channel_id=1, source_target_pairs={{0,1},{1,0},{2,3},{3,2},{4,5},{5,4},{6,7},{7,6},{8,9},{9,8},{10,11... | collective-permute-start | bytes 49160 | tf_op jit(solution)/shard_map/ppermute | solution.py:115
  24.1 4.6 %collective-permute-start.1 = (f32[2,2048]{1,0:T(2,128)S(1)}, f32[2,2048]{1,0:T(2,128)S(1)}, u32[]{:S(2)}, u32[]{:S(2)}) collective-permute-start(f32[2,2048]{1,0:T(2,128)S(1)} %pad_maximum_fusion.4), channel_id=1, source_target_pairs={{0,2},{1,3},{2,0},{3,1},{4,6},{5,7},{6,4},{7,5},{8,10},{9,11},{10,... | collective-permute-start | bytes 49160 | tf_op jit(solution)/shard_map/ppermute | solution.py:115
  27.4 10.2 %copy-start.3 = (f32[1,2048]{1,0:T(1,128)S(1)}, f32[1,2048]{1,0:T(1,128)}, u32[]{:S(2)}) copy-start(f32[1,2048]{1,0:T(1,128)} %get-tuple-element.8) | copy-start | bytes 24580
  27.4 10.2 %copy-start.4 = (f32[1,2048]{1,0:T(1,128)S(1)}, f32[1,2048]{1,0:T(1,128)}, u32[]{:S(2)}) copy-start(f32[1,2048]{1,0:T(1,128)} %get-tuple-element.9) | copy-start | bytes 24580
  28.8 3.9 %collective-permute-start.2 = (f32[2,2048]{1,0:T(2,128)S(1)}, f32[2,2048]{1,0:T(2,128)S(1)}, u32[]{:S(2)}, u32[]{:S(2)}) collective-permute-start(f32[2,2048]{1,0:T(2,128)S(1)} %pad_maximum_fusion.5), channel_id=1, source_target_pairs={{0,4},{1,5},{2,6},{3,7},{4,0},{5,1},{6,2},{7,3},{8,12},{9,13},{10,... | collective-permute-start | bytes 49160 | tf_op jit(solution)/shard_map/ppermute | solution.py:115
  32.7 4.8 %collective-permute-start.3 = (f32[2,2048]{1,0:T(2,128)S(1)}, f32[2,2048]{1,0:T(2,128)S(1)}, u32[]{:S(2)}, u32[]{:S(2)}) collective-permute-start(f32[2,2048]{1,0:T(2,128)S(1)} %pad_maximum_fusion.6), channel_id=1, source_target_pairs={{0,8},{1,9},{2,10},{3,11},{4,12},{5,13},{6,14},{7,15},{8,0},{9,1},... | collective-permute-start | bytes 49160 | tf_op jit(solution)/shard_map/ppermute | solution.py:115
  38.9 8.7 %copy-start.2 = (f32[2048]{0:T(1024)S(1)}, f32[2048]{0:T(1024)}, u32[]{:S(2)}) copy-start(f32[2048]{0:T(1024)} %get-tuple-element.36) | copy-start | bytes 24580
  50.9 5.7 %copy-start.1 = (f32[2048,256]{1,0:T(8,128)S(1)}, f32[2048,256]{1,0:T(8,128)}, u32[]{:S(2)}) copy-start(f32[2048,256]{1,0:T(8,128)} %shard_map.77) | copy-start | bytes 6291460
  60.2 2.0 %collective-permute-start.4 = (f32[1026,128]{1,0:T(8,128)S(1)}, f32[1026,128]{1,0:T(8,128)S(1)}, u32[]{:S(2)}, u32[]{:S(2)}) collective-permute-start(f32[1026,128]{1,0:T(8,128)S(1)} %concatenate.17), channel_id=1, source_target_pairs={{0,1},{1,0},{2,3},{3,2},{4,5},{5,4},{6,7},{7,6},{8,9},{9,8},{10,11... | collective-permute-start | bytes 1575944 | tf_op jit(solution)/shard_map/ppermute | solution.py:115
  62.4 8.6 %collective-permute-start.5 = (f32[514,128]{1,0:T(8,128)S(1)}, f32[514,128]{1,0:T(8,128)S(1)}, u32[]{:S(2)}, u32[]{:S(2)}) collective-permute-start(f32[514,128]{1,0:T(8,128)S(1)} %pad_maximum_fusion), channel_id=1, source_target_pairs={{0,2},{1,3},{2,0},{3,1},{4,6},{5,7},{6,4},{7,5},{8,10},{9,11},{10,... | collective-permute-start | bytes 789512 | tf_op jit(solution)/shard_map/ppermute | solution.py:115
  71.1 5.1 %collective-permute-start.6 = (f32[258,128]{1,0:T(8,128)S(1)}, f32[258,128]{1,0:T(8,128)S(1)}, u32[]{:S(2)}, u32[]{:S(2)}) collective-permute-start(f32[258,128]{1,0:T(8,128)S(1)} %pad_maximum_fusion.1), channel_id=1, source_target_pairs={{0,4},{1,5},{2,6},{3,7},{4,0},{5,1},{6,2},{7,3},{8,12},{9,13},{10,... | collective-permute-start | bytes 396296 | tf_op jit(solution)/shard_map/ppermute | solution.py:115
  76.3 5.3 %collective-permute-start.7 = (f32[130,128]{1,0:T(8,128)S(1)}, f32[130,128]{1,0:T(8,128)S(1)}, u32[]{:S(2)}, u32[]{:S(2)}) collective-permute-start(f32[130,128]{1,0:T(8,128)S(1)} %pad_maximum_fusion.2), channel_id=1, source_target_pairs={{0,8},{1,9},{2,10},{3,11},{4,12},{5,13},{6,14},{7,15},{8,0},{9,1},... | collective-permute-start | bytes 199688 | tf_op jit(solution)/shard_map/ppermute | solution.py:115

commit v7 on v6

--- a/solution.py
+++ b/solution.py
@@ -1,3 +1,4 @@
+import numpy as np
 import jax
 import jax.numpy as jnp
 from jax import lax
@@ -111,6 +112,11 @@
     )(expd_low, scale, query_aug)
 
 
+def bit_reversed(n):
+    bits = n.bit_length() - 1
+    return np.array([int(format(p, f"0{bits}b")[::-1], 2) if bits else 0 for p in range(n)], np.int32)
+
+
 def exchange(x, n_dev, step):
     return lax.ppermute(x, "ref", [(i, i ^ step) for i in range(n_dev)])
 
@@ -133,11 +139,10 @@
     blocks = rows.reshape(n_dev, -1, n_feat)
     step = 1
     while step < n_dev:
-        lead = n_dev // (2 * step)
-        split = blocks.reshape(lead, 2, -1, n_feat)
+        half = blocks.shape[0] // 2
         bit = (me // step) % 2
-        keep = lax.dynamic_index_in_dim(split, bit, axis=1, keepdims=False)
-        send = lax.dynamic_index_in_dim(split, 1 - bit, axis=1, keepdims=False)
+        keep = lax.dynamic_slice_in_dim(blocks, bit * half, half, 0)
+        send = lax.dynamic_slice_in_dim(blocks, (1 - bit) * half, half, 0)
         n_send = send.shape[0] * send.shape[1]
         got = exchange(jnp.concatenate([send.reshape(n_send, n_feat), extra]), n_dev, step)
         blocks = keep + got[:n_send].reshape(keep.shape)
@@ -151,6 +156,11 @@
     n_feat = queries.shape[1]
     n_ref = references.shape[0]
     n_dev = lax.axis_size("ref")
+    own_rows = n_query // n_dev
+    order = bit_reversed(n_dev)
+    reorder = lambda x: x.reshape((n_dev, own_rows) + x.shape[1:])[order].reshape(x.shape)
+    all_queries, all_cotangent = queries, cotangent
+    queries, query_ids, cotangent = reorder(queries), reorder(query_ids), reorder(cotangent)
     inv = 1.0 / (spread * spread)
     ref_start = lax.axis_index("ref") * n_ref
     local_ids = (query_ids - ref_start)[None, :]
@@ -168,10 +178,9 @@
     reference_grad = (pushed - references * column[:, None]) * inv
     local_terms = jnp.stack([jnp.sum(queries * pulled, axis=0), jnp.sum(references * reference_grad, axis=0)])
     own_pulled, summed_terms = halving_scatter(pulled, local_terms, n_dev)
-    own_rows = n_query // n_dev
     own_start = lax.axis_index("ref") * own_rows
-    own_queries = lax.dynamic_slice_in_dim(queries, own_start, own_rows, 0)
-    own_cot = lax.dynamic_slice_in_dim(cotangent, own_start, own_rows, 0)
+    own_queries = lax.dynamic_slice_in_dim(all_queries, own_start, own_rows, 0)
+    own_cot = lax.dynamic_slice_in_dim(all_cotangent, own_start, own_rows, 0)
     query_grad = (own_pulled - own_queries * own_cot[:, None]) * inv
     self_terms = jnp.sum(queries * queries * cotangent[:, None], axis=0)
     summed = (summed_terms[0] - self_terms) * inv + summed_terms[1]

time: 84 us -> 78.1 us (0.930)
  local copies, waits for them, and re-layouts: 12.1 us -> 7.75 us
  other arithmetic: 13.1 us -> 11.5 us
    dynamic_slice x5 -> x4, local copies, waits for them, and re-layouts: 5.79 us -> 0.16 us  [the longest x3 0.08 us: halving_scatter(): send = lax.dynamic_slice_in_dim(blocks, (1 - bit) * half, half, 0)]
    gather x0 -> x3, local copies, waits for them, and re-layouts: none -> 3.94 us  [on_device(): x.reshape((n_dev, own_rows) + x.shape[1:])[order].reshape(x.shape)]
    another operation x1 -> x0, local copies, waits for them, and re-layouts: 1.86 us -> none  [halving_scatter(): split = blocks.reshape(lead, 2, -1, n_feat)]
    reduce_sum x1, other arithmetic: 2.54 us -> 1.31 us  [on_device(): jnp.sum(references * reference_grad, axis=0)]
    reduce_sum x1, other arithmetic: 1.43 us -> 0.35 us  [on_device(): jnp.sum(queries * pulled, axis=0)]
    concatenate x1, local copies, waits for them, and re-layouts: 1.08 us -> 0.14 us  [halving_scatter(): jnp.concatenate([send.reshape(n_send, n_feat), extra])]
    mul x1, other arithmetic: 0.72 us -> 1.56 us  [on_device(): query_grad = (own_pulled - own_queries * own_cot[:, None]) * inv]
where the time goes in v7:
time: 78.1 us; the launch traced here: 77.7 us
  Pallas kernels  25.1 us (32%)
  waiting for transfers between devices  17 us (22%)
  starting transfers between devices  15.4 us (20%)
  other arithmetic  11.5 us (15%)
  local copies, waits for them, and re-layouts  7.75 us (10%)
  between operations  0.94 us (1%)
    pallas_call x1, Pallas kernels, local_forward(): pl.pallas_call(forward_kernel, grid=(n_query // tile,), in_specs=[pl.Bloc...  18 us
    ppermute x8, waiting for transfers between devices, exchange(): return lax.ppermute(x, 'ref', [(i, i ^ step) for i in range(n_dev)])  17 us
    ppermute x8, starting transfers between devices, exchange(): return lax.ppermute(x, 'ref', [(i, i ^ step) for i in range(n_dev)])  15.4 us
    pallas_call x1, Pallas kernels, local_backward(): pl.pallas_call(backward_kernel, grid=(n_query // tile,), in_specs=[pl.Blo...  7.1 us
    gather x3, local copies, waits for them, and re-layouts, on_device(): x.reshape((n_dev, own_rows) + x.shape[1:])[order].reshape(x.shape)  3.94 us
  transfers between devices with their start and end apart: 8, of which 8 were waited for; matrix products, arithmetic and copies ran while one was open for 4% of the time, Pallas kernels for 0%

profile of v7, /device:TPU:0, one launch (start us, length us, event | category | flops | bytes accessed | tf_op | source)
XLA Modules:
  0.0 77.7 jit_solution(4165559076055780069)
XLA Ops:
  1.3 1.2 %fusion.17.inv_ref = f32[1,128]{1,0:T(1,128)} fusion(f32[128]{0:T(128)} %param.12), kind=kLoop, calls=%fused_computation.60 | loop fusion | flops 256 | bytes 1024 | tf_op jit(solution)/shard_map/broadcast_in_dim | solution.py:167
  2.5 2.8 %gather_fusion = f32[16,128,128]{2,1,0:T(8,128)} fusion(f32[16,128,128]{2,1,0:T(8,128)} %bitcast.64, s32[1024]{0:T(1024)S(1)} %pad_clamp_fusion), kind=kCustom, calls=%fused_computation | custom fusion | bytes 2097216 | tf_op jit(solution)/shard_map/gather | solution.py:161
  6.5 18.0 %shard_map.112 = (bf16[2048,2048]{1,0:T(8,128)(2,1)}, f32[128,2048]{1,0:T(8,128)}, f32[1,2048]{1,0:T(1,128)}, f32[1,2048]{1,0:T(1,128)}) custom-call(f32[2048,128]{1,0:T(8,128)} %bitcast.59, f32[1,128]{1,0:T(1,128)} %fusion.17.inv_ref, s32[1,2048]{1,0:T(1,128)} %bitcast.72, f32[2048,128]{1,0:T(8,128)} %r_ref.1), custom_call_target="tpu_custom_call" | custom-call | tf_op jit(solution)/shard_map/pallas_call | solution.py:67
  24.5 0.8 %pad_maximum_fusion.3 = f32[2,2048]{1,0:T(2,128)S(1)} fusion(f32[1,2048]{1,0:T(1,128)} %get-tuple-element.9, f32[1,2048]{1,0:T(1,128)} %get-tuple-element.8), kind=kLoop, calls=%fused_computation.24 | loop fusion | flops 4096 | bytes 32768 | tf_op jit(solution)/shard_map/stack | solution.py:127
  26.7 0.7 fusion.10
  27.5 2.9 %collective-permute-start.1 = (f32[2,2048]{1,0:T(2,128)S(1)}, f32[2,2048]{1,0:T(2,128)S(1)}, u32[]{:S(2)}, u32[]{:S(2)}) collective-permute-start(f32[2,2048]{1,0:T(2,128)S(1)} %pad_maximum_fusion.4), channel_id=1, source_target_pairs={{0,2},{1,3},{2,0},{3,1},{4,6},{5,7},{6,4},{7,5},{8,10},{9,11},{10,... | collective-permute-start | bytes 49160 | tf_op jit(solution)/shard_map/ppermute | solution.py:121
  30.9 1.3 %collective-permute-done.1 = f32[2,2048]{1,0:T(2,128)S(1)} collective-permute-done((f32[2,2048]{1,0:T(2,128)S(1)}, f32[2,2048]{1,0:T(2,128)S(1)}, u32[]{:S(2)}, u32[]{:S(2)}) %collective-permute-start.1) | collective-permute-done | bytes 16416 | tf_op jit(solution)/shard_map/ppermute | solution.py:121
  32.2 2.1 %collective-permute-start.2 = (f32[2,2048]{1,0:T(2,128)S(1)}, f32[2,2048]{1,0:T(2,128)S(1)}, u32[]{:S(2)}, u32[]{:S(2)}) collective-permute-start(f32[2,2048]{1,0:T(2,128)S(1)} %pad_maximum_fusion.5), channel_id=1, source_target_pairs={{0,4},{1,5},{2,6},{3,7},{4,0},{5,1},{6,2},{7,3},{8,12},{9,13},{10,... | collective-permute-start | bytes 49160 | tf_op jit(solution)/shard_map/ppermute | solution.py:121
  34.3 1.1 %maximum_maximum_fusion.qa_ref = bf16[2048,256]{1,0:T(8,128)(2,1)} fusion(bf16[2048,128]{1,0:T(8,128)(2,1)S(1)} %get-tuple-element.22, bf16[256]{0:T(256)(128)(2,1)S(1)} %pad.10.clone, bf16[256]{0:T(256)(128)(2,1)S(1)} %pad.9.clone), kind=kLoop, calls=%fused_computation.6 | loop fusion | flops 3145728 | bytes 1573888 | tf_op jit(solution)/shard_map/concatenate | solution.py:172
  36.1 3.1 %collective-permute-start.3 = (f32[2,2048]{1,0:T(2,128)S(1)}, f32[2,2048]{1,0:T(2,128)S(1)}, u32[]{:S(2)}, u32[]{:S(2)}) collective-permute-start(f32[2,2048]{1,0:T(2,128)S(1)} %pad_maximum_fusion.6), channel_id=1, source_target_pairs={{0,8},{1,9},{2,10},{3,11},{4,12},{5,13},{6,14},{7,15},{8,0},{9,1},... | collective-permute-start | bytes 49160 | tf_op jit(solution)/shard_map/ppermute | solution.py:121
  39.6 1.4 %collective-permute-done.3 = f32[2,2048]{1,0:T(2,128)S(1)} collective-permute-done((f32[2,2048]{1,0:T(2,128)S(1)}, f32[2,2048]{1,0:T(2,128)S(1)}, u32[]{:S(2)}, u32[]{:S(2)}) %collective-permute-start.3) | collective-permute-done | bytes 16416 | tf_op jit(solution)/shard_map/ppermute | solution.py:121
  41.6 7.1 %shard_map.113 = f32[2048,256]{1,0:T(8,128)} custom-call(bf16[2048,2048]{1,0:T(8,128)(2,1)} %get-tuple-element.10.e_ref, f32[1,2048]{1,0:T(1,128)} %fusion.7.sc_ref, bf16[2048,256]{1,0:T(8,128)(2,1)} %maximum_maximum_fusion.qa_ref), custom_call_target="tpu_custom_call" | custom-call | tf_op jit(solution)/shard_map/pallas_call | solution.py:101
  48.7 1.6 %slice_reduce_fusion = f32[2048]{0:T(1024)S(1)} fusion(f32[2048,256]{1,0:T(8,128)} %shard_map.113), kind=kLoop, calls=%fused_computation.3 | loop fusion | bytes 16384 | tf_op jit(solution)/shard_map/slice | solution.py:177
  50.7 1.2 %copy-done.2 = f32[2048,256]{1,0:T(8,128)S(1)} copy-done((f32[2048,256]{1,0:T(8,128)S(1)}, f32[2048,256]{1,0:T(8,128)}, u32[]{:S(2)}) %copy-start.2) | copy-done | bytes 2097176
  52.1 1.3 %multiply_reduce_fusion.1 = (f32[128]{0:T(128)S(1)}, f32[2048,128]{1,0:T(8,128)}) fusion(f32[2048,128]{1,0:T(8,128)S(1)} %copy-done.3, f32[128]{0:T(128)S(1)} %multiply_divide_fusion, f32[2048]{0:T(1024)S(1)} %slice_reduce_fusion, f32[2048,256]{1,0:T(8,128)S(1)} %copy-done.2), kind=kLoop, calls=%fused_computation.10 | loop fusion | flops 1310592 | bytes 3154944 | tf_op jit(solution)/shard_map/reduce_sum | solution.py:179
  53.7 1.9 %collective-permute-done.4 = f32[1026,128]{1,0:T(8,128)S(1)} collective-permute-done((f32[1026,128]{1,0:T(8,128)S(1)}, f32[1026,128]{1,0:T(8,128)S(1)}, u32[]{:S(2)}, u32[]{:S(2)}) %collective-permute-start.4) | collective-permute-done | bytes 525344 | tf_op jit(solution)/shard_map/ppermute | solution.py:121
  55.7 1.9 %collective-permute-start.5 = (f32[514,128]{1,0:T(8,128)S(1)}, f32[514,128]{1,0:T(8,128)S(1)}, u32[]{:S(2)}, u32[]{:S(2)}) collective-permute-start(f32[514,128]{1,0:T(8,128)S(1)} %pad_maximum_fusion), channel_id=1, source_target_pairs={{0,2},{1,3},{2,0},{3,1},{4,6},{5,7},{6,4},{7,5},{8,10},{9,11},{10,... | collective-permute-start | bytes 789512 | tf_op jit(solution)/shard_map/ppermute | solution.py:121
  57.7 6.7 %collective-permute-done.5 = f32[514,128]{1,0:T(8,128)S(1)} collective-permute-done((f32[514,128]{1,0:T(8,128)S(1)}, f32[514,128]{1,0:T(8,128)S(1)}, u32[]{:S(2)}, u32[]{:S(2)}) %collective-permute-start.5) | collective-permute-done | bytes 263200 | tf_op jit(solution)/shard_map/ppermute | solution.py:121
  64.5 1.9 %collective-permute-start.6 = (f32[258,128]{1,0:T(8,128)S(1)}, f32[258,128]{1,0:T(8,128)S(1)}, u32[]{:S(2)}, u32[]{:S(2)}) collective-permute-start(f32[258,128]{1,0:T(8,128)S(1)} %pad_maximum_fusion.1), channel_id=1, source_target_pairs={{0,4},{1,5},{2,6},{3,7},{4,0},{5,1},{6,2},{7,3},{8,12},{9,13},{10,... | collective-permute-start | bytes 396296 | tf_op jit(solution)/shard_map/ppermute | solution.py:121
  66.3 3.2 %collective-permute-done.6 = f32[258,128]{1,0:T(8,128)S(1)} collective-permute-done((f32[258,128]{1,0:T(8,128)S(1)}, f32[258,128]{1,0:T(8,128)S(1)}, u32[]{:S(2)}, u32[]{:S(2)}) %collective-permute-start.6) | collective-permute-done | bytes 132128 | tf_op jit(solution)/shard_map/ppermute | solution.py:121
  69.6 2.9 %collective-permute-start.7 = (f32[130,128]{1,0:T(8,128)S(1)}, f32[130,128]{1,0:T(8,128)S(1)}, u32[]{:S(2)}, u32[]{:S(2)}) collective-permute-start(f32[130,128]{1,0:T(8,128)S(1)} %pad_maximum_fusion.2), channel_id=1, source_target_pairs={{0,8},{1,9},{2,10},{3,11},{4,12},{5,13},{6,14},{7,15},{8,0},{9,1},... | collective-permute-start | bytes 199688 | tf_op jit(solution)/shard_map/ppermute | solution.py:121
  73.2 1.7 %collective-permute-done.7 = f32[130,128]{1,0:T(8,128)S(1)} collective-permute-done((f32[130,128]{1,0:T(8,128)S(1)}, f32[130,128]{1,0:T(8,128)S(1)}, u32[]{:S(2)}, u32[]{:S(2)}) %collective-permute-start.7) | collective-permute-done | bytes 66592 | tf_op jit(solution)/shard_map/ppermute | solution.py:121
  74.9 1.2 %divide_subtract_fusion = f32[128]{0:T(128)} fusion(f32[128]{0:T(128)S(1)} %copy-done.8, f32[128]{0:T(128)S(1)} %get-tuple-element.21, f32[2,128]{1,0:T(2,128)S(1)} %slice_add_fusion, f32[]{:T(128)} %reduce_sum.39), kind=kLoop, calls=%fused_computation.52 | loop fusion | flops 1152 | bytes 2564 | tf_op jit(solution)/shard_map/sub | solution.py:188
  76.1 1.6 %fusion.5 = f32[128,128]{1,0:T(8,128)} fusion(f32[130,128]{1,0:T(8,128)S(1)} %collective-permute-done.7, f32[2048,128]{1,0:T(8,128)} %param.9, s32[]{:T(128)S(6)} %select_n.85, f32[2,128,128]{2,1,0:T(8,128)S(1)} %dynamic-slice_add_fusion.2, s32[]{:T(128)S(6)} %select_n.83, f32[128]{0:T(128)S(1)} %multiply_divide_fusion, f32[128]{0:T(128)S(1)} %dynamic_slice.39), kind=kLoop, calls=%fused_computation.22 | loop fusion | flops 65536 | bytes 263176 | tf_op jit(solution)/shard_map/mul | solution.py:184
  (58 shorter events, 7.2 us)
Async XLA Ops:
  0.6 4.7 %copy-start = (s32[2048]{0:T(1024)S(1)}, s32[2048]{0:T(1024)}, u32[]{:S(2)}) copy-start(s32[2048]{0:T(1024)} %param.11) | copy-start | bytes 24580
  2.5 23.4 %copy-start.5 = (f32[2048]{0:T(1024)S(1)}, f32[2048]{0:T(1024)}, u32[]{:S(2)}) copy-start(f32[2048]{0:T(1024)} %param.13) | copy-start | bytes 24580
  5.3 25.1 %copy-start.1 = (f32[16,128,128]{2,1,0:T(8,128)S(1)}, f32[16,128,128]{2,1,0:T(8,128)}, u32[]{:S(2)}) copy-start(f32[16,128,128]{2,1,0:T(8,128)} %gather_fusion) | copy-start | bytes 3145732
  24.5 14.7 %copy-start.8 = (f32[128]{0:T(128)S(1)}, f32[128]{0:T(128)}, u32[]{:S(2)}) copy-start(f32[128]{0:T(128)} %param.12) | copy-start | bytes 1540
  24.5 14.7 %copy-start.4 = (f32[128,2048]{1,0:T(8,128)S(1)}, f32[128,2048]{1,0:T(8,128)}, u32[]{:S(2)}) copy-start(f32[128,2048]{1,0:T(8,128)} %get-tuple-element.7) | copy-start | bytes 3145732
  25.3 1.4 %collective-permute-start = (f32[2,2048]{1,0:T(2,128)S(1)}, f32[2,2048]{1,0:T(2,128)S(1)}, u32[]{:S(2)}, u32[]{:S(2)}) collective-permute-start(f32[2,2048]{1,0:T(2,128)S(1)} %pad_maximum_fusion.3), channel_id=1, source_target_pairs={{0,1},{1,0},{2,3},{3,2},{4,5},{5,4},{6,7},{7,6},{8,9},{9,8},{10,11... | collective-permute-start | bytes 49160 | tf_op jit(solution)/shard_map/ppermute | solution.py:121
  27.5 4.6 %collective-permute-start.1 = (f32[2,2048]{1,0:T(2,128)S(1)}, f32[2,2048]{1,0:T(2,128)S(1)}, u32[]{:S(2)}, u32[]{:S(2)}) collective-permute-start(f32[2,2048]{1,0:T(2,128)S(1)} %pad_maximum_fusion.4), channel_id=1, source_target_pairs={{0,2},{1,3},{2,0},{3,1},{4,6},{5,7},{6,4},{7,5},{8,10},{9,11},{10,... | collective-permute-start | bytes 49160 | tf_op jit(solution)/shard_map/ppermute | solution.py:121
  30.8 10.2 %copy-start.7 = (f32[1,2048]{1,0:T(1,128)S(1)}, f32[1,2048]{1,0:T(1,128)}, u32[]{:S(2)}) copy-start(f32[1,2048]{1,0:T(1,128)} %get-tuple-element.8) | copy-start | bytes 24580
  32.2 3.9 %collective-permute-start.2 = (f32[2,2048]{1,0:T(2,128)S(1)}, f32[2,2048]{1,0:T(2,128)S(1)}, u32[]{:S(2)}, u32[]{:S(2)}) collective-permute-start(f32[2,2048]{1,0:T(2,128)S(1)} %pad_maximum_fusion.5), channel_id=1, source_target_pairs={{0,4},{1,5},{2,6},{3,7},{4,0},{5,1},{6,2},{7,3},{8,12},{9,13},{10,... | collective-permute-start | bytes 49160 | tf_op jit(solution)/shard_map/ppermute | solution.py:121
  36.1 4.8 %collective-permute-start.3 = (f32[2,2048]{1,0:T(2,128)S(1)}, f32[2,2048]{1,0:T(2,128)S(1)}, u32[]{:S(2)}, u32[]{:S(2)}) collective-permute-start(f32[2,2048]{1,0:T(2,128)S(1)} %pad_maximum_fusion.6), channel_id=1, source_target_pairs={{0,8},{1,9},{2,10},{3,11},{4,12},{5,13},{6,14},{7,15},{8,0},{9,1},... | collective-permute-start | bytes 49160 | tf_op jit(solution)/shard_map/ppermute | solution.py:121
  41.6 8.7 %copy-start.6 = (f32[1,2048]{1,0:T(1,128)S(1)}, f32[1,2048]{1,0:T(1,128)}, u32[]{:S(2)}) copy-start(f32[1,2048]{1,0:T(1,128)} %fusion.7.sc_ref) | copy-start | bytes 24580
  50.3 1.6 %copy-start.2 = (f32[2048,256]{1,0:T(8,128)S(1)}, f32[2048,256]{1,0:T(8,128)}, u32[]{:S(2)}) copy-start(f32[2048,256]{1,0:T(8,128)} %shard_map.113) | copy-start | bytes 6291460
  50.3 1.8 %copy-start.3 = (f32[2048,128]{1,0:T(8,128)S(1)}, f32[2048,128]{1,0:T(8,128)}, u32[]{:S(2)}) copy-start(f32[2048,128]{1,0:T(8,128)} %r_ref.1) | copy-start | bytes 3145732
  53.6 2.0 %collective-permute-start.4 = (f32[1026,128]{1,0:T(8,128)S(1)}, f32[1026,128]{1,0:T(8,128)S(1)}, u32[]{:S(2)}, u32[]{:S(2)}) collective-permute-start(f32[1026,128]{1,0:T(8,128)S(1)} %concatenate.17), channel_id=1, source_target_pairs={{0,1},{1,0},{2,3},{3,2},{4,5},{5,4},{6,7},{7,6},{8,9},{9,8},{10,11... | collective-permute-start | bytes 1575944 | tf_op jit(solution)/shard_map/ppermute | solution.py:121
  55.7 8.6 %collective-permute-start.5 = (f32[514,128]{1,0:T(8,128)S(1)}, f32[514,128]{1,0:T(8,128)S(1)}, u32[]{:S(2)}, u32[]{:S(2)}) collective-permute-start(f32[514,128]{1,0:T(8,128)S(1)} %pad_maximum_fusion), channel_id=1, source_target_pairs={{0,2},{1,3},{2,0},{3,1},{4,6},{5,7},{6,4},{7,5},{8,10},{9,11},{10,... | collective-permute-start | bytes 789512 | tf_op jit(solution)/shard_map/ppermute | solution.py:121
  64.5 5.1 %collective-permute-start.6 = (f32[258,128]{1,0:T(8,128)S(1)}, f32[258,128]{1,0:T(8,128)S(1)}, u32[]{:S(2)}, u32[]{:S(2)}) collective-permute-start(f32[258,128]{1,0:T(8,128)S(1)} %pad_maximum_fusion.1), channel_id=1, source_target_pairs={{0,4},{1,5},{2,6},{3,7},{4,0},{5,1},{6,2},{7,3},{8,12},{9,13},{10,... | collective-permute-start | bytes 396296 | tf_op jit(solution)/shard_map/ppermute | solution.py:121
  69.6 5.3 %collective-permute-start.7 = (f32[130,128]{1,0:T(8,128)S(1)}, f32[130,128]{1,0:T(8,128)S(1)}, u32[]{:S(2)}, u32[]{:S(2)}) collective-permute-start(f32[130,128]{1,0:T(8,128)S(1)} %pad_maximum_fusion.2), channel_id=1, source_target_pairs={{0,8},{1,9},{2,10},{3,11},{4,12},{5,13},{6,14},{7,15},{8,0},{9,1},... | collective-permute-start | bytes 199688 | tf_op jit(solution)/shard_map/ppermute | solution.py:121

commit v8 on v7

--- a/solution.py
+++ b/solution.py
@@ -39,25 +39,42 @@
         rs_sc[...], jnp.concatenate([q1, q2, q3, q1, q2, q1], axis=1), (((1,), (1,)), ((), ())),
         preferred_element_type=jnp.float32,
     )
-    score = cross - 0.5 * qnorm - rn_sc[...]
-    row = lax.broadcasted_iota(jnp.int32, score.shape, 0)
-    score = jnp.where(row == lid_ref[...], -jnp.inf, score)
-    peak = jnp.max(score, axis=0, keepdims=True)
-    expd = jnp.exp(score - peak)
-    p_ref[...] = peak
+    shifted = cross - rn_sc[...]
+    row = lax.broadcasted_iota(jnp.int32, shifted.shape, 0)
+    shifted = jnp.where(row == lid_ref[...], -jnp.inf, shifted)
+    top = jnp.max(shifted, axis=0, keepdims=True)
+    expd = jnp.exp(shifted - top)
+    p_ref[...] = top - 0.5 * qnorm
     t_ref[...] = jnp.sum(expd, axis=0, keepdims=True)
     expd_low = expd.astype(jnp.bfloat16)
     e_ref[...] = expd_low
     ut_ref[...] = jnp.dot(rlt_sc[...], expd_low, preferred_element_type=jnp.float32)
 
 
-def backward_kernel(e_ref, sc_ref, qa_ref, pa_ref):
-    @pl.when(pl.program_id(0) == 0)
+def backward_kernel(e_ref, sc_ref, qa_ref, ut_ref, q_ref, r_ref, inv_ref, rg_ref, pull_ref, terms_ref, acc_sc, qt_sc):
+    step = pl.program_id(0)
+    n_feat = q_ref.shape[1]
+
+    @pl.when(step == 0)
     def _():
-        pa_ref[...] = jnp.zeros_like(pa_ref)
-
-    weight = (e_ref[...].astype(jnp.float32) * sc_ref[...]).astype(jnp.bfloat16)
-    pa_ref[...] += jnp.dot(weight, qa_ref[...], preferred_element_type=jnp.float32)
+        acc_sc[...] = jnp.zeros_like(acc_sc)
+        qt_sc[...] = jnp.zeros_like(qt_sc)
+
+    scale = sc_ref[...]
+    weight = (e_ref[...].astype(jnp.float32) * scale).astype(jnp.bfloat16)
+    acc_sc[...] += jnp.dot(weight, qa_ref[...], preferred_element_type=jnp.float32)
+    pulled = (ut_ref[...] * scale).T
+    pull_ref[...] = pulled
+    qt_sc[...] += jnp.sum(q_ref[...] * pulled, axis=0, keepdims=True)
+
+    @pl.when(step == pl.num_programs(0) - 1)
+    def _():
+        acc = acc_sc[...]
+        refs = r_ref[...]
+        rgrad = (acc[:, :n_feat] - refs * acc[:, n_feat:n_feat + 1]) * inv_ref[...]
+        rg_ref[...] = rgrad
+        rterm = jnp.sum(refs * rgrad, axis=0, keepdims=True)
+        terms_ref[...] = jnp.concatenate([qt_sc[...], rterm, jnp.zeros((6, n_feat), jnp.float32)], axis=0)
 
 
 def local_forward(queries, inv, local_ids, references):
@@ -94,10 +111,12 @@
     )(queries, inv, local_ids, references)
 
 
-def local_backward(expd_low, scale, query_aug):
+def local_backward(expd_low, scale, query_aug, unscaled_t, queries, references, inv):
     n_ref, n_query = expd_low.shape
+    n_feat = queries.shape[1]
     width = query_aug.shape[1]
     tile = min(TILE, n_query)
+    whole = lambda i: (0, 0)
     return pl.pallas_call(
         backward_kernel,
         grid=(n_query // tile,),
@@ -105,11 +124,27 @@
             pl.BlockSpec((n_ref, tile), lambda i: (0, i)),
             pl.BlockSpec((1, tile), lambda i: (0, i)),
             pl.BlockSpec((tile, width), lambda i: (i, 0)),
-        ],
-        out_specs=pl.BlockSpec((n_ref, width), lambda i: (0, 0)),
-        out_shape=jax.ShapeDtypeStruct((n_ref, width), jnp.float32),
+            pl.BlockSpec((n_feat, tile), lambda i: (0, i)),
+            pl.BlockSpec((tile, n_feat), lambda i: (i, 0)),
+            pl.BlockSpec((n_ref, n_feat), whole),
+            pl.BlockSpec((1, n_feat), whole),
+        ],
+        out_specs=[
+            pl.BlockSpec((n_ref, n_feat), whole),
+            pl.BlockSpec((tile, n_feat), lambda i: (i, 0)),
+            pl.BlockSpec((8, n_feat), whole),
+        ],
+        out_shape=[
+            jax.ShapeDtypeStruct((n_ref, n_feat), jnp.float32),
+            jax.ShapeDtypeStruct((n_query, n_feat), jnp.float32),
+            jax.ShapeDtypeStruct((8, n_feat), jnp.float32),
+        ],
+        scratch_shapes=[
+            pltpu.VMEM((n_ref, width), jnp.float32),
+            pltpu.VMEM((1, n_feat), jnp.float32),
+        ],
         compiler_params=pltpu.CompilerParams(dimension_semantics=("arbitrary",)),
-    )(expd_low, scale, query_aug)
+    )(expd_low, scale, query_aug, unscaled_t, queries, references, inv)
 
 
 def bit_reversed(n):
@@ -167,16 +202,13 @@
     expd_low, unscaled_t, local_peak, local_total = local_forward(queries, inv[None, :], local_ids, references)
     peak, total = butterfly_stats(local_peak[0], local_total[0], n_dev)
     scale = cotangent * jnp.exp(local_peak[0] - peak) / total
-    pulled = (unscaled_t * scale[None, :]).T
     query_low = queries.astype(jnp.bfloat16)
     query_aug = jnp.concatenate(
         [query_low, jnp.ones((n_query, 1), jnp.bfloat16), jnp.zeros((n_query, n_feat - 1), jnp.bfloat16)], axis=1
     )
-    pushed_aug = local_backward(expd_low, scale[None, :], query_aug)
-    pushed = pushed_aug[:, :n_feat]
-    column = pushed_aug[:, n_feat]
-    reference_grad = (pushed - references * column[:, None]) * inv
-    local_terms = jnp.stack([jnp.sum(queries * pulled, axis=0), jnp.sum(references * reference_grad, axis=0)])
+    reference_grad, pulled, local_terms = local_backward(
+        expd_low, scale[None, :], query_aug, unscaled_t, queries, references, inv[None, :]
+    )
     own_pulled, summed_terms = halving_scatter(pulled, local_terms, n_dev)
     own_start = lax.axis_index("ref") * own_rows
     own_queries = lax.dynamic_slice_in_dim(all_queries, own_start, own_rows, 0)

time: 78.1 us -> 76 us (0.973)
  local copies, waits for them, and re-layouts: 7.75 us -> 5.51 us
  other arithmetic: 11.5 us -> 10.5 us
    reduce_sum x2 -> x0, other arithmetic: 1.66 us -> none  [the longest x1 1.31 us: on_device(): jnp.sum(references * reference_grad, axis=0)]
    slice x1 -> x0, local copies, waits for them, and re-layouts: 1.56 us -> none  [on_device(): column = pushed_aug[:, n_feat]]
    unnamed x18 -> x14, local copies, waits for them, and re-layouts: 1.47 us -> 0.04 us
    dynamic_slice x3, local copies, waits for them, and re-layouts: 0.08 us -> 1.21 us  [halving_scatter(): send = lax.dynamic_slice_in_dim(blocks, (1 - bit) * half, half, 0)]
    pallas_call x1, Pallas kernels: 7.1 us -> 8.2 us  [local_backward(): pl.pallas_call(backward_kernel, grid=(n_query // tile,), in_specs=[pl.Blo...]
    concatenate x3 -> x4, other arithmetic: 0.04 us -> 0.82 us  [halving_scatter(): jnp.concatenate([send.reshape(n_send, n_feat), extra])]
where the time goes in v8:
time: 76 us; the launch traced here: 75.5 us
  Pallas kernels  25.8 us (34%)
  waiting for transfers between devices  17.3 us (23%)
  starting transfers between devices  15.4 us (20%)
  other arithmetic  10.5 us (14%)
  local copies, waits for them, and re-layouts  5.51 us (7%)
  between operations  0.91 us (1%)
    pallas_call x1, Pallas kernels, local_forward(): pl.pallas_call(forward_kernel, grid=(n_query // tile,), in_specs=[pl.Bloc...  17.6 us
    ppermute x8, waiting for transfers between devices, exchange(): return lax.ppermute(x, 'ref', [(i, i ^ step) for i in range(n_dev)])  17.3 us
    ppermute x8, starting transfers between devices, exchange(): return lax.ppermute(x, 'ref', [(i, i ^ step) for i in range(n_dev)])  15.4 us
    pallas_call x1, Pallas kernels, local_backward(): pl.pallas_call(backward_kernel, grid=(n_query // tile,), in_specs=[pl.Blo...  8.2 us
    gather x3, local copies, waits for them, and re-layouts, on_device(): x.reshape((n_dev, own_rows) + x.shape[1:])[order].reshape(x.shape)  4.02 us
    mul x1, other arithmetic, on_device(): query_grad = (own_pulled - own_queries * own_cot[:, None]) * inv  1.56 us
  transfers between devices with their start and end apart: 8, of which 8 were waited for; matrix products, arithmetic and copies ran while one was open for 4% of the time, Pallas kernels for 0%

profile of v8, /device:TPU:0, one launch (start us, length us, event | category | flops | bytes accessed | tf_op | source)
XLA Modules:
  0.0 75.5 jit_solution(2986394531497657545)
XLA Ops:
  0.6 1.2 %fusion.14.inv_ref = f32[1,128]{1,0:T(1,128)} fusion(f32[128]{0:T(128)} %param.12), kind=kLoop, calls=%fused_computation.54 | loop fusion | flops 256 | bytes 1024 | tf_op jit(solution)/shard_map/broadcast_in_dim | solution.py:202
  3.1 2.9 %gather_fusion = f32[16,128,128]{2,1,0:T(8,128)} fusion(f32[16,128,128]{2,1,0:T(8,128)} %bitcast.54, s32[1024]{0:T(1024)S(1)} %pad_clamp_fusion), kind=kCustom, calls=%fused_computation | custom fusion | bytes 2097216 | tf_op jit(solution)/shard_map/gather | solution.py:196
  6.6 17.6 %shard_map.112 = (bf16[2048,2048]{1,0:T(8,128)(2,1)}, f32[128,2048]{1,0:T(8,128)}, f32[1,2048]{1,0:T(1,128)}, f32[1,2048]{1,0:T(1,128)}) custom-call(f32[2048,128]{1,0:T(8,128)} %bitcast.50, f32[1,128]{1,0:T(1,128)} %fusion.14.inv_ref, s32[1,2048]{1,0:T(1,128)} %bitcast.63, f32[2048,128]{1,0:T(8,128)} %r_ref.3), custom_call_target="tpu_custom_call" | custom-call | tf_op jit(solution)/shard_map/pallas_call | solution.py:84
  24.2 0.8 %pad_maximum_fusion.4 = f32[2,2048]{1,0:T(2,128)S(1)} fusion(f32[1,2048]{1,0:T(1,128)} %get-tuple-element.12, f32[1,2048]{1,0:T(1,128)} %get-tuple-element.11), kind=kLoop, calls=%fused_computation.18 | loop fusion | flops 4096 | bytes 32768 | tf_op jit(solution)/shard_map/stack | solution.py:162
  25.6 0.8 %collective-permute-done = f32[2,2048]{1,0:T(2,128)S(1)} collective-permute-done((f32[2,2048]{1,0:T(2,128)S(1)}, f32[2,2048]{1,0:T(2,128)S(1)}, u32[]{:S(2)}, u32[]{:S(2)}) %collective-permute-start) | collective-permute-done | bytes 16416 | tf_op jit(solution)/shard_map/ppermute | solution.py:156
  26.4 0.7 fusion.8
  27.2 2.9 %collective-permute-start.1 = (f32[2,2048]{1,0:T(2,128)S(1)}, f32[2,2048]{1,0:T(2,128)S(1)}, u32[]{:S(2)}, u32[]{:S(2)}) collective-permute-start(f32[2,2048]{1,0:T(2,128)S(1)} %pad_maximum_fusion.5), channel_id=1, source_target_pairs={{0,2},{1,3},{2,0},{3,1},{4,6},{5,7},{6,4},{7,5},{8,10},{9,11},{10,... | collective-permute-start | bytes 49160 | tf_op jit(solution)/shard_map/ppermute | solution.py:156
  30.6 1.2 %collective-permute-done.1 = f32[2,2048]{1,0:T(2,128)S(1)} collective-permute-done((f32[2,2048]{1,0:T(2,128)S(1)}, f32[2,2048]{1,0:T(2,128)S(1)}, u32[]{:S(2)}, u32[]{:S(2)}) %collective-permute-start.1) | collective-permute-done | bytes 16416 | tf_op jit(solution)/shard_map/ppermute | solution.py:156
  31.9 2.1 %collective-permute-start.2 = (f32[2,2048]{1,0:T(2,128)S(1)}, f32[2,2048]{1,0:T(2,128)S(1)}, u32[]{:S(2)}, u32[]{:S(2)}) collective-permute-start(f32[2,2048]{1,0:T(2,128)S(1)} %pad_maximum_fusion.6), channel_id=1, source_target_pairs={{0,4},{1,5},{2,6},{3,7},{4,0},{5,1},{6,2},{7,3},{8,12},{9,13},{10,... | collective-permute-start | bytes 49160 | tf_op jit(solution)/shard_map/ppermute | solution.py:156
  34.5 1.3 %collective-permute-done.2 = f32[2,2048]{1,0:T(2,128)S(1)} collective-permute-done((f32[2,2048]{1,0:T(2,128)S(1)}, f32[2,2048]{1,0:T(2,128)S(1)}, u32[]{:S(2)}, u32[]{:S(2)}) %collective-permute-start.2) | collective-permute-done | bytes 16416 | tf_op jit(solution)/shard_map/ppermute | solution.py:156
  35.8 3.1 %collective-permute-start.3 = (f32[2,2048]{1,0:T(2,128)S(1)}, f32[2,2048]{1,0:T(2,128)S(1)}, u32[]{:S(2)}, u32[]{:S(2)}) collective-permute-start(f32[2,2048]{1,0:T(2,128)S(1)} %pad_maximum_fusion.7), channel_id=1, source_target_pairs={{0,8},{1,9},{2,10},{3,11},{4,12},{5,13},{6,14},{7,15},{8,0},{9,1},... | collective-permute-start | bytes 49160 | tf_op jit(solution)/shard_map/ppermute | solution.py:156
  38.9 1.1 %maximum_maximum_fusion.qa_ref = bf16[2048,256]{1,0:T(8,128)(2,1)} fusion(bf16[2048,128]{1,0:T(8,128)(2,1)S(1)} %get-tuple-element.24, bf16[256]{0:T(256)(128)(2,1)S(1)} %pad.10.clone, bf16[256]{0:T(256)(128)(2,1)S(1)} %pad.9.clone), kind=kLoop, calls=%fused_computation.3 | loop fusion | flops 3145728 | bytes 1573888 | tf_op jit(solution)/shard_map/concatenate | solution.py:206
  41.3 8.2 %shard_map.113 = (f32[2048,128]{1,0:T(8,128)}, f32[2048,128]{1,0:T(8,128)}, f32[8,128]{1,0:T(8,128)}) custom-call(bf16[2048,2048]{1,0:T(8,128)(2,1)} %get-tuple-element.10.e_ref, f32[1,2048]{1,0:T(1,128)} %fusion.5.sc_ref, bf16[2048,256]{1,0:T(8,128)(2,1)} %maximum_maximum_fusion.qa_ref, f32[128,2048]{1,0:T(8,128)} %get-tuple-element.13.ut_ref, ...), custom_call_target="tpu_custom_call" | custom-call | tf_op jit(solution)/shard_map/pallas_call | solution.py:120
  49.5 1.2 %constant_dynamic-slice_fusion.2 = f32[8,128,128]{2,1,0:T(8,128)S(1)} fusion(f32[16,128,128]{2,1,0:T(8,128)} %bitcast.56, s32[]{:T(128)S(6)} %select_n.72), kind=kLoop, calls=%fused_computation.45 | loop fusion | bytes 1048580 | tf_op jit(solution)/shard_map/dynamic_slice | solution.py:180
  50.6 0.8 %pad_maximum_fusion = f32[1032,128]{1,0:T(8,128)S(1)} fusion(f32[8,128]{1,0:T(8,128)} %get-tuple-element.15, f32[1024,128]{1,0:T(8,128)S(1)} %bitcast.53), kind=kLoop, calls=%fused_computation.5 | loop fusion | flops 132096 | bytes 1056768 | tf_op jit(solution)/shard_map/concatenate | solution.py:182
  51.6 1.9 %collective-permute-done.4 = f32[1032,128]{1,0:T(8,128)S(1)} collective-permute-done((f32[1032,128]{1,0:T(8,128)S(1)}, f32[1032,128]{1,0:T(8,128)S(1)}, u32[]{:S(2)}, u32[]{:S(2)}) %collective-permute-start.4) | collective-permute-done | bytes 528416 | tf_op jit(solution)/shard_map/ppermute | solution.py:156
  53.6 1.9 %collective-permute-start.5 = (f32[520,128]{1,0:T(8,128)S(1)}, f32[520,128]{1,0:T(8,128)S(1)}, u32[]{:S(2)}, u32[]{:S(2)}) collective-permute-start(f32[520,128]{1,0:T(8,128)S(1)} %pad_maximum_fusion.1), channel_id=1, source_target_pairs={{0,2},{1,3},{2,0},{3,1},{4,6},{5,7},{6,4},{7,5},{8,10},{9,11},{10,... | collective-permute-start | bytes 798728 | tf_op jit(solution)/shard_map/ppermute | solution.py:156
  55.6 6.7 %collective-permute-done.5 = f32[520,128]{1,0:T(8,128)S(1)} collective-permute-done((f32[520,128]{1,0:T(8,128)S(1)}, f32[520,128]{1,0:T(8,128)S(1)}, u32[]{:S(2)}, u32[]{:S(2)}) %collective-permute-start.5) | collective-permute-done | bytes 266272 | tf_op jit(solution)/shard_map/ppermute | solution.py:156
  62.4 1.9 %collective-permute-start.6 = (f32[264,128]{1,0:T(8,128)S(1)}, f32[264,128]{1,0:T(8,128)S(1)}, u32[]{:S(2)}, u32[]{:S(2)}) collective-permute-start(f32[264,128]{1,0:T(8,128)S(1)} %pad_maximum_fusion.2), channel_id=1, source_target_pairs={{0,4},{1,5},{2,6},{3,7},{4,0},{5,1},{6,2},{7,3},{8,12},{9,13},{10,... | collective-permute-start | bytes 405512 | tf_op jit(solution)/shard_map/ppermute | solution.py:156
  64.2 3.2 %collective-permute-done.6 = f32[264,128]{1,0:T(8,128)S(1)} collective-permute-done((f32[264,128]{1,0:T(8,128)S(1)}, f32[264,128]{1,0:T(8,128)S(1)}, u32[]{:S(2)}, u32[]{:S(2)}) %collective-permute-start.6) | collective-permute-done | bytes 135200 | tf_op jit(solution)/shard_map/ppermute | solution.py:156
  67.5 2.9 %collective-permute-start.7 = (f32[136,128]{1,0:T(8,128)S(1)}, f32[136,128]{1,0:T(8,128)S(1)}, u32[]{:S(2)}, u32[]{:S(2)}) collective-permute-start(f32[136,128]{1,0:T(8,128)S(1)} %pad_maximum_fusion.3), channel_id=1, source_target_pairs={{0,8},{1,9},{2,10},{3,11},{4,12},{5,13},{6,14},{7,15},{8,0},{9,1},... | collective-permute-start | bytes 208904 | tf_op jit(solution)/shard_map/ppermute | solution.py:156
  71.1 1.7 %collective-permute-done.7 = f32[136,128]{1,0:T(8,128)S(1)} collective-permute-done((f32[136,128]{1,0:T(8,128)S(1)}, f32[136,128]{1,0:T(8,128)S(1)}, u32[]{:S(2)}, u32[]{:S(2)}) %collective-permute-start.7) | collective-permute-done | bytes 69664 | tf_op jit(solution)/shard_map/ppermute | solution.py:156
  72.8 1.2 %divide_subtract_fusion = f32[128]{0:T(128)} fusion(f32[128]{0:T(128)S(1)} %copy-done.6, f32[128]{0:T(128)S(1)} %get-tuple-element.23, f32[8,128]{1,0:T(8,128)S(1)} %slice_add_fusion, f32[]{:T(128)} %reduce_sum.19), kind=kLoop, calls=%fused_computation.46 | loop fusion | flops 1152 | bytes 2564 | tf_op jit(solution)/shard_map/sub | solution.py:220
  74.0 1.6 %fusion.3 = f32[128,128]{1,0:T(8,128)} fusion(f32[136,128]{1,0:T(8,128)S(1)} %collective-permute-done.7, f32[2048,128]{1,0:T(8,128)} %param.9, s32[]{:T(128)S(6)} %select_n.85, f32[2,128,128]{2,1,0:T(8,128)S(1)} %dynamic-slice_add_fusion.2, s32[]{:T(128)S(6)} %select_n.83, f32[128]{0:T(128)S(1)} %multiply_divide_fusion, f32[128]{0:T(128)S(1)} %dynamic_slice.39), kind=kLoop, calls=%fused_computation.16 | loop fusion | flops 65536 | bytes 263176 | tf_op jit(solution)/shard_map/mul | solution.py:216
  (50 shorter events, 5.9 us)
Async XLA Ops:
  0.6 1.9 %copy-start = (s32[2048]{0:T(1024)S(1)}, s32[2048]{0:T(1024)}, u32[]{:S(2)}) copy-start(s32[2048]{0:T(1024)} %param.11) | copy-start | bytes 24580
  3.0 27.0 %copy-start.3 = (f32[2048]{0:T(1024)S(1)}, f32[2048]{0:T(1024)}, u32[]{:S(2)}) copy-start(f32[2048]{0:T(1024)} %param.13) | copy-start | bytes 24580
  6.0 28.0 %copy-start.1 = (f32[16,128,128]{2,1,0:T(8,128)S(1)}, f32[16,128,128]{2,1,0:T(8,128)}, u32[]{:S(2)}) copy-start(f32[16,128,128]{2,1,0:T(8,128)} %gather_fusion) | copy-start | bytes 3145732
  24.2 16.4 %copy-start.4 = (f32[1,2048]{1,0:T(1,128)S(1)}, f32[1,2048]{1,0:T(1,128)}, u32[]{:S(2)}) copy-start(f32[1,2048]{1,0:T(1,128)} %get-tuple-element.11) | copy-start | bytes 24580
  25.0 1.4 %collective-permute-start = (f32[2,2048]{1,0:T(2,128)S(1)}, f32[2,2048]{1,0:T(2,128)S(1)}, u32[]{:S(2)}, u32[]{:S(2)}) collective-permute-start(f32[2,2048]{1,0:T(2,128)S(1)} %pad_maximum_fusion.4), channel_id=1, source_target_pairs={{0,1},{1,0},{2,3},{3,2},{4,5},{5,4},{6,7},{7,6},{8,9},{9,8},{10,11... | collective-permute-start | bytes 49160 | tf_op jit(solution)/shard_map/ppermute | solution.py:156
  27.2 4.6 %collective-permute-start.1 = (f32[2,2048]{1,0:T(2,128)S(1)}, f32[2,2048]{1,0:T(2,128)S(1)}, u32[]{:S(2)}, u32[]{:S(2)}) collective-permute-start(f32[2,2048]{1,0:T(2,128)S(1)} %pad_maximum_fusion.5), channel_id=1, source_target_pairs={{0,2},{1,3},{2,0},{3,1},{4,6},{5,7},{6,4},{7,5},{8,10},{9,11},{10,... | collective-permute-start | bytes 49160 | tf_op jit(solution)/shard_map/ppermute | solution.py:156
  31.9 3.9 %collective-permute-start.2 = (f32[2,2048]{1,0:T(2,128)S(1)}, f32[2,2048]{1,0:T(2,128)S(1)}, u32[]{:S(2)}, u32[]{:S(2)}) collective-permute-start(f32[2,2048]{1,0:T(2,128)S(1)} %pad_maximum_fusion.6), channel_id=1, source_target_pairs={{0,4},{1,5},{2,6},{3,7},{4,0},{5,1},{6,2},{7,3},{8,12},{9,13},{10,... | collective-permute-start | bytes 49160 | tf_op jit(solution)/shard_map/ppermute | solution.py:156
  35.8 4.8 %collective-permute-start.3 = (f32[2,2048]{1,0:T(2,128)S(1)}, f32[2,2048]{1,0:T(2,128)S(1)}, u32[]{:S(2)}, u32[]{:S(2)}) collective-permute-start(f32[2,2048]{1,0:T(2,128)S(1)} %pad_maximum_fusion.7), channel_id=1, source_target_pairs={{0,8},{1,9},{2,10},{3,11},{4,12},{5,13},{6,14},{7,15},{8,0},{9,1},... | collective-permute-start | bytes 49160 | tf_op jit(solution)/shard_map/ppermute | solution.py:156
  49.5 4.0 %copy-start.2 = (f32[2048,128]{1,0:T(8,128)S(1)}, f32[2048,128]{1,0:T(8,128)}, u32[]{:S(2)}) copy-start(f32[2048,128]{1,0:T(8,128)} %get-tuple-element.14) | copy-start | bytes 3145732
  50.6 3.0 %copy-start.5 = (f32[8,128]{1,0:T(8,128)S(1)}, f32[8,128]{1,0:T(8,128)}, u32[]{:S(2)}) copy-start(f32[8,128]{1,0:T(8,128)} %get-tuple-element.15) | copy-start | bytes 12292
  51.4 2.0 %collective-permute-start.4 = (f32[1032,128]{1,0:T(8,128)S(1)}, f32[1032,128]{1,0:T(8,128)S(1)}, u32[]{:S(2)}, u32[]{:S(2)}) collective-permute-start(f32[1032,128]{1,0:T(8,128)S(1)} %pad_maximum_fusion), channel_id=1, source_target_pairs={{0,1},{1,0},{2,3},{3,2},{4,5},{5,4},{6,7},{7,6},{8,9},{9,8},{10,11... | collective-permute-start | bytes 1585160 | tf_op jit(solution)/shard_map/ppermute | solution.py:156
  53.5 16.9 %copy-start.6 = (f32[128]{0:T(128)S(1)}, f32[128]{0:T(128)}, u32[]{:S(2)}) copy-start(f32[128]{0:T(128)} %param.12) | copy-start | bytes 1540
  53.6 8.6 %collective-permute-start.5 = (f32[520,128]{1,0:T(8,128)S(1)}, f32[520,128]{1,0:T(8,128)S(1)}, u32[]{:S(2)}, u32[]{:S(2)}) collective-permute-start(f32[520,128]{1,0:T(8,128)S(1)} %pad_maximum_fusion.1), channel_id=1, source_target_pairs={{0,2},{1,3},{2,0},{3,1},{4,6},{5,7},{6,4},{7,5},{8,10},{9,11},{10,... | collective-permute-start | bytes 798728 | tf_op jit(solution)/shard_map/ppermute | solution.py:156
  62.4 5.1 %collective-permute-start.6 = (f32[264,128]{1,0:T(8,128)S(1)}, f32[264,128]{1,0:T(8,128)S(1)}, u32[]{:S(2)}, u32[]{:S(2)}) collective-permute-start(f32[264,128]{1,0:T(8,128)S(1)} %pad_maximum_fusion.2), channel_id=1, source_target_pairs={{0,4},{1,5},{2,6},{3,7},{4,0},{5,1},{6,2},{7,3},{8,12},{9,13},{10,... | collective-permute-start | bytes 405512 | tf_op jit(solution)/shard_map/ppermute | solution.py:156
  67.5 5.3 %collective-permute-start.7 = (f32[136,128]{1,0:T(8,128)S(1)}, f32[136,128]{1,0:T(8,128)S(1)}, u32[]{:S(2)}, u32[]{:S(2)}) collective-permute-start(f32[136,128]{1,0:T(8,128)S(1)} %pad_maximum_fusion.3), channel_id=1, source_target_pairs={{0,8},{1,9},{2,10},{3,11},{4,12},{5,13},{6,14},{7,15},{8,0},{9,1},... | collective-permute-start | bytes 208904 | tf_op jit(solution)/shard_map/ppermute | solution.py:156

commit v9 on v8

--- a/solution.py
+++ b/solution.py
@@ -1,3 +1,5 @@
+import functools
+
 import numpy as np
 import jax
 import jax.numpy as jnp
@@ -51,14 +53,18 @@
     ut_ref[...] = jnp.dot(rlt_sc[...], expd_low, preferred_element_type=jnp.float32)
 
 
-def backward_kernel(e_ref, sc_ref, qa_ref, ut_ref, q_ref, r_ref, inv_ref, rg_ref, pull_ref, terms_ref, acc_sc, qt_sc):
+def backward_kernel(final, e_ref, sc_ref, qa_ref, ut_ref, q_ref, r_ref, inv_ref, acc_ref, qt_ref, *rest):
+    if final:
+        rg_ref, pull_ref, terms_ref, acc_sc, qt_sc = rest
+    else:
+        pull_ref, acc_out, qt_out, acc_sc, qt_sc = rest
     step = pl.program_id(0)
     n_feat = q_ref.shape[1]
 
     @pl.when(step == 0)
     def _():
-        acc_sc[...] = jnp.zeros_like(acc_sc)
-        qt_sc[...] = jnp.zeros_like(qt_sc)
+        acc_sc[...] = acc_ref[...]
+        qt_sc[...] = qt_ref[...]
 
     scale = sc_ref[...]
     weight = (e_ref[...].astype(jnp.float32) * scale).astype(jnp.bfloat16)
@@ -69,12 +75,16 @@
 
     @pl.when(step == pl.num_programs(0) - 1)
     def _():
-        acc = acc_sc[...]
-        refs = r_ref[...]
-        rgrad = (acc[:, :n_feat] - refs * acc[:, n_feat:n_feat + 1]) * inv_ref[...]
-        rg_ref[...] = rgrad
-        rterm = jnp.sum(refs * rgrad, axis=0, keepdims=True)
-        terms_ref[...] = jnp.concatenate([qt_sc[...], rterm, jnp.zeros((6, n_feat), jnp.float32)], axis=0)
+        if final:
+            acc = acc_sc[...]
+            refs = r_ref[...]
+            rgrad = (acc[:, :n_feat] - refs * acc[:, n_feat:n_feat + 1]) * inv_ref[...]
+            rg_ref[...] = rgrad
+            rterm = jnp.sum(refs * rgrad, axis=0, keepdims=True)
+            terms_ref[...] = jnp.concatenate([qt_sc[...], rterm, jnp.zeros((6, n_feat), jnp.float32)], axis=0)
+        else:
+            acc_out[...] = acc_sc[...]
+            qt_out[...] = qt_sc[...]
 
 
 def local_forward(queries, inv, local_ids, references):
@@ -111,14 +121,26 @@
     )(queries, inv, local_ids, references)
 
 
-def local_backward(expd_low, scale, query_aug, unscaled_t, queries, references, inv):
+def local_backward(final, expd_low, scale, query_aug, unscaled_t, queries, references, inv, acc, qterm):
     n_ref, n_query = expd_low.shape
     n_feat = queries.shape[1]
     width = query_aug.shape[1]
     tile = min(TILE, n_query)
     whole = lambda i: (0, 0)
+    if final:
+        out_specs = [pl.BlockSpec((n_ref, n_feat), whole), pl.BlockSpec((tile, n_feat), lambda i: (i, 0)),
+                     pl.BlockSpec((8, n_feat), whole)]
+        out_shape = [jax.ShapeDtypeStruct((n_ref, n_feat), jnp.float32),
+                     jax.ShapeDtypeStruct((n_query, n_feat), jnp.float32),
+                     jax.ShapeDtypeStruct((8, n_feat), jnp.float32)]
+    else:
+        out_specs = [pl.BlockSpec((tile, n_feat), lambda i: (i, 0)), pl.BlockSpec((n_ref, width), whole),
+                     pl.BlockSpec((1, n_feat), whole)]
+        out_shape = [jax.ShapeDtypeStruct((n_query, n_feat), jnp.float32),
+                     jax.ShapeDtypeStruct((n_ref, width), jnp.float32),
+                     jax.ShapeDtypeStruct((1, n_feat), jnp.float32)]
     return pl.pallas_call(
-        backward_kernel,
+        functools.partial(backward_kernel, final),
         grid=(n_query // tile,),
         in_specs=[
             pl.BlockSpec((n_ref, tile), lambda i: (0, i)),
@@ -128,23 +150,17 @@
             pl.BlockSpec((tile, n_feat), lambda i: (i, 0)),
             pl.BlockSpec((n_ref, n_feat), whole),
             pl.BlockSpec((1, n_feat), whole),
-        ],
-        out_specs=[
-            pl.BlockSpec((n_ref, n_feat), whole),
-            pl.BlockSpec((tile, n_feat), lambda i: (i, 0)),
-            pl.BlockSpec((8, n_feat), whole),
-        ],
-        out_shape=[
-            jax.ShapeDtypeStruct((n_ref, n_feat), jnp.float32),
-            jax.ShapeDtypeStruct((n_query, n_feat), jnp.float32),
-            jax.ShapeDtypeStruct((8, n_feat), jnp.float32),
-        ],
+            pl.BlockSpec((n_ref, width), whole),
+            pl.BlockSpec((1, n_feat), whole),
+        ],
+        out_specs=out_specs,
+        out_shape=out_shape,
         scratch_shapes=[
             pltpu.VMEM((n_ref, width), jnp.float32),
             pltpu.VMEM((1, n_feat), jnp.float32),
         ],
         compiler_params=pltpu.CompilerParams(dimension_semantics=("arbitrary",)),
-    )(expd_low, scale, query_aug, unscaled_t, queries, references, inv)
+    )(expd_low, scale, query_aug, unscaled_t, queries, references, inv, acc, qterm)
 
 
 def bit_reversed(n):
@@ -199,16 +215,31 @@
     inv = 1.0 / (spread * spread)
     ref_start = lax.axis_index("ref") * n_ref
     local_ids = (query_ids - ref_start)[None, :]
-    expd_low, unscaled_t, local_peak, local_total = local_forward(queries, inv[None, :], local_ids, references)
-    peak, total = butterfly_stats(local_peak[0], local_total[0], n_dev)
-    scale = cotangent * jnp.exp(local_peak[0] - peak) / total
     query_low = queries.astype(jnp.bfloat16)
     query_aug = jnp.concatenate(
         [query_low, jnp.ones((n_query, 1), jnp.bfloat16), jnp.zeros((n_query, n_feat - 1), jnp.bfloat16)], axis=1
     )
-    reference_grad, pulled, local_terms = local_backward(
-        expd_low, scale[None, :], query_aug, unscaled_t, queries, references, inv[None, :]
-    )
+    n_half = 2 if n_query % (2 * TILE) == 0 else 1
+    rows = n_query // n_half
+    halves = [slice(h * rows, (h + 1) * rows) for h in range(n_half)]
+    forwards = [local_forward(queries[part], inv[None, :], local_ids[:, part], references) for part in halves]
+    acc = jnp.zeros((n_ref, query_aug.shape[1]), jnp.float32)
+    qterm = jnp.zeros((1, n_feat), jnp.float32)
+    pulled_parts = []
+    for h, part in enumerate(halves):
+        expd_low, unscaled_t, local_peak, local_total = forwards[h]
+        peak, total = butterfly_stats(local_peak[0], local_total[0], n_dev)
+        scale = cotangent[part] * jnp.exp(local_peak[0] - peak) / total
+        outs = local_backward(
+            h == n_half - 1, expd_low, scale[None, :], query_aug[part], unscaled_t, queries[part],
+            references, inv[None, :], acc, qterm,
+        )
+        if h == n_half - 1:
+            reference_grad, pulled_part, local_terms = outs
+        else:
+            pulled_part, acc, qterm = outs
+        pulled_parts.append(pulled_part)
+    pulled = jnp.concatenate(pulled_parts, axis=0)
     own_pulled, summed_terms = halving_scatter(pulled, local_terms, n_dev)
     own_start = lax.axis_index("ref") * own_rows
     own_queries = lax.dynamic_slice_in_dim(all_queries, own_start, own_rows, 0)

time: 76 us -> 85.7 us (1.13)
  Pallas kernels: 25.8 us -> 33 us
  starting transfers between devices: 15.4 us -> 18.9 us
  local copies, waits for them, and re-layouts: 5.51 us -> 8.14 us
  waiting for transfers between devices: 17.3 us -> 14.9 us
  other arithmetic: 10.5 us -> 9.29 us
    pallas_call x1 -> x2, Pallas kernels: 8.2 us -> 12.2 us  [local_backward(): pl.pallas_call(functools.partial(backward_kernel, final), grid=(n_query /...]
    ppermute x8 -> x12, starting transfers between devices: 15.4 us -> 18.9 us  [exchange(): return lax.ppermute(x, 'ref', [(i, i ^ step) for i in range(n_dev)])]
    pallas_call x1 -> x2, Pallas kernels: 17.6 us -> 20.9 us  [local_forward(): pl.pallas_call(forward_kernel, grid=(n_query // tile,), in_specs=[pl.Bloc...]
    slice x0 -> x4, local copies, waits for them, and re-layouts: none -> 2.77 us  [the longest x1 1.12 us: on_device(): queries[part]]
    ppermute x8 -> x12, waiting for transfers between devices: 17.3 us -> 14.9 us  [exchange(): return lax.ppermute(x, 'ref', [(i, i ^ step) for i in range(n_dev)])]
    broadcast_in_dim x0 -> x2, local copies, waits for them, and re-layouts: none -> 2.01 us  [the longest x1 1.49 us: on_device(): acc = jnp.zeros((n_ref, query_aug.shape[1]), jnp.float32)]
    dynamic_slice x3, local copies, waits for them, and re-layouts: 1.21 us -> 0.09 us  [halving_scatter(): send = lax.dynamic_slice_in_dim(blocks, (1 - bit) * half, half, 0)]
    concatenate x0 -> x1, other arithmetic: none -> 1.11 us  [on_device(): pulled = jnp.concatenate(pulled_parts, axis=0)]
  transfers between devices with their start and end apart: 8 -> 12, of which waited for: 8 -> 5; matrix products, arithmetic and copies ran while one was open for 4% -> 8% of each run, Pallas kernels for 0% -> 19%
where the time goes in v9:
time: 85.7 us; the launch traced here: 85.3 us
  Pallas kernels  33 us (39%)
  starting transfers between devices  18.9 us (22%)
  waiting for transfers between devices  14.9 us (17%)
  other arithmetic  9.29 us (11%)
  local copies, waits for them, and re-layouts  8.14 us (9%)
  between operations  1.02 us (1%)
    pallas_call x2, Pallas kernels, local_forward(): pl.pallas_call(forward_kernel, grid=(n_query // tile,), in_specs=[pl.Bloc...  20.9 us
    ppermute x12, starting transfers between devices, exchange(): return lax.ppermute(x, 'ref', [(i, i ^ step) for i in range(n_dev)])  18.9 us
    ppermute x12, waiting for transfers between devices, exchange(): return lax.ppermute(x, 'ref', [(i, i ^ step) for i in range(n_dev)])  14.9 us
    pallas_call x2, Pallas kernels, local_backward(): pl.pallas_call(functools.partial(backward_kernel, final), grid=(n_query /...  12.2 us
    gather x3, local copies, waits for them, and re-layouts, on_device(): x.reshape((n_dev, own_rows) + x.shape[1:])[order].reshape(x.shape)  2.97 us
  transfers between devices with their start and end apart: 12, of which 5 were waited for; matrix products, arithmetic and copies ran while one was open for 8% of the time, Pallas kernels for 19%

profile of v9, /device:TPU:0, one launch (start us, length us, event | category | flops | bytes accessed | tf_op | source)
XLA Modules:
  0.0 85.3 jit_solution(15623043429855112244)
XLA Ops:
  2.5 1.9 %gather_fusion = f32[16,128,128]{2,1,0:T(8,128)S(1)} fusion(f32[16,128,128]{2,1,0:T(8,128)} %bitcast.61, s32[1024]{0:T(1024)S(1)} %pad_clamp_fusion), kind=kCustom, calls=%fused_computation | custom fusion | bytes 2097216 | tf_op jit(solution)/shard_map/gather | solution.py:212
  4.4 1.1 %fusion.22 = (f32[8,128,128]{2,1,0:T(8,128)}, f32[8,128,128]{2,1,0:T(8,128)}) fusion(f32[16,128,128]{2,1,0:T(8,128)S(1)} %gather_fusion), kind=kLoop, calls=%fused_computation.74 | loop fusion | bytes 2097152 | tf_op jit(solution)/shard_map/slice | solution.py:225
  6.0 10.5 %shard_map.112 = (bf16[2048,1024]{1,0:T(8,128)(2,1)}, f32[128,1024]{1,0:T(8,128)}, f32[1,1024]{1,0:T(1,128)}, f32[1,1024]{1,0:T(1,128)}) custom-call(f32[1024,128]{1,0:T(8,128)} %bitcast.54, f32[1,128]{1,0:T(1,128)} %fusion.25.inv_ref, s32[1,1024]{1,0:T(1,128)} %get-tuple-element.51.lid_ref, f32[2048,128]{1,0:T(8,128)} %r_ref.7), custom_call_target="tpu_custom_call" | custom-call | tf_op jit(solution)/shard_map/pallas_call | solution.py:94
  17.7 10.4 %shard_map.114 = (bf16[2048,1024]{1,0:T(8,128)(2,1)}, f32[128,1024]{1,0:T(8,128)}, f32[1,1024]{1,0:T(1,128)}, f32[1,1024]{1,0:T(1,128)}) custom-call(f32[1024,128]{1,0:T(8,128)} %bitcast.52, f32[1,128]{1,0:T(1,128)} %fusion.25.inv_ref, s32[1,1024]{1,0:T(1,128)} %get-tuple-element.52.lid_ref, f32[2048,128]{1,0:T(8,128)} %r_ref.7), custom_call_target="tpu_custom_call" | custom-call | tf_op jit(solution)/shard_map/pallas_call | solution.py:94
  30.2 1.1 %fusion.21 = (bf16[1024,256]{1,0:T(8,128)(2,1)}, bf16[1024,256]{1,0:T(8,128)(2,1)}) fusion(bf16[2048,256]{1,0:T(8,128)(2,1)S(1)} %maximum_maximum_fusion), kind=kLoop, calls=%fused_computation.73 | loop fusion | bytes 2097152 | tf_op jit(solution)/shard_map/slice | solution.py:234
  31.3 3.0 %collective-permute-start.1 = (f32[2,1024]{1,0:T(2,128)S(1)}, f32[2,1024]{1,0:T(2,128)S(1)}, u32[]{:S(2)}, u32[]{:S(2)}) collective-permute-start(f32[2,1024]{1,0:T(2,128)S(1)} %pad_maximum_fusion.6), channel_id=1, source_target_pairs={{0,2},{1,3},{2,0},{3,1},{4,6},{5,7},{6,4},{7,5},{8,10},{9,11},{10,... | collective-permute-start | bytes 24584 | tf_op jit(solution)/shard_map/ppermute | solution.py:172
  34.5 1.5 %collective-permute-done.1 = f32[2,1024]{1,0:T(2,128)S(1)} collective-permute-done((f32[2,1024]{1,0:T(2,128)S(1)}, f32[2,1024]{1,0:T(2,128)S(1)}, u32[]{:S(2)}, u32[]{:S(2)}) %collective-permute-start.1) | collective-permute-done | bytes 8224 | tf_op jit(solution)/shard_map/ppermute | solution.py:172
  36.0 2.2 %collective-permute-start.2 = (f32[2,1024]{1,0:T(2,128)S(1)}, f32[2,1024]{1,0:T(2,128)S(1)}, u32[]{:S(2)}, u32[]{:S(2)}) collective-permute-start(f32[2,1024]{1,0:T(2,128)S(1)} %pad_maximum_fusion.7), channel_id=1, source_target_pairs={{0,4},{1,5},{2,6},{3,7},{4,0},{5,1},{6,2},{7,3},{8,12},{9,13},{10,... | collective-permute-start | bytes 24584 | tf_op jit(solution)/shard_map/ppermute | solution.py:172
  38.2 1.6 %collective-permute-start.6 = (f32[2,1024]{1,0:T(2,128)S(1)}, f32[2,1024]{1,0:T(2,128)S(1)}, u32[]{:S(2)}, u32[]{:S(2)}) collective-permute-start(f32[2,1024]{1,0:T(2,128)S(1)} %pad_maximum_fusion.11), channel_id=1, source_target_pairs={{0,4},{1,5},{2,6},{3,7},{4,0},{5,1},{6,2},{7,3},{8,12},{9,13},{10,... | collective-permute-start | bytes 24584 | tf_op jit(solution)/shard_map/ppermute | solution.py:172
  39.8 3.1 %collective-permute-start.3 = (f32[2,1024]{1,0:T(2,128)S(1)}, f32[2,1024]{1,0:T(2,128)S(1)}, u32[]{:S(2)}, u32[]{:S(2)}) collective-permute-start(f32[2,1024]{1,0:T(2,128)S(1)} %pad_maximum_fusion.8), channel_id=1, source_target_pairs={{0,8},{1,9},{2,10},{3,11},{4,12},{5,13},{6,14},{7,15},{8,0},{9,1},... | collective-permute-start | bytes 24584 | tf_op jit(solution)/shard_map/ppermute | solution.py:172
  43.0 1.6 %collective-permute-start.7 = (f32[2,1024]{1,0:T(2,128)S(1)}, f32[2,1024]{1,0:T(2,128)S(1)}, u32[]{:S(2)}, u32[]{:S(2)}) collective-permute-start(f32[2,1024]{1,0:T(2,128)S(1)} %pad_maximum_fusion.12), channel_id=1, source_target_pairs={{0,8},{1,9},{2,10},{3,11},{4,12},{5,13},{6,14},{7,15},{8,0},{9,1},... | collective-permute-start | bytes 24584 | tf_op jit(solution)/shard_map/ppermute | solution.py:172
  45.3 1.5 %broadcast_in_dim.38.acc_ref = f32[2048,256]{1,0:T(8,128)} broadcast(f32[]{:T(128)} %constant.84.clone.1), dimensions={} | broadcast | bytes 2097156 | tf_op jit(solution)/shard_map/broadcast_in_dim | solution.py:226
  47.3 6.1 %shard_map.113 = (f32[1024,128]{1,0:T(8,128)}, f32[2048,256]{1,0:T(8,128)}, f32[1,128]{1,0:T(1,128)}) custom-call(bf16[2048,1024]{1,0:T(8,128)(2,1)} %get-tuple-element.17.e_ref, f32[1,1024]{1,0:T(1,128)} %fusion.10.sc_ref, bf16[1024,256]{1,0:T(8,128)(2,1)} %get-tuple-element.45.qa_ref, f32[128,1024]{1,0:T(8,128)} %get-tuple-element.20.ut_ref, ...), custom_call_target="tpu_custom_call" | custom-call | tf_op jit(solution)/shard_map/pallas_call | solution.py:142
  54.1 6.0 %shard_map.115 = (f32[2048,128]{1,0:T(8,128)}, f32[1024,128]{1,0:T(8,128)}, f32[8,128]{1,0:T(8,128)}) custom-call(bf16[2048,1024]{1,0:T(8,128)(2,1)} %get-tuple-element.22.e_ref, f32[1,1024]{1,0:T(1,128)} %fusion.5.sc_ref, bf16[1024,256]{1,0:T(8,128)(2,1)} %get-tuple-element.46.qa_ref, f32[128,1024]{1,0:T(8,128)} %get-tuple-element.25.ut_ref, ...), custom_call_target="tpu_custom_call" | custom-call | tf_op jit(solution)/shard_map/pallas_call | solution.py:142
  60.1 1.1 %pad_maximum_fusion = f32[2048,128]{1,0:T(8,128)S(1)} fusion(f32[1024,128]{1,0:T(8,128)} %get-tuple-element.28, f32[1024,128]{1,0:T(8,128)S(1)} %copy-done.2), kind=kLoop, calls=%fused_computation.4 | loop fusion | flops 262144 | bytes 2097152 | tf_op jit(solution)/shard_map/concatenate | solution.py:242
  61.5 1.9 %collective-permute-done.8 = f32[1032,128]{1,0:T(8,128)S(1)} collective-permute-done((f32[1032,128]{1,0:T(8,128)S(1)}, f32[1032,128]{1,0:T(8,128)S(1)}, u32[]{:S(2)}, u32[]{:S(2)}) %collective-permute-start.8) | collective-permute-done | bytes 528416 | tf_op jit(solution)/shard_map/ppermute | solution.py:172
  63.5 1.8 %collective-permute-start.9 = (f32[520,128]{1,0:T(8,128)S(1)}, f32[520,128]{1,0:T(8,128)S(1)}, u32[]{:S(2)}, u32[]{:S(2)}) collective-permute-start(f32[520,128]{1,0:T(8,128)S(1)} %pad_maximum_fusion.2), channel_id=1, source_target_pairs={{0,2},{1,3},{2,0},{3,1},{4,6},{5,7},{6,4},{7,5},{8,10},{9,11},{10,... | collective-permute-start | bytes 798728 | tf_op jit(solution)/shard_map/ppermute | solution.py:172
  65.4 6.7 %collective-permute-done.9 = f32[520,128]{1,0:T(8,128)S(1)} collective-permute-done((f32[520,128]{1,0:T(8,128)S(1)}, f32[520,128]{1,0:T(8,128)S(1)}, u32[]{:S(2)}, u32[]{:S(2)}) %collective-permute-start.9) | collective-permute-done | bytes 266272 | tf_op jit(solution)/shard_map/ppermute | solution.py:172
  72.2 1.9 %collective-permute-start.10 = (f32[264,128]{1,0:T(8,128)S(1)}, f32[264,128]{1,0:T(8,128)S(1)}, u32[]{:S(2)}, u32[]{:S(2)}) collective-permute-start(f32[264,128]{1,0:T(8,128)S(1)} %pad_maximum_fusion.3), channel_id=1, source_target_pairs={{0,4},{1,5},{2,6},{3,7},{4,0},{5,1},{6,2},{7,3},{8,12},{9,13},{10,... | collective-permute-start | bytes 405512 | tf_op jit(solution)/shard_map/ppermute | solution.py:172
  74.0 3.2 %collective-permute-done.10 = f32[264,128]{1,0:T(8,128)S(1)} collective-permute-done((f32[264,128]{1,0:T(8,128)S(1)}, f32[264,128]{1,0:T(8,128)S(1)}, u32[]{:S(2)}, u32[]{:S(2)}) %collective-permute-start.10) | collective-permute-done | bytes 135200 | tf_op jit(solution)/shard_map/ppermute | solution.py:172
  77.3 2.9 %collective-permute-start.11 = (f32[136,128]{1,0:T(8,128)S(1)}, f32[136,128]{1,0:T(8,128)S(1)}, u32[]{:S(2)}, u32[]{:S(2)}) collective-permute-start(f32[136,128]{1,0:T(8,128)S(1)} %pad_maximum_fusion.4), channel_id=1, source_target_pairs={{0,8},{1,9},{2,10},{3,11},{4,12},{5,13},{6,14},{7,15},{8,0},{9,1},... | collective-permute-start | bytes 208904 | tf_op jit(solution)/shard_map/ppermute | solution.py:172
  80.9 1.7 %collective-permute-done.11 = f32[136,128]{1,0:T(8,128)S(1)} collective-permute-done((f32[136,128]{1,0:T(8,128)S(1)}, f32[136,128]{1,0:T(8,128)S(1)}, u32[]{:S(2)}, u32[]{:S(2)}) %collective-permute-start.11) | collective-permute-done | bytes 69664 | tf_op jit(solution)/shard_map/ppermute | solution.py:172
  82.6 1.2 %divide_subtract_fusion = f32[128]{0:T(128)} fusion(f32[128]{0:T(128)S(1)} %copy-done.8, f32[128]{0:T(128)S(1)} %get-tuple-element.43, f32[8,128]{1,0:T(8,128)S(1)} %slice_add_fusion, f32[]{:T(128)} %reduce_sum.19), kind=kLoop, calls=%fused_computation.66 | loop fusion | flops 1152 | bytes 2564 | tf_op jit(solution)/shard_map/sub | solution.py:251
  83.8 1.6 %fusion.3 = f32[128,128]{1,0:T(8,128)} fusion(f32[136,128]{1,0:T(8,128)S(1)} %collective-permute-done.11, f32[2048,128]{1,0:T(8,128)} %param.9, s32[]{:T(128)S(6)} %select_n.85, f32[2,128,128]{2,1,0:T(8,128)S(1)} %dynamic-slice_add_fusion.2, s32[]{:T(128)S(6)} %select_n.83, f32[128]{0:T(128)S(1)} %multiply_divide_fusion, f32[128]{0:T(128)S(1)} %dynamic_slice.39), kind=kLoop, calls=%fused_computation.17 | loop fusion | flops 65536 | bytes 263176 | tf_op jit(solution)/shard_map/mul | solution.py:247
  (79 shorter events, 8.9 us)
Async XLA Ops:
  0.6 0.7 copy-start
  2.5 3.0 %copy-start.8 = (f32[128]{0:T(128)S(1)}, f32[128]{0:T(128)}, u32[]{:S(2)}) copy-start(f32[128]{0:T(128)} %param.12) | copy-start | bytes 1540
  5.5 23.4 %copy-start.1 = (f32[2048]{0:T(1024)S(1)}, f32[2048]{0:T(1024)}, u32[]{:S(2)}) copy-start(f32[2048]{0:T(1024)} %param.13) | copy-start | bytes 24580
  17.2 14.1 %collective-permute-start = (f32[2,1024]{1,0:T(2,128)S(1)}, f32[2,1024]{1,0:T(2,128)S(1)}, u32[]{:S(2)}, u32[]{:S(2)}) collective-permute-start(f32[2,1024]{1,0:T(2,128)S(1)} %pad_maximum_fusion.5), channel_id=1, source_target_pairs={{0,1},{1,0},{2,3},{3,2},{4,5},{5,4},{6,7},{7,6},{8,9},{9,8},{10,11... | collective-permute-start | bytes 24584 | tf_op jit(solution)/shard_map/ppermute | solution.py:172
  28.8 5.5 %collective-permute-start.4 = (f32[2,1024]{1,0:T(2,128)S(1)}, f32[2,1024]{1,0:T(2,128)S(1)}, u32[]{:S(2)}, u32[]{:S(2)}) collective-permute-start(f32[2,1024]{1,0:T(2,128)S(1)} %pad_maximum_fusion.9), channel_id=1, source_target_pairs={{0,1},{1,0},{2,3},{3,2},{4,5},{5,4},{6,7},{7,6},{8,9},{9,8},{10,11... | collective-permute-start | bytes 24584 | tf_op jit(solution)/shard_map/ppermute | solution.py:172
  29.9 1.4 %copy-start.4 = (f32[1,1024]{1,0:T(1,128)S(1)}, f32[1,1024]{1,0:T(1,128)}, u32[]{:S(2)}) copy-start(f32[1,1024]{1,0:T(1,128)} %get-tuple-element.18) | copy-start | bytes 12292
  29.9 1.4 %copy-start.7 = (f32[1,1024]{1,0:T(1,128)S(1)}, f32[1,1024]{1,0:T(1,128)}, u32[]{:S(2)}) copy-start(f32[1,1024]{1,0:T(1,128)} %get-tuple-element.19) | copy-start | bytes 12292
  29.9 4.4 %copy-start.3 = (f32[1,1024]{1,0:T(1,128)S(1)}, f32[1,1024]{1,0:T(1,128)}, u32[]{:S(2)}) copy-start(f32[1,1024]{1,0:T(1,128)} %get-tuple-element.23) | copy-start | bytes 12292
  29.9 4.4 %copy-start.6 = (f32[1,1024]{1,0:T(1,128)S(1)}, f32[1,1024]{1,0:T(1,128)}, u32[]{:S(2)}) copy-start(f32[1,1024]{1,0:T(1,128)} %get-tuple-element.24) | copy-start | bytes 12292
  31.3 4.7 %collective-permute-start.1 = (f32[2,1024]{1,0:T(2,128)S(1)}, f32[2,1024]{1,0:T(2,128)S(1)}, u32[]{:S(2)}, u32[]{:S(2)}) collective-permute-start(f32[2,1024]{1,0:T(2,128)S(1)} %pad_maximum_fusion.6), channel_id=1, source_target_pairs={{0,2},{1,3},{2,0},{3,1},{4,6},{5,7},{6,4},{7,5},{8,10},{9,11},{10,... | collective-permute-start | bytes 24584 | tf_op jit(solution)/shard_map/ppermute | solution.py:172
  34.4 3.8 %collective-permute-start.5 = (f32[2,1024]{1,0:T(2,128)S(1)}, f32[2,1024]{1,0:T(2,128)S(1)}, u32[]{:S(2)}, u32[]{:S(2)}) collective-permute-start(f32[2,1024]{1,0:T(2,128)S(1)} %pad_maximum_fusion.10), channel_id=1, source_target_pairs={{0,2},{1,3},{2,0},{3,1},{4,6},{5,7},{6,4},{7,5},{8,10},{9,11},{10,... | collective-permute-start | bytes 24584 | tf_op jit(solution)/shard_map/ppermute | solution.py:172
  36.0 3.8 %collective-permute-start.2 = (f32[2,1024]{1,0:T(2,128)S(1)}, f32[2,1024]{1,0:T(2,128)S(1)}, u32[]{:S(2)}, u32[]{:S(2)}) collective-permute-start(f32[2,1024]{1,0:T(2,128)S(1)} %pad_maximum_fusion.7), channel_id=1, source_target_pairs={{0,4},{1,5},{2,6},{3,7},{4,0},{5,1},{6,2},{7,3},{8,12},{9,13},{10,... | collective-permute-start | bytes 24584 | tf_op jit(solution)/shard_map/ppermute | solution.py:172
  38.2 4.7 %collective-permute-start.6 = (f32[2,1024]{1,0:T(2,128)S(1)}, f32[2,1024]{1,0:T(2,128)S(1)}, u32[]{:S(2)}, u32[]{:S(2)}) collective-permute-start(f32[2,1024]{1,0:T(2,128)S(1)} %pad_maximum_fusion.11), channel_id=1, source_target_pairs={{0,4},{1,5},{2,6},{3,7},{4,0},{5,1},{6,2},{7,3},{8,12},{9,13},{10,... | collective-permute-start | bytes 24584 | tf_op jit(solution)/shard_map/ppermute | solution.py:172
  39.8 4.8 %collective-permute-start.3 = (f32[2,1024]{1,0:T(2,128)S(1)}, f32[2,1024]{1,0:T(2,128)S(1)}, u32[]{:S(2)}, u32[]{:S(2)}) collective-permute-start(f32[2,1024]{1,0:T(2,128)S(1)} %pad_maximum_fusion.8), channel_id=1, source_target_pairs={{0,8},{1,9},{2,10},{3,11},{4,12},{5,13},{6,14},{7,15},{8,0},{9,1},... | collective-permute-start | bytes 24584 | tf_op jit(solution)/shard_map/ppermute | solution.py:172
  43.0 10.4 %collective-permute-start.7 = (f32[2,1024]{1,0:T(2,128)S(1)}, f32[2,1024]{1,0:T(2,128)S(1)}, u32[]{:S(2)}, u32[]{:S(2)}) collective-permute-start(f32[2,1024]{1,0:T(2,128)S(1)} %pad_maximum_fusion.12), channel_id=1, source_target_pairs={{0,8},{1,9},{2,10},{3,11},{4,12},{5,13},{6,14},{7,15},{8,0},{9,1},... | collective-permute-start | bytes 24584 | tf_op jit(solution)/shard_map/ppermute | solution.py:172
  54.1 6.0 %copy-start.2 = (f32[1024,128]{1,0:T(8,128)S(1)}, f32[1024,128]{1,0:T(8,128)}, u32[]{:S(2)}) copy-start(f32[1024,128]{1,0:T(8,128)} %get-tuple-element.21) | copy-start | bytes 1572868
  60.1 1.2 %copy-start.5 = (f32[8,128]{1,0:T(8,128)S(1)}, f32[8,128]{1,0:T(8,128)}, u32[]{:S(2)}) copy-start(f32[8,128]{1,0:T(8,128)} %get-tuple-element.29) | copy-start | bytes 12292
  61.3 2.0 %collective-permute-start.8 = (f32[1032,128]{1,0:T(8,128)S(1)}, f32[1032,128]{1,0:T(8,128)S(1)}, u32[]{:S(2)}, u32[]{:S(2)}) collective-permute-start(f32[1032,128]{1,0:T(8,128)S(1)} %pad_maximum_fusion.1), channel_id=1, source_target_pairs={{0,1},{1,0},{2,3},{3,2},{4,5},{5,4},{6,7},{7,6},{8,9},{9,8},{10,11... | collective-permute-start | bytes 1585160 | tf_op jit(solution)/shard_map/ppermute | solution.py:172
  63.5 8.5 %collective-permute-start.9 = (f32[520,128]{1,0:T(8,128)S(1)}, f32[520,128]{1,0:T(8,128)S(1)}, u32[]{:S(2)}, u32[]{:S(2)}) collective-permute-start(f32[520,128]{1,0:T(8,128)S(1)} %pad_maximum_fusion.2), channel_id=1, source_target_pairs={{0,2},{1,3},{2,0},{3,1},{4,6},{5,7},{6,4},{7,5},{8,10},{9,11},{10,... | collective-permute-start | bytes 798728 | tf_op jit(solution)/shard_map/ppermute | solution.py:172
  72.2 5.1 %collective-permute-start.10 = (f32[264,128]{1,0:T(8,128)S(1)}, f32[264,128]{1,0:T(8,128)S(1)}, u32[]{:S(2)}, u32[]{:S(2)}) collective-permute-start(f32[264,128]{1,0:T(8,128)S(1)} %pad_maximum_fusion.3), channel_id=1, source_target_pairs={{0,4},{1,5},{2,6},{3,7},{4,0},{5,1},{6,2},{7,3},{8,12},{9,13},{10,... | collective-permute-start | bytes 405512 | tf_op jit(solution)/shard_map/ppermute | solution.py:172
  77.3 5.3 %collective-permute-start.11 = (f32[136,128]{1,0:T(8,128)S(1)}, f32[136,128]{1,0:T(8,128)S(1)}, u32[]{:S(2)}, u32[]{:S(2)}) collective-permute-start(f32[136,128]{1,0:T(8,128)S(1)} %pad_maximum_fusion.4), channel_id=1, source_target_pairs={{0,8},{1,9},{2,10},{3,11},{4,12},{5,13},{6,14},{7,15},{8,0},{9,1},... | collective-permute-start | bytes 208904 | tf_op jit(solution)/shard_map/ppermute | solution.py:172

commit v10 on v8

--- a/solution.py
+++ b/solution.py
@@ -61,8 +61,7 @@
         qt_sc[...] = jnp.zeros_like(qt_sc)
 
     scale = sc_ref[...]
-    weight = (e_ref[...].astype(jnp.float32) * scale).astype(jnp.bfloat16)
-    acc_sc[...] += jnp.dot(weight, qa_ref[...], preferred_element_type=jnp.float32)
+    acc_sc[...] += jnp.dot(e_ref[...], qa_ref[...], preferred_element_type=jnp.float32)
     pulled = (ut_ref[...] * scale).T
     pull_ref[...] = pulled
     qt_sc[...] += jnp.sum(q_ref[...] * pulled, axis=0, keepdims=True)
@@ -71,7 +70,8 @@
     def _():
         acc = acc_sc[...]
         refs = r_ref[...]
-        rgrad = (acc[:, :n_feat] - refs * acc[:, n_feat:n_feat + 1]) * inv_ref[...]
+        column = acc[:, n_feat:n_feat + 1] + acc[:, n_feat + 1:n_feat + 2]
+        rgrad = (acc[:, :n_feat] - refs * column) * inv_ref[...]
         rg_ref[...] = rgrad
         rterm = jnp.sum(refs * rgrad, axis=0, keepdims=True)
         terms_ref[...] = jnp.concatenate([qt_sc[...], rterm, jnp.zeros((6, n_feat), jnp.float32)], axis=0)
@@ -192,8 +192,11 @@
     n_ref = references.shape[0]
     n_dev = lax.axis_size("ref")
     own_rows = n_query // n_dev
-    order = bit_reversed(n_dev)
-    reorder = lambda x: x.reshape((n_dev, own_rows) + x.shape[1:])[order].reshape(x.shape)
+    n_bits = n_dev.bit_length() - 1
+    flip = tuple(reversed(range(n_bits)))
+    reorder = lambda x: jnp.transpose(
+        x.reshape((2,) * n_bits + (own_rows,) + x.shape[1:]), flip + tuple(range(n_bits, x.ndim + n_bits))
+    ).reshape(x.shape)
     all_queries, all_cotangent = queries, cotangent
     queries, query_ids, cotangent = reorder(queries), reorder(query_ids), reorder(cotangent)
     inv = 1.0 / (spread * spread)
@@ -202,9 +205,11 @@
     expd_low, unscaled_t, local_peak, local_total = local_forward(queries, inv[None, :], local_ids, references)
     peak, total = butterfly_stats(local_peak[0], local_total[0], n_dev)
     scale = cotangent * jnp.exp(local_peak[0] - peak) / total
-    query_low = queries.astype(jnp.bfloat16)
+    scale_hi = scale.astype(jnp.bfloat16)
+    scale_lo = (scale - scale_hi.astype(jnp.float32)).astype(jnp.bfloat16)
     query_aug = jnp.concatenate(
-        [query_low, jnp.ones((n_query, 1), jnp.bfloat16), jnp.zeros((n_query, n_feat - 1), jnp.bfloat16)], axis=1
+        [(queries * scale[:, None]).astype(jnp.bfloat16), scale_hi[:, None], scale_lo[:, None],
+         jnp.zeros((n_query, n_feat - 2), jnp.bfloat16)], axis=1
     )
     reference_grad, pulled, local_terms = local_backward(
         expd_low, scale[None, :], query_aug, unscaled_t, queries, references, inv[None, :]

time: 76 us -> 93.6 us (1.23)
  local copies, waits for them, and re-layouts: 5.51 us -> 21 us
  starting transfers between devices: 15.4 us -> 10.9 us
  other arithmetic: 10.5 us -> 13.8 us
  waiting for transfers between devices: 17.3 us -> 20.3 us
    squeeze x0 -> x10, local copies, waits for them, and re-layouts: none -> 13 us  [the longest x8 10.9 us: butterfly_stats(): other_peak, other_total = (other[0], other[1])]
    convert_element_type x0 -> x2, other arithmetic: none -> 5.71 us  [the longest x1 5.38 us: on_device(): scale_lo = (scale - scale_hi.astype(jnp.float32)).astype(jnp.bfloat16)]
    ppermute x8, starting transfers between devices: 15.4 us -> 10.9 us  [exchange(): return lax.ppermute(x, 'ref', [(i, i ^ step) for i in range(n_dev)])]
    gather x3 -> x0, local copies, waits for them, and re-layouts: 4.02 us -> none  [on_device(): x.reshape((n_dev, own_rows) + x.shape[1:])[order].reshape(x.shape)]
    reshape x0 -> x2, local copies, waits for them, and re-layouts: none -> 3.75 us  [the longest x1 2.4 us: on_device(): x.reshape((2,) * n_bits + (own_rows,) + x.shape[1:])]
    ppermute x8, waiting for transfers between devices: 17.3 us -> 20.3 us  [exchange(): return lax.ppermute(x, 'ref', [(i, i ^ step) for i in range(n_dev)])]
    slice x0 -> x4, other arithmetic: none -> 1.5 us  [butterfly_stats(): other_peak, other_total = (other[0], other[1])]
    max x0 -> x1, local copies, waits for them, and re-layouts: none -> 1.36 us  [butterfly_stats(): new_peak = jnp.maximum(peak, other_peak)]
  transfers between devices with their start and end apart: 8 -> 8, of which waited for: 8 -> 6; matrix products, arithmetic and copies ran while one was open for 4% -> 15% of each run, Pallas kernels for 0% -> 0%
where the time goes in v10:
time: 93.6 us; the launch traced here: 93.1 us
  Pallas kernels  26.1 us (28%)
  local copies, waits for them, and re-layouts  21 us (22%)
  waiting for transfers between devices  20.3 us (22%)
  other arithmetic  13.8 us (15%)
  starting transfers between devices  10.9 us (12%)
  between operations  0.94 us (1%)
    ppermute x8, waiting for transfers between devices, exchange(): return lax.ppermute(x, 'ref', [(i, i ^ step) for i in range(n_dev)])  20.3 us
    pallas_call x1, Pallas kernels, local_forward(): pl.pallas_call(forward_kernel, grid=(n_query // tile,), in_specs=[pl.Bloc...  17.6 us
    squeeze x8, local copies, waits for them, and re-layouts, butterfly_stats(): other_peak, other_total = (other[0], other[1])  10.9 us
    ppermute x8, starting transfers between devices, exchange(): return lax.ppermute(x, 'ref', [(i, i ^ step) for i in range(n_dev)])  10.9 us
    pallas_call x1, Pallas kernels, local_backward(): pl.pallas_call(backward_kernel, grid=(n_query // tile,), in_specs=[pl.Blo...  8.46 us
    convert_element_type x1, other arithmetic, on_device(): scale_lo = (scale - scale_hi.astype(jnp.float32)).astype(jnp.bfloat16)  5.38 us
    reshape x1, local copies, waits for them, and re-layouts, on_device(): x.reshape((2,) * n_bits + (own_rows,) + x.shape[1:])  2.4 us
  transfers between devices with their start and end apart: 8, of which 6 were waited for; matrix products, arithmetic and copies ran while one was open for 15% of the time, Pallas kernels for 0%

profile of v10, /device:TPU:0, one launch (start us, length us, event | category | flops | bytes accessed | tf_op | source)
XLA Modules:
  0.0 93.1 jit_solution(18320159240492086826)
XLA Ops:
  0.7 2.4 %copy.54 = f32[2,2,2,2,128,128]{5,4,0,1,2,3:T(8,128)} copy(f32[2,2,2,2,128,128]{5,4,3,2,1,0:T(8,128)} %bitcast.95) | data formatting | bytes 2097152 | tf_op jit(solution)/shard_map/reshape | solution.py:198
  4.2 17.6 %shard_map.76 = (bf16[2048,2048]{1,0:T(8,128)(2,1)}, f32[128,2048]{1,0:T(8,128)}, f32[1,2048]{1,0:T(1,128)}, f32[1,2048]{1,0:T(1,128)}) custom-call(f32[2048,128]{1,0:T(8,128)} %bitcast.93, f32[1,128]{1,0:T(1,128)} %fusion.32.inv_ref, s32[1,2048]{1,0:T(1,128)} %bitcast.111, f32[2048,128]{1,0:T(8,128)} %r_ref.3), custom_call_target="tpu_custom_call" | custom-call | tf_op jit(solution)/shard_map/pallas_call | solution.py:84
  24.8 2.9 %collective-permute-start.1 = (f32[2,2048]{1,0:T(2,128)S(1)}, f32[2,2048]{1,0:T(2,128)S(1)}, u32[]{:S(2)}, u32[]{:S(2)}) collective-permute-start(f32[2,2048]{1,0:T(2,128)S(1)} %pad_maximum_fusion.5), channel_id=1, source_target_pairs={{0,2},{1,3},{2,0},{3,1},{4,6},{5,7},{6,4},{7,5},{8,10},{9,11},{10,... | collective-permute-start | bytes 49160 | tf_op jit(solution)/shard_map/ppermute | solution.py:156
  27.7 1.7 %collective-permute-done.1 = f32[2,2048]{1,0:T(2,128)S(1)} collective-permute-done((f32[2,2048]{1,0:T(2,128)S(1)}, f32[2,2048]{1,0:T(2,128)S(1)}, u32[]{:S(2)}, u32[]{:S(2)}) %collective-permute-start.1) | collective-permute-done | bytes 16416 | tf_op jit(solution)/shard_map/ppermute | solution.py:156
  29.5 2.1 %collective-permute-start.2 = (f32[2,2048]{1,0:T(2,128)S(1)}, f32[2,2048]{1,0:T(2,128)S(1)}, u32[]{:S(2)}, u32[]{:S(2)}) collective-permute-start(f32[2,2048]{1,0:T(2,128)S(1)} %pad_maximum_fusion.6), channel_id=1, source_target_pairs={{0,4},{1,5},{2,6},{3,7},{4,0},{5,1},{6,2},{7,3},{8,12},{9,13},{10,... | collective-permute-start | bytes 49160 | tf_op jit(solution)/shard_map/ppermute | solution.py:156
  33.8 1.4 %copy.64 = f32[2048,1]{1,0:T(8,128)} copy(f32[2048,1]{0,1:T(1,128)S(1)} %bitcast.106) | data formatting | bytes 16384 | tf_op jit(solution)/shard_map/reshape | solution.py:199
  35.3 2.6 %collective-permute-start.3 = (f32[2,2048]{1,0:T(2,128)S(1)}, f32[2,2048]{1,0:T(2,128)S(1)}, u32[]{:S(2)}, u32[]{:S(2)}) collective-permute-start(f32[2,2048]{1,0:T(2,128)S(1)} %pad_maximum_fusion.7), channel_id=1, source_target_pairs={{0,8},{1,9},{2,10},{3,11},{4,12},{5,13},{6,14},{7,15},{8,0},{9,1},... | collective-permute-start | bytes 49160 | tf_op jit(solution)/shard_map/ppermute | solution.py:156
  38.0 1.4 %copy.59 = f32[2048,1]{1,0:T(8,128)} copy(f32[2048,1]{0,1:T(1,128)S(1)} %bitcast_maximum_fusion) | data formatting | bytes 16384 | tf_op jit(solution)/shard_map/max | solution.py:164
  39.3 1.4 %copy.70 = f32[2048,1]{1,0:T(8,128)} copy(f32[2048,1]{0,1:T(1,128)S(1)} %get-tuple-element.29) | data formatting | bytes 16384 | tf_op jit(solution)/shard_map/squeeze | solution.py:163
  40.7 1.4 %copy.68 = f32[2048,1]{1,0:T(8,128)} copy(f32[2048,1]{0,1:T(1,128)S(1)} %get-tuple-element.26) | data formatting | bytes 16384 | tf_op jit(solution)/shard_map/squeeze | solution.py:163
  42.0 1.3 %copy.73 = f32[2048,1]{1,0:T(8,128)} copy(f32[2048,1]{0,1:T(1,128)S(1)} %get-tuple-element.35) | data formatting | bytes 16384 | tf_op jit(solution)/shard_map/squeeze | solution.py:163
  43.4 1.4 %copy.60 = f32[2048,1]{1,0:T(8,128)} copy(f32[2048,1]{0,1:T(1,128)S(1)} %get-tuple-element.32) | data formatting | bytes 16384 | tf_op jit(solution)/shard_map/squeeze | solution.py:163
  44.7 1.4 %copy.75 = f32[2048,1]{1,0:T(8,128)} copy(f32[2048,1]{0,1:T(1,128)S(1)} %get-tuple-element.41) | data formatting | bytes 16384 | tf_op jit(solution)/shard_map/squeeze | solution.py:163
  46.1 1.4 %copy.61 = f32[2048,1]{1,0:T(8,128)} copy(f32[2048,1]{0,1:T(1,128)S(1)} %get-tuple-element.38) | data formatting | bytes 16384 | tf_op jit(solution)/shard_map/squeeze | solution.py:163
  48.2 1.3 %copy.77 = f32[2048,1]{1,0:T(8,128)} copy(f32[2048,1]{0,1:T(1,128)S(1)} %get-tuple-element.46) | data formatting | bytes 16384 | tf_op jit(solution)/shard_map/squeeze | solution.py:163
  49.5 1.3 %copy.62 = f32[2048,1]{1,0:T(8,128)} copy(f32[2048,1]{0,1:T(1,128)S(1)} %get-tuple-element.44) | data formatting | bytes 16384 | tf_op jit(solution)/shard_map/squeeze | solution.py:163
  52.1 5.4 %subtract_convert_fusion = (bf16[2048,1]{1,0:T(8,128)(2,1)S(1)}, bf16[2048,1]{1,0:T(8,128)(2,1)S(1)}) fusion(f32[2048,1]{1,0:T(8,128)} %copy.77, f32[2048,1]{1,0:T(8,128)} %copy.62, f32[2048,1]{1,0:T(8,128)} %copy.75, f32[2048,1]{1,0:T(8,128)} %copy.61, f32[2048,1]{1,0:T(8,128)} %copy.73, f32[2048,1]{1,0:T(8,128)} %copy.60, f32[2048,1]{1,0:T(8,128)} %copy.59, ...), kind=kLoop, calls=%fused_computation.4 | loop fusion | flops 61440 | bytes 106496 | tf_op jit(solution)/shard_map/convert_element_type | solution.py:209
  57.5 1.4 %maximum_maximum_fusion.qa_ref = bf16[2048,256]{1,0:T(8,128)(2,1)} fusion(bf16[2048,1]{1,0:T(8,128)(2,1)S(1)} %get-tuple-element.17, bf16[2048,1]{1,0:T(8,128)(2,1)S(1)} %get-tuple-element.18, bf16[2048,128]{1,0:T(8,128)(2,1)S(1)} %multiply_convert_fusion, bf16[256]{0:T(256)(128)(2,1)S(1)} %pad.11.clone), kind=kLoop, calls=%fused_computation | loop fusion | flops 4194304 | bytes 1581568 | tf_op jit(solution)/shard_map/concatenate | solution.py:210
  58.8 8.5 %shard_map.77 = (f32[2048,128]{1,0:T(8,128)}, f32[2048,128]{1,0:T(8,128)}, f32[8,128]{1,0:T(8,128)}) custom-call(bf16[2048,2048]{1,0:T(8,128)(2,1)} %get-tuple-element.10.e_ref, f32[1,2048]{1,0:T(1,128)} %get-tuple-element.45.sc_ref, bf16[2048,256]{1,0:T(8,128)(2,1)} %maximum_maximum_fusion.qa_ref, f32[128,2048]{1,0:T(8,128)} %get-tuple-element.13.ut_ref, ...), custom_call_target="tpu_custom_call" | custom-call | tf_op jit(solution)/shard_map/pallas_call | solution.py:120
  69.4 1.9 %collective-permute-done.4 = f32[1032,128]{1,0:T(8,128)S(1)} collective-permute-done((f32[1032,128]{1,0:T(8,128)S(1)}, f32[1032,128]{1,0:T(8,128)S(1)}, u32[]{:S(2)}, u32[]{:S(2)}) %collective-permute-start.4) | collective-permute-done | bytes 528416 | tf_op jit(solution)/shard_map/ppermute | solution.py:156
  71.5 1.6 %collective-permute-start.5 = (f32[520,128]{1,0:T(8,128)S(1)}, f32[520,128]{1,0:T(8,128)S(1)}, u32[]{:S(2)}, u32[]{:S(2)}) collective-permute-start(f32[520,128]{1,0:T(8,128)S(1)} %pad_maximum_fusion.1), channel_id=1, source_target_pairs={{0,2},{1,3},{2,0},{3,1},{4,6},{5,7},{6,4},{7,5},{8,10},{9,11},{10,... | collective-permute-start | bytes 798728 | tf_op jit(solution)/shard_map/ppermute | solution.py:156
  73.1 6.9 %collective-permute-done.5 = f32[520,128]{1,0:T(8,128)S(1)} collective-permute-done((f32[520,128]{1,0:T(8,128)S(1)}, f32[520,128]{1,0:T(8,128)S(1)}, u32[]{:S(2)}, u32[]{:S(2)}) %collective-permute-start.5) | collective-permute-done | bytes 266272 | tf_op jit(solution)/shard_map/ppermute | solution.py:156
  80.6 4.5 %collective-permute-done.6 = f32[264,128]{1,0:T(8,128)S(1)} collective-permute-done((f32[264,128]{1,0:T(8,128)S(1)}, f32[264,128]{1,0:T(8,128)S(1)}, u32[]{:S(2)}, u32[]{:S(2)}) %collective-permute-start.6) | collective-permute-done | bytes 135200 | tf_op jit(solution)/shard_map/ppermute | solution.py:156
  86.7 4.5 %collective-permute-done.7 = f32[136,128]{1,0:T(8,128)S(1)} collective-permute-done((f32[136,128]{1,0:T(8,128)S(1)}, f32[136,128]{1,0:T(8,128)S(1)}, u32[]{:S(2)}, u32[]{:S(2)}) %collective-permute-start.7) | collective-permute-done | bytes 69664 | tf_op jit(solution)/shard_map/ppermute | solution.py:156
  (70 shorter events, 14.5 us)
Async XLA Ops:
  0.6 2.4 %copy-start.9 = (f32[128]{0:T(128)S(1)}, f32[128]{0:T(128)}, u32[]{:S(2)}) copy-start(f32[128]{0:T(128)} %param.8) | copy-start | bytes 1540
  0.6 2.9 %copy-start.8 = (s32[2048]{0:T(1024)S(1)}, s32[2048]{0:T(1024)}, u32[]{:S(2)}) copy-start(s32[2048]{0:T(1024)} %param.7) | copy-start | bytes 24580
  0.7 31.0 %copy-start.6 = (f32[2048]{0:T(1024)S(1)}, f32[2048]{0:T(1024)}, u32[]{:S(2)}) copy-start(f32[2048]{0:T(1024)} %param.9) | copy-start | bytes 24580
  21.8 16.1 %copy-start.4 = (f32[1,2048]{1,0:T(1,128)S(1)}, f32[1,2048]{1,0:T(1,128)}, u32[]{:S(2)}) copy-start(f32[1,2048]{1,0:T(1,128)} %get-tuple-element.11) | copy-start | bytes 24580
  22.6 1.4 %collective-permute-start = (f32[2,2048]{1,0:T(2,128)S(1)}, f32[2,2048]{1,0:T(2,128)S(1)}, u32[]{:S(2)}, u32[]{:S(2)}) collective-permute-start(f32[2,2048]{1,0:T(2,128)S(1)} %pad_maximum_fusion.4), channel_id=1, source_target_pairs={{0,1},{1,0},{2,3},{3,2},{4,5},{5,4},{6,7},{7,6},{8,9},{9,8},{10,11... | collective-permute-start | bytes 49160 | tf_op jit(solution)/shard_map/ppermute | solution.py:156
  24.8 4.6 %collective-permute-start.1 = (f32[2,2048]{1,0:T(2,128)S(1)}, f32[2,2048]{1,0:T(2,128)S(1)}, u32[]{:S(2)}, u32[]{:S(2)}) collective-permute-start(f32[2,2048]{1,0:T(2,128)S(1)} %pad_maximum_fusion.5), channel_id=1, source_target_pairs={{0,2},{1,3},{2,0},{3,1},{4,6},{5,7},{6,4},{7,5},{8,10},{9,11},{10,... | collective-permute-start | bytes 49160 | tf_op jit(solution)/shard_map/ppermute | solution.py:156
  29.5 5.7 %collective-permute-start.2 = (f32[2,2048]{1,0:T(2,128)S(1)}, f32[2,2048]{1,0:T(2,128)S(1)}, u32[]{:S(2)}, u32[]{:S(2)}) collective-permute-start(f32[2,2048]{1,0:T(2,128)S(1)} %pad_maximum_fusion.6), channel_id=1, source_target_pairs={{0,4},{1,5},{2,6},{3,7},{4,0},{5,1},{6,2},{7,3},{8,12},{9,13},{10,... | collective-permute-start | bytes 49160 | tf_op jit(solution)/shard_map/ppermute | solution.py:156
  35.3 12.2 %collective-permute-start.3 = (f32[2,2048]{1,0:T(2,128)S(1)}, f32[2,2048]{1,0:T(2,128)S(1)}, u32[]{:S(2)}, u32[]{:S(2)}) collective-permute-start(f32[2,2048]{1,0:T(2,128)S(1)} %pad_maximum_fusion.7), channel_id=1, source_target_pairs={{0,8},{1,9},{2,10},{3,11},{4,12},{5,13},{6,14},{7,15},{8,0},{9,1},... | collective-permute-start | bytes 49160 | tf_op jit(solution)/shard_map/ppermute | solution.py:156
  44.7 6.1 %copy-start.5 = (f32[1,2048]{1,0:T(1,128)S(1)}, f32[1,2048]{1,0:T(1,128)}, u32[]{:S(2)}) copy-start(f32[1,2048]{1,0:T(1,128)} %get-tuple-element.12) | copy-start | bytes 24580
  44.7 6.2 %copy-start = (f32[2,2,2,2,128,128]{5,4,0,1,2,3:T(8,128)S(1)}, f32[2,2,2,2,128,128]{5,4,0,1,2,3:T(8,128)}, u32[]{:S(2)}) copy-start(f32[2,2,2,2,128,128]{5,4,0,1,2,3:T(8,128)} %copy.54) | copy-start | bytes 3145732
  50.9 1.2 %copy-start.2 = (f32[2048,1]{1,0:T(8,128)S(1)}, f32[2048,1]{1,0:T(8,128)}, u32[]{:S(2)}) copy-start(f32[2048,1]{1,0:T(8,128)} %copy.64) | copy-start | bytes 24580
  67.3 4.0 %copy-start.3 = (f32[2048,128]{1,0:T(8,128)S(1)}, f32[2048,128]{1,0:T(8,128)}, u32[]{:S(2)}) copy-start(f32[2048,128]{1,0:T(8,128)} %get-tuple-element.14) | copy-start | bytes 3145732
  68.5 3.0 %copy-start.7 = (f32[8,128]{1,0:T(8,128)S(1)}, f32[8,128]{1,0:T(8,128)}, u32[]{:S(2)}) copy-start(f32[8,128]{1,0:T(8,128)} %get-tuple-element.15) | copy-start | bytes 12292
  69.3 2.0 %collective-permute-start.4 = (f32[1032,128]{1,0:T(8,128)S(1)}, f32[1032,128]{1,0:T(8,128)S(1)}, u32[]{:S(2)}, u32[]{:S(2)}) collective-permute-start(f32[1032,128]{1,0:T(8,128)S(1)} %pad_maximum_fusion), channel_id=1, source_target_pairs={{0,1},{1,0},{2,3},{3,2},{4,5},{5,4},{6,7},{7,6},{8,9},{9,8},{10,11... | collective-permute-start | bytes 1585160 | tf_op jit(solution)/shard_map/ppermute | solution.py:156
  71.4 14.3 %copy-start.1 = (f32[2048,128]{1,0:T(8,128)S(1)}, f32[2048,128]{1,0:T(8,128)}, u32[]{:S(2)}) copy-start(f32[2048,128]{1,0:T(8,128)} %param.5) | copy-start | bytes 3145732
  71.5 8.5 %collective-permute-start.5 = (f32[520,128]{1,0:T(8,128)S(1)}, f32[520,128]{1,0:T(8,128)S(1)}, u32[]{:S(2)}, u32[]{:S(2)}) collective-permute-start(f32[520,128]{1,0:T(8,128)S(1)} %pad_maximum_fusion.1), channel_id=1, source_target_pairs={{0,2},{1,3},{2,0},{3,1},{4,6},{5,7},{6,4},{7,5},{8,10},{9,11},{10,... | collective-permute-start | bytes 798728 | tf_op jit(solution)/shard_map/ppermute | solution.py:156
  80.1 5.1 %collective-permute-start.6 = (f32[264,128]{1,0:T(8,128)S(1)}, f32[264,128]{1,0:T(8,128)S(1)}, u32[]{:S(2)}, u32[]{:S(2)}) collective-permute-start(f32[264,128]{1,0:T(8,128)S(1)} %pad_maximum_fusion.2), channel_id=1, source_target_pairs={{0,4},{1,5},{2,6},{3,7},{4,0},{5,1},{6,2},{7,3},{8,12},{9,13},{10,... | collective-permute-start | bytes 405512 | tf_op jit(solution)/shard_map/ppermute | solution.py:156
  85.3 5.9 %collective-permute-start.7 = (f32[136,128]{1,0:T(8,128)S(1)}, f32[136,128]{1,0:T(8,128)S(1)}, u32[]{:S(2)}, u32[]{:S(2)}) collective-permute-start(f32[136,128]{1,0:T(8,128)S(1)} %pad_maximum_fusion.3), channel_id=1, source_target_pairs={{0,8},{1,9},{2,10},{3,11},{4,12},{5,13},{6,14},{7,15},{8,0},{9,1},... | collective-permute-start | bytes 208904 | tf_op jit(solution)/shard_map/ppermute | solution.py:156

commit v11 on v8

--- a/solution.py
+++ b/solution.py
@@ -51,23 +51,29 @@
     ut_ref[...] = jnp.dot(rlt_sc[...], expd_low, preferred_element_type=jnp.float32)
 
 
-def backward_kernel(e_ref, sc_ref, qa_ref, ut_ref, q_ref, r_ref, inv_ref, rg_ref, pull_ref, terms_ref, acc_sc, qt_sc):
-    step = pl.program_id(0)
+def backward_kernel(e_ref, sc_ref, qa_ref, ut_ref, q_ref, r_ref, inv_ref, rg_ref, pull_ref, terms_ref, acc_sc, qt_sc,
+                    pull_sc):
+    step, part = pl.program_id(0), pl.program_id(1)
     n_feat = q_ref.shape[1]
-
-    @pl.when(step == 0)
+    sub = pull_ref.shape[0]
+
+    @pl.when((step == 0) & (part == 0))
     def _():
         acc_sc[...] = jnp.zeros_like(acc_sc)
         qt_sc[...] = jnp.zeros_like(qt_sc)
 
-    scale = sc_ref[...]
-    weight = (e_ref[...].astype(jnp.float32) * scale).astype(jnp.bfloat16)
-    acc_sc[...] += jnp.dot(weight, qa_ref[...], preferred_element_type=jnp.float32)
-    pulled = (ut_ref[...] * scale).T
-    pull_ref[...] = pulled
-    qt_sc[...] += jnp.sum(q_ref[...] * pulled, axis=0, keepdims=True)
-
-    @pl.when(step == pl.num_programs(0) - 1)
+    @pl.when(part == 0)
+    def _():
+        scale = sc_ref[...]
+        weight = (e_ref[...].astype(jnp.float32) * scale).astype(jnp.bfloat16)
+        acc_sc[...] += jnp.dot(weight, qa_ref[...], preferred_element_type=jnp.float32)
+        pulled = (ut_ref[...] * scale).T
+        pull_sc[...] = pulled
+        qt_sc[...] += jnp.sum(q_ref[...] * pulled, axis=0, keepdims=True)
+
+    pull_ref[...] = pull_sc[pl.ds(pl.multiple_of(part * sub, sub), sub), :]
+
+    @pl.when((step == pl.num_programs(0) - 1) & (part == pl.num_programs(1) - 1))
     def _():
         acc = acc_sc[...]
         refs = r_ref[...]
@@ -111,27 +117,37 @@
     )(queries, inv, local_ids, references)
 
 
-def local_backward(expd_low, scale, query_aug, unscaled_t, queries, references, inv):
+def bit_reversed_index(p, n_bits):
+    out = 0
+    for b in range(n_bits):
+        out = out + (p // (2 ** b)) % 2 * (2 ** (n_bits - 1 - b))
+    return out
+
+
+def local_backward(expd_low, scale, query_aug, unscaled_t, queries, references, inv, n_dev):
     n_ref, n_query = expd_low.shape
     n_feat = queries.shape[1]
     width = query_aug.shape[1]
     tile = min(TILE, n_query)
-    whole = lambda i: (0, 0)
+    sub = n_query // n_dev
+    per = tile // sub
+    n_bits = n_dev.bit_length() - 1
+    whole = lambda i, j: (0, 0)
     return pl.pallas_call(
         backward_kernel,
-        grid=(n_query // tile,),
+        grid=(n_query // tile, per),
         in_specs=[
-            pl.BlockSpec((n_ref, tile), lambda i: (0, i)),
-            pl.BlockSpec((1, tile), lambda i: (0, i)),
-            pl.BlockSpec((tile, width), lambda i: (i, 0)),
-            pl.BlockSpec((n_feat, tile), lambda i: (0, i)),
-            pl.BlockSpec((tile, n_feat), lambda i: (i, 0)),
+            pl.BlockSpec((n_ref, tile), lambda i, j: (0, i)),
+            pl.BlockSpec((1, tile), lambda i, j: (0, i)),
+            pl.BlockSpec((tile, width), lambda i, j: (i, 0)),
+            pl.BlockSpec((n_feat, tile), lambda i, j: (0, i)),
+            pl.BlockSpec((tile, n_feat), lambda i, j: (i, 0)),
             pl.BlockSpec((n_ref, n_feat), whole),
             pl.BlockSpec((1, n_feat), whole),
         ],
         out_specs=[
             pl.BlockSpec((n_ref, n_feat), whole),
-            pl.BlockSpec((tile, n_feat), lambda i: (i, 0)),
+            pl.BlockSpec((sub, n_feat), lambda i, j: (bit_reversed_index(i * per + j, n_bits), 0)),
             pl.BlockSpec((8, n_feat), whole),
         ],
         out_shape=[
@@ -142,8 +158,9 @@
         scratch_shapes=[
             pltpu.VMEM((n_ref, width), jnp.float32),
             pltpu.VMEM((1, n_feat), jnp.float32),
-        ],
-        compiler_params=pltpu.CompilerParams(dimension_semantics=("arbitrary",)),
+            pltpu.VMEM((tile, n_feat), jnp.float32),
+        ],
+        compiler_params=pltpu.CompilerParams(dimension_semantics=("arbitrary", "arbitrary")),
     )(expd_low, scale, query_aug, unscaled_t, queries, references, inv)
 
 
@@ -192,10 +209,6 @@
     n_ref = references.shape[0]
     n_dev = lax.axis_size("ref")
     own_rows = n_query // n_dev
-    order = bit_reversed(n_dev)
-    reorder = lambda x: x.reshape((n_dev, own_rows) + x.shape[1:])[order].reshape(x.shape)
-    all_queries, all_cotangent = queries, cotangent
-    queries, query_ids, cotangent = reorder(queries), reorder(query_ids), reorder(cotangent)
     inv = 1.0 / (spread * spread)
     ref_start = lax.axis_index("ref") * n_ref
     local_ids = (query_ids - ref_start)[None, :]
@@ -207,12 +220,12 @@
         [query_low, jnp.ones((n_query, 1), jnp.bfloat16), jnp.zeros((n_query, n_feat - 1), jnp.bfloat16)], axis=1
     )
     reference_grad, pulled, local_terms = local_backward(
-        expd_low, scale[None, :], query_aug, unscaled_t, queries, references, inv[None, :]
+        expd_low, scale[None, :], query_aug, unscaled_t, queries, references, inv[None, :], n_dev
     )
     own_pulled, summed_terms = halving_scatter(pulled, local_terms, n_dev)
     own_start = lax.axis_index("ref") * own_rows
-    own_queries = lax.dynamic_slice_in_dim(all_queries, own_start, own_rows, 0)
-    own_cot = lax.dynamic_slice_in_dim(all_cotangent, own_start, own_rows, 0)
+    own_queries = lax.dynamic_slice_in_dim(queries, own_start, own_rows, 0)
+    own_cot = lax.dynamic_slice_in_dim(cotangent, own_start, own_rows, 0)
     query_grad = (own_pulled - own_queries * own_cot[:, None]) * inv
     self_terms = jnp.sum(queries * queries * cotangent[:, None], axis=0)
     summed = (summed_terms[0] - self_terms) * inv + summed_terms[1]

time: 76 us -> 80.1 us (1.054)
  Pallas kernels: 25.8 us -> 32.7 us
  local copies, waits for them, and re-layouts: 5.51 us -> 1.49 us
  waiting for transfers between devices: 17.3 us -> 18.5 us
    pallas_call x1, Pallas kernels: 8.2 us -> 15 us  [local_backward(): pl.pallas_call(backward_kernel, grid=(n_query // tile, per), in_specs=[pl...]
    gather x3 -> x0, local copies, waits for them, and re-layouts: 4.02 us -> none  [on_device(): x.reshape((n_dev, own_rows) + x.shape[1:])[order].reshape(x.shape)]
    ppermute x8, waiting for transfers between devices: 17.3 us -> 18.5 us  [exchange(): return lax.ppermute(x, 'ref', [(i, i ^ step) for i in range(n_dev)])]
  transfers between devices with their start and end apart: 8 -> 8, of which waited for: 8 -> 8; matrix products, arithmetic and copies ran while one was open for 4% -> 2% of each run, Pallas kernels for 0% -> 0%
where the time goes in v11:
time: 80.1 us; the launch traced here: 79.6 us
  Pallas kernels  32.7 us (41%)
  waiting for transfers between devices  18.5 us (23%)
  starting transfers between devices  15.4 us (19%)
  other arithmetic  10.6 us (13%)
  local copies, waits for them, and re-layouts  1.49 us (2%)
  between operations  0.93 us (1%)
    ppermute x8, waiting for transfers between devices, exchange(): return lax.ppermute(x, 'ref', [(i, i ^ step) for i in range(n_dev)])  18.5 us
    pallas_call x1, Pallas kernels, local_forward(): pl.pallas_call(forward_kernel, grid=(n_query // tile,), in_specs=[pl.Bloc...  17.6 us
    ppermute x8, starting transfers between devices, exchange(): return lax.ppermute(x, 'ref', [(i, i ^ step) for i in range(n_dev)])  15.4 us
    pallas_call x1, Pallas kernels, local_backward(): pl.pallas_call(backward_kernel, grid=(n_query // tile, per), in_specs=[pl...  15 us
  transfers between devices with their start and end apart: 8, of which 8 were waited for; matrix products, arithmetic and copies ran while one was open for 2% of the time, Pallas kernels for 0%

profile of v11, /device:TPU:0, one launch (start us, length us, event | category | flops | bytes accessed | tf_op | source)
XLA Modules:
  0.0 79.6 jit_solution(10295348803849229320)
XLA Ops:
  0.7 1.3 %fusion.20.inv_ref = f32[1,128]{1,0:T(1,128)} fusion(f32[128]{0:T(128)} %param.8), kind=kLoop, calls=%fused_computation.59 | loop fusion | flops 256 | bytes 1024 | tf_op jit(solution)/shard_map/broadcast_in_dim | solution.py:215
  1.9 1.3 %broadcast_subtract_fusion = s32[2048]{0:T(1024)} fusion(s32[2048]{0:T(1024)} %param.7, s32[]{:T(128)S(6)} %mul.109), kind=kLoop, calls=%fused_computation.43 | loop fusion | flops 2048 | bytes 16388 | tf_op jit(solution)/shard_map/sub | solution.py:214
  3.2 17.6 %shard_map.76 = (bf16[2048,2048]{1,0:T(8,128)(2,1)}, f32[128,2048]{1,0:T(8,128)}, f32[1,2048]{1,0:T(1,128)}, f32[1,2048]{1,0:T(1,128)}) custom-call(f32[2048,128]{1,0:T(8,128)} %q_ref.3, f32[1,128]{1,0:T(1,128)} %fusion.20.inv_ref, s32[1,2048]{1,0:T(1,128)} %bitcast.64, f32[2048,128]{1,0:T(8,128)} %r_ref.3), custom_call_target="tpu_custom_call" | custom-call | tf_op jit(solution)/shard_map/pallas_call | solution.py:90
  20.9 0.8 pad_maximum_fusion.4
  22.2 0.8 %collective-permute-done = f32[2,2048]{1,0:T(2,128)S(1)} collective-permute-done((f32[2,2048]{1,0:T(2,128)S(1)}, f32[2,2048]{1,0:T(2,128)S(1)}, u32[]{:S(2)}, u32[]{:S(2)}) %collective-permute-start) | collective-permute-done | bytes 16416 | tf_op jit(solution)/shard_map/ppermute | solution.py:173
  23.8 2.9 %collective-permute-start.1 = (f32[2,2048]{1,0:T(2,128)S(1)}, f32[2,2048]{1,0:T(2,128)S(1)}, u32[]{:S(2)}, u32[]{:S(2)}) collective-permute-start(f32[2,2048]{1,0:T(2,128)S(1)} %pad_maximum_fusion.5), channel_id=1, source_target_pairs={{0,2},{1,3},{2,0},{3,1},{4,6},{5,7},{6,4},{7,5},{8,10},{9,11},{10,... | collective-permute-start | bytes 49160 | tf_op jit(solution)/shard_map/ppermute | solution.py:173
  26.7 1.7 %collective-permute-done.1 = f32[2,2048]{1,0:T(2,128)S(1)} collective-permute-done((f32[2,2048]{1,0:T(2,128)S(1)}, f32[2,2048]{1,0:T(2,128)S(1)}, u32[]{:S(2)}, u32[]{:S(2)}) %collective-permute-start.1) | collective-permute-done | bytes 16416 | tf_op jit(solution)/shard_map/ppermute | solution.py:173
  28.5 2.1 %collective-permute-start.2 = (f32[2,2048]{1,0:T(2,128)S(1)}, f32[2,2048]{1,0:T(2,128)S(1)}, u32[]{:S(2)}, u32[]{:S(2)}) collective-permute-start(f32[2,2048]{1,0:T(2,128)S(1)} %pad_maximum_fusion.6), channel_id=1, source_target_pairs={{0,4},{1,5},{2,6},{3,7},{4,0},{5,1},{6,2},{7,3},{8,12},{9,13},{10,... | collective-permute-start | bytes 49160 | tf_op jit(solution)/shard_map/ppermute | solution.py:173
  31.1 1.3 %collective-permute-done.2 = f32[2,2048]{1,0:T(2,128)S(1)} collective-permute-done((f32[2,2048]{1,0:T(2,128)S(1)}, f32[2,2048]{1,0:T(2,128)S(1)}, u32[]{:S(2)}, u32[]{:S(2)}) %collective-permute-start.2) | collective-permute-done | bytes 16416 | tf_op jit(solution)/shard_map/ppermute | solution.py:173
  32.5 3.1 %collective-permute-start.3 = (f32[2,2048]{1,0:T(2,128)S(1)}, f32[2,2048]{1,0:T(2,128)S(1)}, u32[]{:S(2)}, u32[]{:S(2)}) collective-permute-start(f32[2,2048]{1,0:T(2,128)S(1)} %pad_maximum_fusion.7), channel_id=1, source_target_pairs={{0,8},{1,9},{2,10},{3,11},{4,12},{5,13},{6,14},{7,15},{8,0},{9,1},... | collective-permute-start | bytes 49160 | tf_op jit(solution)/shard_map/ppermute | solution.py:173
  35.5 1.1 %maximum_maximum_fusion.qa_ref = bf16[2048,256]{1,0:T(8,128)(2,1)} fusion(bf16[2048,128]{1,0:T(8,128)(2,1)S(1)} %get-tuple-element.22, bf16[256]{0:T(256)(128)(2,1)S(1)} %pad.10.clone, bf16[256]{0:T(256)(128)(2,1)S(1)} %pad.9.clone), kind=kLoop, calls=%fused_computation | loop fusion | flops 3145728 | bytes 1573888 | tf_op jit(solution)/shard_map/concatenate | solution.py:219
  37.3 1.2 %fusion.19 = (f32[]{:T(128)}, f32[2048]{0:T(1024)}) fusion(f32[2048]{0:T(1024)S(1)} %copy-done.4, f32[2048]{0:T(1024)S(1)} %bitcast.66, f32[2048]{0:T(1024)S(1)} %bitcast.65, f32[2048]{0:T(1024)S(1)} %bitcast.72, f32[2048]{0:T(1024)S(1)} %bitcast.71, f32[2048]{0:T(1024)S(1)} %bitcast.70, f32[2048]{0:T(1024)S(1)} %bitcast.69, f32[2048]{0:T(1024)S(1)} %bitcast.67, ...), kind=kLoop, calls=%fused_computation.58 | loop fusion | flops 57343 | bytes 98308 | tf_op jit(solution)/shard_map/reduce_sum | solution.py:232
  38.5 15.0 %shard_map.77 = (f32[2048,128]{1,0:T(8,128)}, f32[2048,128]{1,0:T(8,128)}, f32[8,128]{1,0:T(8,128)}) custom-call(bf16[2048,2048]{1,0:T(8,128)(2,1)} %get-tuple-element.10.e_ref, f32[1,2048]{1,0:T(1,128)} %bitcast.73, bf16[2048,256]{1,0:T(8,128)(2,1)} %maximum_maximum_fusion.qa_ref, f32[128,2048]{1,0:T(8,128)} %get-tuple-element.13.ut_ref, ...), custom_call_target="tpu_custom_call" | custom-call | tf_op jit(solution)/shard_map/pallas_call | solution.py:136
  53.6 1.2 %constant_dynamic-slice_fusion.2 = f32[8,128,128]{2,1,0:T(8,128)S(1)} fusion(f32[16,128,128]{2,1,0:T(8,128)} %bitcast.57, s32[]{:T(128)S(6)} %select_n.60), kind=kLoop, calls=%fused_computation.46 | loop fusion | bytes 1048580 | tf_op jit(solution)/shard_map/dynamic_slice | solution.py:197
  54.8 0.8 pad_maximum_fusion
  55.7 1.9 %collective-permute-done.4 = f32[1032,128]{1,0:T(8,128)S(1)} collective-permute-done((f32[1032,128]{1,0:T(8,128)S(1)}, f32[1032,128]{1,0:T(8,128)S(1)}, u32[]{:S(2)}, u32[]{:S(2)}) %collective-permute-start.4) | collective-permute-done | bytes 528416 | tf_op jit(solution)/shard_map/ppermute | solution.py:173
  57.8 1.9 %collective-permute-start.5 = (f32[520,128]{1,0:T(8,128)S(1)}, f32[520,128]{1,0:T(8,128)S(1)}, u32[]{:S(2)}, u32[]{:S(2)}) collective-permute-start(f32[520,128]{1,0:T(8,128)S(1)} %pad_maximum_fusion.1), channel_id=1, source_target_pairs={{0,2},{1,3},{2,0},{3,1},{4,6},{5,7},{6,4},{7,5},{8,10},{9,11},{10,... | collective-permute-start | bytes 798728 | tf_op jit(solution)/shard_map/ppermute | solution.py:173
  59.7 6.7 %collective-permute-done.5 = f32[520,128]{1,0:T(8,128)S(1)} collective-permute-done((f32[520,128]{1,0:T(8,128)S(1)}, f32[520,128]{1,0:T(8,128)S(1)}, u32[]{:S(2)}, u32[]{:S(2)}) %collective-permute-start.5) | collective-permute-done | bytes 266272 | tf_op jit(solution)/shard_map/ppermute | solution.py:173
  66.5 1.9 %collective-permute-start.6 = (f32[264,128]{1,0:T(8,128)S(1)}, f32[264,128]{1,0:T(8,128)S(1)}, u32[]{:S(2)}, u32[]{:S(2)}) collective-permute-start(f32[264,128]{1,0:T(8,128)S(1)} %pad_maximum_fusion.2), channel_id=1, source_target_pairs={{0,4},{1,5},{2,6},{3,7},{4,0},{5,1},{6,2},{7,3},{8,12},{9,13},{10,... | collective-permute-start | bytes 405512 | tf_op jit(solution)/shard_map/ppermute | solution.py:173
  68.4 3.2 %collective-permute-done.6 = f32[264,128]{1,0:T(8,128)S(1)} collective-permute-done((f32[264,128]{1,0:T(8,128)S(1)}, f32[264,128]{1,0:T(8,128)S(1)}, u32[]{:S(2)}, u32[]{:S(2)}) %collective-permute-start.6) | collective-permute-done | bytes 135200 | tf_op jit(solution)/shard_map/ppermute | solution.py:173
  71.7 2.9 %collective-permute-start.7 = (f32[136,128]{1,0:T(8,128)S(1)}, f32[136,128]{1,0:T(8,128)S(1)}, u32[]{:S(2)}, u32[]{:S(2)}) collective-permute-start(f32[136,128]{1,0:T(8,128)S(1)} %pad_maximum_fusion.3), channel_id=1, source_target_pairs={{0,8},{1,9},{2,10},{3,11},{4,12},{5,13},{6,14},{7,15},{8,0},{9,1},... | collective-permute-start | bytes 208904 | tf_op jit(solution)/shard_map/ppermute | solution.py:173
  74.6 2.3 %collective-permute-done.7 = f32[136,128]{1,0:T(8,128)S(1)} collective-permute-done((f32[136,128]{1,0:T(8,128)S(1)}, f32[136,128]{1,0:T(8,128)S(1)}, u32[]{:S(2)}, u32[]{:S(2)}) %collective-permute-start.7) | collective-permute-done | bytes 69664 | tf_op jit(solution)/shard_map/ppermute | solution.py:173
  76.9 1.1 %divide_subtract_fusion = f32[128]{0:T(128)} fusion(f32[128]{0:T(128)S(1)} %copy-done.6, f32[128]{0:T(128)S(1)} %get-tuple-element.21, f32[8,128]{1,0:T(8,128)S(1)} %slice_add_fusion, f32[]{:T(128)} %get-tuple-element.33), kind=kLoop, calls=%fused_computation.47 | loop fusion | flops 1152 | bytes 2564 | tf_op jit(solution)/shard_map/sub | solution.py:233
  78.0 1.6 %fusion.3 = f32[128,128]{1,0:T(8,128)} fusion(f32[136,128]{1,0:T(8,128)S(1)} %collective-permute-done.7, f32[2048,128]{1,0:T(8,128)} %q_ref.3, s32[]{:T(128)S(6)} %select_n.73, f32[2,128,128]{2,1,0:T(8,128)S(1)} %dynamic-slice_add_fusion.2, s32[]{:T(128)S(6)} %select_n.71, f32[128]{0:T(128)S(1)} %multiply_divide_fusion, f32[128]{0:T(128)S(1)} %dynamic_slice.39), kind=kLoop, calls=%fused_computation.13 | loop fusion | flops 65536 | bytes 263176 | tf_op jit(solution)/shard_map/mul | solution.py:229
  (46 shorter events, 3.0 us)
Async XLA Ops:
  0.6 30.0 %copy-start = (f32[2048,128]{1,0:T(8,128)S(1)}, f32[2048,128]{1,0:T(8,128)}, u32[]{:S(2)}) copy-start(f32[2048,128]{1,0:T(8,128)} %q_ref.3) | copy-start | bytes 3145732
  0.6 30.0 %copy-start.4 = (f32[2048]{0:T(1024)S(1)}, f32[2048]{0:T(1024)}, u32[]{:S(2)}) copy-start(f32[2048]{0:T(1024)} %param.9) | copy-start | bytes 24580
  20.8 16.4 %copy-start.2 = (f32[1,2048]{1,0:T(1,128)S(1)}, f32[1,2048]{1,0:T(1,128)}, u32[]{:S(2)}) copy-start(f32[1,2048]{1,0:T(1,128)} %get-tuple-element.11) | copy-start | bytes 24580
  20.8 16.4 %copy-start.3 = (f32[1,2048]{1,0:T(1,128)S(1)}, f32[1,2048]{1,0:T(1,128)}, u32[]{:S(2)}) copy-start(f32[1,2048]{1,0:T(1,128)} %get-tuple-element.12) | copy-start | bytes 24580
  21.6 1.4 %collective-permute-start = (f32[2,2048]{1,0:T(2,128)S(1)}, f32[2,2048]{1,0:T(2,128)S(1)}, u32[]{:S(2)}, u32[]{:S(2)}) collective-permute-start(f32[2,2048]{1,0:T(2,128)S(1)} %pad_maximum_fusion.4), channel_id=1, source_target_pairs={{0,1},{1,0},{2,3},{3,2},{4,5},{5,4},{6,7},{7,6},{8,9},{9,8},{10,11... | collective-permute-start | bytes 49160 | tf_op jit(solution)/shard_map/ppermute | solution.py:173
  23.8 4.6 %collective-permute-start.1 = (f32[2,2048]{1,0:T(2,128)S(1)}, f32[2,2048]{1,0:T(2,128)S(1)}, u32[]{:S(2)}, u32[]{:S(2)}) collective-permute-start(f32[2,2048]{1,0:T(2,128)S(1)} %pad_maximum_fusion.5), channel_id=1, source_target_pairs={{0,2},{1,3},{2,0},{3,1},{4,6},{5,7},{6,4},{7,5},{8,10},{9,11},{10,... | collective-permute-start | bytes 49160 | tf_op jit(solution)/shard_map/ppermute | solution.py:173
  28.5 3.9 %collective-permute-start.2 = (f32[2,2048]{1,0:T(2,128)S(1)}, f32[2,2048]{1,0:T(2,128)S(1)}, u32[]{:S(2)}, u32[]{:S(2)}) collective-permute-start(f32[2,2048]{1,0:T(2,128)S(1)} %pad_maximum_fusion.6), channel_id=1, source_target_pairs={{0,4},{1,5},{2,6},{3,7},{4,0},{5,1},{6,2},{7,3},{8,12},{9,13},{10,... | collective-permute-start | bytes 49160 | tf_op jit(solution)/shard_map/ppermute | solution.py:173
  32.5 4.8 %collective-permute-start.3 = (f32[2,2048]{1,0:T(2,128)S(1)}, f32[2,2048]{1,0:T(2,128)S(1)}, u32[]{:S(2)}, u32[]{:S(2)}) collective-permute-start(f32[2,2048]{1,0:T(2,128)S(1)} %pad_maximum_fusion.7), channel_id=1, source_target_pairs={{0,8},{1,9},{2,10},{3,11},{4,12},{5,13},{6,14},{7,15},{8,0},{9,1},... | collective-permute-start | bytes 49160 | tf_op jit(solution)/shard_map/ppermute | solution.py:173
  53.6 4.0 %copy-start.1 = (f32[2048,128]{1,0:T(8,128)S(1)}, f32[2048,128]{1,0:T(8,128)}, u32[]{:S(2)}) copy-start(f32[2048,128]{1,0:T(8,128)} %get-tuple-element.14) | copy-start | bytes 3145732
  54.8 2.9 %copy-start.5 = (f32[8,128]{1,0:T(8,128)S(1)}, f32[8,128]{1,0:T(8,128)}, u32[]{:S(2)}) copy-start(f32[8,128]{1,0:T(8,128)} %get-tuple-element.15) | copy-start | bytes 12292
  55.5 2.0 %collective-permute-start.4 = (f32[1032,128]{1,0:T(8,128)S(1)}, f32[1032,128]{1,0:T(8,128)S(1)}, u32[]{:S(2)}, u32[]{:S(2)}) collective-permute-start(f32[1032,128]{1,0:T(8,128)S(1)} %pad_maximum_fusion), channel_id=1, source_target_pairs={{0,1},{1,0},{2,3},{3,2},{4,5},{5,4},{6,7},{7,6},{8,9},{9,8},{10,11... | collective-permute-start | bytes 1585160 | tf_op jit(solution)/shard_map/ppermute | solution.py:173
  57.7 16.9 %copy-start.6 = (f32[128]{0:T(128)S(1)}, f32[128]{0:T(128)}, u32[]{:S(2)}) copy-start(f32[128]{0:T(128)} %param.8) | copy-start | bytes 1540
  57.8 8.6 %collective-permute-start.5 = (f32[520,128]{1,0:T(8,128)S(1)}, f32[520,128]{1,0:T(8,128)S(1)}, u32[]{:S(2)}, u32[]{:S(2)}) collective-permute-start(f32[520,128]{1,0:T(8,128)S(1)} %pad_maximum_fusion.1), channel_id=1, source_target_pairs={{0,2},{1,3},{2,0},{3,1},{4,6},{5,7},{6,4},{7,5},{8,10},{9,11},{10,... | collective-permute-start | bytes 798728 | tf_op jit(solution)/shard_map/ppermute | solution.py:173
  66.5 5.1 %collective-permute-start.6 = (f32[264,128]{1,0:T(8,128)S(1)}, f32[264,128]{1,0:T(8,128)S(1)}, u32[]{:S(2)}, u32[]{:S(2)}) collective-permute-start(f32[264,128]{1,0:T(8,128)S(1)} %pad_maximum_fusion.2), channel_id=1, source_target_pairs={{0,4},{1,5},{2,6},{3,7},{4,0},{5,1},{6,2},{7,3},{8,12},{9,13},{10,... | collective-permute-start | bytes 405512 | tf_op jit(solution)/shard_map/ppermute | solution.py:173
  71.7 5.3 %collective-permute-start.7 = (f32[136,128]{1,0:T(8,128)S(1)}, f32[136,128]{1,0:T(8,128)S(1)}, u32[]{:S(2)}, u32[]{:S(2)}) collective-permute-start(f32[136,128]{1,0:T(8,128)S(1)} %pad_maximum_fusion.3), channel_id=1, source_target_pairs={{0,8},{1,9},{2,10},{3,11},{4,12},{5,13},{6,14},{7,15},{8,0},{9,1},... | collective-permute-start | bytes 208904 | tf_op jit(solution)/shard_map/ppermute | solution.py:173

commit v12 on v8

--- a/solution.py
+++ b/solution.py
@@ -1,3 +1,5 @@
+import functools
+
 import numpy as np
 import jax
 import jax.numpy as jnp
@@ -51,9 +53,13 @@
     ut_ref[...] = jnp.dot(rlt_sc[...], expd_low, preferred_element_type=jnp.float32)
 
 
-def backward_kernel(e_ref, sc_ref, qa_ref, ut_ref, q_ref, r_ref, inv_ref, rg_ref, pull_ref, terms_ref, acc_sc, qt_sc):
+def backward_kernel(n_bits, e_ref, sc_ref, qa_ref, ut_ref, q_ref, r_ref, inv_ref, rg_ref, pull_hbm, terms_ref,
+                    acc_sc, qt_sc, pull_sc, sems):
     step = pl.program_id(0)
     n_feat = q_ref.shape[1]
+    tile = pull_sc.shape[0]
+    sub = pull_hbm.shape[0] // (2 ** n_bits)
+    per = tile // sub
 
     @pl.when(step == 0)
     def _():
@@ -61,11 +67,21 @@
         qt_sc[...] = jnp.zeros_like(qt_sc)
 
     scale = sc_ref[...]
+    pulled = (ut_ref[...] * scale).T
+    pull_sc[...] = pulled
+    copies = []
+    for j in range(per):
+        dst = bit_reversed_index(step * per + j, n_bits) * sub
+        copy = pltpu.make_async_copy(
+            pull_sc.at[pl.ds(j * sub, sub)], pull_hbm.at[pl.ds(pl.multiple_of(dst, sub), sub)], sems.at[j]
+        )
+        copy.start()
+        copies.append(copy)
     weight = (e_ref[...].astype(jnp.float32) * scale).astype(jnp.bfloat16)
     acc_sc[...] += jnp.dot(weight, qa_ref[...], preferred_element_type=jnp.float32)
-    pulled = (ut_ref[...] * scale).T
-    pull_ref[...] = pulled
     qt_sc[...] += jnp.sum(q_ref[...] * pulled, axis=0, keepdims=True)
+    for copy in copies:
+        copy.wait()
 
     @pl.when(step == pl.num_programs(0) - 1)
     def _():
@@ -111,14 +127,23 @@
     )(queries, inv, local_ids, references)
 
 
-def local_backward(expd_low, scale, query_aug, unscaled_t, queries, references, inv):
+def bit_reversed_index(p, n_bits):
+    out = 0
+    for b in range(n_bits):
+        out = out + (p // (2 ** b)) % 2 * (2 ** (n_bits - 1 - b))
+    return out
+
+
+def local_backward(expd_low, scale, query_aug, unscaled_t, queries, references, inv, n_dev):
     n_ref, n_query = expd_low.shape
     n_feat = queries.shape[1]
     width = query_aug.shape[1]
     tile = min(TILE, n_query)
+    sub = n_query // n_dev
+    n_bits = n_dev.bit_length() - 1
     whole = lambda i: (0, 0)
     return pl.pallas_call(
-        backward_kernel,
+        functools.partial(backward_kernel, n_bits),
         grid=(n_query // tile,),
         in_specs=[
             pl.BlockSpec((n_ref, tile), lambda i: (0, i)),
@@ -131,7 +156,7 @@
         ],
         out_specs=[
             pl.BlockSpec((n_ref, n_feat), whole),
-            pl.BlockSpec((tile, n_feat), lambda i: (i, 0)),
+            pl.BlockSpec(memory_space=pl.ANY),
             pl.BlockSpec((8, n_feat), whole),
         ],
         out_shape=[
@@ -142,6 +167,8 @@
         scratch_shapes=[
             pltpu.VMEM((n_ref, width), jnp.float32),
             pltpu.VMEM((1, n_feat), jnp.float32),
+            pltpu.VMEM((tile, n_feat), jnp.float32),
+            pltpu.SemaphoreType.DMA((tile // sub,)),
         ],
         compiler_params=pltpu.CompilerParams(dimension_semantics=("arbitrary",)),
     )(expd_low, scale, query_aug, unscaled_t, queries, references, inv)
@@ -192,10 +219,6 @@
     n_ref = references.shape[0]
     n_dev = lax.axis_size("ref")
     own_rows = n_query // n_dev
-    order = bit_reversed(n_dev)
-    reorder = lambda x: x.reshape((n_dev, own_rows) + x.shape[1:])[order].reshape(x.shape)
-    all_queries, all_cotangent = queries, cotangent
-    queries, query_ids, cotangent = reorder(queries), reorder(query_ids), reorder(cotangent)
     inv = 1.0 / (spread * spread)
     ref_start = lax.axis_index("ref") * n_ref
     local_ids = (query_ids - ref_start)[None, :]
@@ -207,12 +230,12 @@
         [query_low, jnp.ones((n_query, 1), jnp.bfloat16), jnp.zeros((n_query, n_feat - 1), jnp.bfloat16)], axis=1
     )
     reference_grad, pulled, local_terms = local_backward(
-        expd_low, scale[None, :], query_aug, unscaled_t, queries, references, inv[None, :]
+        expd_low, scale[None, :], query_aug, unscaled_t, queries, references, inv[None, :], n_dev
     )
     own_pulled, summed_terms = halving_scatter(pulled, local_terms, n_dev)
     own_start = lax.axis_index("ref") * own_rows
-    own_queries = lax.dynamic_slice_in_dim(all_queries, own_start, own_rows, 0)
-    own_cot = lax.dynamic_slice_in_dim(all_cotangent, own_start, own_rows, 0)
+    own_queries = lax.dynamic_slice_in_dim(queries, own_start, own_rows, 0)
+    own_cot = lax.dynamic_slice_in_dim(cotangent, own_start, own_rows, 0)
     query_grad = (own_pulled - own_queries * own_cot[:, None]) * inv
     self_terms = jnp.sum(queries * queries * cotangent[:, None], axis=0)
     summed = (summed_terms[0] - self_terms) * inv + summed_terms[1]

time: 76 us -> 74.8 us (0.984)
  local copies, waits for them, and re-layouts: 5.51 us -> 1.49 us
  Pallas kernels: 25.8 us -> 27.4 us
  waiting for transfers between devices: 17.3 us -> 18.5 us
    gather x3 -> x0, local copies, waits for them, and re-layouts: 4.02 us -> none  [on_device(): x.reshape((n_dev, own_rows) + x.shape[1:])[order].reshape(x.shape)]
    pallas_call x1, Pallas kernels: 8.2 us -> 9.79 us  [local_backward(): pl.pallas_call(functools.partial(backward_kernel, n_bits), grid=(n_query...]
    ppermute x8, waiting for transfers between devices: 17.3 us -> 18.5 us  [exchange(): return lax.ppermute(x, 'ref', [(i, i ^ step) for i in range(n_dev)])]
  transfers between devices with their start and end apart: 8 -> 8, of which waited for: 8 -> 8; matrix products, arithmetic and copies ran while one was open for 4% -> 2% of each run, Pallas kernels for 0% -> 0%
where the time goes in v12:
time: 74.8 us; the launch traced here: 74.3 us
  Pallas kernels  27.4 us (37%)
  waiting for transfers between devices  18.5 us (25%)
  starting transfers between devices  15.4 us (21%)
  other arithmetic  10.6 us (14%)
  local copies, waits for them, and re-layouts  1.49 us (2%)
  between operations  0.94 us (1%)
    ppermute x8, waiting for transfers between devices, exchange(): return lax.ppermute(x, 'ref', [(i, i ^ step) for i in range(n_dev)])  18.5 us
    pallas_call x1, Pallas kernels, local_forward(): pl.pallas_call(forward_kernel, grid=(n_query // tile,), in_specs=[pl.Bloc...  17.6 us
    ppermute x8, starting transfers between devices, exchange(): return lax.ppermute(x, 'ref', [(i, i ^ step) for i in range(n_dev)])  15.4 us
    pallas_call x1, Pallas kernels, local_backward(): pl.pallas_call(functools.partial(backward_kernel, n_bits), grid=(n_query...  9.79 us
    mul x1, other arithmetic, on_device(): query_grad = (own_pulled - own_queries * own_cot[:, None]) * inv  1.56 us
  transfers between devices with their start and end apart: 8, of which 8 were waited for; matrix products, arithmetic and copies ran while one was open for 2% of the time, Pallas kernels for 0%

profile of v12, /device:TPU:0, one launch (start us, length us, event | category | flops | bytes accessed | tf_op | source)
XLA Modules:
  0.0 74.3 jit_solution(2824131733458321583)
XLA Ops:
  0.7 1.3 %fusion.20.inv_ref = f32[1,128]{1,0:T(1,128)} fusion(f32[128]{0:T(128)} %param.8), kind=kLoop, calls=%fused_computation.59 | loop fusion | flops 256 | bytes 1024 | tf_op jit(solution)/shard_map/broadcast_in_dim | solution.py:225
  1.9 1.3 %broadcast_subtract_fusion = s32[2048]{0:T(1024)} fusion(s32[2048]{0:T(1024)} %param.7, s32[]{:T(128)S(6)} %mul.109), kind=kLoop, calls=%fused_computation.43 | loop fusion | flops 2048 | bytes 16388 | tf_op jit(solution)/shard_map/sub | solution.py:224
  3.2 17.6 %shard_map.76 = (bf16[2048,2048]{1,0:T(8,128)(2,1)}, f32[128,2048]{1,0:T(8,128)}, f32[1,2048]{1,0:T(1,128)}, f32[1,2048]{1,0:T(1,128)}) custom-call(f32[2048,128]{1,0:T(8,128)} %q_ref.3, f32[1,128]{1,0:T(1,128)} %fusion.20.inv_ref, s32[1,2048]{1,0:T(1,128)} %bitcast.64, f32[2048,128]{1,0:T(8,128)} %r_ref.3), custom_call_target="tpu_custom_call" | custom-call | tf_op jit(solution)/shard_map/pallas_call | solution.py:100
  20.9 0.8 %pad_maximum_fusion.4 = f32[2,2048]{1,0:T(2,128)S(1)} fusion(f32[1,2048]{1,0:T(1,128)} %get-tuple-element.12, f32[1,2048]{1,0:T(1,128)} %get-tuple-element.11), kind=kLoop, calls=%fused_computation.15 | loop fusion | flops 4096 | bytes 32768 | tf_op jit(solution)/shard_map/stack | solution.py:189
  22.2 0.8 %collective-permute-done = f32[2,2048]{1,0:T(2,128)S(1)} collective-permute-done((f32[2,2048]{1,0:T(2,128)S(1)}, f32[2,2048]{1,0:T(2,128)S(1)}, u32[]{:S(2)}, u32[]{:S(2)}) %collective-permute-start) | collective-permute-done | bytes 16416 | tf_op jit(solution)/shard_map/ppermute | solution.py:183
  23.8 2.9 %collective-permute-start.1 = (f32[2,2048]{1,0:T(2,128)S(1)}, f32[2,2048]{1,0:T(2,128)S(1)}, u32[]{:S(2)}, u32[]{:S(2)}) collective-permute-start(f32[2,2048]{1,0:T(2,128)S(1)} %pad_maximum_fusion.5), channel_id=1, source_target_pairs={{0,2},{1,3},{2,0},{3,1},{4,6},{5,7},{6,4},{7,5},{8,10},{9,11},{10,... | collective-permute-start | bytes 49160 | tf_op jit(solution)/shard_map/ppermute | solution.py:183
  26.7 1.7 %collective-permute-done.1 = f32[2,2048]{1,0:T(2,128)S(1)} collective-permute-done((f32[2,2048]{1,0:T(2,128)S(1)}, f32[2,2048]{1,0:T(2,128)S(1)}, u32[]{:S(2)}, u32[]{:S(2)}) %collective-permute-start.1) | collective-permute-done | bytes 16416 | tf_op jit(solution)/shard_map/ppermute | solution.py:183
  28.5 2.1 %collective-permute-start.2 = (f32[2,2048]{1,0:T(2,128)S(1)}, f32[2,2048]{1,0:T(2,128)S(1)}, u32[]{:S(2)}, u32[]{:S(2)}) collective-permute-start(f32[2,2048]{1,0:T(2,128)S(1)} %pad_maximum_fusion.6), channel_id=1, source_target_pairs={{0,4},{1,5},{2,6},{3,7},{4,0},{5,1},{6,2},{7,3},{8,12},{9,13},{10,... | collective-permute-start | bytes 49160 | tf_op jit(solution)/shard_map/ppermute | solution.py:183
  31.1 1.3 %collective-permute-done.2 = f32[2,2048]{1,0:T(2,128)S(1)} collective-permute-done((f32[2,2048]{1,0:T(2,128)S(1)}, f32[2,2048]{1,0:T(2,128)S(1)}, u32[]{:S(2)}, u32[]{:S(2)}) %collective-permute-start.2) | collective-permute-done | bytes 16416 | tf_op jit(solution)/shard_map/ppermute | solution.py:183
  32.5 3.1 %collective-permute-start.3 = (f32[2,2048]{1,0:T(2,128)S(1)}, f32[2,2048]{1,0:T(2,128)S(1)}, u32[]{:S(2)}, u32[]{:S(2)}) collective-permute-start(f32[2,2048]{1,0:T(2,128)S(1)} %pad_maximum_fusion.7), channel_id=1, source_target_pairs={{0,8},{1,9},{2,10},{3,11},{4,12},{5,13},{6,14},{7,15},{8,0},{9,1},... | collective-permute-start | bytes 49160 | tf_op jit(solution)/shard_map/ppermute | solution.py:183
  35.5 1.1 %maximum_maximum_fusion.qa_ref = bf16[2048,256]{1,0:T(8,128)(2,1)} fusion(bf16[2048,128]{1,0:T(8,128)(2,1)S(1)} %get-tuple-element.22, bf16[256]{0:T(256)(128)(2,1)S(1)} %pad.10.clone, bf16[256]{0:T(256)(128)(2,1)S(1)} %pad.9.clone), kind=kLoop, calls=%fused_computation | loop fusion | flops 3145728 | bytes 1573888 | tf_op jit(solution)/shard_map/concatenate | solution.py:229
  37.3 1.2 %fusion.19 = (f32[]{:T(128)}, f32[2048]{0:T(1024)}) fusion(f32[2048]{0:T(1024)S(1)} %copy-done.4, f32[2048]{0:T(1024)S(1)} %bitcast.66, f32[2048]{0:T(1024)S(1)} %bitcast.65, f32[2048]{0:T(1024)S(1)} %bitcast.72, f32[2048]{0:T(1024)S(1)} %bitcast.71, f32[2048]{0:T(1024)S(1)} %bitcast.70, f32[2048]{0:T(1024)S(1)} %bitcast.69, f32[2048]{0:T(1024)S(1)} %bitcast.67, ...), kind=kLoop, calls=%fused_computation.58 | loop fusion | flops 57343 | bytes 98308 | tf_op jit(solution)/shard_map/reduce_sum | solution.py:242
  38.5 9.8 %shard_map.77 = (f32[2048,128]{1,0:T(8,128)}, f32[2048,128]{1,0:T(8,128)}, f32[8,128]{1,0:T(8,128)}) custom-call(bf16[2048,2048]{1,0:T(8,128)(2,1)} %get-tuple-element.10.e_ref, f32[1,2048]{1,0:T(1,128)} %bitcast.73, bf16[2048,256]{1,0:T(8,128)(2,1)} %maximum_maximum_fusion.qa_ref, f32[128,2048]{1,0:T(8,128)} %get-tuple-element.13.ut_ref, ...), custom_call_target="tpu_custom_call" | custom-call | tf_op jit(solution)/shard_map/pallas_call | solution.py:145
  48.3 1.2 %constant_dynamic-slice_fusion.2 = f32[8,128,128]{2,1,0:T(8,128)S(1)} fusion(f32[16,128,128]{2,1,0:T(8,128)} %bitcast.57, s32[]{:T(128)S(6)} %select_n.60), kind=kLoop, calls=%fused_computation.46 | loop fusion | bytes 1048580 | tf_op jit(solution)/shard_map/dynamic_slice | solution.py:207
  49.5 0.8 %pad_maximum_fusion = f32[1032,128]{1,0:T(8,128)S(1)} fusion(f32[8,128]{1,0:T(8,128)} %get-tuple-element.15, f32[1024,128]{1,0:T(8,128)S(1)} %bitcast.55), kind=kLoop, calls=%fused_computation.2 | loop fusion | flops 132096 | bytes 1056768 | tf_op jit(solution)/shard_map/concatenate | solution.py:209
  50.4 1.9 %collective-permute-done.4 = f32[1032,128]{1,0:T(8,128)S(1)} collective-permute-done((f32[1032,128]{1,0:T(8,128)S(1)}, f32[1032,128]{1,0:T(8,128)S(1)}, u32[]{:S(2)}, u32[]{:S(2)}) %collective-permute-start.4) | collective-permute-done | bytes 528416 | tf_op jit(solution)/shard_map/ppermute | solution.py:183
  52.5 1.9 %collective-permute-start.5 = (f32[520,128]{1,0:T(8,128)S(1)}, f32[520,128]{1,0:T(8,128)S(1)}, u32[]{:S(2)}, u32[]{:S(2)}) collective-permute-start(f32[520,128]{1,0:T(8,128)S(1)} %pad_maximum_fusion.1), channel_id=1, source_target_pairs={{0,2},{1,3},{2,0},{3,1},{4,6},{5,7},{6,4},{7,5},{8,10},{9,11},{10,... | collective-permute-start | bytes 798728 | tf_op jit(solution)/shard_map/ppermute | solution.py:183
  54.4 6.7 %collective-permute-done.5 = f32[520,128]{1,0:T(8,128)S(1)} collective-permute-done((f32[520,128]{1,0:T(8,128)S(1)}, f32[520,128]{1,0:T(8,128)S(1)}, u32[]{:S(2)}, u32[]{:S(2)}) %collective-permute-start.5) | collective-permute-done | bytes 266272 | tf_op jit(solution)/shard_map/ppermute | solution.py:183
  61.2 1.9 %collective-permute-start.6 = (f32[264,128]{1,0:T(8,128)S(1)}, f32[264,128]{1,0:T(8,128)S(1)}, u32[]{:S(2)}, u32[]{:S(2)}) collective-permute-start(f32[264,128]{1,0:T(8,128)S(1)} %pad_maximum_fusion.2), channel_id=1, source_target_pairs={{0,4},{1,5},{2,6},{3,7},{4,0},{5,1},{6,2},{7,3},{8,12},{9,13},{10,... | collective-permute-start | bytes 405512 | tf_op jit(solution)/shard_map/ppermute | solution.py:183
  63.1 3.2 %collective-permute-done.6 = f32[264,128]{1,0:T(8,128)S(1)} collective-permute-done((f32[264,128]{1,0:T(8,128)S(1)}, f32[264,128]{1,0:T(8,128)S(1)}, u32[]{:S(2)}, u32[]{:S(2)}) %collective-permute-start.6) | collective-permute-done | bytes 135200 | tf_op jit(solution)/shard_map/ppermute | solution.py:183
  66.4 2.9 %collective-permute-start.7 = (f32[136,128]{1,0:T(8,128)S(1)}, f32[136,128]{1,0:T(8,128)S(1)}, u32[]{:S(2)}, u32[]{:S(2)}) collective-permute-start(f32[136,128]{1,0:T(8,128)S(1)} %pad_maximum_fusion.3), channel_id=1, source_target_pairs={{0,8},{1,9},{2,10},{3,11},{4,12},{5,13},{6,14},{7,15},{8,0},{9,1},... | collective-permute-start | bytes 208904 | tf_op jit(solution)/shard_map/ppermute | solution.py:183
  69.4 2.3 %collective-permute-done.7 = f32[136,128]{1,0:T(8,128)S(1)} collective-permute-done((f32[136,128]{1,0:T(8,128)S(1)}, f32[136,128]{1,0:T(8,128)S(1)}, u32[]{:S(2)}, u32[]{:S(2)}) %collective-permute-start.7) | collective-permute-done | bytes 69664 | tf_op jit(solution)/shard_map/ppermute | solution.py:183
  71.7 1.1 %divide_subtract_fusion = f32[128]{0:T(128)} fusion(f32[128]{0:T(128)S(1)} %copy-done.6, f32[128]{0:T(128)S(1)} %get-tuple-element.21, f32[8,128]{1,0:T(8,128)S(1)} %slice_add_fusion, f32[]{:T(128)} %get-tuple-element.33), kind=kLoop, calls=%fused_computation.47 | loop fusion | flops 1152 | bytes 2564 | tf_op jit(solution)/shard_map/sub | solution.py:243
  72.8 1.6 %fusion.3 = f32[128,128]{1,0:T(8,128)} fusion(f32[136,128]{1,0:T(8,128)S(1)} %collective-permute-done.7, f32[2048,128]{1,0:T(8,128)} %q_ref.3, s32[]{:T(128)S(6)} %select_n.73, f32[2,128,128]{2,1,0:T(8,128)S(1)} %dynamic-slice_add_fusion.2, s32[]{:T(128)S(6)} %select_n.71, f32[128]{0:T(128)S(1)} %multiply_divide_fusion, f32[128]{0:T(128)S(1)} %dynamic_slice.39), kind=kLoop, calls=%fused_computation.13 | loop fusion | flops 65536 | bytes 263176 | tf_op jit(solution)/shard_map/mul | solution.py:239
  (46 shorter events, 3.0 us)
Async XLA Ops:
  0.6 30.0 %copy-start = (f32[2048,128]{1,0:T(8,128)S(1)}, f32[2048,128]{1,0:T(8,128)}, u32[]{:S(2)}) copy-start(f32[2048,128]{1,0:T(8,128)} %q_ref.3) | copy-start | bytes 3145732
  0.6 30.0 %copy-start.4 = (f32[2048]{0:T(1024)S(1)}, f32[2048]{0:T(1024)}, u32[]{:S(2)}) copy-start(f32[2048]{0:T(1024)} %param.9) | copy-start | bytes 24580
  20.8 16.4 %copy-start.2 = (f32[1,2048]{1,0:T(1,128)S(1)}, f32[1,2048]{1,0:T(1,128)}, u32[]{:S(2)}) copy-start(f32[1,2048]{1,0:T(1,128)} %get-tuple-element.11) | copy-start | bytes 24580
  20.8 16.4 %copy-start.3 = (f32[1,2048]{1,0:T(1,128)S(1)}, f32[1,2048]{1,0:T(1,128)}, u32[]{:S(2)}) copy-start(f32[1,2048]{1,0:T(1,128)} %get-tuple-element.12) | copy-start | bytes 24580
  21.6 1.4 %collective-permute-start = (f32[2,2048]{1,0:T(2,128)S(1)}, f32[2,2048]{1,0:T(2,128)S(1)}, u32[]{:S(2)}, u32[]{:S(2)}) collective-permute-start(f32[2,2048]{1,0:T(2,128)S(1)} %pad_maximum_fusion.4), channel_id=1, source_target_pairs={{0,1},{1,0},{2,3},{3,2},{4,5},{5,4},{6,7},{7,6},{8,9},{9,8},{10,11... | collective-permute-start | bytes 49160 | tf_op jit(solution)/shard_map/ppermute | solution.py:183
  23.8 4.6 %collective-permute-start.1 = (f32[2,2048]{1,0:T(2,128)S(1)}, f32[2,2048]{1,0:T(2,128)S(1)}, u32[]{:S(2)}, u32[]{:S(2)}) collective-permute-start(f32[2,2048]{1,0:T(2,128)S(1)} %pad_maximum_fusion.5), channel_id=1, source_target_pairs={{0,2},{1,3},{2,0},{3,1},{4,6},{5,7},{6,4},{7,5},{8,10},{9,11},{10,... | collective-permute-start | bytes 49160 | tf_op jit(solution)/shard_map/ppermute | solution.py:183
  28.5 3.9 %collective-permute-start.2 = (f32[2,2048]{1,0:T(2,128)S(1)}, f32[2,2048]{1,0:T(2,128)S(1)}, u32[]{:S(2)}, u32[]{:S(2)}) collective-permute-start(f32[2,2048]{1,0:T(2,128)S(1)} %pad_maximum_fusion.6), channel_id=1, source_target_pairs={{0,4},{1,5},{2,6},{3,7},{4,0},{5,1},{6,2},{7,3},{8,12},{9,13},{10,... | collective-permute-start | bytes 49160 | tf_op jit(solution)/shard_map/ppermute | solution.py:183
  32.5 4.8 %collective-permute-start.3 = (f32[2,2048]{1,0:T(2,128)S(1)}, f32[2,2048]{1,0:T(2,128)S(1)}, u32[]{:S(2)}, u32[]{:S(2)}) collective-permute-start(f32[2,2048]{1,0:T(2,128)S(1)} %pad_maximum_fusion.7), channel_id=1, source_target_pairs={{0,8},{1,9},{2,10},{3,11},{4,12},{5,13},{6,14},{7,15},{8,0},{9,1},... | collective-permute-start | bytes 49160 | tf_op jit(solution)/shard_map/ppermute | solution.py:183
  48.3 4.0 %copy-start.1 = (f32[2048,128]{1,0:T(8,128)S(1)}, f32[2048,128]{1,0:T(8,128)}, u32[]{:S(2)}) copy-start(f32[2048,128]{1,0:T(8,128)} %get-tuple-element.14) | copy-start | bytes 3145732
  49.5 2.9 %copy-start.5 = (f32[8,128]{1,0:T(8,128)S(1)}, f32[8,128]{1,0:T(8,128)}, u32[]{:S(2)}) copy-start(f32[8,128]{1,0:T(8,128)} %get-tuple-element.15) | copy-start | bytes 12292
  50.3 2.0 %collective-permute-start.4 = (f32[1032,128]{1,0:T(8,128)S(1)}, f32[1032,128]{1,0:T(8,128)S(1)}, u32[]{:S(2)}, u32[]{:S(2)}) collective-permute-start(f32[1032,128]{1,0:T(8,128)S(1)} %pad_maximum_fusion), channel_id=1, source_target_pairs={{0,1},{1,0},{2,3},{3,2},{4,5},{5,4},{6,7},{7,6},{8,9},{9,8},{10,11... | collective-permute-start | bytes 1585160 | tf_op jit(solution)/shard_map/ppermute | solution.py:183
  52.4 16.9 %copy-start.6 = (f32[128]{0:T(128)S(1)}, f32[128]{0:T(128)}, u32[]{:S(2)}) copy-start(f32[128]{0:T(128)} %param.8) | copy-start | bytes 1540
  52.5 8.6 %collective-permute-start.5 = (f32[520,128]{1,0:T(8,128)S(1)}, f32[520,128]{1,0:T(8,128)S(1)}, u32[]{:S(2)}, u32[]{:S(2)}) collective-permute-start(f32[520,128]{1,0:T(8,128)S(1)} %pad_maximum_fusion.1), channel_id=1, source_target_pairs={{0,2},{1,3},{2,0},{3,1},{4,6},{5,7},{6,4},{7,5},{8,10},{9,11},{10,... | collective-permute-start | bytes 798728 | tf_op jit(solution)/shard_map/ppermute | solution.py:183
  61.2 5.1 %collective-permute-start.6 = (f32[264,128]{1,0:T(8,128)S(1)}, f32[264,128]{1,0:T(8,128)S(1)}, u32[]{:S(2)}, u32[]{:S(2)}) collective-permute-start(f32[264,128]{1,0:T(8,128)S(1)} %pad_maximum_fusion.2), channel_id=1, source_target_pairs={{0,4},{1,5},{2,6},{3,7},{4,0},{5,1},{6,2},{7,3},{8,12},{9,13},{10,... | collective-permute-start | bytes 405512 | tf_op jit(solution)/shard_map/ppermute | solution.py:183
  66.4 5.3 %collective-permute-start.7 = (f32[136,128]{1,0:T(8,128)S(1)}, f32[136,128]{1,0:T(8,128)S(1)}, u32[]{:S(2)}, u32[]{:S(2)}) collective-permute-start(f32[136,128]{1,0:T(8,128)S(1)} %pad_maximum_fusion.3), channel_id=1, source_target_pairs={{0,8},{1,9},{2,10},{3,11},{4,12},{5,13},{6,14},{7,15},{8,0},{9,1},... | collective-permute-start | bytes 208904 | tf_op jit(solution)/shard_map/ppermute | solution.py:183

commit v13 on v12

--- a/solution.py
+++ b/solution.py
@@ -19,7 +19,7 @@
     return x1, x2, x3
 
 
-def forward_kernel(q_ref, inv_ref, lid_ref, r_ref, e_ref, ut_ref, p_ref, t_ref, rn_sc, rlt_sc, rs_sc):
+def forward_kernel(q_ref, inv_ref, lid_ref, r_ref, e_ref, ut_ref, st_ref, rn_sc, rlt_sc, rs_sc):
     inv = inv_ref[...]
 
     @pl.when(pl.program_id(0) == 0)
@@ -46,14 +46,14 @@
     shifted = jnp.where(row == lid_ref[...], -jnp.inf, shifted)
     top = jnp.max(shifted, axis=0, keepdims=True)
     expd = jnp.exp(shifted - top)
-    p_ref[...] = top - 0.5 * qnorm
-    t_ref[...] = jnp.sum(expd, axis=0, keepdims=True)
+    st_ref[0:1, :] = top - 0.5 * qnorm
+    st_ref[1:2, :] = jnp.sum(expd, axis=0, keepdims=True)
     expd_low = expd.astype(jnp.bfloat16)
     e_ref[...] = expd_low
     ut_ref[...] = jnp.dot(rlt_sc[...], expd_low, preferred_element_type=jnp.float32)
 
 
-def backward_kernel(n_bits, e_ref, sc_ref, qa_ref, ut_ref, q_ref, r_ref, inv_ref, rg_ref, pull_hbm, terms_ref,
+def backward_kernel(n_bits, e_ref, sc_ref, ut_ref, q_ref, r_ref, inv_ref, rg_ref, pull_hbm, terms_ref,
                     acc_sc, qt_sc, pull_sc, sems):
     step = pl.program_id(0)
     n_feat = q_ref.shape[1]
@@ -78,8 +78,11 @@
         copy.start()
         copies.append(copy)
     weight = (e_ref[...].astype(jnp.float32) * scale).astype(jnp.bfloat16)
-    acc_sc[...] += jnp.dot(weight, qa_ref[...], preferred_element_type=jnp.float32)
-    qt_sc[...] += jnp.sum(q_ref[...] * pulled, axis=0, keepdims=True)
+    q = q_ref[...]
+    lane = lax.broadcasted_iota(jnp.int32, q.shape, 1)
+    query_aug = jnp.concatenate([q.astype(jnp.bfloat16), jnp.where(lane == 0, 1.0, 0.0).astype(jnp.bfloat16)], axis=1)
+    acc_sc[...] += jnp.dot(weight, query_aug, preferred_element_type=jnp.float32)
+    qt_sc[...] += jnp.sum(q * pulled, axis=0, keepdims=True)
     for copy in copies:
         copy.wait()
 
@@ -109,14 +112,12 @@
         out_specs=[
             pl.BlockSpec((n_ref, tile), lambda i: (0, i)),
             pl.BlockSpec((n_feat, tile), lambda i: (0, i)),
-            pl.BlockSpec((1, tile), lambda i: (0, i)),
-            pl.BlockSpec((1, tile), lambda i: (0, i)),
+            pl.BlockSpec((2, tile), lambda i: (0, i)),
         ],
         out_shape=[
             jax.ShapeDtypeStruct((n_ref, n_query), jnp.bfloat16),
             jax.ShapeDtypeStruct((n_feat, n_query), jnp.float32),
-            jax.ShapeDtypeStruct((1, n_query), jnp.float32),
-            jax.ShapeDtypeStruct((1, n_query), jnp.float32),
+            jax.ShapeDtypeStruct((2, n_query), jnp.float32),
         ],
         scratch_shapes=[
             pltpu.VMEM((n_ref, 1), jnp.float32),
@@ -134,10 +135,10 @@
     return out
 
 
-def local_backward(expd_low, scale, query_aug, unscaled_t, queries, references, inv, n_dev):
+def local_backward(expd_low, scale, unscaled_t, queries, references, inv, n_dev):
     n_ref, n_query = expd_low.shape
     n_feat = queries.shape[1]
-    width = query_aug.shape[1]
+    width = 2 * queries.shape[1]
     tile = min(TILE, n_query)
     sub = n_query // n_dev
     n_bits = n_dev.bit_length() - 1
@@ -148,7 +149,6 @@
         in_specs=[
             pl.BlockSpec((n_ref, tile), lambda i: (0, i)),
             pl.BlockSpec((1, tile), lambda i: (0, i)),
-            pl.BlockSpec((tile, width), lambda i: (i, 0)),
             pl.BlockSpec((n_feat, tile), lambda i: (0, i)),
             pl.BlockSpec((tile, n_feat), lambda i: (i, 0)),
             pl.BlockSpec((n_ref, n_feat), whole),
@@ -171,7 +171,7 @@
             pltpu.SemaphoreType.DMA((tile // sub,)),
         ],
         compiler_params=pltpu.CompilerParams(dimension_semantics=("arbitrary",)),
-    )(expd_low, scale, query_aug, unscaled_t, queries, references, inv)
+    )(expd_low, scale, unscaled_t, queries, references, inv)
 
 
 def bit_reversed(n):
@@ -183,16 +183,16 @@
     return lax.ppermute(x, "ref", [(i, i ^ step) for i in range(n_dev)])
 
 
-def butterfly_stats(peak, total, n_dev):
+def butterfly_stats(stats, n_dev):
     step = 1
     while step < n_dev:
-        other = exchange(jnp.stack([peak, total]), n_dev, step)
-        other_peak, other_total = other[0], other[1]
+        other = exchange(stats, n_dev, step)
+        peak, total, other_peak, other_total = stats[0], stats[1], other[0], other[1]
         new_peak = jnp.maximum(peak, other_peak)
         total = total * jnp.exp(peak - new_peak) + other_total * jnp.exp(other_peak - new_peak)
-        peak = new_peak
+        stats = jnp.stack([new_peak, total])
         step *= 2
-    return peak, total
+    return stats[0], stats[1]
 
 
 def halving_scatter(rows, extra, n_dev):
@@ -222,15 +222,11 @@
     inv = 1.0 / (spread * spread)
     ref_start = lax.axis_index("ref") * n_ref
     local_ids = (query_ids - ref_start)[None, :]
-    expd_low, unscaled_t, local_peak, local_total = local_forward(queries, inv[None, :], local_ids, references)
-    peak, total = butterfly_stats(local_peak[0], local_total[0], n_dev)
-    scale = cotangent * jnp.exp(local_peak[0] - peak) / total
-    query_low = queries.astype(jnp.bfloat16)
-    query_aug = jnp.concatenate(
-        [query_low, jnp.ones((n_query, 1), jnp.bfloat16), jnp.zeros((n_query, n_feat - 1), jnp.bfloat16)], axis=1
-    )
+    expd_low, unscaled_t, local_stats = local_forward(queries, inv[None, :], local_ids, references)
+    peak, total = butterfly_stats(local_stats, n_dev)
+    scale = cotangent * jnp.exp(local_stats[0] - peak) / total
     reference_grad, pulled, local_terms = local_backward(
-        expd_low, scale[None, :], query_aug, unscaled_t, queries, references, inv[None, :], n_dev
+        expd_low, scale[None, :], unscaled_t, queries, references, inv[None, :], n_dev
     )
     own_pulled, summed_terms = halving_scatter(pulled, local_terms, n_dev)
     own_start = lax.axis_index("ref") * own_rows

time: 74.8 us -> 75.7 us (1.012)
  waiting for transfers between devices: 18.5 us -> 19.9 us
    ppermute x8, waiting for transfers between devices: 18.5 us -> 19.9 us  [exchange(): return lax.ppermute(x, 'ref', [(i, i ^ step) for i in range(n_dev)])]
    concatenate x1 -> x0, other arithmetic: 1.13 us -> none  [on_device(): jnp.concatenate([query_low, jnp.ones((n_query, 1), jnp.bfloat16), jnp.zer...]
    add x3, other arithmetic: 0.15 us -> 1.2 us  [halving_scatter(): blocks = keep + got[:n_send].reshape(keep.shape)]
    mul x1, other arithmetic: 1.56 us -> 0.72 us  [on_device(): query_grad = (own_pulled - own_queries * own_cot[:, None]) * inv]
    another operation x4 -> x3, other arithmetic: 0.84 us -> 0.06 us  [butterfly_stats(): stats = jnp.stack([new_peak, total])]
  transfers between devices with their start and end apart: 8 -> 8, of which waited for: 8 -> 8; matrix products, arithmetic and copies ran while one was open for 2% -> 1% of each run, Pallas kernels for 0% -> 0%
where the time goes in v13:
time: 75.7 us; the launch traced here: 75.2 us
  Pallas kernels  27.6 us (36%)
  waiting for transfers between devices  19.9 us (26%)
  starting transfers between devices  15.4 us (20%)
  other arithmetic  10.2 us (13%)
  local copies, waits for them, and re-layouts  1.3 us (2%)
  between operations  0.83 us (1%)
    ppermute x8, waiting for transfers between devices, exchange(): return lax.ppermute(x, 'ref', [(i, i ^ step) for i in range(n_dev)])  19.9 us
    pallas_call x1, Pallas kernels, local_forward(): pl.pallas_call(forward_kernel, grid=(n_query // tile,), in_specs=[pl.Bloc...  17.7 us
    ppermute x8, starting transfers between devices, exchange(): return lax.ppermute(x, 'ref', [(i, i ^ step) for i in range(n_dev)])  15.4 us
    pallas_call x1, Pallas kernels, local_backward(): pl.pallas_call(functools.partial(backward_kernel, n_bits), grid=(n_query...  9.94 us
    reduce_sum x1, other arithmetic, on_device(): weight_total = jnp.sum(cotangent)  1.92 us
  transfers between devices with their start and end apart: 8, of which 8 were waited for; matrix products, arithmetic and copies ran while one was open for 1% of the time, Pallas kernels for 0%

profile of v13, /device:TPU:0, one launch (start us, length us, event | category | flops | bytes accessed | tf_op | source)
XLA Modules:
  0.0 75.2 jit_solution(7666292455145791383)
XLA Ops:
  0.6 1.2 %fusion.20.inv_ref = f32[1,128]{1,0:T(1,128)} fusion(f32[128]{0:T(128)} %param.8), kind=kLoop, calls=%fused_computation.57 | loop fusion | flops 256 | bytes 1024 | tf_op jit(solution)/shard_map/broadcast_in_dim | solution.py:225
  1.8 1.3 %broadcast_subtract_fusion = s32[2048]{0:T(1024)} fusion(s32[2048]{0:T(1024)} %param.7, s32[]{:T(128)S(6)} %mul.109), kind=kLoop, calls=%fused_computation.41 | loop fusion | flops 2048 | bytes 16388 | tf_op jit(solution)/shard_map/sub | solution.py:224
  3.1 17.7 %shard_map.76 = (bf16[2048,2048]{1,0:T(8,128)(2,1)}, f32[128,2048]{1,0:T(8,128)}, f32[2,2048]{1,0:T(2,128)}) custom-call(f32[2048,128]{1,0:T(8,128)} %q_ref.3, f32[1,128]{1,0:T(1,128)} %fusion.20.inv_ref, s32[1,2048]{1,0:T(1,128)} %bitcast.62, f32[2048,128]{1,0:T(8,128)} %r_ref.3), custom_call_target="tpu_custom_call" | custom-call | tf_op jit(solution)/shard_map/pallas_call | solution.py:103
  21.3 1.0 %collective-permute-done = f32[2,2048]{1,0:T(2,128)S(1)} collective-permute-done((f32[2,2048]{1,0:T(2,128)}, f32[2,2048]{1,0:T(2,128)S(1)}, u32[]{:S(2)}, u32[]{:S(2)}) %collective-permute-start) | collective-permute-done | bytes 16416 | tf_op jit(solution)/shard_map/ppermute | solution.py:183
  22.3 0.8 %multiply_add_fusion.2 = (f32[1,2048]{1,0:T(1,128)S(1)}, f32[1,2048]{1,0:T(1,128)S(1)}, f32[1,2048]{1,0:T(1,128)S(1)}, f32[1,2048]{1,0:T(1,128)S(1)}, f32[1,2048]{1,0:T(1,128)S(1)}, /*index=5*/f32[1,2048]{1,0:T(1,128)S(1)}) fusion(f32[2,2048]{1,0:T(2,128)S(1)} %collective-permute-done, f32[2,2048]{1,0:T(2,128)} %get-tuple-element.10), kind=kLoop, calls=%fused_computation.36 | loop fusion | flops 12288 | bytes 81920 | tf_op jit(solution)/shard_map/add | solution.py:192
  23.2 2.9 %collective-permute-start.1 = (f32[2,2048]{1,0:T(2,128)S(1)}, f32[2,2048]{1,0:T(2,128)S(1)}, u32[]{:S(2)}, u32[]{:S(2)}) collective-permute-start(f32[2,2048]{1,0:T(2,128)S(1)} %pad_maximum_fusion.4), channel_id=1, source_target_pairs={{0,2},{1,3},{2,0},{3,1},{4,6},{5,7},{6,4},{7,5},{8,10},{9,11},{10,... | collective-permute-start | bytes 49160 | tf_op jit(solution)/shard_map/ppermute | solution.py:183
  26.1 1.7 %collective-permute-done.1 = f32[2,2048]{1,0:T(2,128)S(1)} collective-permute-done((f32[2,2048]{1,0:T(2,128)S(1)}, f32[2,2048]{1,0:T(2,128)S(1)}, u32[]{:S(2)}, u32[]{:S(2)}) %collective-permute-start.1) | collective-permute-done | bytes 16416 | tf_op jit(solution)/shard_map/ppermute | solution.py:183
  27.9 2.2 %collective-permute-start.2 = (f32[2,2048]{1,0:T(2,128)S(1)}, f32[2,2048]{1,0:T(2,128)S(1)}, u32[]{:S(2)}, u32[]{:S(2)}) collective-permute-start(f32[2,2048]{1,0:T(2,128)S(1)} %pad_maximum_fusion.5), channel_id=1, source_target_pairs={{0,4},{1,5},{2,6},{3,7},{4,0},{5,1},{6,2},{7,3},{8,12},{9,13},{10,... | collective-permute-start | bytes 49160 | tf_op jit(solution)/shard_map/ppermute | solution.py:183
  30.0 1.7 %collective-permute-done.2 = f32[2,2048]{1,0:T(2,128)S(1)} collective-permute-done((f32[2,2048]{1,0:T(2,128)S(1)}, f32[2,2048]{1,0:T(2,128)S(1)}, u32[]{:S(2)}, u32[]{:S(2)}) %collective-permute-start.2) | collective-permute-done | bytes 16416 | tf_op jit(solution)/shard_map/ppermute | solution.py:183
  31.8 3.1 %collective-permute-start.3 = (f32[2,2048]{1,0:T(2,128)S(1)}, f32[2,2048]{1,0:T(2,128)S(1)}, u32[]{:S(2)}, u32[]{:S(2)}) collective-permute-start(f32[2,2048]{1,0:T(2,128)S(1)} %pad_maximum_fusion.6), channel_id=1, source_target_pairs={{0,8},{1,9},{2,10},{3,11},{4,12},{5,13},{6,14},{7,15},{8,0},{9,1},... | collective-permute-start | bytes 49160 | tf_op jit(solution)/shard_map/ppermute | solution.py:183
  34.9 1.7 %collective-permute-done.3 = f32[2,2048]{1,0:T(2,128)S(1)} collective-permute-done((f32[2,2048]{1,0:T(2,128)S(1)}, f32[2,2048]{1,0:T(2,128)S(1)}, u32[]{:S(2)}, u32[]{:S(2)}) %collective-permute-start.3) | collective-permute-done | bytes 16416 | tf_op jit(solution)/shard_map/ppermute | solution.py:183
  36.7 1.9 %fusion.19 = (f32[]{:T(128)}, f32[2048]{0:T(1024)}) fusion(f32[2048]{0:T(1024)} %param.9, f32[2048]{0:T(1024)S(1)} %bitcast.68, f32[2048]{0:T(1024)S(1)} %bitcast.67, f32[2048]{0:T(1024)S(1)} %bitcast.72, f32[2048]{0:T(1024)S(1)} %bitcast.71, f32[2048]{0:T(1024)S(1)} %bitcast.70, f32[2048]{0:T(1024)S(1)} %bitcast.69, f32[2048]{0:T(1024)S(1)} %bitcast.63, ...), kind=kLoop, calls=%fused_computation.56 | loop fusion | flops 57343 | bytes 98308 | tf_op jit(solution)/shard_map/reduce_sum | solution.py:238
  38.6 9.9 %shard_map.77 = (f32[2048,128]{1,0:T(8,128)}, f32[2048,128]{1,0:T(8,128)}, f32[8,128]{1,0:T(8,128)}) custom-call(bf16[2048,2048]{1,0:T(8,128)(2,1)} %get-tuple-element.9.e_ref, f32[1,2048]{1,0:T(1,128)} %bitcast.61, f32[128,2048]{1,0:T(8,128)} %get-tuple-element.11.ut_ref, f32[2048,128]{1,0:T(8,128)} %q_ref.3, f32[2048,128]{1,0:T(8,128)} %r_ref.3, ...), custom_call_target="tpu_custom_call" | custom-call | tf_op jit(solution)/shard_map/pallas_call | solution.py:146
  48.5 1.1 %constant_dynamic-slice_fusion.2 = f32[8,128,128]{2,1,0:T(8,128)S(1)} fusion(f32[16,128,128]{2,1,0:T(8,128)} %bitcast.56, s32[]{:T(128)S(6)} %select_n.60), kind=kLoop, calls=%fused_computation.44 | loop fusion | bytes 1048580 | tf_op jit(solution)/shard_map/dynamic_slice | solution.py:207
  49.6 0.7 pad_maximum_fusion
  50.5 1.9 %collective-permute-done.4 = f32[1032,128]{1,0:T(8,128)S(1)} collective-permute-done((f32[1032,128]{1,0:T(8,128)S(1)}, f32[1032,128]{1,0:T(8,128)S(1)}, u32[]{:S(2)}, u32[]{:S(2)}) %collective-permute-start.4) | collective-permute-done | bytes 528416 | tf_op jit(solution)/shard_map/ppermute | solution.py:183
  52.4 1.1 %dynamic-slice_add_fusion = f32[8,128,128]{2,1,0:T(8,128)S(1)} fusion(f32[8,128,128]{2,1,0:T(8,128)S(1)} %bitcast.53, f32[16,128,128]{2,1,0:T(8,128)} %bitcast.57, s32[]{:T(128)S(6)} %select_n.59), kind=kLoop, calls=%fused_computation.2 | loop fusion | flops 131072 | bytes 1572868 | tf_op jit(solution)/shard_map/add | solution.py:210
  54.3 1.9 %collective-permute-start.5 = (f32[520,128]{1,0:T(8,128)S(1)}, f32[520,128]{1,0:T(8,128)S(1)}, u32[]{:S(2)}, u32[]{:S(2)}) collective-permute-start(f32[520,128]{1,0:T(8,128)S(1)} %pad_maximum_fusion.1), channel_id=1, source_target_pairs={{0,2},{1,3},{2,0},{3,1},{4,6},{5,7},{6,4},{7,5},{8,10},{9,11},{10,... | collective-permute-start | bytes 798728 | tf_op jit(solution)/shard_map/ppermute | solution.py:183
  56.1 6.7 %collective-permute-done.5 = f32[520,128]{1,0:T(8,128)S(1)} collective-permute-done((f32[520,128]{1,0:T(8,128)S(1)}, f32[520,128]{1,0:T(8,128)S(1)}, u32[]{:S(2)}, u32[]{:S(2)}) %collective-permute-start.5) | collective-permute-done | bytes 266272 | tf_op jit(solution)/shard_map/ppermute | solution.py:183
  63.0 1.9 %collective-permute-start.6 = (f32[264,128]{1,0:T(8,128)S(1)}, f32[264,128]{1,0:T(8,128)S(1)}, u32[]{:S(2)}, u32[]{:S(2)}) collective-permute-start(f32[264,128]{1,0:T(8,128)S(1)} %pad_maximum_fusion.2), channel_id=1, source_target_pairs={{0,4},{1,5},{2,6},{3,7},{4,0},{5,1},{6,2},{7,3},{8,12},{9,13},{10,... | collective-permute-start | bytes 405512 | tf_op jit(solution)/shard_map/ppermute | solution.py:183
  64.9 3.2 %collective-permute-done.6 = f32[264,128]{1,0:T(8,128)S(1)} collective-permute-done((f32[264,128]{1,0:T(8,128)S(1)}, f32[264,128]{1,0:T(8,128)S(1)}, u32[]{:S(2)}, u32[]{:S(2)}) %collective-permute-start.6) | collective-permute-done | bytes 135200 | tf_op jit(solution)/shard_map/ppermute | solution.py:183
  68.1 2.9 %collective-permute-start.7 = (f32[136,128]{1,0:T(8,128)S(1)}, f32[136,128]{1,0:T(8,128)S(1)}, u32[]{:S(2)}, u32[]{:S(2)}) collective-permute-start(f32[136,128]{1,0:T(8,128)S(1)} %pad_maximum_fusion.3), channel_id=1, source_target_pairs={{0,8},{1,9},{2,10},{3,11},{4,12},{5,13},{6,14},{7,15},{8,0},{9,1},... | collective-permute-start | bytes 208904 | tf_op jit(solution)/shard_map/ppermute | solution.py:183
  71.5 1.9 %collective-permute-done.7 = f32[136,128]{1,0:T(8,128)S(1)} collective-permute-done((f32[136,128]{1,0:T(8,128)S(1)}, f32[136,128]{1,0:T(8,128)S(1)}, u32[]{:S(2)}, u32[]{:S(2)}) %collective-permute-start.7) | collective-permute-done | bytes 69664 | tf_op jit(solution)/shard_map/ppermute | solution.py:183
  73.4 1.1 %divide_subtract_fusion = f32[128]{0:T(128)} fusion(f32[128]{0:T(128)S(1)} %copy-done.2, f32[128]{0:T(128)S(1)} %multiply_reduce_fusion, f32[8,128]{1,0:T(8,128)S(1)} %slice_add_fusion, f32[]{:T(128)} %get-tuple-element.31), kind=kLoop, calls=%fused_computation.45 | loop fusion | flops 1152 | bytes 2564 | tf_op jit(solution)/shard_map/sub | solution.py:239
  (33 shorter events, 2.8 us)
Async XLA Ops:
  20.8 1.5 %collective-permute-start = (f32[2,2048]{1,0:T(2,128)}, f32[2,2048]{1,0:T(2,128)S(1)}, u32[]{:S(2)}, u32[]{:S(2)}) collective-permute-start(f32[2,2048]{1,0:T(2,128)} %get-tuple-element.10), channel_id=1, source_target_pairs={{0,1},{1,0},{2,3},{3,2},{4,5},{5,4},{6,7},{7,6},{8,9},{9,8},{10,11... | collective-permute-start | bytes 49160 | tf_op jit(solution)/shard_map/ppermute | solution.py:183
  23.2 4.6 %collective-permute-start.1 = (f32[2,2048]{1,0:T(2,128)S(1)}, f32[2,2048]{1,0:T(2,128)S(1)}, u32[]{:S(2)}, u32[]{:S(2)}) collective-permute-start(f32[2,2048]{1,0:T(2,128)S(1)} %pad_maximum_fusion.4), channel_id=1, source_target_pairs={{0,2},{1,3},{2,0},{3,1},{4,6},{5,7},{6,4},{7,5},{8,10},{9,11},{10,... | collective-permute-start | bytes 49160 | tf_op jit(solution)/shard_map/ppermute | solution.py:183
  27.9 3.9 %collective-permute-start.2 = (f32[2,2048]{1,0:T(2,128)S(1)}, f32[2,2048]{1,0:T(2,128)S(1)}, u32[]{:S(2)}, u32[]{:S(2)}) collective-permute-start(f32[2,2048]{1,0:T(2,128)S(1)} %pad_maximum_fusion.5), channel_id=1, source_target_pairs={{0,4},{1,5},{2,6},{3,7},{4,0},{5,1},{6,2},{7,3},{8,12},{9,13},{10,... | collective-permute-start | bytes 49160 | tf_op jit(solution)/shard_map/ppermute | solution.py:183
  31.8 4.8 %collective-permute-start.3 = (f32[2,2048]{1,0:T(2,128)S(1)}, f32[2,2048]{1,0:T(2,128)S(1)}, u32[]{:S(2)}, u32[]{:S(2)}) collective-permute-start(f32[2,2048]{1,0:T(2,128)S(1)} %pad_maximum_fusion.6), channel_id=1, source_target_pairs={{0,8},{1,9},{2,10},{3,11},{4,12},{5,13},{6,14},{7,15},{8,0},{9,1},... | collective-permute-start | bytes 49160 | tf_op jit(solution)/shard_map/ppermute | solution.py:183
  38.6 26.3 %copy-start.2 = (f32[128]{0:T(128)S(1)}, f32[128]{0:T(128)}, u32[]{:S(2)}) copy-start(f32[128]{0:T(128)} %param.8) | copy-start | bytes 1540
  38.6 32.4 %copy-start = (f32[2048,128]{1,0:T(8,128)S(1)}, f32[2048,128]{1,0:T(8,128)}, u32[]{:S(2)}) copy-start(f32[2048,128]{1,0:T(8,128)} %q_ref.3) | copy-start | bytes 3145732
  38.6 32.4 %copy-start.1 = (f32[2048]{0:T(1024)S(1)}, f32[2048]{0:T(1024)}, u32[]{:S(2)}) copy-start(f32[2048]{0:T(1024)} %param.9) | copy-start | bytes 24580
  50.4 2.0 %collective-permute-start.4 = (f32[1032,128]{1,0:T(8,128)S(1)}, f32[1032,128]{1,0:T(8,128)S(1)}, u32[]{:S(2)}, u32[]{:S(2)}) collective-permute-start(f32[1032,128]{1,0:T(8,128)S(1)} %pad_maximum_fusion), channel_id=1, source_target_pairs={{0,1},{1,0},{2,3},{3,2},{4,5},{5,4},{6,7},{7,6},{8,9},{9,8},{10,11... | collective-permute-start | bytes 1585160 | tf_op jit(solution)/shard_map/ppermute | solution.py:183
  54.3 8.6 %collective-permute-start.5 = (f32[520,128]{1,0:T(8,128)S(1)}, f32[520,128]{1,0:T(8,128)S(1)}, u32[]{:S(2)}, u32[]{:S(2)}) collective-permute-start(f32[520,128]{1,0:T(8,128)S(1)} %pad_maximum_fusion.1), channel_id=1, source_target_pairs={{0,2},{1,3},{2,0},{3,1},{4,6},{5,7},{6,4},{7,5},{8,10},{9,11},{10,... | collective-permute-start | bytes 798728 | tf_op jit(solution)/shard_map/ppermute | solution.py:183
  63.0 5.1 %collective-permute-start.6 = (f32[264,128]{1,0:T(8,128)S(1)}, f32[264,128]{1,0:T(8,128)S(1)}, u32[]{:S(2)}, u32[]{:S(2)}) collective-permute-start(f32[264,128]{1,0:T(8,128)S(1)} %pad_maximum_fusion.2), channel_id=1, source_target_pairs={{0,4},{1,5},{2,6},{3,7},{4,0},{5,1},{6,2},{7,3},{8,12},{9,13},{10,... | collective-permute-start | bytes 405512 | tf_op jit(solution)/shard_map/ppermute | solution.py:183
  68.1 5.3 %collective-permute-start.7 = (f32[136,128]{1,0:T(8,128)S(1)}, f32[136,128]{1,0:T(8,128)S(1)}, u32[]{:S(2)}, u32[]{:S(2)}) collective-permute-start(f32[136,128]{1,0:T(8,128)S(1)} %pad_maximum_fusion.3), channel_id=1, source_target_pairs={{0,8},{1,9},{2,10},{3,11},{4,12},{5,13},{6,14},{7,15},{8,0},{9,1},... | collective-permute-start | bytes 208904 | tf_op jit(solution)/shard_map/ppermute | solution.py:183

commit v14 on v12

--- a/solution.py
+++ b/solution.py
@@ -19,8 +19,9 @@
     return x1, x2, x3
 
 
-def forward_kernel(q_ref, inv_ref, lid_ref, r_ref, e_ref, ut_ref, p_ref, t_ref, rn_sc, rlt_sc, rs_sc):
-    inv = inv_ref[...]
+def forward_kernel(q_ref, sp_ref, id_ref, r_ref, e_ref, ut_ref, p_ref, t_ref, rn_sc, rlt_sc, rs_sc):
+    spread = sp_ref[...]
+    inv = 1.0 / (spread * spread)
 
     @pl.when(pl.program_id(0) == 0)
     def _():
@@ -43,7 +44,8 @@
     )
     shifted = cross - rn_sc[...]
     row = lax.broadcasted_iota(jnp.int32, shifted.shape, 0)
-    shifted = jnp.where(row == lid_ref[...], -jnp.inf, shifted)
+    local_ids = id_ref[...] - lax.axis_index("ref") * shifted.shape[0]
+    shifted = jnp.where(row == local_ids, -jnp.inf, shifted)
     top = jnp.max(shifted, axis=0, keepdims=True)
     expd = jnp.exp(shifted - top)
     p_ref[...] = top - 0.5 * qnorm
@@ -93,7 +95,7 @@
         terms_ref[...] = jnp.concatenate([qt_sc[...], rterm, jnp.zeros((6, n_feat), jnp.float32)], axis=0)
 
 
-def local_forward(queries, inv, local_ids, references):
+def local_forward(queries, spread, query_ids, references):
     n_query, n_feat = queries.shape
     n_ref = references.shape[0]
     tile = min(TILE, n_query)
@@ -124,7 +126,7 @@
             pltpu.VMEM((n_ref, 6 * n_feat), jnp.bfloat16),
         ],
         compiler_params=pltpu.CompilerParams(dimension_semantics=("arbitrary",)),
-    )(queries, inv, local_ids, references)
+    )(queries, spread, query_ids, references)
 
 
 def bit_reversed_index(p, n_bits):
@@ -220,9 +222,7 @@
     n_dev = lax.axis_size("ref")
     own_rows = n_query // n_dev
     inv = 1.0 / (spread * spread)
-    ref_start = lax.axis_index("ref") * n_ref
-    local_ids = (query_ids - ref_start)[None, :]
-    expd_low, unscaled_t, local_peak, local_total = local_forward(queries, inv[None, :], local_ids, references)
+    expd_low, unscaled_t, local_peak, local_total = local_forward(queries, spread[None, :], query_ids[None, :], references)
     peak, total = butterfly_stats(local_peak[0], local_total[0], n_dev)
     scale = cotangent * jnp.exp(local_peak[0] - peak) / total
     query_low = queries.astype(jnp.bfloat16)

time: 74.8 us -> 72.2 us (0.965)
  other arithmetic: 10.6 us -> 8.54 us
    sub x1 -> x0, other arithmetic: 1.3 us -> none  [on_device(): local_ids = (query_ids - ref_start)[None, :]]
  transfers between devices with their start and end apart: 8 -> 8, of which waited for: 8 -> 8; matrix products, arithmetic and copies ran while one was open for 2% -> 3% of each run, Pallas kernels for 0% -> 0%
where the time goes in v14:
time: 72.2 us; the launch traced here: 71.8 us
  Pallas kernels  27.4 us (38%)
  waiting for transfers between devices  18 us (25%)
  starting transfers between devices  15.4 us (21%)
  other arithmetic  8.54 us (12%)
  local copies, waits for them, and re-layouts  1.5 us (2%)
  between operations  0.93 us (1%)
    ppermute x8, waiting for transfers between devices, exchange(): return lax.ppermute(x, 'ref', [(i, i ^ step) for i in range(n_dev)])  18 us
    pallas_call x1, Pallas kernels, local_forward(): pl.pallas_call(forward_kernel, grid=(n_query // tile,), in_specs=[pl.Bloc...  17.6 us
    ppermute x8, starting transfers between devices, exchange(): return lax.ppermute(x, 'ref', [(i, i ^ step) for i in range(n_dev)])  15.4 us
    pallas_call x1, Pallas kernels, local_backward(): pl.pallas_call(functools.partial(backward_kernel, n_bits), grid=(n_query...  9.78 us
    mul x1, other arithmetic, on_device(): query_grad = (own_pulled - own_queries * own_cot[:, None]) * inv  1.56 us
  transfers between devices with their start and end apart: 8, of which 8 were waited for; matrix products, arithmetic and copies ran while one was open for 3% of the time, Pallas kernels for 0%

profile of v14, /device:TPU:0, one launch (start us, length us, event | category | flops | bytes accessed | tf_op | source)
XLA Modules:
  0.0 71.8 jit_solution(5921079352918651404)
XLA Ops:
  0.7 17.6 %shard_map.76 = (bf16[2048,2048]{1,0:T(8,128)(2,1)}, f32[128,2048]{1,0:T(8,128)}, f32[1,2048]{1,0:T(1,128)}, f32[1,2048]{1,0:T(1,128)}) custom-call(f32[2048,128]{1,0:T(8,128)} %q_ref.3, f32[1,128]{1,0:T(1,128)} %bitcast.75, s32[1,2048]{1,0:T(1,128)} %bitcast.74, f32[2048,128]{1,0:T(8,128)} %r_ref.3), custom_call_target="tpu_custom_call" | custom-call | tf_op jit(solution)/shard_map/pallas_call | solution.py:102
  18.3 0.8 %pad_maximum_fusion.4 = f32[2,2048]{1,0:T(2,128)S(1)} fusion(f32[1,2048]{1,0:T(1,128)} %get-tuple-element.12, f32[1,2048]{1,0:T(1,128)} %get-tuple-element.11), kind=kLoop, calls=%fused_computation.15 | loop fusion | flops 4096 | bytes 32768 | tf_op jit(solution)/shard_map/stack | solution.py:191
  19.6 0.8 %collective-permute-done = f32[2,2048]{1,0:T(2,128)S(1)} collective-permute-done((f32[2,2048]{1,0:T(2,128)S(1)}, f32[2,2048]{1,0:T(2,128)S(1)}, u32[]{:S(2)}, u32[]{:S(2)}) %collective-permute-start) | collective-permute-done | bytes 16416 | tf_op jit(solution)/shard_map/ppermute | solution.py:185
  20.5 0.8 %multiply_add_fusion.2 = (f32[1,2048]{1,0:T(1,128)S(1)}, f32[1,2048]{1,0:T(1,128)S(1)}, f32[1,2048]{1,0:T(1,128)S(1)}, f32[1,2048]{1,0:T(1,128)S(1)}) fusion(f32[1,2048]{1,0:T(1,128)} %get-tuple-element.12, f32[1,2048]{1,0:T(1,128)} %get-tuple-element.11, f32[2,2048]{1,0:T(2,128)S(1)} %collective-permute-done), kind=kLoop, calls=%fused_computation.38 | loop fusion | flops 12288 | bytes 65536 | tf_op jit(solution)/shard_map/add | solution.py:194
  21.3 2.9 %collective-permute-start.1 = (f32[2,2048]{1,0:T(2,128)S(1)}, f32[2,2048]{1,0:T(2,128)S(1)}, u32[]{:S(2)}, u32[]{:S(2)}) collective-permute-start(f32[2,2048]{1,0:T(2,128)S(1)} %pad_maximum_fusion.5), channel_id=1, source_target_pairs={{0,2},{1,3},{2,0},{3,1},{4,6},{5,7},{6,4},{7,5},{8,10},{9,11},{10,... | collective-permute-start | bytes 49160 | tf_op jit(solution)/shard_map/ppermute | solution.py:185
  24.6 1.3 %collective-permute-done.1 = f32[2,2048]{1,0:T(2,128)S(1)} collective-permute-done((f32[2,2048]{1,0:T(2,128)S(1)}, f32[2,2048]{1,0:T(2,128)S(1)}, u32[]{:S(2)}, u32[]{:S(2)}) %collective-permute-start.1) | collective-permute-done | bytes 16416 | tf_op jit(solution)/shard_map/ppermute | solution.py:185
  26.0 2.1 %collective-permute-start.2 = (f32[2,2048]{1,0:T(2,128)S(1)}, f32[2,2048]{1,0:T(2,128)S(1)}, u32[]{:S(2)}, u32[]{:S(2)}) collective-permute-start(f32[2,2048]{1,0:T(2,128)S(1)} %pad_maximum_fusion.6), channel_id=1, source_target_pairs={{0,4},{1,5},{2,6},{3,7},{4,0},{5,1},{6,2},{7,3},{8,12},{9,13},{10,... | collective-permute-start | bytes 49160 | tf_op jit(solution)/shard_map/ppermute | solution.py:185
  28.1 1.1 %maximum_maximum_fusion.qa_ref = bf16[2048,256]{1,0:T(8,128)(2,1)} fusion(bf16[2048,128]{1,0:T(8,128)(2,1)S(1)} %get-tuple-element.22, bf16[256]{0:T(256)(128)(2,1)S(1)} %pad.10.clone, bf16[256]{0:T(256)(128)(2,1)S(1)} %pad.9.clone), kind=kLoop, calls=%fused_computation | loop fusion | flops 3145728 | bytes 1573888 | tf_op jit(solution)/shard_map/concatenate | solution.py:229
  29.2 0.6 collective-permute-done.2
  29.9 3.1 %collective-permute-start.3 = (f32[2,2048]{1,0:T(2,128)S(1)}, f32[2,2048]{1,0:T(2,128)S(1)}, u32[]{:S(2)}, u32[]{:S(2)}) collective-permute-start(f32[2,2048]{1,0:T(2,128)S(1)} %pad_maximum_fusion.7), channel_id=1, source_target_pairs={{0,8},{1,9},{2,10},{3,11},{4,12},{5,13},{6,14},{7,15},{8,0},{9,1},... | collective-permute-start | bytes 49160 | tf_op jit(solution)/shard_map/ppermute | solution.py:185
  33.5 1.2 %collective-permute-done.3 = f32[2,2048]{1,0:T(2,128)S(1)} collective-permute-done((f32[2,2048]{1,0:T(2,128)S(1)}, f32[2,2048]{1,0:T(2,128)S(1)}, u32[]{:S(2)}, u32[]{:S(2)}) %collective-permute-start.3) | collective-permute-done | bytes 16416 | tf_op jit(solution)/shard_map/ppermute | solution.py:185
  34.8 1.2 %fusion.19 = (f32[]{:T(128)}, f32[2048]{0:T(1024)}) fusion(f32[2048]{0:T(1024)S(1)} %copy-done.4, f32[2048]{0:T(1024)S(1)} %bitcast.66, f32[2048]{0:T(1024)S(1)} %bitcast.65, f32[2048]{0:T(1024)S(1)} %bitcast.72, f32[2048]{0:T(1024)S(1)} %bitcast.71, f32[2048]{0:T(1024)S(1)} %bitcast.70, f32[2048]{0:T(1024)S(1)} %bitcast.69, f32[2048]{0:T(1024)S(1)} %bitcast.67, ...), kind=kLoop, calls=%fused_computation.57 | loop fusion | flops 57343 | bytes 98308 | tf_op jit(solution)/shard_map/reduce_sum | solution.py:242
  36.0 9.8 %shard_map.77 = (f32[2048,128]{1,0:T(8,128)}, f32[2048,128]{1,0:T(8,128)}, f32[8,128]{1,0:T(8,128)}) custom-call(bf16[2048,2048]{1,0:T(8,128)(2,1)} %get-tuple-element.10.e_ref, f32[1,2048]{1,0:T(1,128)} %bitcast.73, bf16[2048,256]{1,0:T(8,128)(2,1)} %maximum_maximum_fusion.qa_ref, f32[128,2048]{1,0:T(8,128)} %get-tuple-element.13.ut_ref, ...), custom_call_target="tpu_custom_call" | custom-call | tf_op jit(solution)/shard_map/pallas_call | solution.py:147
  45.8 1.2 %constant_dynamic-slice_fusion.2 = f32[8,128,128]{2,1,0:T(8,128)S(1)} fusion(f32[16,128,128]{2,1,0:T(8,128)} %bitcast.58, s32[]{:T(128)S(6)} %select_n.60), kind=kLoop, calls=%fused_computation.45 | loop fusion | bytes 1048580 | tf_op jit(solution)/shard_map/dynamic_slice | solution.py:209
  47.0 0.8 %pad_maximum_fusion = f32[1032,128]{1,0:T(8,128)S(1)} fusion(f32[8,128]{1,0:T(8,128)} %get-tuple-element.15, f32[1024,128]{1,0:T(8,128)S(1)} %bitcast.56), kind=kLoop, calls=%fused_computation.2 | loop fusion | flops 132096 | bytes 1056768 | tf_op jit(solution)/shard_map/concatenate | solution.py:211
  47.9 1.9 %collective-permute-done.4 = f32[1032,128]{1,0:T(8,128)S(1)} collective-permute-done((f32[1032,128]{1,0:T(8,128)S(1)}, f32[1032,128]{1,0:T(8,128)S(1)}, u32[]{:S(2)}, u32[]{:S(2)}) %collective-permute-start.4) | collective-permute-done | bytes 528416 | tf_op jit(solution)/shard_map/ppermute | solution.py:185
  49.9 1.9 %collective-permute-start.5 = (f32[520,128]{1,0:T(8,128)S(1)}, f32[520,128]{1,0:T(8,128)S(1)}, u32[]{:S(2)}, u32[]{:S(2)}) collective-permute-start(f32[520,128]{1,0:T(8,128)S(1)} %pad_maximum_fusion.1), channel_id=1, source_target_pairs={{0,2},{1,3},{2,0},{3,1},{4,6},{5,7},{6,4},{7,5},{8,10},{9,11},{10,... | collective-permute-start | bytes 798728 | tf_op jit(solution)/shard_map/ppermute | solution.py:185
  51.9 6.7 %collective-permute-done.5 = f32[520,128]{1,0:T(8,128)S(1)} collective-permute-done((f32[520,128]{1,0:T(8,128)S(1)}, f32[520,128]{1,0:T(8,128)S(1)}, u32[]{:S(2)}, u32[]{:S(2)}) %collective-permute-start.5) | collective-permute-done | bytes 266272 | tf_op jit(solution)/shard_map/ppermute | solution.py:185
  58.7 1.9 %collective-permute-start.6 = (f32[264,128]{1,0:T(8,128)S(1)}, f32[264,128]{1,0:T(8,128)S(1)}, u32[]{:S(2)}, u32[]{:S(2)}) collective-permute-start(f32[264,128]{1,0:T(8,128)S(1)} %pad_maximum_fusion.2), channel_id=1, source_target_pairs={{0,4},{1,5},{2,6},{3,7},{4,0},{5,1},{6,2},{7,3},{8,12},{9,13},{10,... | collective-permute-start | bytes 405512 | tf_op jit(solution)/shard_map/ppermute | solution.py:185
  60.5 3.2 %collective-permute-done.6 = f32[264,128]{1,0:T(8,128)S(1)} collective-permute-done((f32[264,128]{1,0:T(8,128)S(1)}, f32[264,128]{1,0:T(8,128)S(1)}, u32[]{:S(2)}, u32[]{:S(2)}) %collective-permute-start.6) | collective-permute-done | bytes 135200 | tf_op jit(solution)/shard_map/ppermute | solution.py:185
  63.8 2.9 %collective-permute-start.7 = (f32[136,128]{1,0:T(8,128)S(1)}, f32[136,128]{1,0:T(8,128)S(1)}, u32[]{:S(2)}, u32[]{:S(2)}) collective-permute-start(f32[136,128]{1,0:T(8,128)S(1)} %pad_maximum_fusion.3), channel_id=1, source_target_pairs={{0,8},{1,9},{2,10},{3,11},{4,12},{5,13},{6,14},{7,15},{8,0},{9,1},... | collective-permute-start | bytes 208904 | tf_op jit(solution)/shard_map/ppermute | solution.py:185
  66.8 2.3 %collective-permute-done.7 = f32[136,128]{1,0:T(8,128)S(1)} collective-permute-done((f32[136,128]{1,0:T(8,128)S(1)}, f32[136,128]{1,0:T(8,128)S(1)}, u32[]{:S(2)}, u32[]{:S(2)}) %collective-permute-start.7) | collective-permute-done | bytes 69664 | tf_op jit(solution)/shard_map/ppermute | solution.py:185
  69.1 1.1 %divide_subtract_fusion = f32[128]{0:T(128)} fusion(f32[128]{0:T(128)S(1)} %copy-done.6, f32[128]{0:T(128)S(1)} %get-tuple-element.21, f32[8,128]{1,0:T(8,128)S(1)} %slice_add_fusion, f32[]{:T(128)} %get-tuple-element.33), kind=kLoop, calls=%fused_computation.46 | loop fusion | flops 1152 | bytes 2564 | tf_op jit(solution)/shard_map/sub | solution.py:243
  70.2 1.6 %fusion.3 = f32[128,128]{1,0:T(8,128)} fusion(f32[136,128]{1,0:T(8,128)S(1)} %collective-permute-done.7, f32[2048,128]{1,0:T(8,128)} %q_ref.3, s32[]{:T(128)S(6)} %select_n.73, f32[2,128,128]{2,1,0:T(8,128)S(1)} %dynamic-slice_add_fusion.2, s32[]{:T(128)S(6)} %select_n.71, f32[128]{0:T(128)S(1)} %multiply_divide_fusion, f32[128]{0:T(128)S(1)} %dynamic_slice.39), kind=kLoop, calls=%fused_computation.13 | loop fusion | flops 65536 | bytes 263176 | tf_op jit(solution)/shard_map/mul | solution.py:239
  (45 shorter events, 2.2 us)
Async XLA Ops:
  0.6 23.5 %copy-start = (f32[2048,128]{1,0:T(8,128)S(1)}, f32[2048,128]{1,0:T(8,128)}, u32[]{:S(2)}) copy-start(f32[2048,128]{1,0:T(8,128)} %q_ref.3) | copy-start | bytes 3145732
  0.6 23.5 %copy-start.4 = (f32[2048]{0:T(1024)S(1)}, f32[2048]{0:T(1024)}, u32[]{:S(2)}) copy-start(f32[2048]{0:T(1024)} %param.9) | copy-start | bytes 24580
  18.3 14.7 %copy-start.6 = (f32[128]{0:T(128)S(1)}, f32[128]{0:T(128)}, u32[]{:S(2)}) copy-start(f32[128]{0:T(128)} %param.8) | copy-start | bytes 1540
  18.3 16.5 %copy-start.2 = (f32[1,2048]{1,0:T(1,128)S(1)}, f32[1,2048]{1,0:T(1,128)}, u32[]{:S(2)}) copy-start(f32[1,2048]{1,0:T(1,128)} %get-tuple-element.11) | copy-start | bytes 24580
  18.3 16.5 %copy-start.3 = (f32[1,2048]{1,0:T(1,128)S(1)}, f32[1,2048]{1,0:T(1,128)}, u32[]{:S(2)}) copy-start(f32[1,2048]{1,0:T(1,128)} %get-tuple-element.12) | copy-start | bytes 24580
  19.1 1.4 %collective-permute-start = (f32[2,2048]{1,0:T(2,128)S(1)}, f32[2,2048]{1,0:T(2,128)S(1)}, u32[]{:S(2)}, u32[]{:S(2)}) collective-permute-start(f32[2,2048]{1,0:T(2,128)S(1)} %pad_maximum_fusion.4), channel_id=1, source_target_pairs={{0,1},{1,0},{2,3},{3,2},{4,5},{5,4},{6,7},{7,6},{8,9},{9,8},{10,11... | collective-permute-start | bytes 49160 | tf_op jit(solution)/shard_map/ppermute | solution.py:185
  21.3 4.6 %collective-permute-start.1 = (f32[2,2048]{1,0:T(2,128)S(1)}, f32[2,2048]{1,0:T(2,128)S(1)}, u32[]{:S(2)}, u32[]{:S(2)}) collective-permute-start(f32[2,2048]{1,0:T(2,128)S(1)} %pad_maximum_fusion.5), channel_id=1, source_target_pairs={{0,2},{1,3},{2,0},{3,1},{4,6},{5,7},{6,4},{7,5},{8,10},{9,11},{10,... | collective-permute-start | bytes 49160 | tf_op jit(solution)/shard_map/ppermute | solution.py:185
  26.0 3.9 %collective-permute-start.2 = (f32[2,2048]{1,0:T(2,128)S(1)}, f32[2,2048]{1,0:T(2,128)S(1)}, u32[]{:S(2)}, u32[]{:S(2)}) collective-permute-start(f32[2,2048]{1,0:T(2,128)S(1)} %pad_maximum_fusion.6), channel_id=1, source_target_pairs={{0,4},{1,5},{2,6},{3,7},{4,0},{5,1},{6,2},{7,3},{8,12},{9,13},{10,... | collective-permute-start | bytes 49160 | tf_op jit(solution)/shard_map/ppermute | solution.py:185
  29.9 4.8 %collective-permute-start.3 = (f32[2,2048]{1,0:T(2,128)S(1)}, f32[2,2048]{1,0:T(2,128)S(1)}, u32[]{:S(2)}, u32[]{:S(2)}) collective-permute-start(f32[2,2048]{1,0:T(2,128)S(1)} %pad_maximum_fusion.7), channel_id=1, source_target_pairs={{0,8},{1,9},{2,10},{3,11},{4,12},{5,13},{6,14},{7,15},{8,0},{9,1},... | collective-permute-start | bytes 49160 | tf_op jit(solution)/shard_map/ppermute | solution.py:185
  45.8 4.0 %copy-start.1 = (f32[2048,128]{1,0:T(8,128)S(1)}, f32[2048,128]{1,0:T(8,128)}, u32[]{:S(2)}) copy-start(f32[2048,128]{1,0:T(8,128)} %get-tuple-element.14) | copy-start | bytes 3145732
  47.0 2.9 %copy-start.5 = (f32[8,128]{1,0:T(8,128)S(1)}, f32[8,128]{1,0:T(8,128)}, u32[]{:S(2)}) copy-start(f32[8,128]{1,0:T(8,128)} %get-tuple-element.15) | copy-start | bytes 12292
  47.7 2.0 %collective-permute-start.4 = (f32[1032,128]{1,0:T(8,128)S(1)}, f32[1032,128]{1,0:T(8,128)S(1)}, u32[]{:S(2)}, u32[]{:S(2)}) collective-permute-start(f32[1032,128]{1,0:T(8,128)S(1)} %pad_maximum_fusion), channel_id=1, source_target_pairs={{0,1},{1,0},{2,3},{3,2},{4,5},{5,4},{6,7},{7,6},{8,9},{9,8},{10,11... | collective-permute-start | bytes 1585160 | tf_op jit(solution)/shard_map/ppermute | solution.py:185
  49.9 8.6 %collective-permute-start.5 = (f32[520,128]{1,0:T(8,128)S(1)}, f32[520,128]{1,0:T(8,128)S(1)}, u32[]{:S(2)}, u32[]{:S(2)}) collective-permute-start(f32[520,128]{1,0:T(8,128)S(1)} %pad_maximum_fusion.1), channel_id=1, source_target_pairs={{0,2},{1,3},{2,0},{3,1},{4,6},{5,7},{6,4},{7,5},{8,10},{9,11},{10,... | collective-permute-start | bytes 798728 | tf_op jit(solution)/shard_map/ppermute | solution.py:185
  58.7 5.1 %collective-permute-start.6 = (f32[264,128]{1,0:T(8,128)S(1)}, f32[264,128]{1,0:T(8,128)S(1)}, u32[]{:S(2)}, u32[]{:S(2)}) collective-permute-start(f32[264,128]{1,0:T(8,128)S(1)} %pad_maximum_fusion.2), channel_id=1, source_target_pairs={{0,4},{1,5},{2,6},{3,7},{4,0},{5,1},{6,2},{7,3},{8,12},{9,13},{10,... | collective-permute-start | bytes 405512 | tf_op jit(solution)/shard_map/ppermute | solution.py:185
  63.8 5.3 %collective-permute-start.7 = (f32[136,128]{1,0:T(8,128)S(1)}, f32[136,128]{1,0:T(8,128)S(1)}, u32[]{:S(2)}, u32[]{:S(2)}) collective-permute-start(f32[136,128]{1,0:T(8,128)S(1)} %pad_maximum_fusion.3), channel_id=1, source_target_pairs={{0,8},{1,9},{2,10},{3,11},{4,12},{5,13},{6,14},{7,15},{8,0},{9,1},... | collective-permute-start | bytes 208904 | tf_op jit(solution)/shard_map/ppermute | solution.py:185

commit v15 on v14

--- a/solution.py
+++ b/solution.py
@@ -55,13 +55,16 @@
     ut_ref[...] = jnp.dot(rlt_sc[...], expd_low, preferred_element_type=jnp.float32)
 
 
-def backward_kernel(n_bits, e_ref, sc_ref, qa_ref, ut_ref, q_ref, r_ref, inv_ref, rg_ref, pull_hbm, terms_ref,
-                    acc_sc, qt_sc, pull_sc, sems):
+def backward_kernel(n_bits, e_ref, sc_ref, qa_ref, ut_ref, q_ref, r_ref, inv_ref, rg_ref, pull_hbm,
+                    acc_sc, qt_sc, pull_sc, terms_sc, sems, terms_sem):
     step = pl.program_id(0)
     n_feat = q_ref.shape[1]
     tile = pull_sc.shape[0]
-    sub = pull_hbm.shape[0] // (2 ** n_bits)
+    n_rows = pull_hbm.shape[0] - terms_sc.shape[0]
+    n_dev = 2 ** n_bits
+    sub = n_rows // n_dev
     per = tile // sub
+    flip = (lax.axis_index("ref") % 2) * (n_dev // 2)
 
     @pl.when(step == 0)
     def _():
@@ -73,7 +76,7 @@
     pull_sc[...] = pulled
     copies = []
     for j in range(per):
-        dst = bit_reversed_index(step * per + j, n_bits) * sub
+        dst = (bit_reversed_index(step * per + j, n_bits) + flip) % n_dev * sub
         copy = pltpu.make_async_copy(
             pull_sc.at[pl.ds(j * sub, sub)], pull_hbm.at[pl.ds(pl.multiple_of(dst, sub), sub)], sems.at[j]
         )
@@ -92,7 +95,10 @@
         rgrad = (acc[:, :n_feat] - refs * acc[:, n_feat:n_feat + 1]) * inv_ref[...]
         rg_ref[...] = rgrad
         rterm = jnp.sum(refs * rgrad, axis=0, keepdims=True)
-        terms_ref[...] = jnp.concatenate([qt_sc[...], rterm, jnp.zeros((6, n_feat), jnp.float32)], axis=0)
+        terms_sc[...] = jnp.concatenate([qt_sc[...], rterm, jnp.zeros((6, n_feat), jnp.float32)], axis=0)
+        copy = pltpu.make_async_copy(terms_sc, pull_hbm.at[pl.ds(n_rows, terms_sc.shape[0])], terms_sem)
+        copy.start()
+        copy.wait()
 
 
 def local_forward(queries, spread, query_ids, references):
@@ -159,18 +165,18 @@
         out_specs=[
             pl.BlockSpec((n_ref, n_feat), whole),
             pl.BlockSpec(memory_space=pl.ANY),
-            pl.BlockSpec((8, n_feat), whole),
         ],
         out_shape=[
             jax.ShapeDtypeStruct((n_ref, n_feat), jnp.float32),
-            jax.ShapeDtypeStruct((n_query, n_feat), jnp.float32),
-            jax.ShapeDtypeStruct((8, n_feat), jnp.float32),
+            jax.ShapeDtypeStruct((n_query + 8, n_feat), jnp.float32),
         ],
         scratch_shapes=[
             pltpu.VMEM((n_ref, width), jnp.float32),
             pltpu.VMEM((1, n_feat), jnp.float32),
             pltpu.VMEM((tile, n_feat), jnp.float32),
+            pltpu.VMEM((8, n_feat), jnp.float32),
             pltpu.SemaphoreType.DMA((tile // sub,)),
+            pltpu.SemaphoreType.DMA(()),
         ],
         compiler_params=pltpu.CompilerParams(dimension_semantics=("arbitrary",)),
     )(expd_low, scale, query_aug, unscaled_t, queries, references, inv)
@@ -197,11 +203,15 @@
     return peak, total
 
 
-def halving_scatter(rows, extra, n_dev):
+def halving_scatter(packed, n_extra, n_dev):
     me = lax.axis_index("ref")
-    n_feat = rows.shape[-1]
-    blocks = rows.reshape(n_dev, -1, n_feat)
-    step = 1
+    n_feat = packed.shape[-1]
+    n_rows = packed.shape[0] - n_extra
+    half = n_rows // 2
+    got = exchange(packed[half:], n_dev, 1)
+    blocks = (packed[:half] + got[:half]).reshape(n_dev // 2, -1, n_feat)
+    extra = packed[n_rows:] + got[half:]
+    step = 2
     while step < n_dev:
         half = blocks.shape[0] // 2
         bit = (me // step) % 2
@@ -229,10 +239,10 @@
     query_aug = jnp.concatenate(
         [query_low, jnp.ones((n_query, 1), jnp.bfloat16), jnp.zeros((n_query, n_feat - 1), jnp.bfloat16)], axis=1
     )
-    reference_grad, pulled, local_terms = local_backward(
+    reference_grad, packed = local_backward(
         expd_low, scale[None, :], query_aug, unscaled_t, queries, references, inv[None, :], n_dev
     )
-    own_pulled, summed_terms = halving_scatter(pulled, local_terms, n_dev)
+    own_pulled, summed_terms = halving_scatter(packed, 8, n_dev)
     own_start = lax.axis_index("ref") * own_rows
     own_queries = lax.dynamic_slice_in_dim(queries, own_start, own_rows, 0)
     own_cot = lax.dynamic_slice_in_dim(cotangent, own_start, own_rows, 0)

time: 72.2 us -> 73.7 us (1.021)
  other arithmetic: 8.54 us -> 9.54 us
    add x0 -> x2, other arithmetic: none -> 1.78 us  [the longest x1 1.1 us: halving_scatter(): blocks = (packed[:half] + got[:half]).reshape(n_dev // 2, -1, n_feat)]
    dynamic_slice x3 -> x2, local copies, waits for them, and re-layouts: 1.21 us -> 0.04 us  [halving_scatter(): send = lax.dynamic_slice_in_dim(blocks, (1 - bit) * half, half, 0)]
    slice x0 -> x1, local copies, waits for them, and re-layouts: none -> 1.08 us  [halving_scatter(): got = exchange(packed[half:], n_dev, 1)]
    concatenate x4 -> x3, other arithmetic: 0.81 us -> 0.04 us  [halving_scatter(): jnp.concatenate([send.reshape(n_send, n_feat), extra])]
where the time goes in v15:
time: 73.7 us; the launch traced here: 73.2 us
  Pallas kernels  28 us (38%)
  waiting for transfers between devices  18 us (24%)
  starting transfers between devices  15.4 us (21%)
  other arithmetic  9.54 us (13%)
  local copies, waits for them, and re-layouts  1.36 us (2%)
  between operations  0.87 us (1%)
    ppermute x8, waiting for transfers between devices, exchange(): return lax.ppermute(x, 'ref', [(i, i ^ step) for i in range(n_dev)])  18 us
    pallas_call x1, Pallas kernels, local_forward(): pl.pallas_call(forward_kernel, grid=(n_query // tile,), in_specs=[pl.Bloc...  17.6 us
    ppermute x8, starting transfers between devices, exchange(): return lax.ppermute(x, 'ref', [(i, i ^ step) for i in range(n_dev)])  15.4 us
    pallas_call x1, Pallas kernels, local_backward(): pl.pallas_call(functools.partial(backward_kernel, n_bits), grid=(n_query...  10.4 us
    mul x1, other arithmetic, on_device(): query_grad = (own_pulled - own_queries * own_cot[:, None]) * inv  1.56 us
  transfers between devices with their start and end apart: 8, of which 8 were waited for; matrix products, arithmetic and copies ran while one was open for 3% of the time, Pallas kernels for 0%

profile of v15, /device:TPU:0, one launch (start us, length us, event | category | flops | bytes accessed | tf_op | source)
XLA Modules:
  0.0 73.2 jit_solution(11180983656568114778)
XLA Ops:
  0.7 17.6 %shard_map.76 = (bf16[2048,2048]{1,0:T(8,128)(2,1)}, f32[128,2048]{1,0:T(8,128)}, f32[1,2048]{1,0:T(1,128)}, f32[1,2048]{1,0:T(1,128)}) custom-call(f32[2048,128]{1,0:T(8,128)} %q_ref.3, f32[1,128]{1,0:T(1,128)} %bitcast.71, s32[1,2048]{1,0:T(1,128)} %bitcast.70, f32[2048,128]{1,0:T(8,128)} %r_ref.3), custom_call_target="tpu_custom_call" | custom-call | tf_op jit(solution)/shard_map/pallas_call | solution.py:108
  18.3 0.8 %pad_maximum_fusion.3 = f32[2,2048]{1,0:T(2,128)S(1)} fusion(f32[1,2048]{1,0:T(1,128)} %get-tuple-element.11, f32[1,2048]{1,0:T(1,128)} %get-tuple-element.10), kind=kLoop, calls=%fused_computation.14 | loop fusion | flops 4096 | bytes 32768 | tf_op jit(solution)/shard_map/stack | solution.py:197
  19.7 0.8 %collective-permute-done = f32[2,2048]{1,0:T(2,128)S(1)} collective-permute-done((f32[2,2048]{1,0:T(2,128)S(1)}, f32[2,2048]{1,0:T(2,128)S(1)}, u32[]{:S(2)}, u32[]{:S(2)}) %collective-permute-start) | collective-permute-done | bytes 16416 | tf_op jit(solution)/shard_map/ppermute | solution.py:191
  20.5 0.8 %multiply_add_fusion.2 = (f32[1,2048]{1,0:T(1,128)S(1)}, f32[1,2048]{1,0:T(1,128)S(1)}, f32[1,2048]{1,0:T(1,128)S(1)}, f32[1,2048]{1,0:T(1,128)S(1)}) fusion(f32[1,2048]{1,0:T(1,128)} %get-tuple-element.11, f32[1,2048]{1,0:T(1,128)} %get-tuple-element.10, f32[2,2048]{1,0:T(2,128)S(1)} %collective-permute-done), kind=kLoop, calls=%fused_computation.37 | loop fusion | flops 12288 | bytes 65536 | tf_op jit(solution)/shard_map/add | solution.py:200
  21.3 2.9 %collective-permute-start.1 = (f32[2,2048]{1,0:T(2,128)S(1)}, f32[2,2048]{1,0:T(2,128)S(1)}, u32[]{:S(2)}, u32[]{:S(2)}) collective-permute-start(f32[2,2048]{1,0:T(2,128)S(1)} %pad_maximum_fusion.4), channel_id=1, source_target_pairs={{0,2},{1,3},{2,0},{3,1},{4,6},{5,7},{6,4},{7,5},{8,10},{9,11},{10,... | collective-permute-start | bytes 49160 | tf_op jit(solution)/shard_map/ppermute | solution.py:191
  24.7 1.3 %collective-permute-done.1 = f32[2,2048]{1,0:T(2,128)S(1)} collective-permute-done((f32[2,2048]{1,0:T(2,128)S(1)}, f32[2,2048]{1,0:T(2,128)S(1)}, u32[]{:S(2)}, u32[]{:S(2)}) %collective-permute-start.1) | collective-permute-done | bytes 16416 | tf_op jit(solution)/shard_map/ppermute | solution.py:191
  26.0 2.1 %collective-permute-start.2 = (f32[2,2048]{1,0:T(2,128)S(1)}, f32[2,2048]{1,0:T(2,128)S(1)}, u32[]{:S(2)}, u32[]{:S(2)}) collective-permute-start(f32[2,2048]{1,0:T(2,128)S(1)} %pad_maximum_fusion.5), channel_id=1, source_target_pairs={{0,4},{1,5},{2,6},{3,7},{4,0},{5,1},{6,2},{7,3},{8,12},{9,13},{10,... | collective-permute-start | bytes 49160 | tf_op jit(solution)/shard_map/ppermute | solution.py:191
  28.1 1.1 %maximum_maximum_fusion.qa_ref = bf16[2048,256]{1,0:T(8,128)(2,1)} fusion(bf16[2048,128]{1,0:T(8,128)(2,1)S(1)} %get-tuple-element.20, bf16[256]{0:T(256)(128)(2,1)S(1)} %pad.8.clone, bf16[256]{0:T(256)(128)(2,1)S(1)} %pad.7.clone), kind=kLoop, calls=%fused_computation | loop fusion | flops 3145728 | bytes 1573888 | tf_op jit(solution)/shard_map/concatenate | solution.py:239
  29.9 3.1 %collective-permute-start.3 = (f32[2,2048]{1,0:T(2,128)S(1)}, f32[2,2048]{1,0:T(2,128)S(1)}, u32[]{:S(2)}, u32[]{:S(2)}) collective-permute-start(f32[2,2048]{1,0:T(2,128)S(1)} %pad_maximum_fusion.6), channel_id=1, source_target_pairs={{0,8},{1,9},{2,10},{3,11},{4,12},{5,13},{6,14},{7,15},{8,0},{9,1},... | collective-permute-start | bytes 49160 | tf_op jit(solution)/shard_map/ppermute | solution.py:191
  33.5 1.2 %collective-permute-done.3 = f32[2,2048]{1,0:T(2,128)S(1)} collective-permute-done((f32[2,2048]{1,0:T(2,128)S(1)}, f32[2,2048]{1,0:T(2,128)S(1)}, u32[]{:S(2)}, u32[]{:S(2)}) %collective-permute-start.3) | collective-permute-done | bytes 16416 | tf_op jit(solution)/shard_map/ppermute | solution.py:191
  34.8 1.3 %fusion.19 = (f32[]{:T(128)}, f32[2048]{0:T(1024)}) fusion(f32[2048]{0:T(1024)S(1)} %copy-done.3, f32[2048]{0:T(1024)S(1)} %bitcast.62, f32[2048]{0:T(1024)S(1)} %bitcast.61, f32[2048]{0:T(1024)S(1)} %bitcast.68, f32[2048]{0:T(1024)S(1)} %bitcast.67, f32[2048]{0:T(1024)S(1)} %bitcast.66, f32[2048]{0:T(1024)S(1)} %bitcast.65, f32[2048]{0:T(1024)S(1)} %bitcast.63, ...), kind=kLoop, calls=%fused_computation.55 | loop fusion | flops 57343 | bytes 98308 | tf_op jit(solution)/shard_map/reduce_sum | solution.py:252
  36.0 10.4 %shard_map.77 = (f32[2048,128]{1,0:T(8,128)}, f32[2056,128]{1,0:T(8,128)}) custom-call(bf16[2048,2048]{1,0:T(8,128)(2,1)} %get-tuple-element.9.e_ref, f32[1,2048]{1,0:T(1,128)} %bitcast.69, bf16[2048,256]{1,0:T(8,128)(2,1)} %maximum_maximum_fusion.qa_ref, f32[128,2048]{1,0:T(8,128)} %get-tuple-element.12.ut_ref, f32[2048,128]{1,0:T(8,128)} %q_ref.3, ...), custom_call_target="tpu_custom_call" | custom-call | tf_op jit(solution)/shard_map/pallas_call | solution.py:153
  46.4 1.1 %slice.72 = f32[1032,128]{1,0:T(8,128)S(1)} slice(f32[2056,128]{1,0:T(8,128)} %get-tuple-element.13), slice={[1024:2056], [0:128]} | slice | bytes 1056768 | tf_op jit(solution)/shard_map/slice | solution.py:211
  47.6 1.9 %collective-permute-done.4 = f32[1032,128]{1,0:T(8,128)S(1)} collective-permute-done((f32[1032,128]{1,0:T(8,128)S(1)}, f32[1032,128]{1,0:T(8,128)S(1)}, u32[]{:S(2)}, u32[]{:S(2)}) %collective-permute-start.4) | collective-permute-done | bytes 528416 | tf_op jit(solution)/shard_map/ppermute | solution.py:191
  49.5 1.1 %slice_add_fusion = f32[1024,128]{1,0:T(8,128)S(1)} fusion(f32[1032,128]{1,0:T(8,128)S(1)} %collective-permute-done.4, f32[2056,128]{1,0:T(8,128)} %get-tuple-element.13), kind=kLoop, calls=%fused_computation.2 | loop fusion | flops 131072 | bytes 1572864 | tf_op jit(solution)/shard_map/add | solution.py:212
  50.6 0.7 slice_add_fusion.4
  51.3 1.9 %collective-permute-start.5 = (f32[520,128]{1,0:T(8,128)S(1)}, f32[520,128]{1,0:T(8,128)S(1)}, u32[]{:S(2)}, u32[]{:S(2)}) collective-permute-start(f32[520,128]{1,0:T(8,128)S(1)} %pad_maximum_fusion), channel_id=1, source_target_pairs={{0,2},{1,3},{2,0},{3,1},{4,6},{5,7},{6,4},{7,5},{8,10},{9,11},{10,... | collective-permute-start | bytes 798728 | tf_op jit(solution)/shard_map/ppermute | solution.py:191
  53.2 6.7 %collective-permute-done.5 = f32[520,128]{1,0:T(8,128)S(1)} collective-permute-done((f32[520,128]{1,0:T(8,128)S(1)}, f32[520,128]{1,0:T(8,128)S(1)}, u32[]{:S(2)}, u32[]{:S(2)}) %collective-permute-start.5) | collective-permute-done | bytes 266272 | tf_op jit(solution)/shard_map/ppermute | solution.py:191
  60.1 1.9 %collective-permute-start.6 = (f32[264,128]{1,0:T(8,128)S(1)}, f32[264,128]{1,0:T(8,128)S(1)}, u32[]{:S(2)}, u32[]{:S(2)}) collective-permute-start(f32[264,128]{1,0:T(8,128)S(1)} %pad_maximum_fusion.1), channel_id=1, source_target_pairs={{0,4},{1,5},{2,6},{3,7},{4,0},{5,1},{6,2},{7,3},{8,12},{9,13},{10,... | collective-permute-start | bytes 405512 | tf_op jit(solution)/shard_map/ppermute | solution.py:191
  61.9 3.2 %collective-permute-done.6 = f32[264,128]{1,0:T(8,128)S(1)} collective-permute-done((f32[264,128]{1,0:T(8,128)S(1)}, f32[264,128]{1,0:T(8,128)S(1)}, u32[]{:S(2)}, u32[]{:S(2)}) %collective-permute-start.6) | collective-permute-done | bytes 135200 | tf_op jit(solution)/shard_map/ppermute | solution.py:191
  65.2 2.9 %collective-permute-start.7 = (f32[136,128]{1,0:T(8,128)S(1)}, f32[136,128]{1,0:T(8,128)S(1)}, u32[]{:S(2)}, u32[]{:S(2)}) collective-permute-start(f32[136,128]{1,0:T(8,128)S(1)} %pad_maximum_fusion.2), channel_id=1, source_target_pairs={{0,8},{1,9},{2,10},{3,11},{4,12},{5,13},{6,14},{7,15},{8,0},{9,1},... | collective-permute-start | bytes 208904 | tf_op jit(solution)/shard_map/ppermute | solution.py:191
  68.2 2.3 %collective-permute-done.7 = f32[136,128]{1,0:T(8,128)S(1)} collective-permute-done((f32[136,128]{1,0:T(8,128)S(1)}, f32[136,128]{1,0:T(8,128)S(1)}, u32[]{:S(2)}, u32[]{:S(2)}) %collective-permute-start.7) | collective-permute-done | bytes 69664 | tf_op jit(solution)/shard_map/ppermute | solution.py:191
  70.5 1.2 %divide_subtract_fusion = f32[128]{0:T(128)} fusion(f32[128]{0:T(128)S(1)} %copy-done.4, f32[128]{0:T(128)S(1)} %get-tuple-element.19, f32[8,128]{1,0:T(8,128)S(1)} %slice_add_fusion.1, f32[]{:T(128)} %get-tuple-element.31), kind=kLoop, calls=%fused_computation.44 | loop fusion | flops 1152 | bytes 2564 | tf_op jit(solution)/shard_map/sub | solution.py:253
  71.7 1.6 %fusion.3 = f32[128,128]{1,0:T(8,128)} fusion(f32[136,128]{1,0:T(8,128)S(1)} %collective-permute-done.7, f32[2048,128]{1,0:T(8,128)} %q_ref.3, s32[]{:T(128)S(6)} %select_n.59, f32[2,128,128]{2,1,0:T(8,128)S(1)} %dynamic-slice_add_fusion.1, s32[]{:T(128)S(6)} %select_n.57, f32[128]{0:T(128)S(1)} %multiply_divide_fusion, f32[128]{0:T(128)S(1)} %dynamic_slice.31), kind=kLoop, calls=%fused_computation.12 | loop fusion | flops 65536 | bytes 263176 | tf_op jit(solution)/shard_map/mul | solution.py:249
  (39 shorter events, 2.6 us)
Async XLA Ops:
  0.6 23.6 %copy-start = (f32[2048,128]{1,0:T(8,128)S(1)}, f32[2048,128]{1,0:T(8,128)}, u32[]{:S(2)}) copy-start(f32[2048,128]{1,0:T(8,128)} %q_ref.3) | copy-start | bytes 3145732
  0.6 23.6 %copy-start.3 = (f32[2048]{0:T(1024)S(1)}, f32[2048]{0:T(1024)}, u32[]{:S(2)}) copy-start(f32[2048]{0:T(1024)} %param.9) | copy-start | bytes 24580
  18.3 14.7 %copy-start.4 = (f32[128]{0:T(128)S(1)}, f32[128]{0:T(128)}, u32[]{:S(2)}) copy-start(f32[128]{0:T(128)} %param.8) | copy-start | bytes 1540
  18.3 16.5 %copy-start.1 = (f32[1,2048]{1,0:T(1,128)S(1)}, f32[1,2048]{1,0:T(1,128)}, u32[]{:S(2)}) copy-start(f32[1,2048]{1,0:T(1,128)} %get-tuple-element.10) | copy-start | bytes 24580
  18.3 16.5 %copy-start.2 = (f32[1,2048]{1,0:T(1,128)S(1)}, f32[1,2048]{1,0:T(1,128)}, u32[]{:S(2)}) copy-start(f32[1,2048]{1,0:T(1,128)} %get-tuple-element.11) | copy-start | bytes 24580
  19.1 1.4 %collective-permute-start = (f32[2,2048]{1,0:T(2,128)S(1)}, f32[2,2048]{1,0:T(2,128)S(1)}, u32[]{:S(2)}, u32[]{:S(2)}) collective-permute-start(f32[2,2048]{1,0:T(2,128)S(1)} %pad_maximum_fusion.3), channel_id=1, source_target_pairs={{0,1},{1,0},{2,3},{3,2},{4,5},{5,4},{6,7},{7,6},{8,9},{9,8},{10,11... | collective-permute-start | bytes 49160 | tf_op jit(solution)/shard_map/ppermute | solution.py:191
  21.3 4.6 %collective-permute-start.1 = (f32[2,2048]{1,0:T(2,128)S(1)}, f32[2,2048]{1,0:T(2,128)S(1)}, u32[]{:S(2)}, u32[]{:S(2)}) collective-permute-start(f32[2,2048]{1,0:T(2,128)S(1)} %pad_maximum_fusion.4), channel_id=1, source_target_pairs={{0,2},{1,3},{2,0},{3,1},{4,6},{5,7},{6,4},{7,5},{8,10},{9,11},{10,... | collective-permute-start | bytes 49160 | tf_op jit(solution)/shard_map/ppermute | solution.py:191
  26.0 3.9 %collective-permute-start.2 = (f32[2,2048]{1,0:T(2,128)S(1)}, f32[2,2048]{1,0:T(2,128)S(1)}, u32[]{:S(2)}, u32[]{:S(2)}) collective-permute-start(f32[2,2048]{1,0:T(2,128)S(1)} %pad_maximum_fusion.5), channel_id=1, source_target_pairs={{0,4},{1,5},{2,6},{3,7},{4,0},{5,1},{6,2},{7,3},{8,12},{9,13},{10,... | collective-permute-start | bytes 49160 | tf_op jit(solution)/shard_map/ppermute | solution.py:191
  29.9 4.8 %collective-permute-start.3 = (f32[2,2048]{1,0:T(2,128)S(1)}, f32[2,2048]{1,0:T(2,128)S(1)}, u32[]{:S(2)}, u32[]{:S(2)}) collective-permute-start(f32[2,2048]{1,0:T(2,128)S(1)} %pad_maximum_fusion.6), channel_id=1, source_target_pairs={{0,8},{1,9},{2,10},{3,11},{4,12},{5,13},{6,14},{7,15},{8,0},{9,1},... | collective-permute-start | bytes 49160 | tf_op jit(solution)/shard_map/ppermute | solution.py:191
  47.5 2.0 %collective-permute-start.4 = (f32[1032,128]{1,0:T(8,128)S(1)}, f32[1032,128]{1,0:T(8,128)S(1)}, u32[]{:S(2)}, u32[]{:S(2)}) collective-permute-start(f32[1032,128]{1,0:T(8,128)S(1)} %slice.72), channel_id=1, source_target_pairs={{0,1},{1,0},{2,3},{3,2},{4,5},{5,4},{6,7},{7,6},{8,9},{9,8},{10,11... | collective-permute-start | bytes 1585160 | tf_op jit(solution)/shard_map/ppermute | solution.py:191
  51.3 8.6 %collective-permute-start.5 = (f32[520,128]{1,0:T(8,128)S(1)}, f32[520,128]{1,0:T(8,128)S(1)}, u32[]{:S(2)}, u32[]{:S(2)}) collective-permute-start(f32[520,128]{1,0:T(8,128)S(1)} %pad_maximum_fusion), channel_id=1, source_target_pairs={{0,2},{1,3},{2,0},{3,1},{4,6},{5,7},{6,4},{7,5},{8,10},{9,11},{10,... | collective-permute-start | bytes 798728 | tf_op jit(solution)/shard_map/ppermute | solution.py:191
  60.1 5.1 %collective-permute-start.6 = (f32[264,128]{1,0:T(8,128)S(1)}, f32[264,128]{1,0:T(8,128)S(1)}, u32[]{:S(2)}, u32[]{:S(2)}) collective-permute-start(f32[264,128]{1,0:T(8,128)S(1)} %pad_maximum_fusion.1), channel_id=1, source_target_pairs={{0,4},{1,5},{2,6},{3,7},{4,0},{5,1},{6,2},{7,3},{8,12},{9,13},{10,... | collective-permute-start | bytes 405512 | tf_op jit(solution)/shard_map/ppermute | solution.py:191
  65.2 5.3 %collective-permute-start.7 = (f32[136,128]{1,0:T(8,128)S(1)}, f32[136,128]{1,0:T(8,128)S(1)}, u32[]{:S(2)}, u32[]{:S(2)}) collective-permute-start(f32[136,128]{1,0:T(8,128)S(1)} %pad_maximum_fusion.2), channel_id=1, source_target_pairs={{0,8},{1,9},{2,10},{3,11},{4,12},{5,13},{6,14},{7,15},{8,0},{9,1},... | collective-permute-start | bytes 208904 | tf_op jit(solution)/shard_map/ppermute | solution.py:191

commit v16 on v14

--- a/solution.py
+++ b/solution.py
@@ -8,7 +8,7 @@
 from jax.experimental.pallas import tpu as pltpu
 from jax.sharding import PartitionSpec as P
 
-TILE = 512
+TILE = 1024
 
 
 def split3(x):

time: 72.2 us -> 71.2 us (0.986)
  Pallas kernels: 27.4 us -> 26.4 us
    pallas_call x1, Pallas kernels: 9.78 us -> 8.87 us  [local_backward(): pl.pallas_call(functools.partial(backward_kernel, n_bits), grid=(n_query...]
where the time goes in v16:
time: 71.2 us; the launch traced here: 70.8 us
  Pallas kernels  26.4 us (37%)
  waiting for transfers between devices  18 us (25%)
  starting transfers between devices  15.4 us (22%)
  other arithmetic  8.54 us (12%)
  local copies, waits for them, and re-layouts  1.5 us (2%)
  between operations  0.93 us (1%)
    ppermute x8, waiting for transfers between devices, exchange(): return lax.ppermute(x, 'ref', [(i, i ^ step) for i in range(n_dev)])  18 us
    pallas_call x1, Pallas kernels, local_forward(): pl.pallas_call(forward_kernel, grid=(n_query // tile,), in_specs=[pl.Bloc...  17.6 us
    ppermute x8, starting transfers between devices, exchange(): return lax.ppermute(x, 'ref', [(i, i ^ step) for i in range(n_dev)])  15.4 us
    pallas_call x1, Pallas kernels, local_backward(): pl.pallas_call(functools.partial(backward_kernel, n_bits), grid=(n_query...  8.87 us
    mul x1, other arithmetic, on_device(): query_grad = (own_pulled - own_queries * own_cot[:, None]) * inv  1.56 us
  transfers between devices with their start and end apart: 8, of which 8 were waited for; matrix products, arithmetic and copies ran while one was open for 3% of the time, Pallas kernels for 0%

profile of v16, /device:TPU:0, one launch (start us, length us, event | category | flops | bytes accessed | tf_op | source)
XLA Modules:
  0.0 70.8 jit_solution(7105748092780193898)
XLA Ops:
  0.7 17.6 %shard_map.76 = (bf16[2048,2048]{1,0:T(8,128)(2,1)}, f32[128,2048]{1,0:T(8,128)}, f32[1,2048]{1,0:T(1,128)}, f32[1,2048]{1,0:T(1,128)}) custom-call(f32[2048,128]{1,0:T(8,128)} %q_ref.3, f32[1,128]{1,0:T(1,128)} %bitcast.75, s32[1,2048]{1,0:T(1,128)} %bitcast.74, f32[2048,128]{1,0:T(8,128)} %r_ref.3), custom_call_target="tpu_custom_call" | custom-call | tf_op jit(solution)/shard_map/pallas_call | solution.py:102
  18.2 0.8 %pad_maximum_fusion.4 = f32[2,2048]{1,0:T(2,128)S(1)} fusion(f32[1,2048]{1,0:T(1,128)} %get-tuple-element.12, f32[1,2048]{1,0:T(1,128)} %get-tuple-element.11), kind=kLoop, calls=%fused_computation.15 | loop fusion | flops 4096 | bytes 32768 | tf_op jit(solution)/shard_map/stack | solution.py:191
  19.6 0.8 %collective-permute-done = f32[2,2048]{1,0:T(2,128)S(1)} collective-permute-done((f32[2,2048]{1,0:T(2,128)S(1)}, f32[2,2048]{1,0:T(2,128)S(1)}, u32[]{:S(2)}, u32[]{:S(2)}) %collective-permute-start) | collective-permute-done | bytes 16416 | tf_op jit(solution)/shard_map/ppermute | solution.py:185
  20.4 0.8 %multiply_add_fusion.2 = (f32[1,2048]{1,0:T(1,128)S(1)}, f32[1,2048]{1,0:T(1,128)S(1)}, f32[1,2048]{1,0:T(1,128)S(1)}, f32[1,2048]{1,0:T(1,128)S(1)}) fusion(f32[1,2048]{1,0:T(1,128)} %get-tuple-element.12, f32[1,2048]{1,0:T(1,128)} %get-tuple-element.11, f32[2,2048]{1,0:T(2,128)S(1)} %collective-permute-done), kind=kLoop, calls=%fused_computation.38 | loop fusion | flops 12288 | bytes 65536 | tf_op jit(solution)/shard_map/add | solution.py:194
  21.2 2.9 %collective-permute-start.1 = (f32[2,2048]{1,0:T(2,128)S(1)}, f32[2,2048]{1,0:T(2,128)S(1)}, u32[]{:S(2)}, u32[]{:S(2)}) collective-permute-start(f32[2,2048]{1,0:T(2,128)S(1)} %pad_maximum_fusion.5), channel_id=1, source_target_pairs={{0,2},{1,3},{2,0},{3,1},{4,6},{5,7},{6,4},{7,5},{8,10},{9,11},{10,... | collective-permute-start | bytes 49160 | tf_op jit(solution)/shard_map/ppermute | solution.py:185
  24.6 1.3 %collective-permute-done.1 = f32[2,2048]{1,0:T(2,128)S(1)} collective-permute-done((f32[2,2048]{1,0:T(2,128)S(1)}, f32[2,2048]{1,0:T(2,128)S(1)}, u32[]{:S(2)}, u32[]{:S(2)}) %collective-permute-start.1) | collective-permute-done | bytes 16416 | tf_op jit(solution)/shard_map/ppermute | solution.py:185
  25.9 2.1 %collective-permute-start.2 = (f32[2,2048]{1,0:T(2,128)S(1)}, f32[2,2048]{1,0:T(2,128)S(1)}, u32[]{:S(2)}, u32[]{:S(2)}) collective-permute-start(f32[2,2048]{1,0:T(2,128)S(1)} %pad_maximum_fusion.6), channel_id=1, source_target_pairs={{0,4},{1,5},{2,6},{3,7},{4,0},{5,1},{6,2},{7,3},{8,12},{9,13},{10,... | collective-permute-start | bytes 49160 | tf_op jit(solution)/shard_map/ppermute | solution.py:185
  28.0 1.1 %maximum_maximum_fusion.qa_ref = bf16[2048,256]{1,0:T(8,128)(2,1)} fusion(bf16[2048,128]{1,0:T(8,128)(2,1)S(1)} %get-tuple-element.22, bf16[256]{0:T(256)(128)(2,1)S(1)} %pad.10.clone, bf16[256]{0:T(256)(128)(2,1)S(1)} %pad.9.clone), kind=kLoop, calls=%fused_computation | loop fusion | flops 3145728 | bytes 1573888 | tf_op jit(solution)/shard_map/concatenate | solution.py:229
  29.2 0.6 collective-permute-done.2
  29.8 3.1 %collective-permute-start.3 = (f32[2,2048]{1,0:T(2,128)S(1)}, f32[2,2048]{1,0:T(2,128)S(1)}, u32[]{:S(2)}, u32[]{:S(2)}) collective-permute-start(f32[2,2048]{1,0:T(2,128)S(1)} %pad_maximum_fusion.7), channel_id=1, source_target_pairs={{0,8},{1,9},{2,10},{3,11},{4,12},{5,13},{6,14},{7,15},{8,0},{9,1},... | collective-permute-start | bytes 49160 | tf_op jit(solution)/shard_map/ppermute | solution.py:185
  33.5 1.2 %collective-permute-done.3 = f32[2,2048]{1,0:T(2,128)S(1)} collective-permute-done((f32[2,2048]{1,0:T(2,128)S(1)}, f32[2,2048]{1,0:T(2,128)S(1)}, u32[]{:S(2)}, u32[]{:S(2)}) %collective-permute-start.3) | collective-permute-done | bytes 16416 | tf_op jit(solution)/shard_map/ppermute | solution.py:185
  34.7 1.2 %fusion.19 = (f32[]{:T(128)}, f32[2048]{0:T(1024)}) fusion(f32[2048]{0:T(1024)S(1)} %copy-done.4, f32[2048]{0:T(1024)S(1)} %bitcast.66, f32[2048]{0:T(1024)S(1)} %bitcast.65, f32[2048]{0:T(1024)S(1)} %bitcast.72, f32[2048]{0:T(1024)S(1)} %bitcast.71, f32[2048]{0:T(1024)S(1)} %bitcast.70, f32[2048]{0:T(1024)S(1)} %bitcast.69, f32[2048]{0:T(1024)S(1)} %bitcast.67, ...), kind=kLoop, calls=%fused_computation.57 | loop fusion | flops 57343 | bytes 98308 | tf_op jit(solution)/shard_map/reduce_sum | solution.py:242
  35.9 8.9 %shard_map.77 = (f32[2048,128]{1,0:T(8,128)}, f32[2048,128]{1,0:T(8,128)}, f32[8,128]{1,0:T(8,128)}) custom-call(bf16[2048,2048]{1,0:T(8,128)(2,1)} %get-tuple-element.10.e_ref, f32[1,2048]{1,0:T(1,128)} %bitcast.73, bf16[2048,256]{1,0:T(8,128)(2,1)} %maximum_maximum_fusion.qa_ref, f32[128,2048]{1,0:T(8,128)} %get-tuple-element.13.ut_ref, ...), custom_call_target="tpu_custom_call" | custom-call | tf_op jit(solution)/shard_map/pallas_call | solution.py:147
  44.8 1.2 %constant_dynamic-slice_fusion.2 = f32[8,128,128]{2,1,0:T(8,128)S(1)} fusion(f32[16,128,128]{2,1,0:T(8,128)} %bitcast.58, s32[]{:T(128)S(6)} %select_n.60), kind=kLoop, calls=%fused_computation.45 | loop fusion | bytes 1048580 | tf_op jit(solution)/shard_map/dynamic_slice | solution.py:209
  46.0 0.8 %pad_maximum_fusion = f32[1032,128]{1,0:T(8,128)S(1)} fusion(f32[8,128]{1,0:T(8,128)} %get-tuple-element.15, f32[1024,128]{1,0:T(8,128)S(1)} %bitcast.56), kind=kLoop, calls=%fused_computation.2 | loop fusion | flops 132096 | bytes 1056768 | tf_op jit(solution)/shard_map/concatenate | solution.py:211
  46.9 1.9 %collective-permute-done.4 = f32[1032,128]{1,0:T(8,128)S(1)} collective-permute-done((f32[1032,128]{1,0:T(8,128)S(1)}, f32[1032,128]{1,0:T(8,128)S(1)}, u32[]{:S(2)}, u32[]{:S(2)}) %collective-permute-start.4) | collective-permute-done | bytes 528416 | tf_op jit(solution)/shard_map/ppermute | solution.py:185
  49.0 1.9 %collective-permute-start.5 = (f32[520,128]{1,0:T(8,128)S(1)}, f32[520,128]{1,0:T(8,128)S(1)}, u32[]{:S(2)}, u32[]{:S(2)}) collective-permute-start(f32[520,128]{1,0:T(8,128)S(1)} %pad_maximum_fusion.1), channel_id=1, source_target_pairs={{0,2},{1,3},{2,0},{3,1},{4,6},{5,7},{6,4},{7,5},{8,10},{9,11},{10,... | collective-permute-start | bytes 798728 | tf_op jit(solution)/shard_map/ppermute | solution.py:185
  50.9 6.7 %collective-permute-done.5 = f32[520,128]{1,0:T(8,128)S(1)} collective-permute-done((f32[520,128]{1,0:T(8,128)S(1)}, f32[520,128]{1,0:T(8,128)S(1)}, u32[]{:S(2)}, u32[]{:S(2)}) %collective-permute-start.5) | collective-permute-done | bytes 266272 | tf_op jit(solution)/shard_map/ppermute | solution.py:185
  57.7 1.9 %collective-permute-start.6 = (f32[264,128]{1,0:T(8,128)S(1)}, f32[264,128]{1,0:T(8,128)S(1)}, u32[]{:S(2)}, u32[]{:S(2)}) collective-permute-start(f32[264,128]{1,0:T(8,128)S(1)} %pad_maximum_fusion.2), channel_id=1, source_target_pairs={{0,4},{1,5},{2,6},{3,7},{4,0},{5,1},{6,2},{7,3},{8,12},{9,13},{10,... | collective-permute-start | bytes 405512 | tf_op jit(solution)/shard_map/ppermute | solution.py:185
  59.6 3.2 %collective-permute-done.6 = f32[264,128]{1,0:T(8,128)S(1)} collective-permute-done((f32[264,128]{1,0:T(8,128)S(1)}, f32[264,128]{1,0:T(8,128)S(1)}, u32[]{:S(2)}, u32[]{:S(2)}) %collective-permute-start.6) | collective-permute-done | bytes 135200 | tf_op jit(solution)/shard_map/ppermute | solution.py:185
  62.9 2.9 %collective-permute-start.7 = (f32[136,128]{1,0:T(8,128)S(1)}, f32[136,128]{1,0:T(8,128)S(1)}, u32[]{:S(2)}, u32[]{:S(2)}) collective-permute-start(f32[136,128]{1,0:T(8,128)S(1)} %pad_maximum_fusion.3), channel_id=1, source_target_pairs={{0,8},{1,9},{2,10},{3,11},{4,12},{5,13},{6,14},{7,15},{8,0},{9,1},... | collective-permute-start | bytes 208904 | tf_op jit(solution)/shard_map/ppermute | solution.py:185
  65.8 2.3 %collective-permute-done.7 = f32[136,128]{1,0:T(8,128)S(1)} collective-permute-done((f32[136,128]{1,0:T(8,128)S(1)}, f32[136,128]{1,0:T(8,128)S(1)}, u32[]{:S(2)}, u32[]{:S(2)}) %collective-permute-start.7) | collective-permute-done | bytes 69664 | tf_op jit(solution)/shard_map/ppermute | solution.py:185
  68.1 1.1 %divide_subtract_fusion = f32[128]{0:T(128)} fusion(f32[128]{0:T(128)S(1)} %copy-done.6, f32[128]{0:T(128)S(1)} %get-tuple-element.21, f32[8,128]{1,0:T(8,128)S(1)} %slice_add_fusion, f32[]{:T(128)} %get-tuple-element.33), kind=kLoop, calls=%fused_computation.46 | loop fusion | flops 1152 | bytes 2564 | tf_op jit(solution)/shard_map/sub | solution.py:243
  69.2 1.6 %fusion.3 = f32[128,128]{1,0:T(8,128)} fusion(f32[136,128]{1,0:T(8,128)S(1)} %collective-permute-done.7, f32[2048,128]{1,0:T(8,128)} %q_ref.3, s32[]{:T(128)S(6)} %select_n.73, f32[2,128,128]{2,1,0:T(8,128)S(1)} %dynamic-slice_add_fusion.2, s32[]{:T(128)S(6)} %select_n.71, f32[128]{0:T(128)S(1)} %multiply_divide_fusion, f32[128]{0:T(128)S(1)} %dynamic_slice.39), kind=kLoop, calls=%fused_computation.13 | loop fusion | flops 65536 | bytes 263176 | tf_op jit(solution)/shard_map/mul | solution.py:239
  (45 shorter events, 2.2 us)
Async XLA Ops:
  0.6 23.5 %copy-start = (f32[2048,128]{1,0:T(8,128)S(1)}, f32[2048,128]{1,0:T(8,128)}, u32[]{:S(2)}) copy-start(f32[2048,128]{1,0:T(8,128)} %q_ref.3) | copy-start | bytes 3145732
  0.6 23.5 %copy-start.4 = (f32[2048]{0:T(1024)S(1)}, f32[2048]{0:T(1024)}, u32[]{:S(2)}) copy-start(f32[2048]{0:T(1024)} %param.9) | copy-start | bytes 24580
  18.2 14.7 %copy-start.6 = (f32[128]{0:T(128)S(1)}, f32[128]{0:T(128)}, u32[]{:S(2)}) copy-start(f32[128]{0:T(128)} %param.8) | copy-start | bytes 1540
  18.2 16.5 %copy-start.2 = (f32[1,2048]{1,0:T(1,128)S(1)}, f32[1,2048]{1,0:T(1,128)}, u32[]{:S(2)}) copy-start(f32[1,2048]{1,0:T(1,128)} %get-tuple-element.11) | copy-start | bytes 24580
  18.2 16.5 %copy-start.3 = (f32[1,2048]{1,0:T(1,128)S(1)}, f32[1,2048]{1,0:T(1,128)}, u32[]{:S(2)}) copy-start(f32[1,2048]{1,0:T(1,128)} %get-tuple-element.12) | copy-start | bytes 24580
  19.0 1.4 %collective-permute-start = (f32[2,2048]{1,0:T(2,128)S(1)}, f32[2,2048]{1,0:T(2,128)S(1)}, u32[]{:S(2)}, u32[]{:S(2)}) collective-permute-start(f32[2,2048]{1,0:T(2,128)S(1)} %pad_maximum_fusion.4), channel_id=1, source_target_pairs={{0,1},{1,0},{2,3},{3,2},{4,5},{5,4},{6,7},{7,6},{8,9},{9,8},{10,11... | collective-permute-start | bytes 49160 | tf_op jit(solution)/shard_map/ppermute | solution.py:185
  21.2 4.6 %collective-permute-start.1 = (f32[2,2048]{1,0:T(2,128)S(1)}, f32[2,2048]{1,0:T(2,128)S(1)}, u32[]{:S(2)}, u32[]{:S(2)}) collective-permute-start(f32[2,2048]{1,0:T(2,128)S(1)} %pad_maximum_fusion.5), channel_id=1, source_target_pairs={{0,2},{1,3},{2,0},{3,1},{4,6},{5,7},{6,4},{7,5},{8,10},{9,11},{10,... | collective-permute-start | bytes 49160 | tf_op jit(solution)/shard_map/ppermute | solution.py:185
  25.9 3.9 %collective-permute-start.2 = (f32[2,2048]{1,0:T(2,128)S(1)}, f32[2,2048]{1,0:T(2,128)S(1)}, u32[]{:S(2)}, u32[]{:S(2)}) collective-permute-start(f32[2,2048]{1,0:T(2,128)S(1)} %pad_maximum_fusion.6), channel_id=1, source_target_pairs={{0,4},{1,5},{2,6},{3,7},{4,0},{5,1},{6,2},{7,3},{8,12},{9,13},{10,... | collective-permute-start | bytes 49160 | tf_op jit(solution)/shard_map/ppermute | solution.py:185
  29.8 4.8 %collective-permute-start.3 = (f32[2,2048]{1,0:T(2,128)S(1)}, f32[2,2048]{1,0:T(2,128)S(1)}, u32[]{:S(2)}, u32[]{:S(2)}) collective-permute-start(f32[2,2048]{1,0:T(2,128)S(1)} %pad_maximum_fusion.7), channel_id=1, source_target_pairs={{0,8},{1,9},{2,10},{3,11},{4,12},{5,13},{6,14},{7,15},{8,0},{9,1},... | collective-permute-start | bytes 49160 | tf_op jit(solution)/shard_map/ppermute | solution.py:185
  44.8 4.0 %copy-start.1 = (f32[2048,128]{1,0:T(8,128)S(1)}, f32[2048,128]{1,0:T(8,128)}, u32[]{:S(2)}) copy-start(f32[2048,128]{1,0:T(8,128)} %get-tuple-element.14) | copy-start | bytes 3145732
  46.0 2.9 %copy-start.5 = (f32[8,128]{1,0:T(8,128)S(1)}, f32[8,128]{1,0:T(8,128)}, u32[]{:S(2)}) copy-start(f32[8,128]{1,0:T(8,128)} %get-tuple-element.15) | copy-start | bytes 12292
  46.8 2.0 %collective-permute-start.4 = (f32[1032,128]{1,0:T(8,128)S(1)}, f32[1032,128]{1,0:T(8,128)S(1)}, u32[]{:S(2)}, u32[]{:S(2)}) collective-permute-start(f32[1032,128]{1,0:T(8,128)S(1)} %pad_maximum_fusion), channel_id=1, source_target_pairs={{0,1},{1,0},{2,3},{3,2},{4,5},{5,4},{6,7},{7,6},{8,9},{9,8},{10,11... | collective-permute-start | bytes 1585160 | tf_op jit(solution)/shard_map/ppermute | solution.py:185
  49.0 8.6 %collective-permute-start.5 = (f32[520,128]{1,0:T(8,128)S(1)}, f32[520,128]{1,0:T(8,128)S(1)}, u32[]{:S(2)}, u32[]{:S(2)}) collective-permute-start(f32[520,128]{1,0:T(8,128)S(1)} %pad_maximum_fusion.1), channel_id=1, source_target_pairs={{0,2},{1,3},{2,0},{3,1},{4,6},{5,7},{6,4},{7,5},{8,10},{9,11},{10,... | collective-permute-start | bytes 798728 | tf_op jit(solution)/shard_map/ppermute | solution.py:185
  57.7 5.1 %collective-permute-start.6 = (f32[264,128]{1,0:T(8,128)S(1)}, f32[264,128]{1,0:T(8,128)S(1)}, u32[]{:S(2)}, u32[]{:S(2)}) collective-permute-start(f32[264,128]{1,0:T(8,128)S(1)} %pad_maximum_fusion.2), channel_id=1, source_target_pairs={{0,4},{1,5},{2,6},{3,7},{4,0},{5,1},{6,2},{7,3},{8,12},{9,13},{10,... | collective-permute-start | bytes 405512 | tf_op jit(solution)/shard_map/ppermute | solution.py:185
  62.9 5.3 %collective-permute-start.7 = (f32[136,128]{1,0:T(8,128)S(1)}, f32[136,128]{1,0:T(8,128)S(1)}, u32[]{:S(2)}, u32[]{:S(2)}) collective-permute-start(f32[136,128]{1,0:T(8,128)S(1)} %pad_maximum_fusion.3), channel_id=1, source_target_pairs={{0,8},{1,9},{2,10},{3,11},{4,12},{5,13},{6,14},{7,15},{8,0},{9,1},... | collective-permute-start | bytes 208904 | tf_op jit(solution)/shard_map/ppermute | solution.py:185

commit v17 on v16

--- a/solution.py
+++ b/solution.py
@@ -19,7 +19,7 @@
     return x1, x2, x3
 
 
-def forward_kernel(q_ref, sp_ref, id_ref, r_ref, e_ref, ut_ref, p_ref, t_ref, rn_sc, rlt_sc, rs_sc):
+def forward_kernel(q_ref, sp_ref, id_ref, r_ref, e_ref, ut_ref, st_ref, rn_sc, rlt_sc, rs_sc):
     spread = sp_ref[...]
     inv = 1.0 / (spread * spread)
 
@@ -48,8 +48,8 @@
     shifted = jnp.where(row == local_ids, -jnp.inf, shifted)
     top = jnp.max(shifted, axis=0, keepdims=True)
     expd = jnp.exp(shifted - top)
-    p_ref[...] = top - 0.5 * qnorm
-    t_ref[...] = jnp.sum(expd, axis=0, keepdims=True)
+    st_ref[0:1, :] = top - 0.5 * qnorm
+    st_ref[1:2, :] = jnp.sum(expd, axis=0, keepdims=True)
     expd_low = expd.astype(jnp.bfloat16)
     e_ref[...] = expd_low
     ut_ref[...] = jnp.dot(rlt_sc[...], expd_low, preferred_element_type=jnp.float32)
@@ -111,14 +111,12 @@
         out_specs=[
             pl.BlockSpec((n_ref, tile), lambda i: (0, i)),
             pl.BlockSpec((n_feat, tile), lambda i: (0, i)),
-            pl.BlockSpec((1, tile), lambda i: (0, i)),
-            pl.BlockSpec((1, tile), lambda i: (0, i)),
+            pl.BlockSpec((2, tile), lambda i: (0, i)),
         ],
         out_shape=[
             jax.ShapeDtypeStruct((n_ref, n_query), jnp.bfloat16),
             jax.ShapeDtypeStruct((n_feat, n_query), jnp.float32),
-            jax.ShapeDtypeStruct((1, n_query), jnp.float32),
-            jax.ShapeDtypeStruct((1, n_query), jnp.float32),
+            jax.ShapeDtypeStruct((2, n_query), jnp.float32),
         ],
         scratch_shapes=[
             pltpu.VMEM((n_ref, 1), jnp.float32),
@@ -185,14 +183,16 @@
     return lax.ppermute(x, "ref", [(i, i ^ step) for i in range(n_dev)])
 
 
-def butterfly_stats(peak, total, n_dev):
+def butterfly_stats(stats, n_dev):
+    peak, total = stats[0], stats[1]
     step = 1
     while step < n_dev:
-        other = exchange(jnp.stack([peak, total]), n_dev, step)
+        other = exchange(stats, n_dev, step)
         other_peak, other_total = other[0], other[1]
         new_peak = jnp.maximum(peak, other_peak)
         total = total * jnp.exp(peak - new_peak) + other_total * jnp.exp(other_peak - new_peak)
         peak = new_peak
+        stats = jnp.stack([peak, total])
         step *= 2
     return peak, total
 
@@ -222,9 +222,9 @@
     n_dev = lax.axis_size("ref")
     own_rows = n_query // n_dev
     inv = 1.0 / (spread * spread)
-    expd_low, unscaled_t, local_peak, local_total = local_forward(queries, spread[None, :], query_ids[None, :], references)
-    peak, total = butterfly_stats(local_peak[0], local_total[0], n_dev)
-    scale = cotangent * jnp.exp(local_peak[0] - peak) / total
+    expd_low, unscaled_t, local_stats = local_forward(queries, spread[None, :], query_ids[None, :], references)
+    peak, total = butterfly_stats(local_stats, n_dev)
+    scale = cotangent * jnp.exp(local_stats[0] - peak) / total
     query_low = queries.astype(jnp.bfloat16)
     query_aug = jnp.concatenate(
         [query_low, jnp.ones((n_query, 1), jnp.bfloat16), jnp.zeros((n_query, n_feat - 1), jnp.bfloat16)], axis=1

time: 71.2 us -> 70.7 us (level)
    another operation x4 -> x3, other arithmetic: 0.84 us -> 0.06 us  [butterfly_stats(): stats = jnp.stack([peak, total])]
where the time goes in v17:
time: 70.7 us; the launch traced here: 70.4 us
  Pallas kernels  26.5 us (37%)
  waiting for transfers between devices  18.2 us (26%)
  starting transfers between devices  15.4 us (22%)
  other arithmetic  7.92 us (11%)
  local copies, waits for them, and re-layouts  1.48 us (2%)
  between operations  0.89 us (1%)
    ppermute x8, waiting for transfers between devices, exchange(): return lax.ppermute(x, 'ref', [(i, i ^ step) for i in range(n_dev)])  18.2 us
    pallas_call x1, Pallas kernels, local_forward(): pl.pallas_call(forward_kernel, grid=(n_query // tile,), in_specs=[pl.Bloc...  17.6 us
    ppermute x8, starting transfers between devices, exchange(): return lax.ppermute(x, 'ref', [(i, i ^ step) for i in range(n_dev)])  15.4 us
    pallas_call x1, Pallas kernels, local_backward(): pl.pallas_call(functools.partial(backward_kernel, n_bits), grid=(n_query...  8.89 us
    mul x1, other arithmetic, on_device(): query_grad = (own_pulled - own_queries * own_cot[:, None]) * inv  1.56 us
  transfers between devices with their start and end apart: 8, of which 8 were waited for; matrix products, arithmetic and copies ran while one was open for 3% of the time, Pallas kernels for 0%

profile of v17, /device:TPU:0, one launch (start us, length us, event | category | flops | bytes accessed | tf_op | source)
XLA Modules:
  0.0 70.4 jit_solution(6616261721091157516)
XLA Ops:
  0.7 17.6 %shard_map.76 = (bf16[2048,2048]{1,0:T(8,128)(2,1)}, f32[128,2048]{1,0:T(8,128)}, f32[2,2048]{1,0:T(2,128)}) custom-call(f32[2048,128]{1,0:T(8,128)} %q_ref.3, f32[1,128]{1,0:T(1,128)} %bitcast.75, s32[1,2048]{1,0:T(1,128)} %bitcast.74, f32[2048,128]{1,0:T(8,128)} %r_ref.3), custom_call_target="tpu_custom_call" | custom-call | tf_op jit(solution)/shard_map/pallas_call | solution.py:102
  18.3 0.6 collective-permute-start
  18.9 1.0 %collective-permute-done = f32[2,2048]{1,0:T(2,128)S(1)} collective-permute-done((f32[2,2048]{1,0:T(2,128)}, f32[2,2048]{1,0:T(2,128)S(1)}, u32[]{:S(2)}, u32[]{:S(2)}) %collective-permute-start) | collective-permute-done | bytes 16416 | tf_op jit(solution)/shard_map/ppermute | solution.py:183
  19.9 0.8 %multiply_add_fusion.2 = (f32[1,2048]{1,0:T(1,128)S(1)}, f32[1,2048]{1,0:T(1,128)S(1)}, f32[1,2048]{1,0:T(1,128)S(1)}, f32[1,2048]{1,0:T(1,128)S(1)}, f32[1,2048]{1,0:T(1,128)S(1)}, /*index=5*/f32[1,2048]{1,0:T(1,128)S(1)}) fusion(f32[2,2048]{1,0:T(2,128)S(1)} %collective-permute-done, f32[2,2048]{1,0:T(2,128)} %get-tuple-element.10), kind=kLoop, calls=%fused_computation.37 | loop fusion | flops 12288 | bytes 81920 | tf_op jit(solution)/shard_map/add | solution.py:193
  20.8 2.9 %collective-permute-start.1 = (f32[2,2048]{1,0:T(2,128)S(1)}, f32[2,2048]{1,0:T(2,128)S(1)}, u32[]{:S(2)}, u32[]{:S(2)}) collective-permute-start(f32[2,2048]{1,0:T(2,128)S(1)} %pad_maximum_fusion.4), channel_id=1, source_target_pairs={{0,2},{1,3},{2,0},{3,1},{4,6},{5,7},{6,4},{7,5},{8,10},{9,11},{10,... | collective-permute-start | bytes 49160 | tf_op jit(solution)/shard_map/ppermute | solution.py:183
  24.1 1.3 %collective-permute-done.1 = f32[2,2048]{1,0:T(2,128)S(1)} collective-permute-done((f32[2,2048]{1,0:T(2,128)S(1)}, f32[2,2048]{1,0:T(2,128)S(1)}, u32[]{:S(2)}, u32[]{:S(2)}) %collective-permute-start.1) | collective-permute-done | bytes 16416 | tf_op jit(solution)/shard_map/ppermute | solution.py:183
  25.5 2.1 %collective-permute-start.2 = (f32[2,2048]{1,0:T(2,128)S(1)}, f32[2,2048]{1,0:T(2,128)S(1)}, u32[]{:S(2)}, u32[]{:S(2)}) collective-permute-start(f32[2,2048]{1,0:T(2,128)S(1)} %pad_maximum_fusion.5), channel_id=1, source_target_pairs={{0,4},{1,5},{2,6},{3,7},{4,0},{5,1},{6,2},{7,3},{8,12},{9,13},{10,... | collective-permute-start | bytes 49160 | tf_op jit(solution)/shard_map/ppermute | solution.py:183
  27.6 1.1 %maximum_maximum_fusion.qa_ref = bf16[2048,256]{1,0:T(8,128)(2,1)} fusion(bf16[2048,128]{1,0:T(8,128)(2,1)S(1)} %get-tuple-element.20, bf16[256]{0:T(256)(128)(2,1)S(1)} %pad.10.clone, bf16[256]{0:T(256)(128)(2,1)S(1)} %pad.9.clone), kind=kLoop, calls=%fused_computation | loop fusion | flops 3145728 | bytes 1573888 | tf_op jit(solution)/shard_map/concatenate | solution.py:229
  28.7 0.6 collective-permute-done.2
  29.4 3.1 %collective-permute-start.3 = (f32[2,2048]{1,0:T(2,128)S(1)}, f32[2,2048]{1,0:T(2,128)S(1)}, u32[]{:S(2)}, u32[]{:S(2)}) collective-permute-start(f32[2,2048]{1,0:T(2,128)S(1)} %pad_maximum_fusion.6), channel_id=1, source_target_pairs={{0,8},{1,9},{2,10},{3,11},{4,12},{5,13},{6,14},{7,15},{8,0},{9,1},... | collective-permute-start | bytes 49160 | tf_op jit(solution)/shard_map/ppermute | solution.py:183
  33.0 1.2 %collective-permute-done.3 = f32[2,2048]{1,0:T(2,128)S(1)} collective-permute-done((f32[2,2048]{1,0:T(2,128)S(1)}, f32[2,2048]{1,0:T(2,128)S(1)}, u32[]{:S(2)}, u32[]{:S(2)}) %collective-permute-start.3) | collective-permute-done | bytes 16416 | tf_op jit(solution)/shard_map/ppermute | solution.py:183
  34.2 1.3 %fusion.19 = (f32[]{:T(128)}, f32[2048]{0:T(1024)}) fusion(f32[2048]{0:T(1024)S(1)} %copy-done.2, f32[2048]{0:T(1024)S(1)} %bitcast.68, f32[2048]{0:T(1024)S(1)} %bitcast.67, f32[2048]{0:T(1024)S(1)} %bitcast.72, f32[2048]{0:T(1024)S(1)} %bitcast.71, f32[2048]{0:T(1024)S(1)} %bitcast.70, f32[2048]{0:T(1024)S(1)} %bitcast.69, f32[2048]{0:T(1024)S(1)} %bitcast.63, ...), kind=kLoop, calls=%fused_computation.56 | loop fusion | flops 57343 | bytes 98308 | tf_op jit(solution)/shard_map/reduce_sum | solution.py:242
  35.5 8.9 %shard_map.77 = (f32[2048,128]{1,0:T(8,128)}, f32[2048,128]{1,0:T(8,128)}, f32[8,128]{1,0:T(8,128)}) custom-call(bf16[2048,2048]{1,0:T(8,128)(2,1)} %get-tuple-element.9.e_ref, f32[1,2048]{1,0:T(1,128)} %bitcast.73, bf16[2048,256]{1,0:T(8,128)(2,1)} %maximum_maximum_fusion.qa_ref, f32[128,2048]{1,0:T(8,128)} %get-tuple-element.11.ut_ref, f32[2048,128]{1,0:T(8,128)} %q_ref.3, ...), custom_call_target="tpu_custom_call" | custom-call | tf_op jit(solution)/shard_map/pallas_call | solution.py:145
  44.4 1.2 %constant_dynamic-slice_fusion.2 = f32[8,128,128]{2,1,0:T(8,128)S(1)} fusion(f32[16,128,128]{2,1,0:T(8,128)} %bitcast.58, s32[]{:T(128)S(6)} %select_n.60), kind=kLoop, calls=%fused_computation.44 | loop fusion | bytes 1048580 | tf_op jit(solution)/shard_map/dynamic_slice | solution.py:209
  45.6 0.8 %pad_maximum_fusion = f32[1032,128]{1,0:T(8,128)S(1)} fusion(f32[8,128]{1,0:T(8,128)} %get-tuple-element.13, f32[1024,128]{1,0:T(8,128)S(1)} %bitcast.56), kind=kLoop, calls=%fused_computation.2 | loop fusion | flops 132096 | bytes 1056768 | tf_op jit(solution)/shard_map/concatenate | solution.py:211
  46.5 1.9 %collective-permute-done.4 = f32[1032,128]{1,0:T(8,128)S(1)} collective-permute-done((f32[1032,128]{1,0:T(8,128)S(1)}, f32[1032,128]{1,0:T(8,128)S(1)}, u32[]{:S(2)}, u32[]{:S(2)}) %collective-permute-start.4) | collective-permute-done | bytes 528416 | tf_op jit(solution)/shard_map/ppermute | solution.py:183
  48.6 1.9 %collective-permute-start.5 = (f32[520,128]{1,0:T(8,128)S(1)}, f32[520,128]{1,0:T(8,128)S(1)}, u32[]{:S(2)}, u32[]{:S(2)}) collective-permute-start(f32[520,128]{1,0:T(8,128)S(1)} %pad_maximum_fusion.1), channel_id=1, source_target_pairs={{0,2},{1,3},{2,0},{3,1},{4,6},{5,7},{6,4},{7,5},{8,10},{9,11},{10,... | collective-permute-start | bytes 798728 | tf_op jit(solution)/shard_map/ppermute | solution.py:183
  50.5 6.7 %collective-permute-done.5 = f32[520,128]{1,0:T(8,128)S(1)} collective-permute-done((f32[520,128]{1,0:T(8,128)S(1)}, f32[520,128]{1,0:T(8,128)S(1)}, u32[]{:S(2)}, u32[]{:S(2)}) %collective-permute-start.5) | collective-permute-done | bytes 266272 | tf_op jit(solution)/shard_map/ppermute | solution.py:183
  57.3 1.9 %collective-permute-start.6 = (f32[264,128]{1,0:T(8,128)S(1)}, f32[264,128]{1,0:T(8,128)S(1)}, u32[]{:S(2)}, u32[]{:S(2)}) collective-permute-start(f32[264,128]{1,0:T(8,128)S(1)} %pad_maximum_fusion.2), channel_id=1, source_target_pairs={{0,4},{1,5},{2,6},{3,7},{4,0},{5,1},{6,2},{7,3},{8,12},{9,13},{10,... | collective-permute-start | bytes 405512 | tf_op jit(solution)/shard_map/ppermute | solution.py:183
  59.1 3.2 %collective-permute-done.6 = f32[264,128]{1,0:T(8,128)S(1)} collective-permute-done((f32[264,128]{1,0:T(8,128)S(1)}, f32[264,128]{1,0:T(8,128)S(1)}, u32[]{:S(2)}, u32[]{:S(2)}) %collective-permute-start.6) | collective-permute-done | bytes 135200 | tf_op jit(solution)/shard_map/ppermute | solution.py:183
  62.5 2.9 %collective-permute-start.7 = (f32[136,128]{1,0:T(8,128)S(1)}, f32[136,128]{1,0:T(8,128)S(1)}, u32[]{:S(2)}, u32[]{:S(2)}) collective-permute-start(f32[136,128]{1,0:T(8,128)S(1)} %pad_maximum_fusion.3), channel_id=1, source_target_pairs={{0,8},{1,9},{2,10},{3,11},{4,12},{5,13},{6,14},{7,15},{8,0},{9,1},... | collective-permute-start | bytes 208904 | tf_op jit(solution)/shard_map/ppermute | solution.py:183
  65.4 2.3 %collective-permute-done.7 = f32[136,128]{1,0:T(8,128)S(1)} collective-permute-done((f32[136,128]{1,0:T(8,128)S(1)}, f32[136,128]{1,0:T(8,128)S(1)}, u32[]{:S(2)}, u32[]{:S(2)}) %collective-permute-start.7) | collective-permute-done | bytes 69664 | tf_op jit(solution)/shard_map/ppermute | solution.py:183
  67.7 1.2 %divide_subtract_fusion = f32[128]{0:T(128)} fusion(f32[128]{0:T(128)S(1)} %copy-done.4, f32[128]{0:T(128)S(1)} %get-tuple-element.19, f32[8,128]{1,0:T(8,128)S(1)} %slice_add_fusion, f32[]{:T(128)} %get-tuple-element.33), kind=kLoop, calls=%fused_computation.45 | loop fusion | flops 1152 | bytes 2564 | tf_op jit(solution)/shard_map/sub | solution.py:243
  68.9 1.6 %fusion.3 = f32[128,128]{1,0:T(8,128)} fusion(f32[136,128]{1,0:T(8,128)S(1)} %collective-permute-done.7, f32[2048,128]{1,0:T(8,128)} %q_ref.3, s32[]{:T(128)S(6)} %select_n.73, f32[2,128,128]{2,1,0:T(8,128)S(1)} %dynamic-slice_add_fusion.2, s32[]{:T(128)S(6)} %select_n.71, f32[128]{0:T(128)S(1)} %multiply_divide_fusion, f32[128]{0:T(128)S(1)} %dynamic_slice.39), kind=kLoop, calls=%fused_computation.13 | loop fusion | flops 65536 | bytes 263176 | tf_op jit(solution)/shard_map/mul | solution.py:239
  (40 shorter events, 1.6 us)
Async XLA Ops:
  0.6 23.1 %copy-start = (f32[2048,128]{1,0:T(8,128)S(1)}, f32[2048,128]{1,0:T(8,128)}, u32[]{:S(2)}) copy-start(f32[2048,128]{1,0:T(8,128)} %q_ref.3) | copy-start | bytes 3145732
  0.6 23.0 %copy-start.2 = (f32[2048]{0:T(1024)S(1)}, f32[2048]{0:T(1024)}, u32[]{:S(2)}) copy-start(f32[2048]{0:T(1024)} %param.9) | copy-start | bytes 24580
  18.3 14.2 %copy-start.4 = (f32[128]{0:T(128)S(1)}, f32[128]{0:T(128)}, u32[]{:S(2)}) copy-start(f32[128]{0:T(128)} %param.8) | copy-start | bytes 1540
  18.3 1.6 %collective-permute-start = (f32[2,2048]{1,0:T(2,128)}, f32[2,2048]{1,0:T(2,128)S(1)}, u32[]{:S(2)}, u32[]{:S(2)}) collective-permute-start(f32[2,2048]{1,0:T(2,128)} %get-tuple-element.10), channel_id=1, source_target_pairs={{0,1},{1,0},{2,3},{3,2},{4,5},{5,4},{6,7},{7,6},{8,9},{9,8},{10,11... | collective-permute-start | bytes 49160 | tf_op jit(solution)/shard_map/ppermute | solution.py:183
  20.8 4.6 %collective-permute-start.1 = (f32[2,2048]{1,0:T(2,128)S(1)}, f32[2,2048]{1,0:T(2,128)S(1)}, u32[]{:S(2)}, u32[]{:S(2)}) collective-permute-start(f32[2,2048]{1,0:T(2,128)S(1)} %pad_maximum_fusion.4), channel_id=1, source_target_pairs={{0,2},{1,3},{2,0},{3,1},{4,6},{5,7},{6,4},{7,5},{8,10},{9,11},{10,... | collective-permute-start | bytes 49160 | tf_op jit(solution)/shard_map/ppermute | solution.py:183
  25.5 3.9 %collective-permute-start.2 = (f32[2,2048]{1,0:T(2,128)S(1)}, f32[2,2048]{1,0:T(2,128)S(1)}, u32[]{:S(2)}, u32[]{:S(2)}) collective-permute-start(f32[2,2048]{1,0:T(2,128)S(1)} %pad_maximum_fusion.5), channel_id=1, source_target_pairs={{0,4},{1,5},{2,6},{3,7},{4,0},{5,1},{6,2},{7,3},{8,12},{9,13},{10,... | collective-permute-start | bytes 49160 | tf_op jit(solution)/shard_map/ppermute | solution.py:183
  29.4 4.8 %collective-permute-start.3 = (f32[2,2048]{1,0:T(2,128)S(1)}, f32[2,2048]{1,0:T(2,128)S(1)}, u32[]{:S(2)}, u32[]{:S(2)}) collective-permute-start(f32[2,2048]{1,0:T(2,128)S(1)} %pad_maximum_fusion.6), channel_id=1, source_target_pairs={{0,8},{1,9},{2,10},{3,11},{4,12},{5,13},{6,14},{7,15},{8,0},{9,1},... | collective-permute-start | bytes 49160 | tf_op jit(solution)/shard_map/ppermute | solution.py:183
  44.4 4.0 %copy-start.1 = (f32[2048,128]{1,0:T(8,128)S(1)}, f32[2048,128]{1,0:T(8,128)}, u32[]{:S(2)}) copy-start(f32[2048,128]{1,0:T(8,128)} %get-tuple-element.12) | copy-start | bytes 3145732
  45.6 2.9 %copy-start.3 = (f32[8,128]{1,0:T(8,128)S(1)}, f32[8,128]{1,0:T(8,128)}, u32[]{:S(2)}) copy-start(f32[8,128]{1,0:T(8,128)} %get-tuple-element.13) | copy-start | bytes 12292
  46.4 2.0 %collective-permute-start.4 = (f32[1032,128]{1,0:T(8,128)S(1)}, f32[1032,128]{1,0:T(8,128)S(1)}, u32[]{:S(2)}, u32[]{:S(2)}) collective-permute-start(f32[1032,128]{1,0:T(8,128)S(1)} %pad_maximum_fusion), channel_id=1, source_target_pairs={{0,1},{1,0},{2,3},{3,2},{4,5},{5,4},{6,7},{7,6},{8,9},{9,8},{10,11... | collective-permute-start | bytes 1585160 | tf_op jit(solution)/shard_map/ppermute | solution.py:183
  48.6 8.6 %collective-permute-start.5 = (f32[520,128]{1,0:T(8,128)S(1)}, f32[520,128]{1,0:T(8,128)S(1)}, u32[]{:S(2)}, u32[]{:S(2)}) collective-permute-start(f32[520,128]{1,0:T(8,128)S(1)} %pad_maximum_fusion.1), channel_id=1, source_target_pairs={{0,2},{1,3},{2,0},{3,1},{4,6},{5,7},{6,4},{7,5},{8,10},{9,11},{10,... | collective-permute-start | bytes 798728 | tf_op jit(solution)/shard_map/ppermute | solution.py:183
  57.3 5.1 %collective-permute-start.6 = (f32[264,128]{1,0:T(8,128)S(1)}, f32[264,128]{1,0:T(8,128)S(1)}, u32[]{:S(2)}, u32[]{:S(2)}) collective-permute-start(f32[264,128]{1,0:T(8,128)S(1)} %pad_maximum_fusion.2), channel_id=1, source_target_pairs={{0,4},{1,5},{2,6},{3,7},{4,0},{5,1},{6,2},{7,3},{8,12},{9,13},{10,... | collective-permute-start | bytes 405512 | tf_op jit(solution)/shard_map/ppermute | solution.py:183
  62.5 5.3 %collective-permute-start.7 = (f32[136,128]{1,0:T(8,128)S(1)}, f32[136,128]{1,0:T(8,128)S(1)}, u32[]{:S(2)}, u32[]{:S(2)}) collective-permute-start(f32[136,128]{1,0:T(8,128)S(1)} %pad_maximum_fusion.3), channel_id=1, source_target_pairs={{0,8},{1,9},{2,10},{3,11},{4,12},{5,13},{6,14},{7,15},{8,0},{9,1},... | collective-permute-start | bytes 208904 | tf_op jit(solution)/shard_map/ppermute | solution.py:183

commit v18 on v17

--- a/solution.py
+++ b/solution.py
@@ -55,20 +55,23 @@
     ut_ref[...] = jnp.dot(rlt_sc[...], expd_low, preferred_element_type=jnp.float32)
 
 
-def backward_kernel(n_bits, e_ref, sc_ref, qa_ref, ut_ref, q_ref, r_ref, inv_ref, rg_ref, pull_hbm, terms_ref,
-                    acc_sc, qt_sc, pull_sc, sems):
+def backward_kernel(n_bits, e_ref, cot_ref, ls_ref, gs_ref, qa_ref, ut_ref, q_ref, r_hbm, inv_ref, rg_ref, pull_hbm,
+                    terms_ref, acc_sc, qt_sc, pull_sc, r_sc, sems, r_sem):
     step = pl.program_id(0)
     n_feat = q_ref.shape[1]
     tile = pull_sc.shape[0]
     sub = pull_hbm.shape[0] // (2 ** n_bits)
     per = tile // sub
 
+    refs_copy = pltpu.make_async_copy(r_hbm, r_sc, r_sem)
+
     @pl.when(step == 0)
     def _():
+        refs_copy.start()
         acc_sc[...] = jnp.zeros_like(acc_sc)
         qt_sc[...] = jnp.zeros_like(qt_sc)
 
-    scale = sc_ref[...]
+    scale = cot_ref[...] * jnp.exp(ls_ref[0:1, :] - gs_ref[0:1, :]) / gs_ref[1:2, :]
     pulled = (ut_ref[...] * scale).T
     pull_sc[...] = pulled
     copies = []
@@ -87,8 +90,9 @@
 
     @pl.when(step == pl.num_programs(0) - 1)
     def _():
+        refs_copy.wait()
         acc = acc_sc[...]
-        refs = r_ref[...]
+        refs = r_sc[...]
         rgrad = (acc[:, :n_feat] - refs * acc[:, n_feat:n_feat + 1]) * inv_ref[...]
         rg_ref[...] = rgrad
         rterm = jnp.sum(refs * rgrad, axis=0, keepdims=True)
@@ -134,7 +138,7 @@
     return out
 
 
-def local_backward(expd_low, scale, query_aug, unscaled_t, queries, references, inv, n_dev):
+def local_backward(expd_low, cot, local_stats, stats, query_aug, unscaled_t, queries, references, inv, n_dev):
     n_ref, n_query = expd_low.shape
     n_feat = queries.shape[1]
     width = query_aug.shape[1]
@@ -148,10 +152,12 @@
         in_specs=[
             pl.BlockSpec((n_ref, tile), lambda i: (0, i)),
             pl.BlockSpec((1, tile), lambda i: (0, i)),
+            pl.BlockSpec((2, tile), lambda i: (0, i)),
+            pl.BlockSpec((2, tile), lambda i: (0, i)),
             pl.BlockSpec((tile, width), lambda i: (i, 0)),
             pl.BlockSpec((n_feat, tile), lambda i: (0, i)),
             pl.BlockSpec((tile, n_feat), lambda i: (i, 0)),
-            pl.BlockSpec((n_ref, n_feat), whole),
+            pl.BlockSpec(memory_space=pl.ANY),
             pl.BlockSpec((1, n_feat), whole),
         ],
         out_specs=[
@@ -168,10 +174,12 @@
             pltpu.VMEM((n_ref, width), jnp.float32),
             pltpu.VMEM((1, n_feat), jnp.float32),
             pltpu.VMEM((tile, n_feat), jnp.float32),
+            pltpu.VMEM((n_ref, n_feat), jnp.float32),
             pltpu.SemaphoreType.DMA((tile // sub,)),
+            pltpu.SemaphoreType.DMA(()),
         ],
         compiler_params=pltpu.CompilerParams(dimension_semantics=("arbitrary",)),
-    )(expd_low, scale, query_aug, unscaled_t, queries, references, inv)
+    )(expd_low, cot, local_stats, stats, query_aug, unscaled_t, queries, references, inv)
 
 
 def bit_reversed(n):
@@ -194,7 +202,7 @@
         peak = new_peak
         stats = jnp.stack([peak, total])
         step *= 2
-    return peak, total
+    return stats
 
 
 def halving_scatter(rows, extra, n_dev):
@@ -223,14 +231,13 @@
     own_rows = n_query // n_dev
     inv = 1.0 / (spread * spread)
     expd_low, unscaled_t, local_stats = local_forward(queries, spread[None, :], query_ids[None, :], references)
-    peak, total = butterfly_stats(local_stats, n_dev)
-    scale = cotangent * jnp.exp(local_stats[0] - peak) / total
+    stats = butterfly_stats(local_stats, n_dev)
     query_low = queries.astype(jnp.bfloat16)
     query_aug = jnp.concatenate(
         [query_low, jnp.ones((n_query, 1), jnp.bfloat16), jnp.zeros((n_query, n_feat - 1), jnp.bfloat16)], axis=1
     )
     reference_grad, pulled, local_terms = local_backward(
-        expd_low, scale[None, :], query_aug, unscaled_t, queries, references, inv[None, :], n_dev
+        expd_low, cotangent[None, :], local_stats, stats, query_aug, unscaled_t, queries, references, inv[None, :], n_dev
     )
     own_pulled, summed_terms = halving_scatter(pulled, local_terms, n_dev)
     own_start = lax.axis_index("ref") * own_rows

time: 70.7 us -> 69.7 us (0.986)
  transfers between devices with their start and end apart: 8 -> 8, of which waited for: 8 -> 8; matrix products, arithmetic and copies ran while one was open for 3% -> 4% of each run, Pallas kernels for 0% -> 0%
where the time goes in v18:
time: 69.7 us; the launch traced here: 69.4 us
  Pallas kernels  26.1 us (37%)
  waiting for transfers between devices  17.6 us (25%)
  starting transfers between devices  15.4 us (22%)
  other arithmetic  7.94 us (11%)
  local copies, waits for them, and re-layouts  1.48 us (2%)
  between operations  0.9 us (1%)
    pallas_call x1, Pallas kernels, local_forward(): pl.pallas_call(forward_kernel, grid=(n_query // tile,), in_specs=[pl.Bloc...  17.6 us
    ppermute x8, waiting for transfers between devices, exchange(): return lax.ppermute(x, 'ref', [(i, i ^ step) for i in range(n_dev)])  17.6 us
    ppermute x8, starting transfers between devices, exchange(): return lax.ppermute(x, 'ref', [(i, i ^ step) for i in range(n_dev)])  15.4 us
    pallas_call x1, Pallas kernels, local_backward(): pl.pallas_call(functools.partial(backward_kernel, n_bits), grid=(n_query...  8.41 us
    mul x1, other arithmetic, on_device(): query_grad = (own_pulled - own_queries * own_cot[:, None]) * inv  1.56 us
  transfers between devices with their start and end apart: 8, of which 8 were waited for; matrix products, arithmetic and copies ran while one was open for 4% of the time, Pallas kernels for 0%

profile of v18, /device:TPU:0, one launch (start us, length us, event | category | flops | bytes accessed | tf_op | source)
XLA Modules:
  0.0 69.4 jit_solution(4974841263731522613)
XLA Ops:
  0.7 17.6 %shard_map.76 = (bf16[2048,2048]{1,0:T(8,128)(2,1)}, f32[128,2048]{1,0:T(8,128)}, f32[2,2048]{1,0:T(2,128)}) custom-call(f32[2048,128]{1,0:T(8,128)} %q_ref.3, f32[1,128]{1,0:T(1,128)} %bitcast.55, s32[1,2048]{1,0:T(1,128)} %bitcast.54, f32[2048,128]{1,0:T(8,128)} %r_hbm.1), custom_call_target="tpu_custom_call" | custom-call | tf_op jit(solution)/shard_map/pallas_call | solution.py:106
  18.9 1.0 %collective-permute-done = f32[2,2048]{1,0:T(2,128)S(1)} collective-permute-done((f32[2,2048]{1,0:T(2,128)}, f32[2,2048]{1,0:T(2,128)S(1)}, u32[]{:S(2)}, u32[]{:S(2)}) %collective-permute-start) | collective-permute-done | bytes 16416 | tf_op jit(solution)/shard_map/ppermute | solution.py:191
  19.9 0.8 %fusion.7 = (f32[1,2048]{1,0:T(1,128)S(1)}, f32[1,2048]{1,0:T(1,128)S(1)}) fusion(f32[2,2048]{1,0:T(2,128)S(1)} %collective-permute-done, f32[2,2048]{1,0:T(2,128)} %get-tuple-element.10.ls_ref), kind=kLoop, calls=%fused_computation.26 | loop fusion | flops 12288 | bytes 49152 | tf_op jit(solution)/shard_map/add | solution.py:201
  20.8 2.9 %collective-permute-start.1 = (f32[2,2048]{1,0:T(2,128)S(1)}, f32[2,2048]{1,0:T(2,128)S(1)}, u32[]{:S(2)}, u32[]{:S(2)}) collective-permute-start(f32[2,2048]{1,0:T(2,128)S(1)} %pad_maximum_fusion.4), channel_id=1, source_target_pairs={{0,2},{1,3},{2,0},{3,1},{4,6},{5,7},{6,4},{7,5},{8,10},{9,11},{10,... | collective-permute-start | bytes 49160 | tf_op jit(solution)/shard_map/ppermute | solution.py:191
  24.1 1.3 %collective-permute-done.1 = f32[2,2048]{1,0:T(2,128)S(1)} collective-permute-done((f32[2,2048]{1,0:T(2,128)S(1)}, f32[2,2048]{1,0:T(2,128)S(1)}, u32[]{:S(2)}, u32[]{:S(2)}) %collective-permute-start.1) | collective-permute-done | bytes 16416 | tf_op jit(solution)/shard_map/ppermute | solution.py:191
  25.5 2.1 %collective-permute-start.2 = (f32[2,2048]{1,0:T(2,128)S(1)}, f32[2,2048]{1,0:T(2,128)S(1)}, u32[]{:S(2)}, u32[]{:S(2)}) collective-permute-start(f32[2,2048]{1,0:T(2,128)S(1)} %pad_maximum_fusion.5), channel_id=1, source_target_pairs={{0,4},{1,5},{2,6},{3,7},{4,0},{5,1},{6,2},{7,3},{8,12},{9,13},{10,... | collective-permute-start | bytes 49160 | tf_op jit(solution)/shard_map/ppermute | solution.py:191
  27.6 1.1 %maximum_maximum_fusion.qa_ref = bf16[2048,256]{1,0:T(8,128)(2,1)} fusion(bf16[2048,128]{1,0:T(8,128)(2,1)S(1)} %get-tuple-element.22, bf16[256]{0:T(256)(128)(2,1)S(1)} %pad.10.clone, bf16[256]{0:T(256)(128)(2,1)S(1)} %pad.9.clone), kind=kLoop, calls=%fused_computation | loop fusion | flops 3145728 | bytes 1573888 | tf_op jit(solution)/shard_map/concatenate | solution.py:236
  28.7 0.6 collective-permute-done.2
  29.4 3.1 %collective-permute-start.3 = (f32[2,2048]{1,0:T(2,128)S(1)}, f32[2,2048]{1,0:T(2,128)S(1)}, u32[]{:S(2)}, u32[]{:S(2)}) collective-permute-start(f32[2,2048]{1,0:T(2,128)S(1)} %pad_maximum_fusion.6), channel_id=1, source_target_pairs={{0,8},{1,9},{2,10},{3,11},{4,12},{5,13},{6,14},{7,15},{8,0},{9,1},... | collective-permute-start | bytes 49160 | tf_op jit(solution)/shard_map/ppermute | solution.py:191
  33.0 1.2 %collective-permute-done.3 = f32[2,2048]{1,0:T(2,128)S(1)} collective-permute-done((f32[2,2048]{1,0:T(2,128)S(1)}, f32[2,2048]{1,0:T(2,128)S(1)}, u32[]{:S(2)}, u32[]{:S(2)}) %collective-permute-start.3) | collective-permute-done | bytes 16416 | tf_op jit(solution)/shard_map/ppermute | solution.py:191
  34.2 0.6 pad_maximum_fusion.7.gs_ref
  34.9 8.4 %shard_map.77 = (f32[2048,128]{1,0:T(8,128)}, f32[2048,128]{1,0:T(8,128)}, f32[8,128]{1,0:T(8,128)}) custom-call(bf16[2048,2048]{1,0:T(8,128)(2,1)} %get-tuple-element.9.e_ref, f32[1,2048]{1,0:T(1,128)} %bitcast.53, f32[2,2048]{1,0:T(2,128)} %get-tuple-element.10.ls_ref, f32[2,2048]{1,0:T(2,128)} %pad_maximum_fusion.7.gs_ref, ...), custom_call_target="tpu_custom_call" | custom-call | tf_op jit(solution)/shard_map/pallas_call | solution.py:149
  43.3 1.2 %constant_dynamic-slice_fusion.2 = f32[8,128,128]{2,1,0:T(8,128)S(1)} fusion(f32[16,128,128]{2,1,0:T(8,128)} %bitcast.48, s32[]{:T(128)S(6)} %select_n.60), kind=kLoop, calls=%fused_computation.37 | loop fusion | bytes 1048580 | tf_op jit(solution)/shard_map/dynamic_slice | solution.py:217
  44.5 0.8 %pad_maximum_fusion = f32[1032,128]{1,0:T(8,128)S(1)} fusion(f32[8,128]{1,0:T(8,128)} %get-tuple-element.13, f32[1024,128]{1,0:T(8,128)S(1)} %bitcast.46), kind=kLoop, calls=%fused_computation.2 | loop fusion | flops 132096 | bytes 1056768 | tf_op jit(solution)/shard_map/concatenate | solution.py:219
  45.4 1.9 %collective-permute-done.4 = f32[1032,128]{1,0:T(8,128)S(1)} collective-permute-done((f32[1032,128]{1,0:T(8,128)S(1)}, f32[1032,128]{1,0:T(8,128)S(1)}, u32[]{:S(2)}, u32[]{:S(2)}) %collective-permute-start.4) | collective-permute-done | bytes 528416 | tf_op jit(solution)/shard_map/ppermute | solution.py:191
  47.5 1.9 %collective-permute-start.5 = (f32[520,128]{1,0:T(8,128)S(1)}, f32[520,128]{1,0:T(8,128)S(1)}, u32[]{:S(2)}, u32[]{:S(2)}) collective-permute-start(f32[520,128]{1,0:T(8,128)S(1)} %pad_maximum_fusion.1), channel_id=1, source_target_pairs={{0,2},{1,3},{2,0},{3,1},{4,6},{5,7},{6,4},{7,5},{8,10},{9,11},{10,... | collective-permute-start | bytes 798728 | tf_op jit(solution)/shard_map/ppermute | solution.py:191
  49.4 6.7 %collective-permute-done.5 = f32[520,128]{1,0:T(8,128)S(1)} collective-permute-done((f32[520,128]{1,0:T(8,128)S(1)}, f32[520,128]{1,0:T(8,128)S(1)}, u32[]{:S(2)}, u32[]{:S(2)}) %collective-permute-start.5) | collective-permute-done | bytes 266272 | tf_op jit(solution)/shard_map/ppermute | solution.py:191
  56.2 1.9 %collective-permute-start.6 = (f32[264,128]{1,0:T(8,128)S(1)}, f32[264,128]{1,0:T(8,128)S(1)}, u32[]{:S(2)}, u32[]{:S(2)}) collective-permute-start(f32[264,128]{1,0:T(8,128)S(1)} %pad_maximum_fusion.2), channel_id=1, source_target_pairs={{0,4},{1,5},{2,6},{3,7},{4,0},{5,1},{6,2},{7,3},{8,12},{9,13},{10,... | collective-permute-start | bytes 405512 | tf_op jit(solution)/shard_map/ppermute | solution.py:191
  58.1 3.2 %collective-permute-done.6 = f32[264,128]{1,0:T(8,128)S(1)} collective-permute-done((f32[264,128]{1,0:T(8,128)S(1)}, f32[264,128]{1,0:T(8,128)S(1)}, u32[]{:S(2)}, u32[]{:S(2)}) %collective-permute-start.6) | collective-permute-done | bytes 135200 | tf_op jit(solution)/shard_map/ppermute | solution.py:191
  61.4 2.9 %collective-permute-start.7 = (f32[136,128]{1,0:T(8,128)S(1)}, f32[136,128]{1,0:T(8,128)S(1)}, u32[]{:S(2)}, u32[]{:S(2)}) collective-permute-start(f32[136,128]{1,0:T(8,128)S(1)} %pad_maximum_fusion.3), channel_id=1, source_target_pairs={{0,8},{1,9},{2,10},{3,11},{4,12},{5,13},{6,14},{7,15},{8,0},{9,1},... | collective-permute-start | bytes 208904 | tf_op jit(solution)/shard_map/ppermute | solution.py:191
  64.3 0.6 reduce_sum.19
  64.9 1.7 %collective-permute-done.7 = f32[136,128]{1,0:T(8,128)S(1)} collective-permute-done((f32[136,128]{1,0:T(8,128)S(1)}, f32[136,128]{1,0:T(8,128)S(1)}, u32[]{:S(2)}, u32[]{:S(2)}) %collective-permute-start.7) | collective-permute-done | bytes 69664 | tf_op jit(solution)/shard_map/ppermute | solution.py:191
  66.6 1.2 %divide_subtract_fusion = f32[128]{0:T(128)} fusion(f32[128]{0:T(128)S(1)} %copy-done.5, f32[128]{0:T(128)S(1)} %get-tuple-element.21, f32[8,128]{1,0:T(8,128)S(1)} %slice_add_fusion, f32[]{:T(128)} %reduce_sum.19), kind=kLoop, calls=%fused_computation.38 | loop fusion | flops 1152 | bytes 2564 | tf_op jit(solution)/shard_map/sub | solution.py:250
  67.8 1.6 %fusion.3 = f32[128,128]{1,0:T(8,128)} fusion(f32[136,128]{1,0:T(8,128)S(1)} %collective-permute-done.7, f32[2048,128]{1,0:T(8,128)} %q_ref.3, s32[]{:T(128)S(6)} %select_n.73, f32[2,128,128]{2,1,0:T(8,128)S(1)} %dynamic-slice_add_fusion.2, s32[]{:T(128)S(6)} %select_n.71, f32[128]{0:T(128)S(1)} %multiply_divide_fusion, f32[128]{0:T(128)S(1)} %dynamic_slice.39), kind=kLoop, calls=%fused_computation.13 | loop fusion | flops 65536 | bytes 263176 | tf_op jit(solution)/shard_map/mul | solution.py:246
  (43 shorter events, 2.2 us)
Async XLA Ops:
  0.6 23.0 %copy-start = (f32[2048,128]{1,0:T(8,128)S(1)}, f32[2048,128]{1,0:T(8,128)}, u32[]{:S(2)}) copy-start(f32[2048,128]{1,0:T(8,128)} %q_ref.3) | copy-start | bytes 3145732
  0.6 23.0 %copy-start.2 = (f32[2048]{0:T(1024)S(1)}, f32[2048]{0:T(1024)}, u32[]{:S(2)}) copy-start(f32[2048]{0:T(1024)} %param.9) | copy-start | bytes 24580
  18.3 14.2 %copy-start.5 = (f32[128]{0:T(128)S(1)}, f32[128]{0:T(128)}, u32[]{:S(2)}) copy-start(f32[128]{0:T(128)} %param.8) | copy-start | bytes 1540
  18.3 1.6 %collective-permute-start = (f32[2,2048]{1,0:T(2,128)}, f32[2,2048]{1,0:T(2,128)S(1)}, u32[]{:S(2)}, u32[]{:S(2)}) collective-permute-start(f32[2,2048]{1,0:T(2,128)} %get-tuple-element.10.ls_ref), channel_id=1, source_target_pairs={{0,1},{1,0},{2,3},{3,2},{4,5},{5,4},{6,7},{7,6},{8,9},{9,8},{10,11... | collective-permute-start | bytes 49160 | tf_op jit(solution)/shard_map/ppermute | solution.py:191
  20.8 4.6 %collective-permute-start.1 = (f32[2,2048]{1,0:T(2,128)S(1)}, f32[2,2048]{1,0:T(2,128)S(1)}, u32[]{:S(2)}, u32[]{:S(2)}) collective-permute-start(f32[2,2048]{1,0:T(2,128)S(1)} %pad_maximum_fusion.4), channel_id=1, source_target_pairs={{0,2},{1,3},{2,0},{3,1},{4,6},{5,7},{6,4},{7,5},{8,10},{9,11},{10,... | collective-permute-start | bytes 49160 | tf_op jit(solution)/shard_map/ppermute | solution.py:191
  25.5 3.9 %collective-permute-start.2 = (f32[2,2048]{1,0:T(2,128)S(1)}, f32[2,2048]{1,0:T(2,128)S(1)}, u32[]{:S(2)}, u32[]{:S(2)}) collective-permute-start(f32[2,2048]{1,0:T(2,128)S(1)} %pad_maximum_fusion.5), channel_id=1, source_target_pairs={{0,4},{1,5},{2,6},{3,7},{4,0},{5,1},{6,2},{7,3},{8,12},{9,13},{10,... | collective-permute-start | bytes 49160 | tf_op jit(solution)/shard_map/ppermute | solution.py:191
  29.4 4.8 %collective-permute-start.3 = (f32[2,2048]{1,0:T(2,128)S(1)}, f32[2,2048]{1,0:T(2,128)S(1)}, u32[]{:S(2)}, u32[]{:S(2)}) collective-permute-start(f32[2,2048]{1,0:T(2,128)S(1)} %pad_maximum_fusion.6), channel_id=1, source_target_pairs={{0,8},{1,9},{2,10},{3,11},{4,12},{5,13},{6,14},{7,15},{8,0},{9,1},... | collective-permute-start | bytes 49160 | tf_op jit(solution)/shard_map/ppermute | solution.py:191
  43.3 4.0 %copy-start.1 = (f32[2048,128]{1,0:T(8,128)S(1)}, f32[2048,128]{1,0:T(8,128)}, u32[]{:S(2)}) copy-start(f32[2048,128]{1,0:T(8,128)} %get-tuple-element.12) | copy-start | bytes 3145732
  44.5 3.0 %copy-start.4 = (f32[8,128]{1,0:T(8,128)S(1)}, f32[8,128]{1,0:T(8,128)}, u32[]{:S(2)}) copy-start(f32[8,128]{1,0:T(8,128)} %get-tuple-element.13) | copy-start | bytes 12292
  45.3 2.0 %collective-permute-start.4 = (f32[1032,128]{1,0:T(8,128)S(1)}, f32[1032,128]{1,0:T(8,128)S(1)}, u32[]{:S(2)}, u32[]{:S(2)}) collective-permute-start(f32[1032,128]{1,0:T(8,128)S(1)} %pad_maximum_fusion), channel_id=1, source_target_pairs={{0,1},{1,0},{2,3},{3,2},{4,5},{5,4},{6,7},{7,6},{8,9},{9,8},{10,11... | collective-permute-start | bytes 1585160 | tf_op jit(solution)/shard_map/ppermute | solution.py:191
  47.4 16.9 %copy-start.3 = (f32[2048]{0:T(1024)S(1)}, f32[2048]{0:T(1024)}, u32[]{:S(2)}) copy-start(f32[2048]{0:T(1024)} %param.9) | copy-start | bytes 24580
  47.5 8.6 %collective-permute-start.5 = (f32[520,128]{1,0:T(8,128)S(1)}, f32[520,128]{1,0:T(8,128)S(1)}, u32[]{:S(2)}, u32[]{:S(2)}) collective-permute-start(f32[520,128]{1,0:T(8,128)S(1)} %pad_maximum_fusion.1), channel_id=1, source_target_pairs={{0,2},{1,3},{2,0},{3,1},{4,6},{5,7},{6,4},{7,5},{8,10},{9,11},{10,... | collective-permute-start | bytes 798728 | tf_op jit(solution)/shard_map/ppermute | solution.py:191
  56.2 5.1 %collective-permute-start.6 = (f32[264,128]{1,0:T(8,128)S(1)}, f32[264,128]{1,0:T(8,128)S(1)}, u32[]{:S(2)}, u32[]{:S(2)}) collective-permute-start(f32[264,128]{1,0:T(8,128)S(1)} %pad_maximum_fusion.2), channel_id=1, source_target_pairs={{0,4},{1,5},{2,6},{3,7},{4,0},{5,1},{6,2},{7,3},{8,12},{9,13},{10,... | collective-permute-start | bytes 405512 | tf_op jit(solution)/shard_map/ppermute | solution.py:191
  61.4 5.3 %collective-permute-start.7 = (f32[136,128]{1,0:T(8,128)S(1)}, f32[136,128]{1,0:T(8,128)S(1)}, u32[]{:S(2)}, u32[]{:S(2)}) collective-permute-start(f32[136,128]{1,0:T(8,128)S(1)} %pad_maximum_fusion.3), channel_id=1, source_target_pairs={{0,8},{1,9},{2,10},{3,11},{4,12},{5,13},{6,14},{7,15},{8,0},{9,1},... | collective-permute-start | bytes 208904 | tf_op jit(solution)/shard_map/ppermute | solution.py:191

commit v19 on v18

--- a/solution.py
+++ b/solution.py
@@ -55,7 +55,7 @@
     ut_ref[...] = jnp.dot(rlt_sc[...], expd_low, preferred_element_type=jnp.float32)
 
 
-def backward_kernel(n_bits, e_ref, cot_ref, ls_ref, gs_ref, qa_ref, ut_ref, q_ref, r_hbm, inv_ref, rg_ref, pull_hbm,
+def backward_kernel(n_bits, e_ref, cot_ref, ls_ref, gp_ref, gt_ref, qa_ref, ut_ref, q_ref, r_hbm, inv_ref, rg_ref, pull_hbm,
                     terms_ref, acc_sc, qt_sc, pull_sc, r_sc, sems, r_sem):
     step = pl.program_id(0)
     n_feat = q_ref.shape[1]
@@ -71,7 +71,7 @@
         acc_sc[...] = jnp.zeros_like(acc_sc)
         qt_sc[...] = jnp.zeros_like(qt_sc)
 
-    scale = cot_ref[...] * jnp.exp(ls_ref[0:1, :] - gs_ref[0:1, :]) / gs_ref[1:2, :]
+    scale = cot_ref[...] * jnp.exp(ls_ref[0:1, :] - gp_ref[...]) / gt_ref[...]
     pulled = (ut_ref[...] * scale).T
     pull_sc[...] = pulled
     copies = []
@@ -138,7 +138,7 @@
     return out
 
 
-def local_backward(expd_low, cot, local_stats, stats, query_aug, unscaled_t, queries, references, inv, n_dev):
+def local_backward(expd_low, cot, local_stats, peak, total, query_aug, unscaled_t, queries, references, inv, n_dev):
     n_ref, n_query = expd_low.shape
     n_feat = queries.shape[1]
     width = query_aug.shape[1]
@@ -153,7 +153,8 @@
             pl.BlockSpec((n_ref, tile), lambda i: (0, i)),
             pl.BlockSpec((1, tile), lambda i: (0, i)),
             pl.BlockSpec((2, tile), lambda i: (0, i)),
-            pl.BlockSpec((2, tile), lambda i: (0, i)),
+            pl.BlockSpec((1, tile), lambda i: (0, i)),
+            pl.BlockSpec((1, tile), lambda i: (0, i)),
             pl.BlockSpec((tile, width), lambda i: (i, 0)),
             pl.BlockSpec((n_feat, tile), lambda i: (0, i)),
             pl.BlockSpec((tile, n_feat), lambda i: (i, 0)),
@@ -179,7 +180,7 @@
             pltpu.SemaphoreType.DMA(()),
         ],
         compiler_params=pltpu.CompilerParams(dimension_semantics=("arbitrary",)),
-    )(expd_low, cot, local_stats, stats, query_aug, unscaled_t, queries, references, inv)
+    )(expd_low, cot, local_stats, peak, total, query_aug, unscaled_t, queries, references, inv)
 
 
 def bit_reversed(n):
@@ -200,9 +201,10 @@
         new_peak = jnp.maximum(peak, other_peak)
         total = total * jnp.exp(peak - new_peak) + other_total * jnp.exp(other_peak - new_peak)
         peak = new_peak
-        stats = jnp.stack([peak, total])
         step *= 2
-    return stats
+        if step < n_dev:
+            stats = jnp.stack([peak, total])
+    return peak[None, :], total[None, :]
 
 
 def halving_scatter(rows, extra, n_dev):
@@ -231,13 +233,13 @@
     own_rows = n_query // n_dev
     inv = 1.0 / (spread * spread)
     expd_low, unscaled_t, local_stats = local_forward(queries, spread[None, :], query_ids[None, :], references)
-    stats = butterfly_stats(local_stats, n_dev)
+    peak, total = butterfly_stats(local_stats, n_dev)
     query_low = queries.astype(jnp.bfloat16)
     query_aug = jnp.concatenate(
         [query_low, jnp.ones((n_query, 1), jnp.bfloat16), jnp.zeros((n_query, n_feat - 1), jnp.bfloat16)], axis=1
     )
     reference_grad, pulled, local_terms = local_backward(
-        expd_low, cotangent[None, :], local_stats, stats, query_aug, unscaled_t, queries, references, inv[None, :], n_dev
+        expd_low, cotangent[None, :], local_stats, peak, total, query_aug, unscaled_t, queries, references, inv[None, :], n_dev
     )
     own_pulled, summed_terms = halving_scatter(pulled, local_terms, n_dev)
     own_start = lax.axis_index("ref") * own_rows

time: 69.7 us -> 70.7 us (1.014)
  Pallas kernels: 26.1 us -> 27.2 us
    pallas_call x1, Pallas kernels: 8.41 us -> 9.54 us  [local_backward(): pl.pallas_call(functools.partial(backward_kernel, n_bits), grid=(n_query...]
    add x3 -> x4, other arithmetic: 0.9 us -> 1.52 us  [butterfly_stats(): total * jnp.exp(peak - new_peak)]
where the time goes in v19:
time: 70.7 us; the launch traced here: 70.5 us
  Pallas kernels  27.2 us (38%)
  waiting for transfers between devices  17.6 us (25%)
  starting transfers between devices  15.4 us (22%)
  other arithmetic  7.89 us (11%)
  local copies, waits for them, and re-layouts  1.48 us (2%)
  between operations  0.9 us (1%)
    pallas_call x1, Pallas kernels, local_forward(): pl.pallas_call(forward_kernel, grid=(n_query // tile,), in_specs=[pl.Bloc...  17.6 us
    ppermute x8, waiting for transfers between devices, exchange(): return lax.ppermute(x, 'ref', [(i, i ^ step) for i in range(n_dev)])  17.6 us
    ppermute x8, starting transfers between devices, exchange(): return lax.ppermute(x, 'ref', [(i, i ^ step) for i in range(n_dev)])  15.4 us
    pallas_call x1, Pallas kernels, local_backward(): pl.pallas_call(functools.partial(backward_kernel, n_bits), grid=(n_query...  9.54 us
    mul x1, other arithmetic, on_device(): query_grad = (own_pulled - own_queries * own_cot[:, None]) * inv  1.56 us
    add x4, other arithmetic, butterfly_stats(): total * jnp.exp(peak - new_peak)  1.52 us
  transfers between devices with their start and end apart: 8, of which 8 were waited for; matrix products, arithmetic and copies ran while one was open for 4% of the time, Pallas kernels for 0%

profile of v19, /device:TPU:0, one launch (start us, length us, event | category | flops | bytes accessed | tf_op | source)
XLA Modules:
  0.0 70.5 jit_solution(10008597638947527143)
XLA Ops:
  0.7 17.6 %shard_map.76 = (bf16[2048,2048]{1,0:T(8,128)(2,1)}, f32[128,2048]{1,0:T(8,128)}, f32[2,2048]{1,0:T(2,128)}) custom-call(f32[2048,128]{1,0:T(8,128)} %q_ref.3, f32[1,128]{1,0:T(1,128)} %bitcast.55, s32[1,2048]{1,0:T(1,128)} %bitcast.54, f32[2048,128]{1,0:T(8,128)} %r_hbm.1), custom_call_target="tpu_custom_call" | custom-call | tf_op jit(solution)/shard_map/pallas_call | solution.py:106
  18.9 1.0 %collective-permute-done = f32[2,2048]{1,0:T(2,128)S(1)} collective-permute-done((f32[2,2048]{1,0:T(2,128)}, f32[2,2048]{1,0:T(2,128)S(1)}, u32[]{:S(2)}, u32[]{:S(2)}) %collective-permute-start) | collective-permute-done | bytes 16416 | tf_op jit(solution)/shard_map/ppermute | solution.py:192
  19.9 0.8 %fusion.7 = (f32[1,2048]{1,0:T(1,128)S(1)}, f32[1,2048]{1,0:T(1,128)S(1)}) fusion(f32[2,2048]{1,0:T(2,128)S(1)} %collective-permute-done, f32[2,2048]{1,0:T(2,128)} %get-tuple-element.10.ls_ref), kind=kLoop, calls=%fused_computation.25 | loop fusion | flops 12288 | bytes 49152 | tf_op jit(solution)/shard_map/add | solution.py:202
  20.8 2.9 %collective-permute-start.1 = (f32[2,2048]{1,0:T(2,128)S(1)}, f32[2,2048]{1,0:T(2,128)S(1)}, u32[]{:S(2)}, u32[]{:S(2)}) collective-permute-start(f32[2,2048]{1,0:T(2,128)S(1)} %pad_maximum_fusion.4), channel_id=1, source_target_pairs={{0,2},{1,3},{2,0},{3,1},{4,6},{5,7},{6,4},{7,5},{8,10},{9,11},{10,... | collective-permute-start | bytes 49160 | tf_op jit(solution)/shard_map/ppermute | solution.py:192
  24.1 1.3 %collective-permute-done.1 = f32[2,2048]{1,0:T(2,128)S(1)} collective-permute-done((f32[2,2048]{1,0:T(2,128)S(1)}, f32[2,2048]{1,0:T(2,128)S(1)}, u32[]{:S(2)}, u32[]{:S(2)}) %collective-permute-start.1) | collective-permute-done | bytes 16416 | tf_op jit(solution)/shard_map/ppermute | solution.py:192
  25.5 2.1 %collective-permute-start.2 = (f32[2,2048]{1,0:T(2,128)S(1)}, f32[2,2048]{1,0:T(2,128)S(1)}, u32[]{:S(2)}, u32[]{:S(2)}) collective-permute-start(f32[2,2048]{1,0:T(2,128)S(1)} %pad_maximum_fusion.5), channel_id=1, source_target_pairs={{0,4},{1,5},{2,6},{3,7},{4,0},{5,1},{6,2},{7,3},{8,12},{9,13},{10,... | collective-permute-start | bytes 49160 | tf_op jit(solution)/shard_map/ppermute | solution.py:192
  27.6 1.1 %maximum_maximum_fusion.qa_ref = bf16[2048,256]{1,0:T(8,128)(2,1)} fusion(bf16[2048,128]{1,0:T(8,128)(2,1)S(1)} %get-tuple-element.22, bf16[256]{0:T(256)(128)(2,1)S(1)} %pad.10.clone, bf16[256]{0:T(256)(128)(2,1)S(1)} %pad.9.clone), kind=kLoop, calls=%fused_computation | loop fusion | flops 3145728 | bytes 1573888 | tf_op jit(solution)/shard_map/concatenate | solution.py:238
  28.7 0.6 collective-permute-done.2
  29.4 3.1 %collective-permute-start.3 = (f32[2,2048]{1,0:T(2,128)S(1)}, f32[2,2048]{1,0:T(2,128)S(1)}, u32[]{:S(2)}, u32[]{:S(2)}) collective-permute-start(f32[2,2048]{1,0:T(2,128)S(1)} %pad_maximum_fusion.6), channel_id=1, source_target_pairs={{0,8},{1,9},{2,10},{3,11},{4,12},{5,13},{6,14},{7,15},{8,0},{9,1},... | collective-permute-start | bytes 49160 | tf_op jit(solution)/shard_map/ppermute | solution.py:192
  33.0 1.2 %collective-permute-done.3 = f32[2,2048]{1,0:T(2,128)S(1)} collective-permute-done((f32[2,2048]{1,0:T(2,128)S(1)}, f32[2,2048]{1,0:T(2,128)S(1)}, u32[]{:S(2)}, u32[]{:S(2)}) %collective-permute-start.3) | collective-permute-done | bytes 16416 | tf_op jit(solution)/shard_map/ppermute | solution.py:192
  34.2 0.6 fusion.4
  34.8 9.5 %shard_map.77 = (f32[2048,128]{1,0:T(8,128)}, f32[2048,128]{1,0:T(8,128)}, f32[8,128]{1,0:T(8,128)}) custom-call(bf16[2048,2048]{1,0:T(8,128)(2,1)} %get-tuple-element.9.e_ref, f32[1,2048]{1,0:T(1,128)} %bitcast.53, f32[2,2048]{1,0:T(2,128)} %get-tuple-element.10.ls_ref, f32[1,2048]{1,0:T(1,128)} %get-tuple-element.24.gp_ref, ...), custom_call_target="tpu_custom_call" | custom-call | tf_op jit(solution)/shard_map/pallas_call | solution.py:149
  44.4 1.2 %constant_dynamic-slice_fusion.2 = f32[8,128,128]{2,1,0:T(8,128)S(1)} fusion(f32[16,128,128]{2,1,0:T(8,128)} %bitcast.48, s32[]{:T(128)S(6)} %select_n.60), kind=kLoop, calls=%fused_computation.36 | loop fusion | bytes 1048580 | tf_op jit(solution)/shard_map/dynamic_slice | solution.py:219
  45.6 0.8 %pad_maximum_fusion = f32[1032,128]{1,0:T(8,128)S(1)} fusion(f32[8,128]{1,0:T(8,128)} %get-tuple-element.13, f32[1024,128]{1,0:T(8,128)S(1)} %bitcast.46), kind=kLoop, calls=%fused_computation.2 | loop fusion | flops 132096 | bytes 1056768 | tf_op jit(solution)/shard_map/concatenate | solution.py:221
  46.5 1.9 %collective-permute-done.4 = f32[1032,128]{1,0:T(8,128)S(1)} collective-permute-done((f32[1032,128]{1,0:T(8,128)S(1)}, f32[1032,128]{1,0:T(8,128)S(1)}, u32[]{:S(2)}, u32[]{:S(2)}) %collective-permute-start.4) | collective-permute-done | bytes 528416 | tf_op jit(solution)/shard_map/ppermute | solution.py:192
  48.6 1.9 %collective-permute-start.5 = (f32[520,128]{1,0:T(8,128)S(1)}, f32[520,128]{1,0:T(8,128)S(1)}, u32[]{:S(2)}, u32[]{:S(2)}) collective-permute-start(f32[520,128]{1,0:T(8,128)S(1)} %pad_maximum_fusion.1), channel_id=1, source_target_pairs={{0,2},{1,3},{2,0},{3,1},{4,6},{5,7},{6,4},{7,5},{8,10},{9,11},{10,... | collective-permute-start | bytes 798728 | tf_op jit(solution)/shard_map/ppermute | solution.py:192
  50.5 6.7 %collective-permute-done.5 = f32[520,128]{1,0:T(8,128)S(1)} collective-permute-done((f32[520,128]{1,0:T(8,128)S(1)}, f32[520,128]{1,0:T(8,128)S(1)}, u32[]{:S(2)}, u32[]{:S(2)}) %collective-permute-start.5) | collective-permute-done | bytes 266272 | tf_op jit(solution)/shard_map/ppermute | solution.py:192
  57.3 1.9 %collective-permute-start.6 = (f32[264,128]{1,0:T(8,128)S(1)}, f32[264,128]{1,0:T(8,128)S(1)}, u32[]{:S(2)}, u32[]{:S(2)}) collective-permute-start(f32[264,128]{1,0:T(8,128)S(1)} %pad_maximum_fusion.2), channel_id=1, source_target_pairs={{0,4},{1,5},{2,6},{3,7},{4,0},{5,1},{6,2},{7,3},{8,12},{9,13},{10,... | collective-permute-start | bytes 405512 | tf_op jit(solution)/shard_map/ppermute | solution.py:192
  59.2 3.2 %collective-permute-done.6 = f32[264,128]{1,0:T(8,128)S(1)} collective-permute-done((f32[264,128]{1,0:T(8,128)S(1)}, f32[264,128]{1,0:T(8,128)S(1)}, u32[]{:S(2)}, u32[]{:S(2)}) %collective-permute-start.6) | collective-permute-done | bytes 135200 | tf_op jit(solution)/shard_map/ppermute | solution.py:192
  62.5 2.9 %collective-permute-start.7 = (f32[136,128]{1,0:T(8,128)S(1)}, f32[136,128]{1,0:T(8,128)S(1)}, u32[]{:S(2)}, u32[]{:S(2)}) collective-permute-start(f32[136,128]{1,0:T(8,128)S(1)} %pad_maximum_fusion.3), channel_id=1, source_target_pairs={{0,8},{1,9},{2,10},{3,11},{4,12},{5,13},{6,14},{7,15},{8,0},{9,1},... | collective-permute-start | bytes 208904 | tf_op jit(solution)/shard_map/ppermute | solution.py:192
  65.3 0.6 reduce_sum.19
  66.0 1.7 %collective-permute-done.7 = f32[136,128]{1,0:T(8,128)S(1)} collective-permute-done((f32[136,128]{1,0:T(8,128)S(1)}, f32[136,128]{1,0:T(8,128)S(1)}, u32[]{:S(2)}, u32[]{:S(2)}) %collective-permute-start.7) | collective-permute-done | bytes 69664 | tf_op jit(solution)/shard_map/ppermute | solution.py:192
  67.7 1.2 %divide_subtract_fusion = f32[128]{0:T(128)} fusion(f32[128]{0:T(128)S(1)} %copy-done.5, f32[128]{0:T(128)S(1)} %get-tuple-element.21, f32[8,128]{1,0:T(8,128)S(1)} %slice_add_fusion, f32[]{:T(128)} %reduce_sum.19), kind=kLoop, calls=%fused_computation.37 | loop fusion | flops 1152 | bytes 2564 | tf_op jit(solution)/shard_map/sub | solution.py:252
  68.9 1.6 %fusion.3 = f32[128,128]{1,0:T(8,128)} fusion(f32[136,128]{1,0:T(8,128)S(1)} %collective-permute-done.7, f32[2048,128]{1,0:T(8,128)} %q_ref.3, s32[]{:T(128)S(6)} %select_n.73, f32[2,128,128]{2,1,0:T(8,128)S(1)} %dynamic-slice_add_fusion.2, s32[]{:T(128)S(6)} %select_n.71, f32[128]{0:T(128)S(1)} %multiply_divide_fusion, f32[128]{0:T(128)S(1)} %dynamic_slice.39), kind=kLoop, calls=%fused_computation.13 | loop fusion | flops 65536 | bytes 263176 | tf_op jit(solution)/shard_map/mul | solution.py:248
  (42 shorter events, 2.2 us)
Async XLA Ops:
  0.6 23.0 %copy-start = (f32[2048,128]{1,0:T(8,128)S(1)}, f32[2048,128]{1,0:T(8,128)}, u32[]{:S(2)}) copy-start(f32[2048,128]{1,0:T(8,128)} %q_ref.3) | copy-start | bytes 3145732
  0.6 23.0 %copy-start.2 = (f32[2048]{0:T(1024)S(1)}, f32[2048]{0:T(1024)}, u32[]{:S(2)}) copy-start(f32[2048]{0:T(1024)} %param.9) | copy-start | bytes 24580
  18.3 14.2 %copy-start.5 = (f32[128]{0:T(128)S(1)}, f32[128]{0:T(128)}, u32[]{:S(2)}) copy-start(f32[128]{0:T(128)} %param.8) | copy-start | bytes 1540
  18.3 1.6 %collective-permute-start = (f32[2,2048]{1,0:T(2,128)}, f32[2,2048]{1,0:T(2,128)S(1)}, u32[]{:S(2)}, u32[]{:S(2)}) collective-permute-start(f32[2,2048]{1,0:T(2,128)} %get-tuple-element.10.ls_ref), channel_id=1, source_target_pairs={{0,1},{1,0},{2,3},{3,2},{4,5},{5,4},{6,7},{7,6},{8,9},{9,8},{10,11... | collective-permute-start | bytes 49160 | tf_op jit(solution)/shard_map/ppermute | solution.py:192
  20.8 4.6 %collective-permute-start.1 = (f32[2,2048]{1,0:T(2,128)S(1)}, f32[2,2048]{1,0:T(2,128)S(1)}, u32[]{:S(2)}, u32[]{:S(2)}) collective-permute-start(f32[2,2048]{1,0:T(2,128)S(1)} %pad_maximum_fusion.4), channel_id=1, source_target_pairs={{0,2},{1,3},{2,0},{3,1},{4,6},{5,7},{6,4},{7,5},{8,10},{9,11},{10,... | collective-permute-start | bytes 49160 | tf_op jit(solution)/shard_map/ppermute | solution.py:192
  25.5 3.9 %collective-permute-start.2 = (f32[2,2048]{1,0:T(2,128)S(1)}, f32[2,2048]{1,0:T(2,128)S(1)}, u32[]{:S(2)}, u32[]{:S(2)}) collective-permute-start(f32[2,2048]{1,0:T(2,128)S(1)} %pad_maximum_fusion.5), channel_id=1, source_target_pairs={{0,4},{1,5},{2,6},{3,7},{4,0},{5,1},{6,2},{7,3},{8,12},{9,13},{10,... | collective-permute-start | bytes 49160 | tf_op jit(solution)/shard_map/ppermute | solution.py:192
  29.4 4.8 %collective-permute-start.3 = (f32[2,2048]{1,0:T(2,128)S(1)}, f32[2,2048]{1,0:T(2,128)S(1)}, u32[]{:S(2)}, u32[]{:S(2)}) collective-permute-start(f32[2,2048]{1,0:T(2,128)S(1)} %pad_maximum_fusion.6), channel_id=1, source_target_pairs={{0,8},{1,9},{2,10},{3,11},{4,12},{5,13},{6,14},{7,15},{8,0},{9,1},... | collective-permute-start | bytes 49160 | tf_op jit(solution)/shard_map/ppermute | solution.py:192
  44.4 4.0 %copy-start.1 = (f32[2048,128]{1,0:T(8,128)S(1)}, f32[2048,128]{1,0:T(8,128)}, u32[]{:S(2)}) copy-start(f32[2048,128]{1,0:T(8,128)} %get-tuple-element.12) | copy-start | bytes 3145732
  45.6 2.9 %copy-start.4 = (f32[8,128]{1,0:T(8,128)S(1)}, f32[8,128]{1,0:T(8,128)}, u32[]{:S(2)}) copy-start(f32[8,128]{1,0:T(8,128)} %get-tuple-element.13) | copy-start | bytes 12292
  46.3 2.0 %collective-permute-start.4 = (f32[1032,128]{1,0:T(8,128)S(1)}, f32[1032,128]{1,0:T(8,128)S(1)}, u32[]{:S(2)}, u32[]{:S(2)}) collective-permute-start(f32[1032,128]{1,0:T(8,128)S(1)} %pad_maximum_fusion), channel_id=1, source_target_pairs={{0,1},{1,0},{2,3},{3,2},{4,5},{5,4},{6,7},{7,6},{8,9},{9,8},{10,11... | collective-permute-start | bytes 1585160 | tf_op jit(solution)/shard_map/ppermute | solution.py:192
  48.5 16.9 %copy-start.3 = (f32[2048]{0:T(1024)S(1)}, f32[2048]{0:T(1024)}, u32[]{:S(2)}) copy-start(f32[2048]{0:T(1024)} %param.9) | copy-start | bytes 24580
  48.6 8.6 %collective-permute-start.5 = (f32[520,128]{1,0:T(8,128)S(1)}, f32[520,128]{1,0:T(8,128)S(1)}, u32[]{:S(2)}, u32[]{:S(2)}) collective-permute-start(f32[520,128]{1,0:T(8,128)S(1)} %pad_maximum_fusion.1), channel_id=1, source_target_pairs={{0,2},{1,3},{2,0},{3,1},{4,6},{5,7},{6,4},{7,5},{8,10},{9,11},{10,... | collective-permute-start | bytes 798728 | tf_op jit(solution)/shard_map/ppermute | solution.py:192
  57.3 5.1 %collective-permute-start.6 = (f32[264,128]{1,0:T(8,128)S(1)}, f32[264,128]{1,0:T(8,128)S(1)}, u32[]{:S(2)}, u32[]{:S(2)}) collective-permute-start(f32[264,128]{1,0:T(8,128)S(1)} %pad_maximum_fusion.2), channel_id=1, source_target_pairs={{0,4},{1,5},{2,6},{3,7},{4,0},{5,1},{6,2},{7,3},{8,12},{9,13},{10,... | collective-permute-start | bytes 405512 | tf_op jit(solution)/shard_map/ppermute | solution.py:192
  62.5 5.3 %collective-permute-start.7 = (f32[136,128]{1,0:T(8,128)S(1)}, f32[136,128]{1,0:T(8,128)S(1)}, u32[]{:S(2)}, u32[]{:S(2)}) collective-permute-start(f32[136,128]{1,0:T(8,128)S(1)} %pad_maximum_fusion.3), channel_id=1, source_target_pairs={{0,8},{1,9},{2,10},{3,11},{4,12},{5,13},{6,14},{7,15},{8,0},{9,1},... | collective-permute-start | bytes 208904 | tf_op jit(solution)/shard_map/ppermute | solution.py:192
